TPU v7x, 32 devices: a whole 2x2x4 slice. The times are simulated.
32 devices in a mesh: req: 4 (over y, x), seq: 8 (over z, core).
Axes of the slice: x: 2, y: 2, z: 4, core: 2. Of those that a mesh axis runs over, the one named last changes fastest.
Arguments:
- patches: bfloat16 [32, 4, 1280], P('req'), may hold values from -6 to 6
- key_cache: bfloat16 [32, 1024, 1280], P('req', 'seq'), may hold values from -119 to 119
- value_cache: bfloat16 [32, 1024, 1280], P('req', 'seq'), may hold values from -6 to 6
- cache_len: int32 [32], P('req'), may hold values from 16 to 1024, as said below
- attn_gain: float32 [1280], replicated, may hold values from 0.1 to 1.9
- w_qkv: bfloat16 [1280, 3840], replicated, may hold values from -0.15625 to 0.15625
- w_out: bfloat16 [1280, 1280], replicated, may hold values from -0.15625 to 0.15625
- ffn_gain: float32 [1280], replicated, may hold values from 0.1 to 1.9
- w_up: bfloat16 [1280, 1280], replicated, may hold values from -0.15625 to 0.15625
- w_down: bfloat16 [1280, 1280], replicated, may hold values from -0.15625 to 0.15625
Outputs:
- decoded: bfloat16 [32, 4, 1280], P('req')
Inputs may be any that keep to these rules, and one draw needn't show every extreme that they name: `cache_len`: half of the requests hold between 16 and 64 cached patches, the other half between 768 and 1024.
All inputs are finite; a program needn't handle non-finite values.
Results may differ from a plain program's by a relative error of at most 0.012.
The roundings to bfloat16 on the way count: a program that leaves them out, or rounds other values in their place, can miss the bound.
Values may be sent and summed in bfloat16 or wider, within the bound.
No kernel may reach another device: no remote copies, remote signals or barrier semaphores. Data moves between devices by JAX's collectives and lax.ppermute only.
A program may use at most 128 MiB of HBM per device.

v0:
```python
import jax
import jax.numpy as jnp
from jax import lax
from jax.sharding import PartitionSpec as P

HEADS = 16
HD = 80


epsilon = 1e-06
negative_fill = -1e30


def rms_norm(values, gain):
    return values * lax.rsqrt(jnp.mean(values * values, axis=-1, keepdims=True) + epsilon) * gain


def project(token_rows, weight):
    return jnp.dot(token_rows, weight, preferred_element_type=jnp.float32).astype(jnp.bfloat16)


def scale_rows(value_sum, rescale):
    groups, count_tok, model_width = value_sum.shape
    split_heads = value_sum.reshape(groups, count_tok, HEADS, HD) * rescale[..., None]
    return split_heads.reshape(groups, count_tok, model_width)


def gather_partials(partial_set):
    peak_score, weight_sum, value_sum = partial_set
    global_peak = lax.pmax(peak_score, "seq")
    rescale = jnp.exp(peak_score - global_peak)
    weight_total, value_total = (
        lax.psum((weight_sum * rescale).astype(jnp.bfloat16), "seq").astype(jnp.float32),
        lax.psum(scale_rows(value_sum, rescale).astype(jnp.bfloat16), "seq").astype(jnp.float32),
    )
    return (global_peak, weight_total, value_total)


def shards(
    patches, key_cache, value_cache, cache_len, attn_gain, w_qkv, w_out, ffn_gain, w_up, w_down
):
    groups, count_new, model_width = patches.shape
    slots_here = key_cache.shape[1]
    inputs = patches.reshape(groups * count_new, model_width).astype(jnp.float32)
    normed = rms_norm(inputs, attn_gain).astype(jnp.bfloat16)
    projected = project(normed, w_qkv).reshape(groups, count_new, 3, HEADS, HD)
    queries = projected[:, :, 0]
    keys_new = projected[:, :, 1]
    values_new = projected[:, :, 2]
    cache_keys = key_cache.reshape(groups, slots_here, HEADS, HD)
    cache_values = value_cache.reshape(groups, slots_here, HEADS, HD)
    scale_factor = HD ** (-0.5)
    position = lax.axis_index("seq") * slots_here + jnp.arange(slots_here, dtype=jnp.int32)
    live_mask = (position[None, :] < cache_len[:, None])[:, None, None, :]
    cache_scores = (
        jnp.einsum("rthd,rshd->rths", queries, cache_keys, preferred_element_type=jnp.float32)
        * scale_factor
    )
    masked = jnp.where(live_mask, cache_scores, negative_fill)
    peak_score = jnp.max(masked, axis=3)
    weights = jnp.where(live_mask, jnp.exp(masked - peak_score[..., None]), 0.0)
    weight_sum = jnp.sum(weights, axis=3)
    value_sum = jnp.einsum(
        "rths,rshd->rthd",
        weights.astype(jnp.bfloat16),
        cache_values,
        preferred_element_type=jnp.float32,
    )
    peak_score, weight_sum, value_sum = gather_partials(
        (peak_score, weight_sum, value_sum.reshape(groups, cache_scores.shape[1], model_width))
    )
    new_scores = (
        jnp.einsum("rthd,ruhd->rthu", queries, keys_new, preferred_element_type=jnp.float32)
        * scale_factor
    )
    causal = (jnp.arange(count_new)[:, None] >= jnp.arange(count_new)[None, :])[None, :, None, :]
    new_masked = jnp.where(causal, new_scores, negative_fill)
    global_peak = jnp.maximum(peak_score, jnp.max(new_masked, axis=3))
    carry_scale = jnp.exp(peak_score - global_peak)
    new_weights = jnp.where(causal, jnp.exp(new_masked - global_peak[..., None]), 0.0)
    denominator = weight_sum * carry_scale + jnp.sum(new_weights, axis=3)
    new_values = jnp.einsum(
        "rthu,ruhd->rthd",
        new_weights.astype(jnp.bfloat16),
        values_new,
        preferred_element_type=jnp.float32,
    )
    numerator = scale_rows(value_sum, carry_scale) + new_values.reshape(
        groups, count_new, model_width
    )
    attended = scale_rows(numerator, 1.0 / denominator).astype(jnp.bfloat16)
    out_rows = project(attended.reshape(groups * count_new, model_width), w_out)
    mixed_rows = inputs + out_rows.astype(jnp.float32)
    normed_mixed = rms_norm(mixed_rows, ffn_gain).astype(jnp.bfloat16)
    up_rows = project(normed_mixed, w_up)
    hidden = jax.nn.silu(up_rows.astype(jnp.float32)).astype(jnp.bfloat16)
    down_rows = project(hidden, w_down)
    decoded = (mixed_rows + down_rows.astype(jnp.float32)).astype(jnp.bfloat16)
    return decoded.reshape(groups, count_new, model_width)


def solution(mesh):
    placed = (
        P("req", None, None),
        P("req", "seq", None),
        P("req", "seq", None),
        P("req"),
        P(),
        P(),
        P(),
        P(),
        P(),
        P(),
    )
    return jax.shard_map(
        shards, mesh=mesh, in_specs=placed, out_specs=P("req", None, None), check_vma=False
    )
```

profile of v0, /device:TPU:1, one launch (start us, length us, event | category | flops | bytes accessed | tf_op | source)
XLA Modules:
  0.0 143.7 jit_solution(14735307493136979209)
XLA Ops:
  8.7 6.4 %convolution_convert_fusion = bf16[32,3840]{1,0:T(8,128)(2,1)} fusion(bf16[1280,3840]{1,0:T(8,128)(2,1)} %param.15, f32[32,1280]{1,0:T(8,128)S(1)} %reshape.106, f32[1280]{0:T(1024)} %param.14, f32[32]{0:T(128)S(1)} %rsqrt.20), kind=kOutput, calls=%fused_computation | convolution fusion | flops 314818560 | bytes 10245248 | tf_op jit(solution)/shard_map/dot_general | solution.py:19
  15.1 2.3 %reshape.100 = bf16[8,4,3,16,80]{4,3,2,1,0:T(8,128)(2,1)} reshape(bf16[32,3840]{1,0:T(8,128)(2,1)} %convolution_convert_fusion) | data formatting | bytes 491520 | tf_op jit(solution)/shard_map/reshape | solution.py:46
  17.4 1.7 %fusion.29 = (bf16[8,4,1,16,80]{4,3,2,1,0:T(8,128)(2,1)}, bf16[8,4,1,16,80]{4,3,2,1,0:T(8,128)(2,1)S(1)}, bf16[8,4,1,16,80]{4,3,2,1,0:T(8,128)(2,1)S(1)}) fusion(bf16[8,4,3,16,80]{4,3,2,1,0:T(8,128)(2,1)} %reshape.100), kind=kLoop, calls=%fused_computation.54 | loop fusion | bytes 491520 | tf_op jit(solution)/shard_map/slice | solution.py:49
  20.8 1.2 copy.60
  22.0 4.4 %copy.53 = bf16[8,128,1280]{1,2,0:T(8,128)(2,1)} copy(bf16[8,128,1280]{2,1,0:T(8,128)(2,1)} %param.11) | data formatting | bytes 5242880 | tf_op args[1]
  26.5 3.9 %fusion.30 = (f32[8,4,16]{1,2,0:T(8,128)}, f32[8,4,16,128]{3,1,2,0:T(4,128)}) fusion(bf16[8,128,16,80]{1,3,2,0:T(8,128)(2,1)} %bitcast.58, bf16[8,4,1,16,80]{4,3,2,1,0:T(8,128)(2,1)} %copy-done.1, pred[8,128]{1,0:T(8,128)(4,1)S(1)} %broadcast_compare_fusion), kind=kOutput, calls=%fused_computation.55 | convolution fusion | flops 10681856 | bytes 2968576 | tf_op jit(solution)/shard_map/rthd,rshd->rths/dot_general | solution.py:56
  31.4 26.2 %pmax.7 = f32[8,4,16]{2,0,1:T(8,128)S(1)} all-reduce(f32[8,4,16]{2,0,1:T(8,128)S(1)} %copy.56), channel_id=1, replica_groups=mesh['req'=4,'seq'=8] {'seq'}, use_global_device_ids=true, to_apply=%region_2.3 | all-reduce | flops 512 | bytes 4096 | tf_op jit(solution)/shard_map/pmax | solution.py:30
  57.6 2.0 %fusion.10 = f32[8,4,16]{1,2,0:T(8,128)} fusion(f32[8,4,16,128]{3,1,2,0:T(4,128)} %get-tuple-element.16, f32[8,4,16]{1,2,0:T(8,128)} %get-tuple-element.15, pred[8,128]{1,0:T(8,128)(4,1)S(1)} %broadcast_compare_fusion), kind=kLoop, calls=%fused_computation.18 | loop fusion | flops 196096 | bytes 267264 | tf_op jit(solution)/shard_map/reduce_sum | solution.py:62
  59.5 1.6 %copy.64 = f32[8,4,16]{2,0,1:T(8,128)} copy(f32[8,4,16]{1,2,0:T(8,128)} %fusion.10) | data formatting | bytes 4096 | tf_op jit(solution)/shard_map/reduce_sum | solution.py:62
  61.2 1.3 multiply_convert_fusion.7
  62.5 1.5 %copy.57 = f32[8,4,16]{1,2,0:T(8,128)} copy(f32[8,4,16]{2,0,1:T(8,128)} %get-tuple-element.8) | data formatting | bytes 4096 | tf_op jit(solution)/shard_map/exp | solution.py:31
  64.0 4.4 %copy.54 = bf16[8,128,1280]{1,2,0:T(8,128)(2,1)} copy(bf16[8,128,1280]{2,1,0:T(8,128)(2,1)} %param.12) | data formatting | bytes 5242880 | tf_op args[2]
  68.4 3.4 %fusion.9 = bf16[8,4,16,80]{3,1,2,0:T(4,128)(2,1)S(1)} fusion(bf16[8,128,16,80]{1,3,2,0:T(8,128)(2,1)} %bitcast.59, f32[8,4,16,128]{3,1,2,0:T(4,128)} %get-tuple-element.16, f32[8,4,16]{1,2,0:T(8,128)} %copy.57, f32[8,4,16]{1,2,0:T(8,128)} %get-tuple-element.15, pred[8,128]{1,0:T(8,128)(4,1)S(1)} %copy-done.3), kind=kOutput, calls=%fused_computation.16 | convolution fusion | flops 10764288 | bytes 2970624 | tf_op jit(solution)/shard_map/rths,rshd->rthd/dot_general | solution.py:63
  72.4 1.7 %convert_element_type.73 = bf16[8,4,1280]{2,0,1:T(8,128)(2,1)} reshape(bf16[8,4,16,80]{3,2,0,1:T(8,128)(2,1)} %copy.58) | data formatting | bytes 163840 | tf_op jit(solution)/shard_map/convert_element_type | solution.py:34
  74.2 1.3 fusion.26
  75.5 17.4 %psum.15 = bf16[8,4,16]{2,0,1:T(8,128)(2,1)S(1)} all-reduce(bf16[8,4,16]{2,0,1:T(8,128)(2,1)} %get-tuple-element.7), channel_id=1, replica_groups=mesh['req'=4,'seq'=8] {'seq'}, use_global_device_ids=true, to_apply=%region_6.7 | all-reduce | flops 512 | bytes 2048 | tf_op jit(solution)/shard_map/psum | solution.py:33
  92.9 1.7 %copy.62 = bf16[8,4,16,4]{3,1,2,0:T(4,128)(2,1)} copy(bf16[8,4,16,4]{2,0,3,1:T(8,128)(2,1)} %get-tuple-element.12) | data formatting | bytes 8192 | tf_op jit(solution)/shard_map/convert_element_type | solution.py:84
  94.5 1.2 convolution_bitcast_fusion.1
  96.5 1.8 %reshape.103 = f32[8,4,1280]{2,0,1:T(8,128)} reshape(f32[8,4,16,80]{3,2,0,1:T(8,128)} %copy.63) | data formatting | bytes 327680 | tf_op jit(solution)/shard_map/reshape | solution.py:88
  99.1 1.7 %mul.117 = f32[8,4,1280]{2,0,1:T(8,128)} reshape(f32[8,4,16,80]{3,2,0,1:T(8,128)} %mul.116) | data formatting | bytes 327680 | tf_op jit(solution)/shard_map/mul | solution.py:24
  101.7 1.7 %mul.112 = f32[8,4,1280]{2,0,1:T(8,128)} reshape(f32[8,4,16,80]{3,2,0,1:T(8,128)} %mul.111) | data formatting | bytes 327680 | tf_op jit(solution)/shard_map/mul | solution.py:24
  103.4 24.3 %all-reduce.2.cloned.1.call-done = bf16[8,4,1280]{2,0,1:T(8,128)(2,1)} async-done(((bf16[8,4,1280]{2,0,1:T(8,128)(2,1)}), bf16[8,4,1280]{2,0,1:T(8,128)(2,1)}) %all-reduce.2.cloned.1.call-update) | async-done | bytes 81936 | tf_op jit(solution)/shard_map/psum | solution.py:34
  129.6 2.3 %multiply_reduce_fusion = (f32[32]{0:T(128)S(1)}, f32[32,1280]{1,0:T(8,128)}) fusion(f32[32,1280]{1,0:T(8,128)S(1)} %reshape.106, bf16[32,1280]{1,0:T(8,128)(2,1)} %reshape.104, bf16[1280,1280]{1,0:T(8,128)(2,1)S(1)} %copy-done), kind=kOutput, calls=%fused_computation.22 | convolution fusion | flops 105062368 | bytes 3686528 | tf_op jit(solution)/shard_map/dot_general | solution.py:19
  131.9 4.3 %fusion.2 = bf16[32,1280]{1,0:T(8,128)(2,1)S(1)} fusion(f32[32,1280]{1,0:T(8,128)} %get-tuple-element.18, bf16[1280,1280]{1,0:T(8,128)(2,1)} %param.19, bf16[1280,1280]{1,0:T(8,128)(2,1)} %param.18, f32[1280]{0:T(1024)S(1)} %copy-done.4, f32[32]{0:T(128)S(1)} %add_rsqrt_fusion.1), kind=kOutput, calls=%fused_computation.4 | convolution fusion | flops 210288640 | bytes 6804608 | tf_op jit(solution)/shard_map/dot_general | solution.py:19
  (36 shorter events, 10.5 us)
Async XLA Ops:
  6.5 123.0 %copy-start = (bf16[1280,1280]{1,0:T(8,128)(2,1)S(1)}, bf16[1280,1280]{1,0:T(8,128)(2,1)}, u32[]{:S(2)}) copy-start(bf16[1280,1280]{1,0:T(8,128)(2,1)} %param.16) | copy-start | bytes 9830404
  6.5 121.2 %all-reduce.2.cloned.1.call-start = ((), (), s32[]{:S(2)}) async-start(), calls=%async_computation | async-start | bytes 163840 | tf_op jit(solution)/shard_map/psum | solution.py:34
  6.5 54.6 %copy-start.5 = (pred[4,4]{1,0:T(4,128)(4,1)}, pred[4,4]{1,0:T(4,128)(4,1)S(1)}, u32[]{:S(2)}) copy-start(pred[4,4]{1,0:T(4,128)(4,1)S(1)} %iota_compare_fusion) | copy-start | bytes 52
  19.1 0.7 copy-start.1
  19.1 7.3 %copy-start.6 = (s32[8]{0:T(128)S(1)}, s32[8]{0:T(128)}, u32[]{:S(2)}) copy-start(s32[8]{0:T(128)} %param.13) | copy-start | bytes 100
  26.5 34.6 %copy-start.2 = (pred[8,128]{1,0:T(8,128)(4,1)}, pred[8,128]{1,0:T(8,128)(4,1)S(1)}, u32[]{:S(2)}) copy-start(pred[8,128]{1,0:T(8,128)(4,1)S(1)} %broadcast_compare_fusion) | copy-start | bytes 3076
  62.5 5.8 %copy-start.3 = (pred[8,128]{1,0:T(8,128)(4,1)S(1)}, pred[8,128]{1,0:T(8,128)(4,1)}, u32[]{:S(2)}) copy-start(pred[8,128]{1,0:T(8,128)(4,1)} %copy-done.2) | copy-start | bytes 3076
  96.5 35.4 %copy-start.4 = (f32[1280]{0:T(1024)S(1)}, f32[1280]{0:T(1024)}, u32[]{:S(2)}) copy-start(f32[1280]{0:T(1024)} %param.17) | copy-start | bytes 15364
Sparse Core Ops, SparseCore 0:
  74.3 53.3 all-reduce.1
where the time goes:
time: 146 us; the launch traced here: 144 us
  blocking collectives  43.6 us (30%)
  local copies, waits for them, and re-layouts  32.7 us (22%)
  waiting for transfers between devices  24.3 us (17%)
  matrix products  22.6 us (15%)
  between operations  13.5 us (9%)
  other arithmetic  7.13 us (5%)
    pmax x1, blocking collectives, gather_partials(): global_peak = lax.pmax(peak_score, 'seq')  26.2 us
    psum x1, waiting for transfers between devices, gather_partials(): lax.psum(scale_rows(value_sum, rescale).astype(jnp.bfloat16), 'seq')  24.3 us
    psum x1, blocking collectives, gather_partials(): lax.psum((weight_sum * rescale).astype(jnp.bfloat16), 'seq')  17.4 us
    dot_general x3, matrix products, project(): jnp.dot(token_rows, weight, preferred_element_type=jnp.float32)  13 us
    unnamed x16, local copies, waits for them, and re-layouts  9.44 us
    mul x4, local copies, waits for them, and re-layouts, scale_rows(): value_sum.reshape(groups, count_tok, HEADS, HD) * rescale[..., None]  5.13 us
    dot_general x1, matrix products, shards(): jnp.einsum('rthd,rshd->rths', queries, cache_keys, preferred_element_type...  3.94 us
    dot_general x1, matrix products, shards(): jnp.einsum('rths,rshd->rthd', weights.astype(jnp.bfloat16), cache_values,...  3.38 us
  transfers between devices with their start and end apart: 1, of which 1 were waited for; matrix products, arithmetic and copies ran while one was open for 8% of the time, Pallas kernels for 0%

commit v1 on v0

v1 whole, which is shorter than its diff:
```python
import jax
import jax.numpy as jnp
from jax import lax
from jax.sharding import PartitionSpec as P

HEADS = 16
HD = 80


epsilon = 1e-06
negative_fill = -1e30


def rms_norm(values, gain):
    return values * lax.rsqrt(jnp.mean(values * values, axis=-1, keepdims=True) + epsilon) * gain


def project(token_rows, weight):
    return jnp.dot(token_rows, weight, preferred_element_type=jnp.float32).astype(jnp.bfloat16)


def head_mask(heads, width):
    return (jnp.arange(width)[None, :] // HD) == jnp.arange(heads)[:, None]


def per_head_queries(queries, mask):
    groups, count, width = queries.shape
    heads = mask.shape[0]
    blocks = jnp.where(mask[None, None], queries[:, :, None, :], jnp.zeros((), queries.dtype))
    return blocks.reshape(groups, count * heads, width)


def head_diagonal(rows, mask):
    groups, count_heads, width = rows.shape
    heads = mask.shape[0]
    rows = rows.reshape(groups, count_heads // heads, heads, width)
    return jnp.sum(jnp.where(mask[None, None], rows, 0.0), axis=2)


def spread(per_head, width):
    return jnp.repeat(per_head, width // per_head.shape[-1], axis=-1)


def merge(first, second, heads):
    cols = first.shape[-1] - 2 * heads
    v1, m1, l1 = first[..., :cols], first[..., cols:cols + heads], first[..., cols + heads:]
    v2, m2, l2 = second[..., :cols], second[..., cols:cols + heads], second[..., cols + heads:]
    m = jnp.maximum(m1, m2)
    a1 = jnp.exp(m1 - m)
    a2 = jnp.exp(m2 - m)
    l = l1 * a1 + l2 * a2
    v = v1 * spread(a1, cols) + v2 * spread(a2, cols)
    return jnp.concatenate([v, m, l], axis=-1)


def exchange(part, distance, count):
    pairs = [(i, i ^ distance) for i in range(count)]
    return lax.ppermute(part, "seq", pairs)


def combine_over_seq(values, peak, weight_sum, count):
    groups, count_new, width = values.shape
    heads = peak.shape[-1]
    half_cols, half_heads = width // 2, heads // 2
    me = lax.axis_index("seq")
    core = me % 2

    def half(which):
        v = lax.dynamic_slice_in_dim(values, which * half_cols, half_cols, axis=2)
        m = lax.dynamic_slice_in_dim(peak, which * half_heads, half_heads, axis=2)
        l = lax.dynamic_slice_in_dim(weight_sum, which * half_heads, half_heads, axis=2)
        return jnp.concatenate([v, m, l], axis=-1)

    kept = half(core)
    sent = half(1 - core)
    got = exchange(sent, 1, count)
    low_first = core == 0
    state = merge(jnp.where(low_first, kept, got), jnp.where(low_first, got, kept), half_heads)
    distance = 2
    while distance < count:
        got = exchange(state, distance, count)
        low_first = (me & distance) == 0
        state = merge(
            jnp.where(low_first, state, got), jnp.where(low_first, got, state), half_heads
        )
        distance *= 2
    other = exchange(state, 1, count)
    low_half = jnp.where(core == 0, state, other)
    high_half = jnp.where(core == 0, other, state)
    v = jnp.concatenate([low_half[..., :half_cols], high_half[..., :half_cols]], axis=-1)
    m = jnp.concatenate(
        [low_half[..., half_cols:half_cols + half_heads], high_half[..., half_cols:half_cols + half_heads]],
        axis=-1,
    )
    l = jnp.concatenate(
        [low_half[..., half_cols + half_heads:], high_half[..., half_cols + half_heads:]], axis=-1
    )
    return v, m, l


def shards(
    patches, key_cache, value_cache, cache_len, attn_gain, w_qkv, w_out, ffn_gain, w_up, w_down
):
    groups, count_new, model_width = patches.shape
    slots_here = key_cache.shape[1]
    seq_count = lax.axis_size("seq")
    inputs = patches.reshape(groups * count_new, model_width).astype(jnp.float32)
    normed = rms_norm(inputs, attn_gain).astype(jnp.bfloat16)
    projected = project(normed, w_qkv).reshape(groups, count_new, 3 * model_width)
    queries = projected[:, :, :model_width]
    keys_new = projected[:, :, model_width:2 * model_width]
    values_new = projected[:, :, 2 * model_width:]
    mask = head_mask(HEADS, model_width)
    query_rows = per_head_queries(queries, mask)
    scale_factor = HD ** (-0.5)
    position = lax.axis_index("seq") * slots_here + jnp.arange(slots_here, dtype=jnp.int32)
    live_mask = (position[None, :] < cache_len[:, None])[:, None, :]
    cache_scores = (
        jnp.einsum("rqc,rsc->rqs", query_rows, key_cache, preferred_element_type=jnp.float32)
        * scale_factor
    )
    masked = jnp.where(live_mask, cache_scores, negative_fill)
    peak_score = jnp.max(masked, axis=2)
    weights = jnp.where(live_mask, jnp.exp(masked - peak_score[..., None]), 0.0)
    weight_sum = jnp.sum(weights, axis=2)
    value_rows = jnp.einsum(
        "rqs,rsc->rqc", weights.astype(jnp.bfloat16), value_cache, preferred_element_type=jnp.float32
    )
    value_sum = head_diagonal(value_rows, mask)
    value_sum, peak_score, weight_sum = combine_over_seq(
        value_sum,
        peak_score.reshape(groups, count_new, HEADS),
        weight_sum.reshape(groups, count_new, HEADS),
        seq_count,
    )
    new_scores = (
        jnp.einsum("rqc,ruc->rqu", query_rows, keys_new, preferred_element_type=jnp.float32)
        * scale_factor
    ).reshape(groups, count_new, HEADS, count_new)
    causal = (jnp.arange(count_new)[:, None] >= jnp.arange(count_new)[None, :])[None, :, None, :]
    new_masked = jnp.where(causal, new_scores, negative_fill)
    global_peak = jnp.maximum(peak_score, jnp.max(new_masked, axis=3))
    carry_scale = jnp.exp(peak_score - global_peak)
    new_weights = jnp.where(causal, jnp.exp(new_masked - global_peak[..., None]), 0.0)
    denominator = weight_sum * carry_scale + jnp.sum(new_weights, axis=3)
    new_rows = jnp.einsum(
        "rqu,ruc->rqc",
        new_weights.reshape(groups, count_new * HEADS, count_new).astype(jnp.bfloat16),
        values_new,
        preferred_element_type=jnp.float32,
    )
    new_values = head_diagonal(new_rows, mask)
    numerator = value_sum * spread(carry_scale, model_width) + new_values
    attended = (numerator / spread(denominator, model_width)).astype(jnp.bfloat16)
    out_rows = project(attended.reshape(groups * count_new, model_width), w_out)
    mixed_rows = inputs + out_rows.astype(jnp.float32)
    normed_mixed = rms_norm(mixed_rows, ffn_gain).astype(jnp.bfloat16)
    up_rows = project(normed_mixed, w_up)
    hidden = jax.nn.silu(up_rows.astype(jnp.float32)).astype(jnp.bfloat16)
    down_rows = project(hidden, w_down)
    decoded = (mixed_rows + down_rows.astype(jnp.float32)).astype(jnp.bfloat16)
    return decoded.reshape(groups, count_new, model_width)


def solution(mesh):
    placed = (
        P("req", None, None),
        P("req", "seq", None),
        P("req", "seq", None),
        P("req"),
        P(),
        P(),
        P(),
        P(),
        P(),
        P(),
    )
    return jax.shard_map(
        shards, mesh=mesh, in_specs=placed, out_specs=P("req", None, None), check_vma=False
    )
```

time: 146 us -> 88.6 us (0.61)
  blocking collectives: 43.6 us -> 0 us
  waiting for transfers between devices: 24.3 us -> 7.83 us
  between operations: 13.5 us -> 0.27 us
  other arithmetic: 7.13 us -> 16.5 us
  starting transfers between devices: 0.01 us -> 7.13 us
  matrix products: 22.6 us -> 24.7 us
  local copies, waits for them, and re-layouts: 32.7 us -> 30.9 us
    pmax x1 -> x0, blocking collectives: 26.2 us -> none  [gather_partials(): global_peak = lax.pmax(peak_score, 'seq')]
    psum x1 -> x0, waiting for transfers between devices: 24.3 us -> none  [gather_partials(): lax.psum(scale_rows(value_sum, rescale).astype(jnp.bfloat16), 'seq')]
    psum x1 -> x0, blocking collectives: 17.4 us -> none  [gather_partials(): lax.psum((weight_sum * rescale).astype(jnp.bfloat16), 'seq')]
    ppermute x0 -> x4, waiting for transfers between devices: none -> 7.83 us  [exchange(): return lax.ppermute(part, 'seq', pairs)]
    unnamed x16 -> x32, local copies, waits for them, and re-layouts: 9.44 us -> 2.25 us
    ppermute x0 -> x4, starting transfers between devices: none -> 7.13 us  [exchange(): return lax.ppermute(part, 'seq', pairs)]
    reshape x3 -> x11, local copies, waits for them, and re-layouts: 4.75 us -> 11.9 us  [the longest x8 8.06 us: spread(): return jnp.repeat(per_head, width // per_head.shape[-1], axis=-1)]
    add x0 -> x7, other arithmetic: none -> 5.34 us  [the longest x3 3.05 us: merge(): v = v1 * spread(a1, cols) + v2 * spread(a2, cols)]
  transfers between devices with their start and end apart: 1 -> 4, of which waited for: 1 -> 3; matrix products, arithmetic and copies ran while one was open for 8% -> 4% of each run, Pallas kernels for 0% -> 0%
where the time goes in v1:
time: 88.6 us; the launch traced here: 87.3 us
  local copies, waits for them, and re-layouts  30.9 us (35%)
  matrix products  24.7 us (28%)
  other arithmetic  16.5 us (19%)
  waiting for transfers between devices  7.83 us (9%)
  starting transfers between devices  7.13 us (8%)
    dot_general x3, matrix products, project(): jnp.dot(token_rows, weight, preferred_element_type=jnp.float32)  13.3 us
    reshape x8, local copies, waits for them, and re-layouts, spread(): return jnp.repeat(per_head, width // per_head.shape[-1], axis=-1)  8.06 us
    ppermute x4, waiting for transfers between devices, exchange(): return lax.ppermute(part, 'seq', pairs)  7.83 us
    ppermute x4, starting transfers between devices, exchange(): return lax.ppermute(part, 'seq', pairs)  7.13 us
    dot_general x1, matrix products, shards(): jnp.einsum('rqc,rsc->rqs', query_rows, key_cache, preferred_element_type=...  3.43 us
    dot_general x1, matrix products, shards(): jnp.einsum('rqs,rsc->rqc', weights.astype(jnp.bfloat16), value_cache, pre...  3.28 us
    add x3, other arithmetic, merge(): v = v1 * spread(a1, cols) + v2 * spread(a2, cols)  3.05 us
    concatenate x3, other arithmetic, merge(): return jnp.concatenate([v, m, l], axis=-1)  3 us
  transfers between devices with their start and end apart: 4, of which 3 were waited for; matrix products, arithmetic and copies ran while one was open for 4% of the time, Pallas kernels for 0%

profile of v1, /device:TPU:1, one launch (start us, length us, event | category | flops | bytes accessed | tf_op | source)
XLA Modules:
  0.0 87.3 jit_solution(11886176068476991726)
XLA Ops:
  2.3 6.4 %convolution_convert_fusion = bf16[32,3840]{1,0:T(8,128)(2,1)} fusion(bf16[1280,3840]{1,0:T(8,128)(2,1)} %param.15, f32[32,1280]{1,0:T(8,128)S(1)} %reshape.208, f32[1280]{0:T(1024)} %param.14, f32[32]{0:T(128)S(1)} %rsqrt.20), kind=kOutput, calls=%fused_computation | convolution fusion | flops 314818560 | bytes 10245248 | tf_op jit(solution)/shard_map/dot_general | solution.py:19
  8.7 1.7 %reshape.194 = bf16[8,4,3840]{2,1,0:T(4,128)(2,1)} reshape(bf16[32,3840]{1,0:T(8,128)(2,1)} %convolution_convert_fusion) | data formatting | bytes 491520 | tf_op jit(solution)/shard_map/reshape | solution.py:109
  12.6 3.4 %fusion.53 = (f32[8,64]{1,0:T(8,128)}, f32[8,64,128]{2,1,0:T(8,128)S(1)}) fusion(bf16[8,64,1280]{2,1,0:T(8,128)(2,1)S(1)} %bitcast_select_fusion, bf16[8,128,1280]{2,1,0:T(8,128)(2,1)} %param.11, pred[8,128]{1,0:T(8,128)(4,1)S(1)} %broadcast_compare_fusion), kind=kOutput, calls=%fused_computation.119 | convolution fusion | flops 167968256 | bytes 4197376 | tf_op jit(solution)/shard_map/rqc,rsc->rqs/dot_general | solution.py:119
  16.8 1.5 %fusion.8 = f32[8,64]{1,0:T(8,128)} fusion(f32[8,64,128]{2,1,0:T(8,128)S(1)} %get-tuple-element.40, f32[8,64]{1,0:T(8,128)} %get-tuple-element.39, pred[8,128]{1,0:T(8,128)(4,1)} %copy-done.13), kind=kLoop, calls=%fused_computation.18 | loop fusion | flops 196096 | bytes 267264 | tf_op jit(solution)/shard_map/reduce_sum | solution.py:125
  18.4 1.4 %reshape.197 = f32[8,4,16]{2,1,0:T(4,128)} reshape(f32[8,64]{1,0:T(8,128)} %fusion.8) | data formatting | bytes 4096 | tf_op jit(solution)/shard_map/reshape | solution.py:133
  19.7 3.3 %select_reduce_fusion.1 = f32[8,4,1280]{2,1,0:T(4,128)} fusion(pred[16,1280]{1,0:T(8,128)(4,1)} %copy-done.10, bf16[8,128,1280]{2,1,0:T(8,128)(2,1)} %param.12, f32[8,64,128]{2,1,0:T(8,128)S(1)} %get-tuple-element.40, f32[8,64]{1,0:T(8,128)} %get-tuple-element.39, pred[8,128]{1,0:T(8,128)(4,1)} %copy-done.13), kind=kOutput, calls=%fused_computation.2 | convolution fusion | flops 169238528 | bytes 3070976 | tf_op jit(solution)/shard_map/rqs,rsc->rqc/dot_general | solution.py:126
  24.0 1.5 %constant_dynamic-slice_fusion.3 = (f32[8,4,8]{2,1,0:T(4,128)}, f32[8,4,8]{2,1,0:T(4,128)S(1)}, f32[8,4,8]{2,1,0:T(4,128)S(1)}, f32[8,4,8]{2,1,0:T(4,128)}) fusion(f32[8,4,16]{2,1,0:T(4,128)} %reshape.197, s32[]{:T(128)S(6)} %select_n.116, s32[]{:T(128)S(6)} %select_n.118, f32[8,4,16]{2,1,0:T(4,128)S(1)} %reshape.196), kind=kLoop, calls=%fused_computation.106 | loop fusion | bytes 8200 | tf_op jit(solution)/shard_map/dynamic_slice | solution.py:71
  25.6 1.3 %collective-permute-done = f32[8,4,656]{2,1,0:T(4,128)S(1)} collective-permute-done((f32[8,4,656]{2,1,0:T(4,128)S(1)}, f32[8,4,656]{2,1,0:T(4,128)S(1)}, u32[]{:S(2)}, u32[]{:S(2)}) %collective-permute-start) | collective-permute-done | bytes 84000 | tf_op jit(solution)/shard_map/ppermute | solution.py:58
  31.9 2.5 %collective-permute-start.1 = (f32[8,4,656]{2,1,0:T(4,128)S(1)}, f32[8,4,656]{2,1,0:T(4,128)}, u32[]{:S(2)}, u32[]{:S(2)}) collective-permute-start(f32[8,4,656]{2,1,0:T(4,128)S(1)} %pad_maximum_fusion.2), channel_id=1, source_target_pairs={{0,2},{1,3},{2,0},{3,1},{4,6},{5,7},{6,4},{7,5},{8,10},{9,11},{10,... | collective-permute-start | bytes 251912 | tf_op jit(solution)/shard_map/ppermute | solution.py:58
  34.4 2.9 %collective-permute-done.1 = f32[8,4,656]{2,1,0:T(4,128)} collective-permute-done((f32[8,4,656]{2,1,0:T(4,128)S(1)}, f32[8,4,656]{2,1,0:T(4,128)}, u32[]{:S(2)}, u32[]{:S(2)}) %collective-permute-start.1) | collective-permute-done | bytes 84000 | tf_op jit(solution)/shard_map/ppermute | solution.py:58
  42.4 1.4 %pad_maximum_fusion.3 = f32[8,4,656]{2,1,0:T(4,128)} fusion(f32[8,4,8]{2,1,0:T(4,128)S(1)} %get-tuple-element.11, f32[8,4,8]{2,1,0:T(4,128)} %get-tuple-element.14, f32[8,4,640]{2,1,0:T(4,128)S(1)} %fusion.23), kind=kLoop, calls=%fused_computation.36 | loop fusion | flops 41984 | bytes 167936 | tf_op jit(solution)/shard_map/concatenate | solution.py:53
  43.8 2.2 %collective-permute-start.2 = (f32[8,4,656]{2,1,0:T(4,128)}, f32[8,4,656]{2,1,0:T(4,128)S(1)}, u32[]{:S(2)}, u32[]{:S(2)}) collective-permute-start(f32[8,4,656]{2,1,0:T(4,128)} %pad_maximum_fusion.3), channel_id=1, source_target_pairs={{0,4},{1,5},{2,6},{3,7},{4,0},{5,1},{6,2},{7,3},{8,12},{9,13},{10,... | collective-permute-start | bytes 251912 | tf_op jit(solution)/shard_map/ppermute | solution.py:58
  46.2 3.6 %collective-permute-done.2 = f32[8,4,656]{2,1,0:T(4,128)S(1)} collective-permute-done((f32[8,4,656]{2,1,0:T(4,128)}, f32[8,4,656]{2,1,0:T(4,128)S(1)}, u32[]{:S(2)}, u32[]{:S(2)}) %collective-permute-start.2) | collective-permute-done | bytes 84000 | tf_op jit(solution)/shard_map/ppermute | solution.py:58
  54.1 1.5 %pad_maximum_fusion.4 = f32[8,4,656]{2,1,0:T(4,128)} fusion(f32[8,4,8]{2,1,0:T(4,128)} %get-tuple-element.7, f32[8,4,8]{2,1,0:T(4,128)} %get-tuple-element.10, f32[8,4,640]{2,1,0:T(4,128)S(1)} %fusion.22), kind=kLoop, calls=%fused_computation.37 | loop fusion | flops 41984 | bytes 167936 | tf_op jit(solution)/shard_map/concatenate | solution.py:53
  55.6 2.4 %collective-permute-start.3 = (f32[8,4,656]{2,1,0:T(4,128)}, f32[8,4,656]{2,1,0:T(4,128)}, u32[]{:S(2)}, u32[]{:S(2)}) collective-permute-start(f32[8,4,656]{2,1,0:T(4,128)} %pad_maximum_fusion.4), channel_id=1, source_target_pairs={{0,1},{1,0},{2,3},{3,2},{4,5},{5,4},{6,7},{7,6},{8,9},{9,8},{10,11... | collective-permute-start | bytes 251912 | tf_op jit(solution)/shard_map/ppermute | solution.py:58
  58.0 2.4 %fusion.54 = (f32[8,64]{1,0:T(8,128)S(1)}, f32[8,64,4]{1,2,0:T(4,128)}) fusion(bf16[8,64,1280]{2,1,0:T(8,128)(2,1)} %copy-done.1, bf16[8,4,3840]{2,1,0:T(4,128)(2,1)} %reshape.194, pred[64,4]{0,1:T(4,128)(4,1)S(1)} %broadcast_in_dim.150), kind=kOutput, calls=%fused_computation.120 | convolution fusion | flops 5248512 | bytes 1403136 | tf_op jit(solution)/shard_map/rqc,ruc->rqu/dot_general | solution.py:137
  63.6 1.3 %fusion.37 = f32[8,64]{1,0:T(8,128)} fusion(f32[8,64,4]{1,2,0:T(4,128)} %get-tuple-element.42, f32[8,64]{1,0:T(8,128)S(1)} %max.22, pred[64,4]{0,1:T(4,128)(4,1)S(1)} %broadcast_in_dim.150), kind=kLoop, calls=%fused_computation.92 | loop fusion | flops 5632 | bytes 12544 | tf_op jit(solution)/shard_map/reduce_sum | solution.py:145
  65.0 2.4 %select_reduce_fusion = f32[8,4,1280]{2,1,0:T(4,128)} fusion(pred[16,1280]{1,0:T(8,128)(4,1)S(1)} %copy-done.11, bf16[8,4,3840]{2,1,0:T(4,128)(2,1)} %reshape.194, f32[8,64,4]{1,2,0:T(4,128)} %get-tuple-element.42, f32[8,64]{1,0:T(8,128)S(1)} %max.22, pred[64,4]{0,1:T(4,128)(4,1)S(1)} %broadcast_in_dim.150), kind=kOutput, calls=%fused_computation.1 | convolution fusion | flops 6518784 | bytes 284928 | tf_op jit(solution)/shard_map/rqu,ruc->rqc/dot_general | solution.py:146
  68.2 1.5 %slice.127 = f32[8,4,640]{2,1,0:T(4,128)} slice(f32[8,4,656]{2,1,0:T(4,128)} %copy-done.4), slice={[0:8], [0:4], [0:640]} | slice | bytes 163840 | tf_op jit(solution)/shard_map/slice | solution.py:90
  72.2 1.7 %reshape.206 = f32[32,1280]{1,0:T(8,128)} reshape(f32[8,4,16,80]{3,2,1,0:T(8,128)} %broadcast_in_dim.155) | data formatting | bytes 327680 | tf_op jit(solution)/shard_map/reshape | solution.py:41
  74.0 1.6 %reduce_sum.62 = f32[32,1280]{1,0:T(8,128)} reshape(f32[8,4,1280]{2,1,0:T(4,128)} %select_reduce_fusion) | data formatting | bytes 327680 | tf_op jit(solution)/shard_map/reduce_sum | solution.py:37
  76.4 1.8 %reshape.204 = f32[32,1280]{1,0:T(8,128)} reshape(f32[8,4,16,80]{3,2,1,0:T(8,128)} %broadcast_in_dim.153) | data formatting | bytes 327680 | tf_op jit(solution)/shard_map/reshape | solution.py:41
  79.8 2.6 %multiply_reduce_fusion = (f32[32]{0:T(128)S(1)}, f32[32,1280]{1,0:T(8,128)}) fusion(f32[32,1280]{1,0:T(8,128)S(1)} %copy-done.3, bf16[1280,1280]{1,0:T(8,128)(2,1)S(1)} %copy-done, f32[32,1280]{1,0:T(8,128)} %reshape.206, f32[32,1280]{1,0:T(8,128)} %reduce_sum.62, f32[32,1280]{1,0:T(8,128)} %reshape.204, f32[32,640]{1,0:T(8,128)} %concatenate.46, ...), kind=kOutput, calls=%fused_computation.25 | convolution fusion | flops 105267168 | bytes 4259968 | tf_op jit(solution)/shard_map/dot_general | solution.py:19
  82.4 4.3 %fusion.2 = bf16[32,1280]{1,0:T(8,128)(2,1)S(1)} fusion(f32[32,1280]{1,0:T(8,128)} %get-tuple-element.44, bf16[1280,1280]{1,0:T(8,128)(2,1)} %param.19, bf16[1280,1280]{1,0:T(8,128)(2,1)} %param.18, f32[1280]{0:T(1024)S(1)} %copy-done.14, f32[32]{0:T(128)S(1)} %add_rsqrt_fusion.1), kind=kOutput, calls=%fused_computation.6 | convolution fusion | flops 210288640 | bytes 6804608 | tf_op jit(solution)/shard_map/dot_general | solution.py:19
  (89 shorter events, 30.4 us)
Async XLA Ops:
  0.0 79.8 %copy-start = (bf16[1280,1280]{1,0:T(8,128)(2,1)S(1)}, bf16[1280,1280]{1,0:T(8,128)(2,1)}, u32[]{:S(2)}) copy-start(bf16[1280,1280]{1,0:T(8,128)(2,1)} %param.16) | copy-start | bytes 9830404
  1.1 7.6 %copy-start.2 = (f32[32,1280]{1,0:T(8,128)}, f32[32,1280]{1,0:T(8,128)S(1)}, u32[]{:S(2)}) copy-start(f32[32,1280]{1,0:T(8,128)S(1)} %reshape.208) | copy-start | bytes 491524
  2.2 9.1 %copy-start.10 = (pred[16,1280]{1,0:T(8,128)(4,1)}, pred[16,1280]{1,0:T(8,128)(4,1)S(1)}, u32[]{:S(2)}) copy-start(pred[16,1280]{1,0:T(8,128)(4,1)S(1)} %iota_compare_fusion) | copy-start | bytes 61444
  2.3 9.2 %copy-start.15 = (s32[8]{0:T(128)S(1)}, s32[8]{0:T(128)}, u32[]{:S(2)}) copy-start(s32[8]{0:T(128)} %param.13) | copy-start | bytes 100
  11.5 1.1 %copy-start.1 = (bf16[8,64,1280]{2,1,0:T(8,128)(2,1)}, bf16[8,64,1280]{2,1,0:T(8,128)(2,1)S(1)}, u32[]{:S(2)}) copy-start(bf16[8,64,1280]{2,1,0:T(8,128)(2,1)S(1)} %bitcast_select_fusion) | copy-start | bytes 3932164
  12.6 3.4 %copy-start.13 = (pred[8,128]{1,0:T(8,128)(4,1)}, pred[8,128]{1,0:T(8,128)(4,1)S(1)}, u32[]{:S(2)}) copy-start(pred[8,128]{1,0:T(8,128)(4,1)S(1)} %broadcast_compare_fusion) | copy-start | bytes 3076
  25.5 1.3 %collective-permute-start = (f32[8,4,656]{2,1,0:T(4,128)S(1)}, f32[8,4,656]{2,1,0:T(4,128)S(1)}, u32[]{:S(2)}, u32[]{:S(2)}) collective-permute-start(f32[8,4,656]{2,1,0:T(4,128)S(1)} %pad_maximum_fusion.1), channel_id=1, source_target_pairs={{0,1},{1,0},{2,3},{3,2},{4,5},{5,4},{6,7},{7,6},{8,9},{9,8},{10,11... | collective-permute-start | bytes 251912 | tf_op jit(solution)/shard_map/ppermute | solution.py:58
  26.9 0.6 copy-start.12
  28.5 0.6 copy-start.9
  31.9 5.4 %collective-permute-start.1 = (f32[8,4,656]{2,1,0:T(4,128)S(1)}, f32[8,4,656]{2,1,0:T(4,128)}, u32[]{:S(2)}, u32[]{:S(2)}) collective-permute-start(f32[8,4,656]{2,1,0:T(4,128)S(1)} %pad_maximum_fusion.2), channel_id=1, source_target_pairs={{0,2},{1,3},{2,0},{3,1},{4,6},{5,7},{6,4},{7,5},{8,10},{9,11},{10,... | collective-permute-start | bytes 251912 | tf_op jit(solution)/shard_map/ppermute | solution.py:58
  38.3 0.7 copy-start.6
  39.1 25.9 %copy-start.11 = (pred[16,1280]{1,0:T(8,128)(4,1)S(1)}, pred[16,1280]{1,0:T(8,128)(4,1)}, u32[]{:S(2)}) copy-start(pred[16,1280]{1,0:T(8,128)(4,1)} %copy-done.10) | copy-start | bytes 61444
  43.8 6.0 %collective-permute-start.2 = (f32[8,4,656]{2,1,0:T(4,128)}, f32[8,4,656]{2,1,0:T(4,128)S(1)}, u32[]{:S(2)}, u32[]{:S(2)}) collective-permute-start(f32[8,4,656]{2,1,0:T(4,128)} %pad_maximum_fusion.3), channel_id=1, source_target_pairs={{0,4},{1,5},{2,6},{3,7},{4,0},{5,1},{6,2},{7,3},{8,12},{9,13},{10,... | collective-permute-start | bytes 251912 | tf_op jit(solution)/shard_map/ppermute | solution.py:58
  50.6 0.7 copy-start.7
  50.6 0.7 copy-start.8
  54.1 25.7 %copy-start.3 = (f32[32,1280]{1,0:T(8,128)S(1)}, f32[32,1280]{1,0:T(8,128)}, u32[]{:S(2)}) copy-start(f32[32,1280]{1,0:T(8,128)} %copy-done.2) | copy-start | bytes 491524
  55.6 5.5 %collective-permute-start.3 = (f32[8,4,656]{2,1,0:T(4,128)}, f32[8,4,656]{2,1,0:T(4,128)}, u32[]{:S(2)}, u32[]{:S(2)}) collective-permute-start(f32[8,4,656]{2,1,0:T(4,128)} %pad_maximum_fusion.4), channel_id=1, source_target_pairs={{0,1},{1,0},{2,3},{3,2},{4,5},{5,4},{6,7},{7,6},{8,9},{9,8},{10,11... | collective-permute-start | bytes 251912 | tf_op jit(solution)/shard_map/ppermute | solution.py:58
  62.1 0.7 copy-start.4
  62.1 1.4 %copy-start.5 = (f32[8,4,656]{2,1,0:T(4,128)}, f32[8,4,656]{2,1,0:T(4,128)S(1)}, u32[]{:S(2)}) copy-start(f32[8,4,656]{2,1,0:T(4,128)S(1)} %get-tuple-element.22) | copy-start | bytes 251908
  75.6 6.8 %copy-start.14 = (f32[1280]{0:T(1024)S(1)}, f32[1280]{0:T(1024)}, u32[]{:S(2)}) copy-start(f32[1280]{0:T(1024)} %param.17) | copy-start | bytes 15364

commit v2 on v1

--- a/solution.py
+++ b/solution.py
@@ -37,20 +37,23 @@
     return jnp.sum(jnp.where(mask[None, None], rows, 0.0), axis=2)
 
 
-def spread(per_head, width):
-    return jnp.repeat(per_head, width // per_head.shape[-1], axis=-1)
+LANES = 128
 
 
-def merge(first, second, heads):
-    cols = first.shape[-1] - 2 * heads
-    v1, m1, l1 = first[..., :cols], first[..., cols:cols + heads], first[..., cols + heads:]
-    v2, m2, l2 = second[..., :cols], second[..., cols:cols + heads], second[..., cols + heads:]
+def pack(values, peak, weight_sum):
+    pad = jnp.zeros(values.shape[:-1] + (LANES - HD - 2,), jnp.float32)
+    return jnp.concatenate([values, peak[..., None], weight_sum[..., None], pad], axis=-1)
+
+
+def merge(first, second):
+    m1 = first[..., HD:HD + 1]
+    m2 = second[..., HD:HD + 1]
     m = jnp.maximum(m1, m2)
     a1 = jnp.exp(m1 - m)
     a2 = jnp.exp(m2 - m)
-    l = l1 * a1 + l2 * a2
-    v = v1 * spread(a1, cols) + v2 * spread(a2, cols)
-    return jnp.concatenate([v, m, l], axis=-1)
+    merged = first * a1 + second * a2
+    lane = lax.broadcasted_iota(jnp.int32, merged.shape, merged.ndim - 1)
+    return jnp.where(lane == HD, m, merged)
 
 
 def exchange(part, distance, count):
@@ -58,44 +61,26 @@
     return lax.ppermute(part, "seq", pairs)
 
 
-def combine_over_seq(values, peak, weight_sum, count):
-    groups, count_new, width = values.shape
-    heads = peak.shape[-1]
-    half_cols, half_heads = width // 2, heads // 2
+def combine_over_seq(packed, count):
+    heads = packed.shape[1]
+    half_heads = heads // 2
     me = lax.axis_index("seq")
     core = me % 2
-
-    def half(which):
-        v = lax.dynamic_slice_in_dim(values, which * half_cols, half_cols, axis=2)
-        m = lax.dynamic_slice_in_dim(peak, which * half_heads, half_heads, axis=2)
-        l = lax.dynamic_slice_in_dim(weight_sum, which * half_heads, half_heads, axis=2)
-        return jnp.concatenate([v, m, l], axis=-1)
-
-    kept = half(core)
-    sent = half(1 - core)
+    kept = lax.dynamic_slice_in_dim(packed, core * half_heads, half_heads, axis=1)
+    sent = lax.dynamic_slice_in_dim(packed, (1 - core) * half_heads, half_heads, axis=1)
     got = exchange(sent, 1, count)
     low_first = core == 0
-    state = merge(jnp.where(low_first, kept, got), jnp.where(low_first, got, kept), half_heads)
+    state = merge(jnp.where(low_first, kept, got), jnp.where(low_first, got, kept))
     distance = 2
     while distance < count:
         got = exchange(state, distance, count)
-        low_first = (me & distance) == 0
-        state = merge(
-            jnp.where(low_first, state, got), jnp.where(low_first, got, state), half_heads
-        )
+        low_first = (me // distance) % 2 == 0
+        state = merge(jnp.where(low_first, state, got), jnp.where(low_first, got, state))
         distance *= 2
     other = exchange(state, 1, count)
     low_half = jnp.where(core == 0, state, other)
     high_half = jnp.where(core == 0, other, state)
-    v = jnp.concatenate([low_half[..., :half_cols], high_half[..., :half_cols]], axis=-1)
-    m = jnp.concatenate(
-        [low_half[..., half_cols:half_cols + half_heads], high_half[..., half_cols:half_cols + half_heads]],
-        axis=-1,
-    )
-    l = jnp.concatenate(
-        [low_half[..., half_cols + half_heads:], high_half[..., half_cols + half_heads:]], axis=-1
-    )
-    return v, m, l
+    return jnp.concatenate([low_half, high_half], axis=1)
 
 
 def shards(
@@ -127,31 +112,37 @@
         "rqs,rsc->rqc", weights.astype(jnp.bfloat16), value_cache, preferred_element_type=jnp.float32
     )
     value_sum = head_diagonal(value_rows, mask)
-    value_sum, peak_score, weight_sum = combine_over_seq(
-        value_sum,
-        peak_score.reshape(groups, count_new, HEADS),
-        weight_sum.reshape(groups, count_new, HEADS),
-        seq_count,
+    rows = groups * count_new
+    packed = pack(
+        value_sum.reshape(rows, HEADS, HD),
+        peak_score.reshape(rows, HEADS),
+        weight_sum.reshape(rows, HEADS),
     )
+    total = combine_over_seq(packed, seq_count).reshape(groups, count_new, HEADS, LANES)
+    value_total = total[..., :HD]
+    peak_total = total[..., HD]
+    weight_total = total[..., HD + 1]
+    query_heads = queries.reshape(groups, count_new, HEADS, HD)
+    key_heads = keys_new.reshape(groups, count_new, HEADS, HD)
+    value_heads = values_new.reshape(groups, count_new, HEADS, HD)
     new_scores = (
-        jnp.einsum("rqc,ruc->rqu", query_rows, keys_new, preferred_element_type=jnp.float32)
+        jnp.einsum("rthd,ruhd->rthu", query_heads, key_heads, preferred_element_type=jnp.float32)
         * scale_factor
-    ).reshape(groups, count_new, HEADS, count_new)
+    )
     causal = (jnp.arange(count_new)[:, None] >= jnp.arange(count_new)[None, :])[None, :, None, :]
     new_masked = jnp.where(causal, new_scores, negative_fill)
-    global_peak = jnp.maximum(peak_score, jnp.max(new_masked, axis=3))
-    carry_scale = jnp.exp(peak_score - global_peak)
+    global_peak = jnp.maximum(peak_total, jnp.max(new_masked, axis=3))
+    carry_scale = jnp.exp(peak_total - global_peak)
     new_weights = jnp.where(causal, jnp.exp(new_masked - global_peak[..., None]), 0.0)
-    denominator = weight_sum * carry_scale + jnp.sum(new_weights, axis=3)
-    new_rows = jnp.einsum(
-        "rqu,ruc->rqc",
-        new_weights.reshape(groups, count_new * HEADS, count_new).astype(jnp.bfloat16),
-        values_new,
+    denominator = weight_total * carry_scale + jnp.sum(new_weights, axis=3)
+    new_values = jnp.einsum(
+        "rthu,ruhd->rthd",
+        new_weights.astype(jnp.bfloat16),
+        value_heads,
         preferred_element_type=jnp.float32,
     )
-    new_values = head_diagonal(new_rows, mask)
-    numerator = value_sum * spread(carry_scale, model_width) + new_values
-    attended = (numerator / spread(denominator, model_width)).astype(jnp.bfloat16)
+    numerator = value_total * carry_scale[..., None] + new_values
+    attended = (numerator / denominator[..., None]).astype(jnp.bfloat16)
     out_rows = project(attended.reshape(groups * count_new, model_width), w_out)
     mixed_rows = inputs + out_rows.astype(jnp.float32)
     normed_mixed = rms_norm(mixed_rows, ffn_gain).astype(jnp.bfloat16)

time: 88.6 us -> 112 us (1.26)
  waiting for transfers between devices: 7.83 us -> 34.7 us
  matrix products: 24.7 us -> 21.4 us
    ppermute x4, waiting for transfers between devices: 7.83 us -> 34.7 us  [exchange(): return lax.ppermute(part, 'seq', pairs)]
    add x7 -> x0, other arithmetic: 5.34 us -> none  [the longest x3 3.05 us: merge(): v = v1 * spread(a1, cols) + v2 * spread(a2, cols)]
    reshape x10 -> x6, local copies, waits for them, and re-layouts: 10.2 us -> 4.94 us  [the longest x2 2.25 us: shards(): value_sum.reshape(rows, HEADS, HD)]
    another operation x0 -> x4, local copies, waits for them, and re-layouts: none -> 4.14 us  [the longest x2 2.73 us: pack(): weight_sum[..., None]]
    select_n x0 -> x2, local copies, waits for them, and re-layouts: none -> 3.74 us  [the longest x1 1.87 us: combine_over_seq(): high_half = jnp.where(core == 0, other, state)]
    broadcast_in_dim x10 -> x1, local copies, waits for them, and re-layouts: 3.08 us -> 0.01 us  [pack(): pad = jnp.zeros(values.shape[:-1] + (LANES - HD - 2,), jnp.float32)]
    select_n x0 -> x3, other arithmetic: none -> 2.92 us  [merge(): return jnp.where(lane == HD, m, merged)]
    unnamed x32 -> x40, local copies, waits for them, and re-layouts: 2.25 us -> 5.04 us
where the time goes in v2:
time: 112 us; the launch traced here: 111 us
  waiting for transfers between devices  34.7 us (31%)
  local copies, waits for them, and re-layouts  30.9 us (28%)
  matrix products  21.4 us (19%)
  other arithmetic  17.3 us (15%)
  starting transfers between devices  6.09 us (5%)
    ppermute x4, waiting for transfers between devices, exchange(): return lax.ppermute(part, 'seq', pairs)  34.7 us
    dot_general x3, matrix products, project(): jnp.dot(token_rows, weight, preferred_element_type=jnp.float32)  12.3 us
    ppermute x4, starting transfers between devices, exchange(): return lax.ppermute(part, 'seq', pairs)  6.09 us
    unnamed x40, local copies, waits for them, and re-layouts  5.04 us
    dot_general x1, matrix products, shards(): jnp.einsum('rqc,rsc->rqs', query_rows, key_cache, preferred_element_type=...  3.43 us
    dot_general x1, matrix products, shards(): jnp.einsum('rqs,rsc->rqc', weights.astype(jnp.bfloat16), value_cache, pre...  3.28 us
    select_n x3, other arithmetic, merge(): return jnp.where(lane == HD, m, merged)  2.92 us
    another operation x2, local copies, waits for them, and re-layouts, pack(): weight_sum[..., None]  2.73 us
  transfers between devices with their start and end apart: 4, of which 3 were waited for; matrix products, arithmetic and copies ran while one was open for 4% of the time, Pallas kernels for 0%

profile of v2, /device:TPU:1, one launch (start us, length us, event | category | flops | bytes accessed | tf_op | source)
XLA Modules:
  0.0 110.6 jit_solution(1728909805358950464)
XLA Ops:
  2.2 6.4 %convolution_convert_fusion = bf16[32,3840]{1,0:T(8,128)(2,1)} fusion(bf16[1280,3840]{1,0:T(8,128)(2,1)} %param.15, f32[32,1280]{1,0:T(8,128)S(1)} %reshape.157, f32[1280]{0:T(1024)} %param.14, f32[32]{0:T(128)S(1)} %rsqrt.20), kind=kOutput, calls=%fused_computation | convolution fusion | flops 314818560 | bytes 10245248 | tf_op jit(solution)/shard_map/dot_general | solution.py:19
  8.6 1.7 %reshape.148 = bf16[8,4,3840]{2,1,0:T(4,128)(2,1)} reshape(bf16[32,3840]{1,0:T(8,128)(2,1)} %convolution_convert_fusion) | data formatting | bytes 491520 | tf_op jit(solution)/shard_map/reshape | solution.py:94
  10.3 1.7 %fusion.43 = (bf16[8,4,1280]{2,1,0:T(4,128)(2,1)}, bf16[8,4,1280]{2,1,0:T(4,128)(2,1)}, bf16[8,4,1280]{2,1,0:T(4,128)(2,1)S(1)}) fusion(bf16[8,4,3840]{2,1,0:T(4,128)(2,1)} %reshape.148), kind=kLoop, calls=%fused_computation.94 | loop fusion | bytes 491520 | tf_op jit(solution)/shard_map/slice | solution.py:97
  12.8 3.4 %fusion.44 = (f32[8,64]{1,0:T(8,128)}, f32[8,64,128]{2,1,0:T(8,128)S(1)}) fusion(bf16[8,64,1280]{2,1,0:T(8,128)(2,1)S(1)} %bitcast_select_fusion, bf16[8,128,1280]{2,1,0:T(8,128)(2,1)} %param.11, pred[8,128]{1,0:T(8,128)(4,1)S(1)} %broadcast_compare_fusion), kind=kOutput, calls=%fused_computation.95 | convolution fusion | flops 167968256 | bytes 4197376 | tf_op jit(solution)/shard_map/rqc,rsc->rqs/dot_general | solution.py:104
  17.0 1.6 %fusion.10 = f32[8,64]{1,0:T(8,128)} fusion(f32[8,64,128]{2,1,0:T(8,128)S(1)} %get-tuple-element.32, f32[8,64]{1,0:T(8,128)} %get-tuple-element.31, pred[8,128]{1,0:T(8,128)(4,1)} %copy-done.13), kind=kLoop, calls=%fused_computation.33 | loop fusion | flops 196096 | bytes 267264 | tf_op jit(solution)/shard_map/reduce_sum | solution.py:110
  19.9 1.4 %copy.164 = f32[32,16,1]{0,1,2:T(8,128)} copy(f32[32,16,1]{1,0,2:T(8,128)} %broadcast_in_dim_reshape.7) | data formatting | bytes 4096 | tf_op jit(solution)/shard_map/broadcast_in_dim;reshape | solution.py:45
  21.9 3.3 %select_reduce_fusion = f32[8,4,1280]{2,1,0:T(4,128)} fusion(pred[16,1280]{1,0:T(8,128)(4,1)} %copy-done.8, bf16[8,128,1280]{2,1,0:T(8,128)(2,1)} %param.12, f32[8,64,128]{2,1,0:T(8,128)S(1)} %get-tuple-element.32, f32[8,64]{1,0:T(8,128)} %get-tuple-element.31, pred[8,128]{1,0:T(8,128)(4,1)} %copy-done.13), kind=kOutput, calls=%fused_computation.1 | convolution fusion | flops 169238528 | bytes 3070976 | tf_op jit(solution)/shard_map/rqs,rsc->rqc/dot_general | solution.py:111
  30.7 2.2 %collective-permute-done = f32[32,8,128]{0,1,2:T(8,128)} collective-permute-done((f32[32,8,128]{0,1,2:T(8,128)}, f32[32,8,128]{0,1,2:T(8,128)}, u32[]{:S(2)}, u32[]{:S(2)}) %collective-permute-start) | collective-permute-done | bytes 131104 | tf_op jit(solution)/shard_map/ppermute | solution.py:61
  35.2 2.4 %collective-permute-start.1 = (f32[32,8,128]{0,1,2:T(8,128)}, f32[32,8,128]{0,1,2:T(8,128)}, u32[]{:S(2)}, u32[]{:S(2)}) collective-permute-start(f32[32,8,128]{0,1,2:T(8,128)} %add_select_fusion.2), channel_id=1, source_target_pairs={{0,2},{1,3},{2,0},{3,1},{4,6},{5,7},{6,4},{7,5},{8,10},{9,11},{10,... | collective-permute-start | bytes 393224 | tf_op jit(solution)/shard_map/ppermute | solution.py:61
  39.3 10.6 %collective-permute-done.1 = f32[32,8,128]{0,1,2:T(8,128)} collective-permute-done((f32[32,8,128]{0,1,2:T(8,128)}, f32[32,8,128]{0,1,2:T(8,128)}, u32[]{:S(2)}, u32[]{:S(2)}) %collective-permute-start.1) | collective-permute-done | bytes 131104 | tf_op jit(solution)/shard_map/ppermute | solution.py:61
  52.1 2.3 %collective-permute-start.2 = (f32[32,8,128]{0,1,2:T(8,128)S(1)}, f32[32,8,128]{0,1,2:T(8,128)S(1)}, u32[]{:S(2)}, u32[]{:S(2)}) collective-permute-start(f32[32,8,128]{0,1,2:T(8,128)S(1)} %add_select_fusion.1), channel_id=1, source_target_pairs={{0,4},{1,5},{2,6},{3,7},{4,0},{5,1},{6,2},{7,3},{8,12},{9,13},{10,... | collective-permute-start | bytes 393224 | tf_op jit(solution)/shard_map/ppermute | solution.py:61
  55.4 21.9 %collective-permute-done.2 = f32[32,8,128]{0,1,2:T(8,128)S(1)} collective-permute-done((f32[32,8,128]{0,1,2:T(8,128)S(1)}, f32[32,8,128]{0,1,2:T(8,128)S(1)}, u32[]{:S(2)}, u32[]{:S(2)}) %collective-permute-start.2) | collective-permute-done | bytes 131104 | tf_op jit(solution)/shard_map/ppermute | solution.py:61
  78.3 1.4 %collective-permute-start.3 = (f32[32,8,128]{0,1,2:T(8,128)}, f32[32,8,128]{0,1,2:T(8,128)}, u32[]{:S(2)}, u32[]{:S(2)}) collective-permute-start(f32[32,8,128]{0,1,2:T(8,128)} %add_select_fusion), channel_id=1, source_target_pairs={{0,1},{1,0},{2,3},{3,2},{4,5},{5,4},{6,7},{7,6},{8,9},{9,8},{10,11... | collective-permute-start | bytes 393224 | tf_op jit(solution)/shard_map/ppermute | solution.py:61
  81.9 2.3 %broadcast_select_fusion.5 = (f32[32,8,128]{0,1,2:T(8,128)}, f32[32,8,128]{0,1,2:T(8,128)}) fusion(f32[32,8,128]{0,1,2:T(8,128)} %add_select_fusion, f32[32,8,128]{0,1,2:T(8,128)} %collective-permute-done.3, pred[]{:T(512)S(6)} %eq.48), kind=kLoop, calls=%fused_computation.32 | loop fusion | flops 65536 | bytes 524289 | tf_op jit(solution)/shard_map/jit(_where)/select_n | solution.py:81
  84.2 1.9 %copy.166 = f32[32,8,128]{2,1,0:T(8,128)} copy(f32[32,8,128]{0,1,2:T(8,128)} %get-tuple-element.8) | data formatting | bytes 262144 | tf_op jit(solution)/shard_map/jit(_where)/select_n | solution.py:82
  86.1 1.9 %copy.165 = f32[32,8,128]{2,1,0:T(8,128)} copy(f32[32,8,128]{0,1,2:T(8,128)} %get-tuple-element.7) | data formatting | bytes 262144 | tf_op jit(solution)/shard_map/jit(_where)/select_n | solution.py:81
  89.9 1.8 %copy.188 = f32[8,4,16,1]{2,0,3,1:T(8,128)} copy(f32[8,4,16,1]{3,2,1,0:T(8,128)} %get-tuple-element.23) | data formatting | bytes 4096
  92.4 2.2 %fusion.29 = (f32[8,4,16]{2,0,1:T(8,128)}, bf16[8,4,16,4]{2,0,3,1:T(8,128)(2,1)}) fusion(f32[8,16,4,4]{1,0,2,3:T(8,128)} %copy-done.5, f32[8,4,16]{2,0,1:T(8,128)S(1)} %fusion.32, pred[4,4]{1,0:T(4,128)(4,1)} %copy-done.17), kind=kLoop, calls=%fused_computation.57 | loop fusion | flops 11776 | bytes 16400 | tf_op jit(solution)/shard_map/reduce_sum | solution.py:137
  94.6 1.7 %copy.178 = bf16[8,4,16,4]{3,1,2,0:T(4,128)(2,1)} copy(bf16[8,4,16,4]{2,0,3,1:T(8,128)(2,1)} %get-tuple-element.28) | data formatting | bytes 8192 | tf_op jit(solution)/shard_map/convert_element_type | solution.py:140
  96.3 1.8 %copy.191 = f32[8,4,16,1]{2,0,3,1:T(8,128)} copy(f32[8,4,16,1]{3,2,1,0:T(8,128)} %get-tuple-element.22) | data formatting | bytes 4096
  99.5 1.5 %copy.182 = f32[8,4,16]{1,2,0:T(8,128)} copy(f32[8,4,16]{2,0,1:T(8,128)} %get-tuple-element.30) | data formatting | bytes 4096 | tf_op jit(solution)/shard_map/div | solution.py:145
  100.9 1.5 %copy.175 = f32[8,4,16]{1,2,0:T(8,128)} copy(f32[8,4,16]{2,0,1:T(8,128)} %get-tuple-element.29) | data formatting | bytes 4096 | tf_op jit(solution)/shard_map/mul | solution.py:144
  104.0 1.7 %multiply_reduce_fusion = (f32[32]{0:T(128)S(1)}, f32[32,1280]{1,0:T(8,128)S(1)}) fusion(f32[32,1280]{1,0:T(8,128)} %copy-done.2, bf16[32,1280]{1,0:T(8,128)(2,1)S(1)} %reshape.155, bf16[1280,1280]{1,0:T(8,128)(2,1)S(1)} %copy-done), kind=kOutput, calls=%fused_computation.37 | convolution fusion | flops 105062368 | bytes 3686528 | tf_op jit(solution)/shard_map/dot_general | solution.py:19
  105.7 4.2 %fusion.2 = bf16[32,1280]{1,0:T(8,128)(2,1)S(1)} fusion(f32[32,1280]{1,0:T(8,128)S(1)} %get-tuple-element.34, bf16[1280,1280]{1,0:T(8,128)(2,1)} %param.19, bf16[1280,1280]{1,0:T(8,128)(2,1)} %param.18, f32[1280]{0:T(1024)S(1)} %copy-done.14, f32[32]{0:T(128)S(1)} %add_rsqrt_fusion.1), kind=kOutput, calls=%fused_computation.5 | convolution fusion | flops 210288640 | bytes 6804608 | tf_op jit(solution)/shard_map/dot_general | solution.py:19
  (85 shorter events, 27.9 us)
Async XLA Ops:
  0.0 104.0 %copy-start = (bf16[1280,1280]{1,0:T(8,128)(2,1)S(1)}, bf16[1280,1280]{1,0:T(8,128)(2,1)}, u32[]{:S(2)}) copy-start(bf16[1280,1280]{1,0:T(8,128)(2,1)} %param.16) | copy-start | bytes 9830404
  1.1 7.6 %copy-start.2 = (f32[32,1280]{1,0:T(8,128)}, f32[32,1280]{1,0:T(8,128)S(1)}, u32[]{:S(2)}) copy-start(f32[32,1280]{1,0:T(8,128)S(1)} %reshape.157) | copy-start | bytes 491524
  2.2 10.5 %copy-start.18 = (s32[8]{0:T(128)S(1)}, s32[8]{0:T(128)}, u32[]{:S(2)}) copy-start(s32[8]{0:T(128)} %param.13) | copy-start | bytes 100
  12.1 0.6 copy-start.3
  12.1 0.6 copy-start.8
  12.8 3.4 %copy-start.13 = (pred[8,128]{1,0:T(8,128)(4,1)}, pred[8,128]{1,0:T(8,128)(4,1)S(1)}, u32[]{:S(2)}) copy-start(pred[8,128]{1,0:T(8,128)(4,1)S(1)} %broadcast_compare_fusion) | copy-start | bytes 3076
  21.9 5.6 %copy-start.11 = (f32[32,16,1]{0,1,2:T(8,128)S(1)}, f32[32,16,1]{0,1,2:T(8,128)}, u32[]{:S(2)}) copy-start(f32[32,16,1]{0,1,2:T(8,128)} %copy.164) | copy-start | bytes 6148
  21.9 5.6 %copy-start.12 = (f32[32,16,1]{0,1,2:T(8,128)S(1)}, f32[32,16,1]{0,1,2:T(8,128)}, u32[]{:S(2)}) copy-start(f32[32,16,1]{0,1,2:T(8,128)} %copy.163) | copy-start | bytes 6148
  28.8 1.0 copy-start.1
  29.8 7.8 %copy-start.4 = (bf16[8,4,1280]{2,1,0:T(4,128)(2,1)S(1)}, bf16[8,4,1280]{2,1,0:T(4,128)(2,1)}, u32[]{:S(2)}) copy-start(bf16[8,4,1280]{2,1,0:T(4,128)(2,1)} %copy-done.3) | copy-start | bytes 245764
  29.8 8.6 %copy-start.7 = (bf16[8,4,1280]{2,1,0:T(4,128)(2,1)S(1)}, bf16[8,4,1280]{2,1,0:T(4,128)(2,1)}, u32[]{:S(2)}) copy-start(bf16[8,4,1280]{2,1,0:T(4,128)(2,1)} %get-tuple-element.25) | copy-start | bytes 245764
  30.6 2.3 %collective-permute-start = (f32[32,8,128]{0,1,2:T(8,128)}, f32[32,8,128]{0,1,2:T(8,128)}, u32[]{:S(2)}, u32[]{:S(2)}) collective-permute-start(f32[32,8,128]{0,1,2:T(8,128)} %constant_dynamic-slice_fusion), channel_id=1, source_target_pairs={{0,1},{1,0},{2,3},{3,2},{4,5},{5,4},{6,7},{7,6},{8,9},{9,8},{10,11... | collective-permute-start | bytes 393224 | tf_op jit(solution)/shard_map/ppermute | solution.py:61
  30.7 4.5 %copy-start.15 = (pred[128]{0:T(512)(128)(4,1)}, pred[128]{0:T(512)(128)(4,1)S(1)}, u32[]{:S(2)}) copy-start(pred[128]{0:T(512)(128)(4,1)S(1)} %iota_compare_fusion.2) | copy-start | bytes 388
  35.2 14.7 %collective-permute-start.1 = (f32[32,8,128]{0,1,2:T(8,128)}, f32[32,8,128]{0,1,2:T(8,128)}, u32[]{:S(2)}, u32[]{:S(2)}) collective-permute-start(f32[32,8,128]{0,1,2:T(8,128)} %add_select_fusion.2), channel_id=1, source_target_pairs={{0,2},{1,3},{2,0},{3,1},{4,6},{5,7},{6,4},{7,5},{8,10},{9,11},{10,... | collective-permute-start | bytes 393224 | tf_op jit(solution)/shard_map/ppermute | solution.py:61
  39.3 15.1 %copy-start.9 = (bf16[8,4,16,80]{3,2,1,0:T(8,128)(2,1)S(1)}, bf16[8,4,16,80]{3,2,1,0:T(8,128)(2,1)}, u32[]{:S(2)}) copy-start(bf16[8,4,16,80]{3,2,1,0:T(8,128)(2,1)} %reshape.159) | copy-start | bytes 245764
  39.3 15.1 %copy-start.10 = (bf16[8,4,16,80]{3,2,1,0:T(8,128)(2,1)S(1)}, bf16[8,4,16,80]{3,2,1,0:T(8,128)(2,1)}, u32[]{:S(2)}) copy-start(bf16[8,4,16,80]{3,2,1,0:T(8,128)(2,1)} %reshape.158) | copy-start | bytes 245764
  51.1 26.2 %copy-start.16 = (pred[128]{0:T(512)(128)(4,1)S(1)}, pred[128]{0:T(512)(128)(4,1)}, u32[]{:S(2)}) copy-start(pred[128]{0:T(512)(128)(4,1)} %copy-done.15) | copy-start | bytes 388
  52.1 28.9 %copy-start.6 = (bf16[8,4,1280]{2,1,0:T(4,128)(2,1)S(1)}, bf16[8,4,1280]{2,1,0:T(4,128)(2,1)}, u32[]{:S(2)}) copy-start(bf16[8,4,1280]{2,1,0:T(4,128)(2,1)} %get-tuple-element.24) | copy-start | bytes 245764
  52.1 25.1 %collective-permute-start.2 = (f32[32,8,128]{0,1,2:T(8,128)S(1)}, f32[32,8,128]{0,1,2:T(8,128)S(1)}, u32[]{:S(2)}, u32[]{:S(2)}) collective-permute-start(f32[32,8,128]{0,1,2:T(8,128)S(1)} %add_select_fusion.1), channel_id=1, source_target_pairs={{0,4},{1,5},{2,6},{3,7},{4,0},{5,1},{6,2},{7,3},{8,12},{9,13},{10,... | collective-permute-start | bytes 393224 | tf_op jit(solution)/shard_map/ppermute | solution.py:61
  78.3 3.6 %collective-permute-start.3 = (f32[32,8,128]{0,1,2:T(8,128)}, f32[32,8,128]{0,1,2:T(8,128)}, u32[]{:S(2)}, u32[]{:S(2)}) collective-permute-start(f32[32,8,128]{0,1,2:T(8,128)} %add_select_fusion), channel_id=1, source_target_pairs={{0,1},{1,0},{2,3},{3,2},{4,5},{5,4},{6,7},{7,6},{8,9},{9,8},{10,11... | collective-permute-start | bytes 393224 | tf_op jit(solution)/shard_map/ppermute | solution.py:61
  79.7 6.3 %copy-start.17 = (pred[4,4]{1,0:T(4,128)(4,1)}, pred[4,4]{1,0:T(4,128)(4,1)S(1)}, u32[]{:S(2)}) copy-start(pred[4,4]{1,0:T(4,128)(4,1)S(1)} %iota_compare_fusion.1) | copy-start | bytes 52
  81.0 5.1 %copy-start.5 = (f32[8,16,4,4]{1,0,2,3:T(8,128)}, f32[8,16,4,4]{1,0,2,3:T(8,128)S(1)}, u32[]{:S(2)}) copy-start(f32[8,16,4,4]{1,0,2,3:T(8,128)S(1)} %copy.172) | copy-start | bytes 24580
  103.8 2.0 %copy-start.14 = (f32[1280]{0:T(1024)S(1)}, f32[1280]{0:T(1024)}, u32[]{:S(2)}) copy-start(f32[1280]{0:T(1024)} %param.17) | copy-start | bytes 15364

commit v3 on v2

--- a/solution.py
+++ b/solution.py
@@ -62,12 +62,13 @@
 
 
 def combine_over_seq(packed, count):
-    heads = packed.shape[1]
+    heads, rows, lanes = packed.shape
     half_heads = heads // 2
     me = lax.axis_index("seq")
     core = me % 2
-    kept = lax.dynamic_slice_in_dim(packed, core * half_heads, half_heads, axis=1)
-    sent = lax.dynamic_slice_in_dim(packed, (1 - core) * half_heads, half_heads, axis=1)
+    halves = packed.reshape(2, half_heads * rows, lanes)
+    kept = lax.dynamic_index_in_dim(halves, core, axis=0, keepdims=False)
+    sent = lax.dynamic_index_in_dim(halves, 1 - core, axis=0, keepdims=False)
     got = exchange(sent, 1, count)
     low_first = core == 0
     state = merge(jnp.where(low_first, kept, got), jnp.where(low_first, got, kept))
@@ -80,7 +81,7 @@
     other = exchange(state, 1, count)
     low_half = jnp.where(core == 0, state, other)
     high_half = jnp.where(core == 0, other, state)
-    return jnp.concatenate([low_half, high_half], axis=1)
+    return jnp.concatenate([low_half, high_half], axis=0).reshape(heads, rows, lanes)
 
 
 def shards(
@@ -114,11 +115,12 @@
     value_sum = head_diagonal(value_rows, mask)
     rows = groups * count_new
     packed = pack(
-        value_sum.reshape(rows, HEADS, HD),
-        peak_score.reshape(rows, HEADS),
-        weight_sum.reshape(rows, HEADS),
+        value_sum.reshape(rows, HEADS, HD).transpose(1, 0, 2),
+        peak_score.reshape(rows, HEADS).T,
+        weight_sum.reshape(rows, HEADS).T,
     )
-    total = combine_over_seq(packed, seq_count).reshape(groups, count_new, HEADS, LANES)
+    total = combine_over_seq(packed, seq_count).transpose(1, 0, 2)
+    total = total.reshape(groups, count_new, HEADS, LANES)
     value_total = total[..., :HD]
     peak_total = total[..., HD]
     weight_total = total[..., HD + 1]

time: 112 us -> 82.1 us (0.73)
  waiting for transfers between devices: 34.7 us -> 5.92 us
  other arithmetic: 17.3 us -> 15.4 us
    ppermute x4, waiting for transfers between devices: 34.7 us -> 5.92 us  [exchange(): return lax.ppermute(part, 'seq', pairs)]
    another operation x4 -> x0, local copies, waits for them, and re-layouts: 4.14 us -> none  [the longest x2 2.73 us: pack(): weight_sum[..., None]]
    select_n x2 -> x0, local copies, waits for them, and re-layouts: 3.74 us -> none  [the longest x1 1.87 us: combine_over_seq(): high_half = jnp.where(core == 0, other, state)]
    concatenate x1 -> x3, local copies, waits for them, and re-layouts: 0.08 us -> 3.38 us  [pack(): jnp.concatenate([values, peak[..., None], weight_sum[..., None], pad], ax...]
    transpose x0 -> x4, local copies, waits for them, and re-layouts: none -> 2.99 us  [the longest x1 1.38 us: shards(): weight_sum.reshape(rows, HEADS)]
    select_n x1, other arithmetic: 2.25 us -> 0.93 us  [combine_over_seq(): low_half = jnp.where(core == 0, state, other)]
    unnamed x40 -> x22, local copies, waits for them, and re-layouts: 5.04 us -> 4.05 us
    reshape x2 -> x3, local copies, waits for them, and re-layouts: 2.25 us -> 3.18 us  [the longest x1 1.35 us: shards(): weight_sum.reshape(rows, HEADS)]
  transfers between devices with their start and end apart: 4 -> 4, of which waited for: 3 -> 3; matrix products, arithmetic and copies ran while one was open for 4% -> 11% of each run, Pallas kernels for 0% -> 0%
where the time goes in v3:
time: 82.1 us; the launch traced here: 80.9 us
  local copies, waits for them, and re-layouts  30.8 us (38%)
  matrix products  22.4 us (27%)
  other arithmetic  15.4 us (19%)
  starting transfers between devices  6.22 us (8%)
  waiting for transfers between devices  5.92 us (7%)
    dot_general x3, matrix products, project(): jnp.dot(token_rows, weight, preferred_element_type=jnp.float32)  12.3 us
    ppermute x4, starting transfers between devices, exchange(): return lax.ppermute(part, 'seq', pairs)  6.22 us
    ppermute x4, waiting for transfers between devices, exchange(): return lax.ppermute(part, 'seq', pairs)  5.92 us
    unnamed x22, local copies, waits for them, and re-layouts  4.05 us
    dot_general x1, matrix products, shards(): jnp.einsum('rqc,rsc->rqs', query_rows, key_cache, preferred_element_type=...  3.42 us
    concatenate x3, local copies, waits for them, and re-layouts, pack(): jnp.concatenate([values, peak[..., None], weight_sum[..., None], pad], ax...  3.38 us
    dot_general x1, matrix products, shards(): jnp.einsum('rqs,rsc->rqc', weights.astype(jnp.bfloat16), value_cache, pre...  3.28 us
    reduce_sum x1, other arithmetic, shards(): denominator = weight_total * carry_scale + jnp.sum(new_weights, axis=3)  2.15 us
  transfers between devices with their start and end apart: 4, of which 3 were waited for; matrix products, arithmetic and copies ran while one was open for 11% of the time, Pallas kernels for 0%

profile of v3, /device:TPU:1, one launch (start us, length us, event | category | flops | bytes accessed | tf_op | source)
XLA Modules:
  0.0 80.9 jit_solution(5570833118305471013)
XLA Ops:
  2.2 6.4 %convolution_convert_fusion = bf16[32,3840]{1,0:T(8,128)(2,1)} fusion(bf16[1280,3840]{1,0:T(8,128)(2,1)} %param.15, f32[32,1280]{1,0:T(8,128)S(1)} %reshape.176, f32[1280]{0:T(1024)} %param.14, f32[32]{0:T(128)S(1)} %rsqrt.20), kind=kOutput, calls=%fused_computation | convolution fusion | flops 314818560 | bytes 10245248 | tf_op jit(solution)/shard_map/dot_general | solution.py:19
  8.6 1.7 %reshape.164 = bf16[8,4,3840]{2,1,0:T(4,128)(2,1)} reshape(bf16[32,3840]{1,0:T(8,128)(2,1)} %convolution_convert_fusion) | data formatting | bytes 491520 | tf_op jit(solution)/shard_map/reshape | solution.py:95
  10.3 1.7 %fusion.43 = (bf16[8,4,1280]{2,1,0:T(4,128)(2,1)}, bf16[8,4,1280]{2,1,0:T(4,128)(2,1)}, bf16[8,4,1280]{2,1,0:T(4,128)(2,1)S(1)}) fusion(bf16[8,4,3840]{2,1,0:T(4,128)(2,1)} %reshape.164), kind=kLoop, calls=%fused_computation.94 | loop fusion | bytes 491520 | tf_op jit(solution)/shard_map/slice | solution.py:98
  12.8 3.4 %fusion.44 = (f32[8,64]{1,0:T(8,128)}, f32[8,64,128]{2,1,0:T(8,128)S(1)}) fusion(bf16[8,64,1280]{2,1,0:T(8,128)(2,1)S(1)} %bitcast_select_fusion, bf16[8,128,1280]{2,1,0:T(8,128)(2,1)} %param.11, pred[8,128]{1,0:T(8,128)(4,1)S(1)} %broadcast_compare_fusion), kind=kOutput, calls=%fused_computation.95 | convolution fusion | flops 167968256 | bytes 4197376 | tf_op jit(solution)/shard_map/rqc,rsc->rqs/dot_general | solution.py:105
  16.9 1.5 %fusion.10 = f32[8,64]{1,0:T(8,128)} fusion(f32[8,64,128]{2,1,0:T(8,128)S(1)} %get-tuple-element.32, f32[8,64]{1,0:T(8,128)} %get-tuple-element.31, pred[8,128]{1,0:T(8,128)(4,1)} %copy-done.6), kind=kLoop, calls=%fused_computation.22 | loop fusion | flops 196096 | bytes 267264 | tf_op jit(solution)/shard_map/reduce_sum | solution.py:111
  21.2 1.6 %concatenate.19 = f32[2,256,1]{2,1,0:T(8,128)} reshape(f32[16,32]{1,0:T(8,128)} %copy.88) | data formatting | bytes 4096 | tf_op jit(solution)/shard_map/concatenate | solution.py:45
  23.5 1.7 %concatenate.18 = f32[2,256,1]{2,1,0:T(8,128)} reshape(f32[16,32]{1,0:T(8,128)} %copy.87) | data formatting | bytes 4096 | tf_op jit(solution)/shard_map/concatenate | solution.py:45
  25.2 3.3 %select_reduce_fusion = f32[8,4,1280]{2,1,0:T(4,128)} fusion(pred[16,1280]{1,0:T(8,128)(4,1)} %copy-done.5, bf16[8,128,1280]{2,1,0:T(8,128)(2,1)} %param.12, f32[8,64,128]{2,1,0:T(8,128)S(1)} %get-tuple-element.32, f32[8,64]{1,0:T(8,128)} %get-tuple-element.31, pred[8,128]{1,0:T(8,128)(4,1)} %copy-done.6), kind=kOutput, calls=%fused_computation.1 | convolution fusion | flops 169238528 | bytes 3070976 | tf_op jit(solution)/shard_map/rqs,rsc->rqc/dot_general | solution.py:112
  32.4 1.7 %collective-permute-done = f32[256,128]{1,0:T(8,128)} collective-permute-done((f32[256,128]{1,0:T(8,128)}, f32[256,128]{1,0:T(8,128)}, u32[]{:S(2)}, u32[]{:S(2)}) %collective-permute-start) | collective-permute-done | bytes 131104 | tf_op jit(solution)/shard_map/ppermute | solution.py:61
  35.5 2.5 %collective-permute-start.1 = (f32[256,128]{1,0:T(8,128)S(1)}, f32[256,128]{1,0:T(8,128)}, u32[]{:S(2)}, u32[]{:S(2)}) collective-permute-start(f32[256,128]{1,0:T(8,128)S(1)} %add_select_fusion.2), channel_id=1, source_target_pairs={{0,2},{1,3},{2,0},{3,1},{4,6},{5,7},{6,4},{7,5},{8,10},{9,11},{10,... | collective-permute-start | bytes 393224 | tf_op jit(solution)/shard_map/ppermute | solution.py:61
  38.0 1.7 %reshape.187 = bf16[8,4,16,80]{3,2,1,0:T(8,128)(2,1)} reshape(bf16[8,4,1280]{2,1,0:T(4,128)(2,1)} %copy-done.2) | data formatting | bytes 163840 | tf_op jit(solution)/shard_map/reshape | solution.py:127
  39.7 1.7 %reshape.186 = bf16[8,4,16,80]{3,2,1,0:T(8,128)(2,1)} reshape(bf16[8,4,1280]{2,1,0:T(4,128)(2,1)} %get-tuple-element.25) | data formatting | bytes 163840 | tf_op jit(solution)/shard_map/reshape | solution.py:128
  43.7 2.3 %collective-permute-start.2 = (f32[256,128]{1,0:T(8,128)S(1)}, f32[256,128]{1,0:T(8,128)S(1)}, u32[]{:S(2)}, u32[]{:S(2)}) collective-permute-start(f32[256,128]{1,0:T(8,128)S(1)} %add_select_fusion.1), channel_id=1, source_target_pairs={{0,4},{1,5},{2,6},{3,7},{4,0},{5,1},{6,2},{7,3},{8,12},{9,13},{10,... | collective-permute-start | bytes 393224 | tf_op jit(solution)/shard_map/ppermute | solution.py:61
  45.9 1.9 %fusion.15 = f32[8,16,4,4]{3,2,1,0:T(4,128)} fusion(bf16[8,4,16,80]{3,2,1,0:T(8,128)(2,1)} %reshape.187, bf16[8,4,16,80]{3,2,1,0:T(8,128)(2,1)} %reshape.186), kind=kOutput, calls=%fused_computation.31 | convolution fusion | flops 327680 | bytes 172032 | tf_op jit(solution)/shard_map/rthd,ruhd->rthu/dot_general | solution.py:131
  47.9 4.1 %collective-permute-done.2 = f32[256,128]{1,0:T(8,128)S(1)} collective-permute-done((f32[256,128]{1,0:T(8,128)S(1)}, f32[256,128]{1,0:T(8,128)S(1)}, u32[]{:S(2)}, u32[]{:S(2)}) %collective-permute-start.2) | collective-permute-done | bytes 131104 | tf_op jit(solution)/shard_map/ppermute | solution.py:61
  53.1 1.5 %collective-permute-start.3 = (f32[256,128]{1,0:T(8,128)S(1)}, f32[256,128]{1,0:T(8,128)}, u32[]{:S(2)}, u32[]{:S(2)}) collective-permute-start(f32[256,128]{1,0:T(8,128)S(1)} %add_select_fusion), channel_id=1, source_target_pairs={{0,1},{1,0},{2,3},{3,2},{4,5},{5,4},{6,7},{7,6},{8,9},{9,8},{10,11... | collective-permute-start | bytes 393224 | tf_op jit(solution)/shard_map/ppermute | solution.py:61
  60.2 1.8 %copy.113 = f32[8,4,16,1]{2,0,3,1:T(8,128)} copy(f32[8,4,16,1]{3,2,1,0:T(8,128)} %get-tuple-element.17) | data formatting | bytes 4096
  62.7 2.2 %fusion.29 = (f32[8,4,16]{2,0,1:T(8,128)}, bf16[8,4,16,4]{2,0,3,1:T(8,128)(2,1)}) fusion(f32[8,16,4,4]{1,0,2,3:T(8,128)} %copy-done.3, f32[8,4,16]{2,0,1:T(8,128)S(1)} %fusion.32, pred[4,4]{1,0:T(4,128)(4,1)} %iota_compare_fusion.1), kind=kLoop, calls=%fused_computation.67 | loop fusion | flops 11776 | bytes 16400 | tf_op jit(solution)/shard_map/reduce_sum | solution.py:139
  64.9 1.7 %copy.103 = bf16[8,4,16,4]{3,1,2,0:T(4,128)(2,1)} copy(bf16[8,4,16,4]{2,0,3,1:T(8,128)(2,1)} %get-tuple-element.28) | data formatting | bytes 8192 | tf_op jit(solution)/shard_map/convert_element_type | solution.py:142
  66.5 1.8 %copy.116 = f32[8,4,16,1]{2,0,3,1:T(8,128)} copy(f32[8,4,16,1]{3,2,1,0:T(8,128)} %get-tuple-element.16) | data formatting | bytes 4096
  69.7 1.5 %copy.107 = f32[8,4,16]{1,2,0:T(8,128)} copy(f32[8,4,16]{2,0,1:T(8,128)} %get-tuple-element.30) | data formatting | bytes 4096 | tf_op jit(solution)/shard_map/div | solution.py:147
  71.2 1.5 %copy.100 = f32[8,4,16]{1,2,0:T(8,128)} copy(f32[8,4,16]{2,0,1:T(8,128)} %get-tuple-element.29) | data formatting | bytes 4096 | tf_op jit(solution)/shard_map/mul | solution.py:146
  74.2 1.7 %multiply_reduce_fusion = (f32[32]{0:T(128)S(1)}, f32[32,1280]{1,0:T(8,128)S(1)}) fusion(f32[32,1280]{1,0:T(8,128)} %copy-done.1, bf16[32,1280]{1,0:T(8,128)(2,1)S(1)} %reshape.174, bf16[1280,1280]{1,0:T(8,128)(2,1)S(1)} %copy-done), kind=kOutput, calls=%fused_computation.26 | convolution fusion | flops 105062368 | bytes 3686528 | tf_op jit(solution)/shard_map/dot_general | solution.py:19
  76.0 4.2 %fusion.2 = bf16[32,1280]{1,0:T(8,128)(2,1)S(1)} fusion(f32[32,1280]{1,0:T(8,128)S(1)} %get-tuple-element.34, bf16[1280,1280]{1,0:T(8,128)(2,1)} %param.19, bf16[1280,1280]{1,0:T(8,128)(2,1)} %param.18, f32[1280]{0:T(1024)S(1)} %copy-done.7, f32[32]{0:T(128)S(1)} %add_rsqrt_fusion.1), kind=kOutput, calls=%fused_computation.5 | convolution fusion | flops 210288640 | bytes 6804608 | tf_op jit(solution)/shard_map/dot_general | solution.py:19
  (68 shorter events, 25.6 us)
Async XLA Ops:
  0.0 74.2 %copy-start = (bf16[1280,1280]{1,0:T(8,128)(2,1)S(1)}, bf16[1280,1280]{1,0:T(8,128)(2,1)}, u32[]{:S(2)}) copy-start(bf16[1280,1280]{1,0:T(8,128)(2,1)} %param.16) | copy-start | bytes 9830404
  1.1 7.6 %copy-start.1 = (f32[32,1280]{1,0:T(8,128)}, f32[32,1280]{1,0:T(8,128)S(1)}, u32[]{:S(2)}) copy-start(f32[32,1280]{1,0:T(8,128)S(1)} %reshape.176) | copy-start | bytes 491524
  2.2 10.4 %copy-start.9 = (s32[8]{0:T(128)S(1)}, s32[8]{0:T(128)}, u32[]{:S(2)}) copy-start(s32[8]{0:T(128)} %param.13) | copy-start | bytes 100
  12.0 0.6 copy-start.2
  12.1 0.6 copy-start.5
  12.8 3.4 %copy-start.6 = (pred[8,128]{1,0:T(8,128)(4,1)}, pred[8,128]{1,0:T(8,128)(4,1)S(1)}, u32[]{:S(2)}) copy-start(pred[8,128]{1,0:T(8,128)(4,1)S(1)} %broadcast_compare_fusion) | copy-start | bytes 3076
  32.4 1.7 %collective-permute-start = (f32[256,128]{1,0:T(8,128)}, f32[256,128]{1,0:T(8,128)}, u32[]{:S(2)}, u32[]{:S(2)}) collective-permute-start(f32[256,128]{1,0:T(8,128)} %dynamic-slice_bitcast_fusion), channel_id=1, source_target_pairs={{0,1},{1,0},{2,3},{3,2},{4,5},{5,4},{6,7},{7,6},{8,9},{9,8},{10,11... | collective-permute-start | bytes 393224 | tf_op jit(solution)/shard_map/ppermute | solution.py:61
  32.4 3.1 %copy-start.8 = (pred[128]{0:T(512)(128)(4,1)}, pred[128]{0:T(512)(128)(4,1)S(1)}, u32[]{:S(2)}) copy-start(pred[128]{0:T(512)(128)(4,1)S(1)} %iota_compare_fusion.2) | copy-start | bytes 388
  35.0 21.4 %copy-start.4 = (bf16[8,4,1280]{2,1,0:T(4,128)(2,1)S(1)}, bf16[8,4,1280]{2,1,0:T(4,128)(2,1)}, u32[]{:S(2)}) copy-start(bf16[8,4,1280]{2,1,0:T(4,128)(2,1)} %get-tuple-element.24) | copy-start | bytes 245764
  35.5 6.1 %collective-permute-start.1 = (f32[256,128]{1,0:T(8,128)S(1)}, f32[256,128]{1,0:T(8,128)}, u32[]{:S(2)}, u32[]{:S(2)}) collective-permute-start(f32[256,128]{1,0:T(8,128)S(1)} %add_select_fusion.2), channel_id=1, source_target_pairs={{0,2},{1,3},{2,0},{3,1},{4,6},{5,7},{6,4},{7,5},{8,10},{9,11},{10,... | collective-permute-start | bytes 393224 | tf_op jit(solution)/shard_map/ppermute | solution.py:61
  43.7 8.3 %collective-permute-start.2 = (f32[256,128]{1,0:T(8,128)S(1)}, f32[256,128]{1,0:T(8,128)S(1)}, u32[]{:S(2)}, u32[]{:S(2)}) collective-permute-start(f32[256,128]{1,0:T(8,128)S(1)} %add_select_fusion.1), channel_id=1, source_target_pairs={{0,4},{1,5},{2,6},{3,7},{4,0},{5,1},{6,2},{7,3},{8,12},{9,13},{10,... | collective-permute-start | bytes 393224 | tf_op jit(solution)/shard_map/ppermute | solution.py:61
  53.1 4.9 %collective-permute-start.3 = (f32[256,128]{1,0:T(8,128)S(1)}, f32[256,128]{1,0:T(8,128)}, u32[]{:S(2)}, u32[]{:S(2)}) collective-permute-start(f32[256,128]{1,0:T(8,128)S(1)} %add_select_fusion), channel_id=1, source_target_pairs={{0,1},{1,0},{2,3},{3,2},{4,5},{5,4},{6,7},{7,6},{8,9},{9,8},{10,11... | collective-permute-start | bytes 393224 | tf_op jit(solution)/shard_map/ppermute | solution.py:61
  56.4 2.6 %copy-start.3 = (f32[8,16,4,4]{1,0,2,3:T(8,128)}, f32[8,16,4,4]{1,0,2,3:T(8,128)S(1)}, u32[]{:S(2)}) copy-start(f32[8,16,4,4]{1,0,2,3:T(8,128)S(1)} %copy.97) | copy-start | bytes 24580
  74.0 2.0 %copy-start.7 = (f32[1280]{0:T(1024)S(1)}, f32[1280]{0:T(1024)}, u32[]{:S(2)}) copy-start(f32[1280]{0:T(1024)} %param.17) | copy-start | bytes 15364

commit v4 on v3

--- a/solution.py
+++ b/solution.py
@@ -119,11 +119,6 @@
         peak_score.reshape(rows, HEADS).T,
         weight_sum.reshape(rows, HEADS).T,
     )
-    total = combine_over_seq(packed, seq_count).transpose(1, 0, 2)
-    total = total.reshape(groups, count_new, HEADS, LANES)
-    value_total = total[..., :HD]
-    peak_total = total[..., HD]
-    weight_total = total[..., HD + 1]
     query_heads = queries.reshape(groups, count_new, HEADS, HD)
     key_heads = keys_new.reshape(groups, count_new, HEADS, HD)
     value_heads = values_new.reshape(groups, count_new, HEADS, HD)
@@ -133,19 +128,24 @@
     )
     causal = (jnp.arange(count_new)[:, None] >= jnp.arange(count_new)[None, :])[None, :, None, :]
     new_masked = jnp.where(causal, new_scores, negative_fill)
-    global_peak = jnp.maximum(peak_total, jnp.max(new_masked, axis=3))
-    carry_scale = jnp.exp(peak_total - global_peak)
-    new_weights = jnp.where(causal, jnp.exp(new_masked - global_peak[..., None]), 0.0)
-    denominator = weight_total * carry_scale + jnp.sum(new_weights, axis=3)
+    new_peak = jnp.max(new_masked, axis=3)
+    new_weights = jnp.where(causal, jnp.exp(new_masked - new_peak[..., None]), 0.0)
+    new_sum = jnp.sum(new_weights, axis=3)
     new_values = jnp.einsum(
         "rthu,ruhd->rthd",
         new_weights.astype(jnp.bfloat16),
         value_heads,
         preferred_element_type=jnp.float32,
     )
-    numerator = value_total * carry_scale[..., None] + new_values
-    attended = (numerator / denominator[..., None]).astype(jnp.bfloat16)
-    out_rows = project(attended.reshape(groups * count_new, model_width), w_out)
+    new_packed = pack(
+        new_values.reshape(rows, HEADS, HD).transpose(1, 0, 2),
+        new_peak.reshape(rows, HEADS).T,
+        new_sum.reshape(rows, HEADS).T,
+    )
+    total = merge(combine_over_seq(packed, seq_count), new_packed)
+    attended_heads = total[..., :HD] / total[..., HD + 1:HD + 2]
+    attended = attended_heads.transpose(1, 0, 2).reshape(rows, model_width).astype(jnp.bfloat16)
+    out_rows = project(attended, w_out)
     mixed_rows = inputs + out_rows.astype(jnp.float32)
     normed_mixed = rms_norm(mixed_rows, ffn_gain).astype(jnp.bfloat16)
     up_rows = project(normed_mixed, w_up)

time: 82.1 us -> 73.9 us (0.900)
  local copies, waits for them, and re-layouts: 30.8 us -> 25.1 us
  waiting for transfers between devices: 5.92 us -> 2.06 us
  other arithmetic: 15.4 us -> 16.9 us
    ppermute x4, waiting for transfers between devices: 5.92 us -> 2.06 us  [exchange(): return lax.ppermute(part, 'seq', pairs)]
    select_n x3 -> x4, other arithmetic: 1.88 us -> 5.16 us  [merge(): return jnp.where(lane == HD, m, merged)]
    unnamed x22 -> x26, local copies, waits for them, and re-layouts: 4.05 us -> 1.24 us
    convert_element_type x0 -> x2, other arithmetic: none -> 2.27 us  [the longest x1 2.13 us: shards(): new_weights.astype(jnp.bfloat16)]
    reduce_sum x1 -> x0, other arithmetic: 2.15 us -> none  [shards(): denominator = weight_total * carry_scale + jnp.sum(new_weights, axis=3)]
    broadcast_in_dim x1 -> x2, local copies, waits for them, and re-layouts: 0.01 us -> 1.89 us  [the longest x1 1.02 us: pack(): weight_sum[..., None]]
    div x1 -> x0, local copies, waits for them, and re-layouts: 1.46 us -> none  [shards(): attended = (numerator / denominator[..., None]).astype(jnp.bfloat16)]
    mul x1 -> x0, local copies, waits for them, and re-layouts: 1.45 us -> none  [shards(): numerator = value_total * carry_scale[..., None] + new_values]
  transfers between devices with their start and end apart: 4 -> 4, of which waited for: 3 -> 2; matrix products, arithmetic and copies ran while one was open for 11% -> 22% of each run, Pallas kernels for 0% -> 0%
where the time goes in v4:
time: 73.9 us; the launch traced here: 72.9 us
  local copies, waits for them, and re-layouts  25.1 us (34%)
  matrix products  22.1 us (30%)
  other arithmetic  16.9 us (23%)
  starting transfers between devices  6.44 us (9%)
  waiting for transfers between devices  2.06 us (3%)
    dot_general x3, matrix products, project(): jnp.dot(token_rows, weight, preferred_element_type=jnp.float32)  12.3 us
    ppermute x4, starting transfers between devices, exchange(): return lax.ppermute(part, 'seq', pairs)  6.44 us
    select_n x4, other arithmetic, merge(): return jnp.where(lane == HD, m, merged)  5.16 us
    dot_general x1, matrix products, shards(): jnp.einsum('rqc,rsc->rqs', query_rows, key_cache, preferred_element_type=...  3.42 us
    dot_general x1, matrix products, shards(): jnp.einsum('rqs,rsc->rqc', weights.astype(jnp.bfloat16), value_cache, pre...  3.27 us
    concatenate x4, local copies, waits for them, and re-layouts, pack(): jnp.concatenate([values, peak[..., None], weight_sum[..., None], pad], ax...  2.68 us
    convert_element_type x1, other arithmetic, shards(): new_weights.astype(jnp.bfloat16)  2.13 us
    ppermute x4, waiting for transfers between devices, exchange(): return lax.ppermute(part, 'seq', pairs)  2.06 us
  transfers between devices with their start and end apart: 4, of which 2 were waited for; matrix products, arithmetic and copies ran while one was open for 22% of the time, Pallas kernels for 0%

profile of v4, /device:TPU:1, one launch (start us, length us, event | category | flops | bytes accessed | tf_op | source)
XLA Modules:
  0.0 72.9 jit_solution(564254086758647708)
XLA Ops:
  2.3 6.4 %convolution_convert_fusion = bf16[32,3840]{1,0:T(8,128)(2,1)} fusion(bf16[1280,3840]{1,0:T(8,128)(2,1)} %param.15, f32[32,1280]{1,0:T(8,128)S(1)} %reshape.179, f32[1280]{0:T(1024)} %param.14, f32[32]{0:T(128)S(1)} %rsqrt.20), kind=kOutput, calls=%fused_computation | convolution fusion | flops 314818560 | bytes 10245248 | tf_op jit(solution)/shard_map/dot_general | solution.py:19
  8.7 1.7 %reshape.166 = bf16[8,4,3840]{2,1,0:T(4,128)(2,1)} reshape(bf16[32,3840]{1,0:T(8,128)(2,1)} %convolution_convert_fusion) | data formatting | bytes 491520 | tf_op jit(solution)/shard_map/reshape | solution.py:95
  10.3 1.7 %fusion.41 = (bf16[8,4,1280]{2,1,0:T(4,128)(2,1)}, bf16[8,4,1280]{2,1,0:T(4,128)(2,1)}, bf16[8,4,1280]{2,1,0:T(4,128)(2,1)S(1)}) fusion(bf16[8,4,3840]{2,1,0:T(4,128)(2,1)} %reshape.166), kind=kLoop, calls=%fused_computation.95 | loop fusion | bytes 491520 | tf_op jit(solution)/shard_map/slice | solution.py:98
  12.9 3.4 %fusion.42 = (f32[8,64]{1,0:T(8,128)}, f32[8,64,128]{2,1,0:T(8,128)S(1)}) fusion(bf16[8,64,1280]{2,1,0:T(8,128)(2,1)S(1)} %bitcast_select_fusion, bf16[8,128,1280]{2,1,0:T(8,128)(2,1)} %param.11, pred[8,128]{1,0:T(8,128)(4,1)S(1)} %broadcast_compare_fusion), kind=kOutput, calls=%fused_computation.96 | convolution fusion | flops 167968256 | bytes 4197376 | tf_op jit(solution)/shard_map/rqc,rsc->rqs/dot_general | solution.py:105
  17.0 1.5 %fusion.10 = f32[8,64]{1,0:T(8,128)} fusion(f32[8,64,128]{2,1,0:T(8,128)S(1)} %get-tuple-element.31, f32[8,64]{1,0:T(8,128)} %get-tuple-element.30, pred[8,128]{1,0:T(8,128)(4,1)} %copy-done.7), kind=kLoop, calls=%fused_computation.28 | loop fusion | flops 196096 | bytes 267264 | tf_op jit(solution)/shard_map/reduce_sum | solution.py:111
  18.6 3.3 %select_reduce_fusion = f32[8,4,1280]{2,1,0:T(4,128)} fusion(pred[16,1280]{1,0:T(8,128)(4,1)} %copy-done.5, bf16[8,128,1280]{2,1,0:T(8,128)(2,1)} %param.12, f32[8,64,128]{2,1,0:T(8,128)S(1)} %get-tuple-element.31, f32[8,64]{1,0:T(8,128)} %get-tuple-element.30, pred[8,128]{1,0:T(8,128)(4,1)} %copy-done.7), kind=kOutput, calls=%fused_computation.1 | convolution fusion | flops 169238528 | bytes 3070976 | tf_op jit(solution)/shard_map/rqs,rsc->rqc/dot_general | solution.py:112
  26.7 1.7 %concatenate.25 = f32[2,256,1]{2,1,0:T(8,128)} reshape(f32[16,32]{1,0:T(8,128)} %copy.80) | data formatting | bytes 4096 | tf_op jit(solution)/shard_map/concatenate | solution.py:45
  28.5 1.2 %maximum_maximum_fusion = f32[2,256,128]{2,1,0:T(8,128)S(1)} fusion(f32[2,256,1]{2,1,0:T(8,128)S(1)} %concatenate.26, f32[2,256,1]{2,1,0:T(8,128)} %concatenate.25, f32[2,256,80]{2,1,0:T(8,128)} %bitcast.56, f32[128]{0:T(128)S(1)} %pad.9.clone), kind=kLoop, calls=%fused_computation.18 | loop fusion | flops 196608 | bytes 430592 | tf_op jit(solution)/shard_map/concatenate | solution.py:45
  31.6 1.7 %reshape.180 = bf16[8,4,16,80]{3,2,1,0:T(8,128)(2,1)} reshape(bf16[8,4,1280]{2,1,0:T(4,128)(2,1)} %get-tuple-element.26) | data formatting | bytes 163840 | tf_op jit(solution)/shard_map/reshape | solution.py:123
  33.3 1.9 %fusion.14 = f32[8,16,4,4]{3,2,1,0:T(4,128)} fusion(bf16[8,4,16,80]{3,2,1,0:T(8,128)(2,1)S(1)} %reshape.195, bf16[8,4,16,80]{3,2,1,0:T(8,128)(2,1)} %reshape.180), kind=kOutput, calls=%fused_computation.36 | convolution fusion | flops 327680 | bytes 172032 | tf_op jit(solution)/shard_map/rthd,ruhd->rthu/dot_general | solution.py:126
  37.3 2.8 %collective-permute-start.1 = (f32[256,128]{1,0:T(8,128)}, f32[256,128]{1,0:T(8,128)}, u32[]{:S(2)}, u32[]{:S(2)}) collective-permute-start(f32[256,128]{1,0:T(8,128)} %add_select_fusion.2), channel_id=1, source_target_pairs={{0,2},{1,3},{2,0},{3,1},{4,6},{5,7},{6,4},{7,5},{8,10},{9,11},{10,... | collective-permute-start | bytes 393224 | tf_op jit(solution)/shard_map/ppermute | solution.py:61
  40.1 1.2 %copy.87 = f32[8,16,4,4]{1,0,2,3:T(8,128)S(1)} copy(f32[8,16,4,4]{3,2,1,0:T(4,128)} %fusion.14) | data formatting | bytes 16384 | tf_op jit(solution)/shard_map/rthd,ruhd->rthu/dot_general | solution.py:126
  43.0 1.3 %collective-permute-done.1 = f32[256,128]{1,0:T(8,128)} collective-permute-done((f32[256,128]{1,0:T(8,128)}, f32[256,128]{1,0:T(8,128)}, u32[]{:S(2)}, u32[]{:S(2)}) %collective-permute-start.1) | collective-permute-done | bytes 131104 | tf_op jit(solution)/shard_map/ppermute | solution.py:61
  45.6 1.4 %add_select_fusion.1 = f32[256,128]{1,0:T(8,128)} fusion(f32[256,128]{1,0:T(8,128)S(1)} %get-tuple-element.24, f32[256,128]{1,0:T(8,128)S(1)} %get-tuple-element.23, f32[256]{0:T(256)S(1)} %get-tuple-element.13, f32[256]{0:T(256)S(1)} %get-tuple-element.12, f32[256]{0:T(256)S(1)} %get-tuple-element.11, pred[128]{0:T(512)(128)(4,1)} %copy-done.9), kind=kLoop, calls=%fused_computation.45 | loop fusion | flops 131072 | bytes 396416 | tf_op jit(solution)/shard_map/jit(_where)/select_n | solution.py:56
  47.0 2.2 %collective-permute-start.2 = (f32[256,128]{1,0:T(8,128)}, f32[256,128]{1,0:T(8,128)}, u32[]{:S(2)}, u32[]{:S(2)}) collective-permute-start(f32[256,128]{1,0:T(8,128)} %add_select_fusion.1), channel_id=1, source_target_pairs={{0,4},{1,5},{2,6},{3,7},{4,0},{5,1},{6,2},{7,3},{8,12},{9,13},{10,... | collective-permute-start | bytes 393224 | tf_op jit(solution)/shard_map/ppermute | solution.py:61
  49.2 2.1 %fusion.32 = (bf16[8,4,16,4]{2,0,3,1:T(8,128)(2,1)}, f32[8,4,16]{2,0,1:T(8,128)}) fusion(f32[8,16,4,4]{1,0,2,3:T(8,128)} %copy-done.4, f32[8,4,16]{2,0,1:T(8,128)S(1)} %fusion.30, pred[4,4]{1,0:T(4,128)(4,1)} %copy-done.11), kind=kLoop, calls=%fused_computation.76 | loop fusion | flops 11776 | bytes 16400 | tf_op jit(solution)/shard_map/convert_element_type | solution.py:136
  51.3 1.7 %copy.95 = bf16[8,4,16,4]{3,1,2,0:T(4,128)(2,1)} copy(bf16[8,4,16,4]{2,0,3,1:T(8,128)(2,1)} %get-tuple-element.28) | data formatting | bytes 8192 | tf_op jit(solution)/shard_map/convert_element_type | solution.py:136
  53.0 1.7 %reshape.192 = bf16[8,4,16,80]{3,2,1,0:T(8,128)(2,1)} reshape(bf16[8,4,1280]{2,1,0:T(4,128)(2,1)} %get-tuple-element.25) | data formatting | bytes 163840 | tf_op jit(solution)/shard_map/reshape | solution.py:124
  56.8 1.4 %add_select_fusion = f32[256,128]{1,0:T(8,128)} fusion(f32[256,128]{1,0:T(8,128)S(1)} %get-tuple-element.22, f32[256,128]{1,0:T(8,128)S(1)} %get-tuple-element.21, f32[256]{0:T(256)S(1)} %get-tuple-element.10, f32[256]{0:T(256)S(1)} %get-tuple-element.9, f32[256]{0:T(256)S(1)} %get-tuple-element.8, pred[128]{0:T(512)(128)(4,1)} %copy-done.9), kind=kLoop, calls=%fused_computation.42 | loop fusion | flops 131072 | bytes 396416 | tf_op jit(solution)/shard_map/jit(_where)/select_n | solution.py:56
  58.3 1.4 %collective-permute-start.3 = (f32[256,128]{1,0:T(8,128)}, f32[256,128]{1,0:T(8,128)}, u32[]{:S(2)}, u32[]{:S(2)}) collective-permute-start(f32[256,128]{1,0:T(8,128)} %add_select_fusion), channel_id=1, source_target_pairs={{0,1},{1,0},{2,3},{3,2},{4,5},{5,4},{6,7},{7,6},{8,9},{9,8},{10,11... | collective-permute-start | bytes 393224 | tf_op jit(solution)/shard_map/ppermute | solution.py:61
  59.7 1.2 %convolution_bitcast_fusion = f32[8,4,16,80]{3,1,2,0:T(4,128)S(1)} fusion(bf16[8,4,16,4]{3,1,2,0:T(4,128)(2,1)} %copy.95, bf16[8,4,16,80]{3,2,1,0:T(8,128)(2,1)} %reshape.192), kind=kOutput, calls=%fused_computation.13 | convolution fusion | flops 327680 | bytes 249856 | tf_op jit(solution)/shard_map/rthu,ruhd->rthd/dot_general | solution.py:134
  64.2 1.4 %fusion.9 = f32[16,32,128]{2,1,0:T(8,128)S(1)} fusion(f32[16,32,1]{2,1,0:T(8,128)} %copy.102, f32[16,32,1]{2,1,0:T(8,128)S(1)} %copy.91, f32[16,32,80]{2,1,0:T(8,128)} %bitcast.55, f32[128]{0:T(128)} %copy-done.10, f32[16,32]{1,0:T(8,128)S(1)} %get-tuple-element.7, f32[16,32]{1,0:T(8,128)S(1)} %get-tuple-element.6, f32[16,32]{1,0:T(8,128)S(1)} %get-tuple-element.5, ...), kind=kLoop, calls=%fused_computation.22 | loop fusion | flops 524288 | bytes 699008 | tf_op jit(solution)/shard_map/jit(_where)/select_n | solution.py:56
  66.3 1.7 %multiply_reduce_fusion = (f32[32]{0:T(128)S(1)}, f32[32,1280]{1,0:T(8,128)S(1)}) fusion(f32[32,1280]{1,0:T(8,128)} %copy-done.1, bf16[32,1280]{1,0:T(8,128)(2,1)S(1)} %convert_element_type.66, bf16[1280,1280]{1,0:T(8,128)(2,1)S(1)} %copy-done), kind=kOutput, calls=%fused_computation.32 | convolution fusion | flops 105062368 | bytes 3686528 | tf_op jit(solution)/shard_map/dot_general | solution.py:19
  68.0 4.2 %fusion.2 = bf16[32,1280]{1,0:T(8,128)(2,1)S(1)} fusion(f32[32,1280]{1,0:T(8,128)S(1)} %get-tuple-element.33, bf16[1280,1280]{1,0:T(8,128)(2,1)} %param.19, bf16[1280,1280]{1,0:T(8,128)(2,1)} %param.18, f32[1280]{0:T(1024)S(1)} %copy-done.8, f32[32]{0:T(128)S(1)} %add_rsqrt_fusion.1), kind=kOutput, calls=%fused_computation.5 | convolution fusion | flops 210288640 | bytes 6804608 | tf_op jit(solution)/shard_map/dot_general | solution.py:19
  (77 shorter events, 22.2 us)
Async XLA Ops:
  0.0 66.3 %copy-start = (bf16[1280,1280]{1,0:T(8,128)(2,1)S(1)}, bf16[1280,1280]{1,0:T(8,128)(2,1)}, u32[]{:S(2)}) copy-start(bf16[1280,1280]{1,0:T(8,128)(2,1)} %param.16) | copy-start | bytes 9830404
  1.1 7.6 %copy-start.1 = (f32[32,1280]{1,0:T(8,128)}, f32[32,1280]{1,0:T(8,128)S(1)}, u32[]{:S(2)}) copy-start(f32[32,1280]{1,0:T(8,128)S(1)} %reshape.179) | copy-start | bytes 491524
  2.3 9.8 %copy-start.12 = (s32[8]{0:T(128)S(1)}, s32[8]{0:T(128)}, u32[]{:S(2)}) copy-start(s32[8]{0:T(128)} %param.13) | copy-start | bytes 100
  12.1 0.6 copy-start.3
  12.1 0.6 copy-start.5
  12.2 4.1 %copy-start.7 = (pred[8,128]{1,0:T(8,128)(4,1)}, pred[8,128]{1,0:T(8,128)(4,1)S(1)}, u32[]{:S(2)}) copy-start(pred[8,128]{1,0:T(8,128)(4,1)S(1)} %broadcast_compare_fusion) | copy-start | bytes 3076
  28.5 2.0 %copy-start.10 = (f32[128]{0:T(128)}, f32[128]{0:T(128)S(1)}, u32[]{:S(2)}) copy-start(f32[128]{0:T(128)S(1)} %pad.9.clone) | copy-start | bytes 1540
  29.7 0.7 copy-start.2
  30.4 4.8 %collective-permute-start = (f32[256,128]{1,0:T(8,128)S(1)}, f32[256,128]{1,0:T(8,128)}, u32[]{:S(2)}, u32[]{:S(2)}) collective-permute-start(f32[256,128]{1,0:T(8,128)S(1)} %dynamic-slice_bitcast_fusion), channel_id=1, source_target_pairs={{0,1},{1,0},{2,3},{3,2},{4,5},{5,4},{6,7},{7,6},{8,9},{9,8},{10,11... | collective-permute-start | bytes 393224 | tf_op jit(solution)/shard_map/ppermute | solution.py:61
  35.2 2.1 %copy-start.9 = (pred[128]{0:T(512)(128)(4,1)}, pred[128]{0:T(512)(128)(4,1)S(1)}, u32[]{:S(2)}) copy-start(pred[128]{0:T(512)(128)(4,1)S(1)} %iota_compare_fusion.2) | copy-start | bytes 388
  37.3 6.9 %collective-permute-start.1 = (f32[256,128]{1,0:T(8,128)}, f32[256,128]{1,0:T(8,128)}, u32[]{:S(2)}, u32[]{:S(2)}) collective-permute-start(f32[256,128]{1,0:T(8,128)} %add_select_fusion.2), channel_id=1, source_target_pairs={{0,2},{1,3},{2,0},{3,1},{4,6},{5,7},{6,4},{7,5},{8,10},{9,11},{10,... | collective-permute-start | bytes 393224 | tf_op jit(solution)/shard_map/ppermute | solution.py:61
  40.1 1.2 %copy-start.11 = (pred[4,4]{1,0:T(4,128)(4,1)}, pred[4,4]{1,0:T(4,128)(4,1)S(1)}, u32[]{:S(2)}) copy-start(pred[4,4]{1,0:T(4,128)(4,1)S(1)} %iota_compare_fusion.1) | copy-start | bytes 52
  41.4 0.8 %copy-start.4 = (f32[8,16,4,4]{1,0,2,3:T(8,128)}, f32[8,16,4,4]{1,0,2,3:T(8,128)S(1)}, u32[]{:S(2)}) copy-start(f32[8,16,4,4]{1,0,2,3:T(8,128)S(1)} %copy.87) | copy-start | bytes 24580
  47.0 8.5 %collective-permute-start.2 = (f32[256,128]{1,0:T(8,128)}, f32[256,128]{1,0:T(8,128)}, u32[]{:S(2)}, u32[]{:S(2)}) collective-permute-start(f32[256,128]{1,0:T(8,128)} %add_select_fusion.1), channel_id=1, source_target_pairs={{0,4},{1,5},{2,6},{3,7},{4,0},{5,1},{6,2},{7,3},{8,12},{9,13},{10,... | collective-permute-start | bytes 393224 | tf_op jit(solution)/shard_map/ppermute | solution.py:61
  54.7 7.0 %copy-start.6 = (f32[8,4,16]{2,0,1:T(8,128)S(1)}, f32[8,4,16]{2,0,1:T(8,128)}, u32[]{:S(2)}) copy-start(f32[8,4,16]{2,0,1:T(8,128)} %get-tuple-element.29) | copy-start | bytes 6148
  58.3 4.5 %collective-permute-start.3 = (f32[256,128]{1,0:T(8,128)}, f32[256,128]{1,0:T(8,128)}, u32[]{:S(2)}, u32[]{:S(2)}) collective-permute-start(f32[256,128]{1,0:T(8,128)} %add_select_fusion), channel_id=1, source_target_pairs={{0,1},{1,0},{2,3},{3,2},{4,5},{5,4},{6,7},{7,6},{8,9},{9,8},{10,11... | collective-permute-start | bytes 393224 | tf_op jit(solution)/shard_map/ppermute | solution.py:61
  65.6 2.4 %copy-start.8 = (f32[1280]{0:T(1024)S(1)}, f32[1280]{0:T(1024)}, u32[]{:S(2)}) copy-start(f32[1280]{0:T(1024)} %param.17) | copy-start | bytes 15364

commit v5 on v4

--- a/solution.py
+++ b/solution.py
@@ -2,6 +2,8 @@
 import jax.numpy as jnp
 from jax import lax
 from jax.sharding import PartitionSpec as P
+from jax.experimental import pallas as pl
+from jax.experimental.pallas import tpu as pltpu
 
 HEADS = 16
 HD = 80
@@ -84,6 +86,54 @@
     return jnp.concatenate([low_half, high_half], axis=0).reshape(heads, rows, lanes)
 
 
+def cache_partial_kernel(offset_ref, length_ref, proj_ref, key_ref, value_ref, qmask_ref, fold_ref, out_ref):
+    groups, slots, width = key_ref.shape
+    heads = out_ref.shape[0]
+    count = out_ref.shape[1] // groups
+    scale_factor = HD ** (-0.5)
+    qmask = qmask_ref[...]
+    fold = fold_ref[...]
+    position = offset_ref[0] + lax.broadcasted_iota(jnp.int32, (1, slots), 1)
+    lane = lax.broadcasted_iota(jnp.int32, (heads * count, LANES), 1)
+    for r in range(groups):
+        queries = proj_ref[pl.ds(r * count, count), pl.ds(0, width)]
+        query_rows = jnp.concatenate([queries] * heads, axis=0) * qmask
+        scores = lax.dot_general(
+            query_rows, key_ref[r], (((1,), (1,)), ((), ())), preferred_element_type=jnp.float32
+        ) * scale_factor
+        live = position < length_ref[r]
+        masked = jnp.where(live, scores, negative_fill)
+        peak = jnp.max(masked, axis=1, keepdims=True)
+        weights = jnp.where(live, jnp.exp(masked - peak), 0.0)
+        total = jnp.sum(weights, axis=1, keepdims=True)
+        value_rows = jnp.dot(
+            weights.astype(jnp.bfloat16), value_ref[r], preferred_element_type=jnp.float32
+        )
+        own = value_rows * qmask.astype(jnp.float32)
+        folded = jnp.dot(own, fold, precision=lax.Precision.HIGHEST, preferred_element_type=jnp.float32)
+        folded = jnp.where(lane == HD, peak, jnp.where(lane == HD + 1, total, folded))
+        for h in range(heads):
+            out_ref[h, pl.ds(r * count, count), :] = folded[h * count:(h + 1) * count, :]
+
+
+def cache_partials(offset, cache_len, projected_rows, key_cache, value_cache):
+    groups, slots, width = key_cache.shape
+    rows = projected_rows.shape[0]
+    count = rows // groups
+    row_head = jnp.arange(HEADS * count)[:, None] // count
+    col_head = jnp.arange(width)[None, :] // HD
+    qmask = (row_head == col_head).astype(jnp.bfloat16)
+    fold = (jnp.arange(width)[:, None] % HD == jnp.arange(LANES)[None, :]).astype(jnp.float32)
+    smem = pl.BlockSpec(memory_space=pltpu.SMEM)
+    vmem = pl.BlockSpec(memory_space=pltpu.VMEM)
+    return pl.pallas_call(
+        cache_partial_kernel,
+        out_shape=jax.ShapeDtypeStruct((HEADS, rows, LANES), jnp.float32),
+        in_specs=[smem, smem, vmem, vmem, vmem, vmem, vmem],
+        out_specs=vmem,
+    )(offset, cache_len, projected_rows, key_cache, value_cache, qmask, fold)
+
+
 def shards(
     patches, key_cache, value_cache, cache_len, attn_gain, w_qkv, w_out, ffn_gain, w_up, w_down
 ):
@@ -96,28 +146,11 @@
     queries = projected[:, :, :model_width]
     keys_new = projected[:, :, model_width:2 * model_width]
     values_new = projected[:, :, 2 * model_width:]
-    mask = head_mask(HEADS, model_width)
-    query_rows = per_head_queries(queries, mask)
     scale_factor = HD ** (-0.5)
-    position = lax.axis_index("seq") * slots_here + jnp.arange(slots_here, dtype=jnp.int32)
-    live_mask = (position[None, :] < cache_len[:, None])[:, None, :]
-    cache_scores = (
-        jnp.einsum("rqc,rsc->rqs", query_rows, key_cache, preferred_element_type=jnp.float32)
-        * scale_factor
-    )
-    masked = jnp.where(live_mask, cache_scores, negative_fill)
-    peak_score = jnp.max(masked, axis=2)
-    weights = jnp.where(live_mask, jnp.exp(masked - peak_score[..., None]), 0.0)
-    weight_sum = jnp.sum(weights, axis=2)
-    value_rows = jnp.einsum(
-        "rqs,rsc->rqc", weights.astype(jnp.bfloat16), value_cache, preferred_element_type=jnp.float32
-    )
-    value_sum = head_diagonal(value_rows, mask)
     rows = groups * count_new
-    packed = pack(
-        value_sum.reshape(rows, HEADS, HD).transpose(1, 0, 2),
-        peak_score.reshape(rows, HEADS).T,
-        weight_sum.reshape(rows, HEADS).T,
+    offset = (lax.axis_index("seq") * slots_here).astype(jnp.int32).reshape(1)
+    packed = cache_partials(
+        offset, cache_len, projected.reshape(rows, 3 * model_width), key_cache, value_cache
     )
     query_heads = queries.reshape(groups, count_new, HEADS, HD)
     key_heads = keys_new.reshape(groups, count_new, HEADS, HD)

time: 73.9 us -> 66.7 us (0.903)
  Pallas kernels: 0 us -> 10.1 us
  local copies, waits for them, and re-layouts: 25.1 us -> 16.1 us
  matrix products: 22.1 us -> 15.4 us
  other arithmetic: 16.9 us -> 15.7 us
    pallas_call x0 -> x1, Pallas kernels: none -> 10.1 us  [cache_partials(): pl.pallas_call(cache_partial_kernel, out_shape=jax.ShapeDtypeStruct((HEAD...]
    dot_general x2 -> x0, matrix products: 6.69 us -> none  [the longest x1 3.42 us: shards(): jnp.einsum('rqc,rsc->rqs', query_rows, key_cache, preferred_element_type=...]
    concatenate x4 -> x1, local copies, waits for them, and re-layouts: 2.68 us -> 0.08 us  [pack(): jnp.concatenate([values, peak[..., None], weight_sum[..., None], pad], ax...]
    reshape x3 -> x0, local copies, waits for them, and re-layouts: 2.58 us -> none  [the longest x1 1.1 us: shards(): value_sum.reshape(rows, HEADS, HD).transpose(1, 0, 2)]
    transpose x3 -> x0, local copies, waits for them, and re-layouts: 2.1 us -> none  [the longest x1 0.77 us: shards(): value_sum.reshape(rows, HEADS, HD).transpose(1, 0, 2)]
    convert_element_type x0 -> x2, other arithmetic: none -> 1.85 us  [the longest x1 1.07 us: cache_partials(): (jnp.arange(width)[:, None] % HD == jnp.arange(LANES)[None, :]).astype(jn...]
    squeeze x1, local copies, waits for them, and re-layouts: 0.01 us -> 1.56 us  [combine_over_seq(): sent = lax.dynamic_index_in_dim(halves, 1 - core, axis=0, keepdims=False)]
    reduce_sum x1 -> x0, other arithmetic: 1.53 us -> none  [shards(): weight_sum = jnp.sum(weights, axis=2)]
  transfers between devices with their start and end apart: 4 -> 4, of which waited for: 2 -> 2; matrix products, arithmetic and copies ran while one was open for 22% -> 27% of each run, Pallas kernels for 0% -> 0%
where the time goes in v5:
time: 66.7 us; the launch traced here: 66.1 us
  local copies, waits for them, and re-layouts  16.1 us (24%)
  other arithmetic  15.7 us (24%)
  matrix products  15.4 us (23%)
  Pallas kernels  10.1 us (15%)
  starting transfers between devices  6.38 us (10%)
  waiting for transfers between devices  2.08 us (3%)
    dot_general x3, matrix products, project(): jnp.dot(token_rows, weight, preferred_element_type=jnp.float32)  12.3 us
    pallas_call x1, Pallas kernels, cache_partials(): pl.pallas_call(cache_partial_kernel, out_shape=jax.ShapeDtypeStruct((HEAD...  10.1 us
    ppermute x4, starting transfers between devices, exchange(): return lax.ppermute(part, 'seq', pairs)  6.38 us
    select_n x4, other arithmetic, merge(): return jnp.where(lane == HD, m, merged)  5.17 us
    convert_element_type x1, other arithmetic, shards(): new_weights.astype(jnp.bfloat16)  2.14 us
    ppermute x4, waiting for transfers between devices, exchange(): return lax.ppermute(part, 'seq', pairs)  2.08 us
    select_n x2, other arithmetic, combine_over_seq(): jnp.where(low_first, state, got)  1.97 us
    dot_general x1, matrix products, shards(): jnp.einsum('rthd,ruhd->rthu', query_heads, key_heads, preferred_element_t...  1.88 us
  transfers between devices with their start and end apart: 4, of which 2 were waited for; matrix products, arithmetic and copies ran while one was open for 27% of the time, Pallas kernels for 0%

profile of v5, /device:TPU:1, one launch (start us, length us, event | category | flops | bytes accessed | tf_op | source)
XLA Modules:
  0.0 66.1 jit_solution(5121262225686785008)
XLA Ops:
  0.0 1.0 %reshape.164 = f32[32,1280]{1,0:T(8,128)S(1)} reshape(bf16[8,4,1280]{2,1,0:T(4,128)(2,1)} %param.10) | data formatting | bytes 245760 | tf_op jit(solution)/shard_map/convert_element_type | solution.py:143
  1.1 1.1 %multiply_reduce_fusion.1 = f32[8,4]{1,0:T(8,128)S(1)} fusion(bf16[8,4,1280]{2,1,0:T(4,128)(2,1)} %param.10), kind=kLoop, calls=%fused_computation.29 | loop fusion | flops 122848 | bytes 82048 | tf_op jit(solution)/shard_map/reduce_sum | solution.py:17
  2.3 1.1 %fusion.6.fold_ref = f32[1280,128]{1,0:T(8,128)} fusion(s32[1280]{0:T(1024)S(1)} %fusion.26), kind=kLoop, calls=%fused_computation.12 | loop fusion | flops 327680 | bytes 660480 | tf_op jit(solution)/shard_map/convert_element_type | solution.py:126
  4.1 6.4 %convolution_convert_fusion.proj_ref = bf16[32,3840]{1,0:T(8,128)(2,1)} fusion(bf16[1280,3840]{1,0:T(8,128)(2,1)} %param.15, f32[32,1280]{1,0:T(8,128)S(1)} %reshape.164, f32[1280]{0:T(1024)} %param.14, f32[32]{0:T(128)S(1)} %rsqrt.20), kind=kOutput, calls=%fused_computation | convolution fusion | flops 314818560 | bytes 10245248 | tf_op jit(solution)/shard_map/dot_general | solution.py:21
  10.5 10.1 %shard_map.100 = f32[16,32,128]{2,1,0:T(8,128)} custom-call(s32[1]{0:T(128)} %bitcast.offset_ref, s32[8]{0:T(128)} %length_ref.1, bf16[32,3840]{1,0:T(8,128)(2,1)} %convolution_convert_fusion.proj_ref, bf16[8,128,1280]{2,1,0:T(8,128)(2,1)} %key_ref.1, bf16[8,128,1280]{2,1,0:T(8,128)(2,1)} %value_ref.1, bf16[64,1280]{1,0:T(8,128)(2,1)} %compare_convert_fusion.qmask_ref, ...), custom_call_target="tpu_custom_call" | custom-call | tf_op jit(solution)/shard_map/pallas_call | solution.py:129
  20.6 1.6 %dynamic-slice_bitcast_fusion = f32[256,128]{1,0:T(8,128)} fusion(f32[2,256,128]{2,1,0:T(8,128)} %bitcast.42, s32[]{:T(128)S(6)} %select_n.133), kind=kLoop, calls=%fused_computation.45 | loop fusion | bytes 262148 | tf_op jit(solution)/shard_map/jit(dynamic_index_in_dim)/squeeze | solution.py:73
  22.9 1.7 %fusion.37 = (bf16[8,4,1280]{2,1,0:T(4,128)(2,1)}, bf16[8,4,1280]{2,1,0:T(4,128)(2,1)S(1)}, bf16[8,4,1280]{2,1,0:T(4,128)(2,1)S(1)}) fusion(bf16[8,4,3840]{2,1,0:T(4,128)(2,1)} %reshape.156), kind=kLoop, calls=%fused_computation.90 | loop fusion | bytes 491520 | tf_op jit(solution)/shard_map/slice | solution.py:148
  25.7 1.9 %fusion.11 = f32[8,16,4,4]{3,2,1,0:T(4,128)} fusion(bf16[8,4,16,80]{3,2,1,0:T(8,128)(2,1)S(1)} %reshape.166, bf16[8,4,16,80]{3,2,1,0:T(8,128)(2,1)} %reshape.165), kind=kOutput, calls=%fused_computation.31 | convolution fusion | flops 327680 | bytes 172032 | tf_op jit(solution)/shard_map/rthd,ruhd->rthu/dot_general | solution.py:159
  27.5 1.0 %bitcast_select_fusion.1 = (f32[256,128]{1,0:T(8,128)S(1)}, f32[256,128]{1,0:T(8,128)S(1)}) fusion(f32[256,128]{1,0:T(8,128)} %collective-permute-done, f32[2,256,128]{2,1,0:T(8,128)} %bitcast.43, s32[]{:T(128)S(6)} %select_n.132, pred[]{:T(512)S(6)} %eq.62), kind=kLoop, calls=%fused_computation.35 | loop fusion | flops 65536 | bytes 524293 | tf_op jit(solution)/shard_map/jit(_where)/select_n | solution.py:76
  29.7 2.8 %collective-permute-start.1 = (f32[256,128]{1,0:T(8,128)}, f32[256,128]{1,0:T(8,128)}, u32[]{:S(2)}, u32[]{:S(2)}) collective-permute-start(f32[256,128]{1,0:T(8,128)} %add_select_fusion.2), channel_id=1, source_target_pairs={{0,2},{1,3},{2,0},{3,1},{4,6},{5,7},{6,4},{7,5},{8,10},{9,11},{10,... | collective-permute-start | bytes 393224 | tf_op jit(solution)/shard_map/ppermute | solution.py:63
  32.4 1.2 %copy.66 = f32[8,16,4,4]{1,0,2,3:T(8,128)S(1)} copy(f32[8,16,4,4]{3,2,1,0:T(4,128)} %fusion.11) | data formatting | bytes 16384 | tf_op jit(solution)/shard_map/rthd,ruhd->rthu/dot_general | solution.py:159
  35.3 1.3 %collective-permute-done.1 = f32[256,128]{1,0:T(8,128)} collective-permute-done((f32[256,128]{1,0:T(8,128)}, f32[256,128]{1,0:T(8,128)}, u32[]{:S(2)}, u32[]{:S(2)}) %collective-permute-start.1) | collective-permute-done | bytes 131104 | tf_op jit(solution)/shard_map/ppermute | solution.py:63
  37.9 1.4 %add_select_fusion.1 = f32[256,128]{1,0:T(8,128)} fusion(f32[256,128]{1,0:T(8,128)S(1)} %get-tuple-element.24, f32[256,128]{1,0:T(8,128)S(1)} %get-tuple-element.23, f32[256]{0:T(256)S(1)} %get-tuple-element.13, f32[256]{0:T(256)S(1)} %get-tuple-element.12, f32[256]{0:T(256)S(1)} %get-tuple-element.11, pred[128]{0:T(512)(128)(4,1)} %copy-done.5), kind=kLoop, calls=%fused_computation.39 | loop fusion | flops 131072 | bytes 396416 | tf_op jit(solution)/shard_map/jit(_where)/select_n | solution.py:58
  39.3 2.2 %collective-permute-start.2 = (f32[256,128]{1,0:T(8,128)}, f32[256,128]{1,0:T(8,128)}, u32[]{:S(2)}, u32[]{:S(2)}) collective-permute-start(f32[256,128]{1,0:T(8,128)} %add_select_fusion.1), channel_id=1, source_target_pairs={{0,4},{1,5},{2,6},{3,7},{4,0},{5,1},{6,2},{7,3},{8,12},{9,13},{10,... | collective-permute-start | bytes 393224 | tf_op jit(solution)/shard_map/ppermute | solution.py:63
  41.5 2.1 %fusion.25 = (bf16[8,4,16,4]{2,0,3,1:T(8,128)(2,1)}, f32[8,4,16]{2,0,1:T(8,128)}) fusion(f32[8,16,4,4]{1,0,2,3:T(8,128)} %copy-done.3, f32[8,4,16]{2,0,1:T(8,128)S(1)} %fusion.23, pred[4,4]{1,0:T(4,128)(4,1)} %copy-done.6), kind=kLoop, calls=%fused_computation.66 | loop fusion | flops 11776 | bytes 16400 | tf_op jit(solution)/shard_map/convert_element_type | solution.py:169
  43.7 1.7 %copy.74 = bf16[8,4,16,4]{3,1,2,0:T(4,128)(2,1)} copy(bf16[8,4,16,4]{2,0,3,1:T(8,128)(2,1)} %get-tuple-element.28) | data formatting | bytes 8192 | tf_op jit(solution)/shard_map/convert_element_type | solution.py:169
  45.4 1.7 %reshape.178 = bf16[8,4,16,80]{3,2,1,0:T(8,128)(2,1)} reshape(bf16[8,4,1280]{2,1,0:T(4,128)(2,1)} %get-tuple-element.25) | data formatting | bytes 163840 | tf_op jit(solution)/shard_map/reshape | solution.py:157
  49.2 1.5 %add_select_fusion = f32[256,128]{1,0:T(8,128)} fusion(f32[256,128]{1,0:T(8,128)S(1)} %get-tuple-element.22, f32[256,128]{1,0:T(8,128)S(1)} %get-tuple-element.21, f32[256]{0:T(256)S(1)} %get-tuple-element.10, f32[256]{0:T(256)S(1)} %get-tuple-element.9, f32[256]{0:T(256)S(1)} %get-tuple-element.8, pred[128]{0:T(512)(128)(4,1)} %copy-done.5), kind=kLoop, calls=%fused_computation.36 | loop fusion | flops 131072 | bytes 396416 | tf_op jit(solution)/shard_map/jit(_where)/select_n | solution.py:58
  50.6 1.4 %collective-permute-start.3 = (f32[256,128]{1,0:T(8,128)}, f32[256,128]{1,0:T(8,128)}, u32[]{:S(2)}, u32[]{:S(2)}) collective-permute-start(f32[256,128]{1,0:T(8,128)} %add_select_fusion), channel_id=1, source_target_pairs={{0,1},{1,0},{2,3},{3,2},{4,5},{5,4},{6,7},{7,6},{8,9},{9,8},{10,11... | collective-permute-start | bytes 393224 | tf_op jit(solution)/shard_map/ppermute | solution.py:63
  52.0 1.2 %convolution_bitcast_fusion = f32[8,4,16,80]{3,1,2,0:T(4,128)S(1)} fusion(bf16[8,4,16,4]{3,1,2,0:T(4,128)(2,1)} %copy.74, bf16[8,4,16,80]{3,2,1,0:T(8,128)(2,1)} %reshape.178), kind=kOutput, calls=%fused_computation.10 | convolution fusion | flops 327680 | bytes 249856 | tf_op jit(solution)/shard_map/rthu,ruhd->rthd/dot_general | solution.py:167
  54.8 1.0 %copy.81 = f32[16,32,1]{2,1,0:T(8,128)} copy(f32[16,32,1]{0,1,2:T(8,128)S(1)} %bitcast.47) | data formatting | bytes 4096 | tf_op jit(solution)/shard_map/broadcast_in_dim | solution.py:47
  57.3 1.4 %fusion.9 = f32[16,32,128]{2,1,0:T(8,128)S(1)} fusion(f32[16,32,1]{2,1,0:T(8,128)} %copy.81, f32[16,32,1]{2,1,0:T(8,128)S(1)} %copy.70, f32[16,32,80]{2,1,0:T(8,128)} %bitcast.46, f32[128]{0:T(128)S(1)} %pad.3.clone, f32[16,32]{1,0:T(8,128)S(1)} %get-tuple-element.7, f32[16,32]{1,0:T(8,128)S(1)} %get-tuple-element.6, f32[16,32]{1,0:T(8,128)S(1)} %get-tuple-element.5, ...), kind=kLoop, calls=%fused_computation.20 | loop fusion | flops 524288 | bytes 699008 | tf_op jit(solution)/shard_map/jit(_where)/select_n | solution.py:58
  59.4 1.7 %multiply_reduce_fusion = (f32[32]{0:T(128)S(1)}, f32[32,1280]{1,0:T(8,128)S(1)}) fusion(f32[32,1280]{1,0:T(8,128)} %copy-done.2, bf16[32,1280]{1,0:T(8,128)(2,1)S(1)} %convert_element_type.70, bf16[1280,1280]{1,0:T(8,128)(2,1)S(1)} %copy-done), kind=kOutput, calls=%fused_computation.27 | convolution fusion | flops 105062368 | bytes 3686528 | tf_op jit(solution)/shard_map/dot_general | solution.py:21
  61.2 4.2 %fusion.2 = bf16[32,1280]{1,0:T(8,128)(2,1)S(1)} fusion(f32[32,1280]{1,0:T(8,128)S(1)} %get-tuple-element.31, bf16[1280,1280]{1,0:T(8,128)(2,1)} %param.19, bf16[1280,1280]{1,0:T(8,128)(2,1)} %param.18, f32[1280]{0:T(1024)S(1)} %copy-done.4, f32[32]{0:T(128)S(1)} %add_rsqrt_fusion.1), kind=kOutput, calls=%fused_computation.4 | convolution fusion | flops 210288640 | bytes 6804608 | tf_op jit(solution)/shard_map/dot_general | solution.py:21
  (53 shorter events, 13.1 us)
Async XLA Ops:
  0.0 59.4 %copy-start = (bf16[1280,1280]{1,0:T(8,128)(2,1)S(1)}, bf16[1280,1280]{1,0:T(8,128)(2,1)}, u32[]{:S(2)}) copy-start(bf16[1280,1280]{1,0:T(8,128)(2,1)} %param.16) | copy-start | bytes 9830404
  1.1 9.4 %copy-start.2 = (f32[32,1280]{1,0:T(8,128)}, f32[32,1280]{1,0:T(8,128)S(1)}, u32[]{:S(2)}) copy-start(f32[32,1280]{1,0:T(8,128)S(1)} %reshape.164) | copy-start | bytes 491524
  10.5 11.7 %copy-start.1 = (bf16[32,3840]{1,0:T(8,128)(2,1)S(1)}, bf16[32,3840]{1,0:T(8,128)(2,1)}, u32[]{:S(2)}) copy-start(bf16[32,3840]{1,0:T(8,128)(2,1)} %convolution_convert_fusion.proj_ref) | copy-start | bytes 737284
  22.2 5.4 %collective-permute-start = (f32[256,128]{1,0:T(8,128)}, f32[256,128]{1,0:T(8,128)}, u32[]{:S(2)}, u32[]{:S(2)}) collective-permute-start(f32[256,128]{1,0:T(8,128)} %dynamic-slice_bitcast_fusion), channel_id=1, source_target_pairs={{0,1},{1,0},{2,3},{3,2},{4,5},{5,4},{6,7},{7,6},{8,9},{9,8},{10,11... | collective-permute-start | bytes 393224 | tf_op jit(solution)/shard_map/ppermute | solution.py:63
  27.5 2.1 %copy-start.5 = (pred[128]{0:T(512)(128)(4,1)}, pred[128]{0:T(512)(128)(4,1)S(1)}, u32[]{:S(2)}) copy-start(pred[128]{0:T(512)(128)(4,1)S(1)} %iota_compare_fusion.2) | copy-start | bytes 388
  29.7 7.0 %collective-permute-start.1 = (f32[256,128]{1,0:T(8,128)}, f32[256,128]{1,0:T(8,128)}, u32[]{:S(2)}, u32[]{:S(2)}) collective-permute-start(f32[256,128]{1,0:T(8,128)} %add_select_fusion.2), channel_id=1, source_target_pairs={{0,2},{1,3},{2,0},{3,1},{4,6},{5,7},{6,4},{7,5},{8,10},{9,11},{10,... | collective-permute-start | bytes 393224 | tf_op jit(solution)/shard_map/ppermute | solution.py:63
  32.4 1.2 %copy-start.6 = (pred[4,4]{1,0:T(4,128)(4,1)}, pred[4,4]{1,0:T(4,128)(4,1)S(1)}, u32[]{:S(2)}) copy-start(pred[4,4]{1,0:T(4,128)(4,1)S(1)} %iota_compare_fusion.1) | copy-start | bytes 52
  33.7 0.8 %copy-start.3 = (f32[8,16,4,4]{1,0,2,3:T(8,128)}, f32[8,16,4,4]{1,0,2,3:T(8,128)S(1)}, u32[]{:S(2)}) copy-start(f32[8,16,4,4]{1,0,2,3:T(8,128)S(1)} %copy.66) | copy-start | bytes 24580
  39.3 8.5 %collective-permute-start.2 = (f32[256,128]{1,0:T(8,128)}, f32[256,128]{1,0:T(8,128)}, u32[]{:S(2)}, u32[]{:S(2)}) collective-permute-start(f32[256,128]{1,0:T(8,128)} %add_select_fusion.1), channel_id=1, source_target_pairs={{0,4},{1,5},{2,6},{3,7},{4,0},{5,1},{6,2},{7,3},{8,12},{9,13},{10,... | collective-permute-start | bytes 393224 | tf_op jit(solution)/shard_map/ppermute | solution.py:63
  50.6 5.3 %collective-permute-start.3 = (f32[256,128]{1,0:T(8,128)}, f32[256,128]{1,0:T(8,128)}, u32[]{:S(2)}, u32[]{:S(2)}) collective-permute-start(f32[256,128]{1,0:T(8,128)} %add_select_fusion), channel_id=1, source_target_pairs={{0,1},{1,0},{2,3},{3,2},{4,5},{5,4},{6,7},{7,6},{8,9},{9,8},{10,11... | collective-permute-start | bytes 393224 | tf_op jit(solution)/shard_map/ppermute | solution.py:63
  56.9 4.2 %copy-start.4 = (f32[1280]{0:T(1024)S(1)}, f32[1280]{0:T(1024)}, u32[]{:S(2)}) copy-start(f32[1280]{0:T(1024)} %param.17) | copy-start | bytes 15364

commit v6 on v5

--- a/solution.py
+++ b/solution.py
@@ -1,3 +1,4 @@
+import numpy as np
 import jax
 import jax.numpy as jnp
 from jax import lax
@@ -86,15 +87,28 @@
     return jnp.concatenate([low_half, high_half], axis=0).reshape(heads, rows, lanes)
 
 
-def cache_partial_kernel(offset_ref, length_ref, proj_ref, key_ref, value_ref, qmask_ref, fold_ref, out_ref):
+def cache_partial_kernel(
+    offset_ref, length_ref, proj_ref, key_ref, value_ref, qmask_ref, fold_ref, out_ref, new_ref
+):
     groups, slots, width = key_ref.shape
     heads = out_ref.shape[0]
     count = out_ref.shape[1] // groups
     scale_factor = HD ** (-0.5)
     qmask = qmask_ref[...]
+    qmask_float = qmask.astype(jnp.float32)
     fold = fold_ref[...]
     position = offset_ref[0] + lax.broadcasted_iota(jnp.int32, (1, slots), 1)
     lane = lax.broadcasted_iota(jnp.int32, (heads * count, LANES), 1)
+    patch = lax.broadcasted_iota(jnp.int32, (heads * count, 1), 0) & (count - 1)
+
+    def emit(target, r, rows, peak, total):
+        folded = jnp.dot(
+            rows * qmask_float, fold, precision=lax.Precision.HIGHEST, preferred_element_type=jnp.float32
+        )
+        folded = jnp.where(lane == HD, peak, jnp.where(lane == HD + 1, total, folded))
+        for h in range(heads):
+            target[h, pl.ds(r * count, count), :] = folded[h * count:(h + 1) * count, :]
+
     for r in range(groups):
         queries = proj_ref[pl.ds(r * count, count), pl.ds(0, width)]
         query_rows = jnp.concatenate([queries] * heads, axis=0) * qmask
@@ -109,28 +123,44 @@
         value_rows = jnp.dot(
             weights.astype(jnp.bfloat16), value_ref[r], preferred_element_type=jnp.float32
         )
-        own = value_rows * qmask.astype(jnp.float32)
-        folded = jnp.dot(own, fold, precision=lax.Precision.HIGHEST, preferred_element_type=jnp.float32)
-        folded = jnp.where(lane == HD, peak, jnp.where(lane == HD + 1, total, folded))
-        for h in range(heads):
-            out_ref[h, pl.ds(r * count, count), :] = folded[h * count:(h + 1) * count, :]
+        emit(out_ref, r, value_rows, peak, total)
+
+        query_float = query_rows.astype(jnp.float32)
+        keys_new = proj_ref[pl.ds(r * count, count), pl.ds(width, width)].astype(jnp.float32)
+        values_new = proj_ref[pl.ds(r * count, count), pl.ds(2 * width, width)].astype(jnp.float32)
+        new_scores = []
+        for u in range(count):
+            score = jnp.sum(query_float * keys_new[u:u + 1, :], axis=1, keepdims=True) * scale_factor
+            new_scores.append(jnp.where(patch >= u, score, negative_fill))
+        new_peak = new_scores[0]
+        for score in new_scores[1:]:
+            new_peak = jnp.maximum(new_peak, score)
+        new_total = jnp.zeros_like(new_peak)
+        new_rows = jnp.zeros((heads * count, width), jnp.float32)
+        for u in range(count):
+            weight = jnp.where(patch >= u, jnp.exp(new_scores[u] - new_peak), 0.0)
+            new_total = new_total + weight
+            weight = weight.astype(jnp.bfloat16).astype(jnp.float32)
+            new_rows = new_rows + weight * values_new[u:u + 1, :]
+        emit(new_ref, r, new_rows, new_peak, new_total)
 
 
 def cache_partials(offset, cache_len, projected_rows, key_cache, value_cache):
     groups, slots, width = key_cache.shape
     rows = projected_rows.shape[0]
     count = rows // groups
-    row_head = jnp.arange(HEADS * count)[:, None] // count
-    col_head = jnp.arange(width)[None, :] // HD
-    qmask = (row_head == col_head).astype(jnp.bfloat16)
-    fold = (jnp.arange(width)[:, None] % HD == jnp.arange(LANES)[None, :]).astype(jnp.float32)
+    row_head = np.arange(HEADS * count)[:, None] // count
+    col_head = np.arange(width)[None, :] // HD
+    qmask = jnp.asarray((row_head == col_head).astype(np.float32), dtype=jnp.bfloat16)
+    fold = jnp.asarray((np.arange(width)[:, None] % HD == np.arange(LANES)[None, :]).astype(np.float32))
     smem = pl.BlockSpec(memory_space=pltpu.SMEM)
     vmem = pl.BlockSpec(memory_space=pltpu.VMEM)
+    packed = jax.ShapeDtypeStruct((HEADS, rows, LANES), jnp.float32)
     return pl.pallas_call(
         cache_partial_kernel,
-        out_shape=jax.ShapeDtypeStruct((HEADS, rows, LANES), jnp.float32),
+        out_shape=(packed, packed),
         in_specs=[smem, smem, vmem, vmem, vmem, vmem, vmem],
-        out_specs=vmem,
+        out_specs=(vmem, vmem),
     )(offset, cache_len, projected_rows, key_cache, value_cache, qmask, fold)
 
 
@@ -149,31 +179,8 @@
     scale_factor = HD ** (-0.5)
     rows = groups * count_new
     offset = (lax.axis_index("seq") * slots_here).astype(jnp.int32).reshape(1)
-    packed = cache_partials(
+    packed, new_packed = cache_partials(
         offset, cache_len, projected.reshape(rows, 3 * model_width), key_cache, value_cache
-    )
-    query_heads = queries.reshape(groups, count_new, HEADS, HD)
-    key_heads = keys_new.reshape(groups, count_new, HEADS, HD)
-    value_heads = values_new.reshape(groups, count_new, HEADS, HD)
-    new_scores = (
-        jnp.einsum("rthd,ruhd->rthu", query_heads, key_heads, preferred_element_type=jnp.float32)
-        * scale_factor
-    )
-    causal = (jnp.arange(count_new)[:, None] >= jnp.arange(count_new)[None, :])[None, :, None, :]
-    new_masked = jnp.where(causal, new_scores, negative_fill)
-    new_peak = jnp.max(new_masked, axis=3)
-    new_weights = jnp.where(causal, jnp.exp(new_masked - new_peak[..., None]), 0.0)
-    new_sum = jnp.sum(new_weights, axis=3)
-    new_values = jnp.einsum(
-        "rthu,ruhd->rthd",
-        new_weights.astype(jnp.bfloat16),
-        value_heads,
-        preferred_element_type=jnp.float32,
-    )
-    new_packed = pack(
-        new_values.reshape(rows, HEADS, HD).transpose(1, 0, 2),
-        new_peak.reshape(rows, HEADS).T,
-        new_sum.reshape(rows, HEADS).T,
     )
     total = merge(combine_over_seq(packed, seq_count), new_packed)
     attended_heads = total[..., :HD] / total[..., HD + 1:HD + 2]

time: 66.7 us -> 55.2 us (0.83)
  local copies, waits for them, and re-layouts: 16.1 us -> 5.07 us
  waiting for transfers between devices: 2.08 us -> 12.1 us
  other arithmetic: 15.7 us -> 5.97 us
  matrix products: 15.4 us -> 12.3 us
  Pallas kernels: 10.1 us -> 12.7 us
    ppermute x4, waiting for transfers between devices: 2.08 us -> 12.1 us  [exchange(): return lax.ppermute(part, 'seq', pairs)]
    reshape x5 -> x0, local copies, waits for them, and re-layouts: 4.27 us -> none  [the longest x1 1.72 us: shards(): value_heads = values_new.reshape(groups, count_new, HEADS, HD)]
    convert_element_type x3 -> x0, other arithmetic: 3.98 us -> none  [the longest x1 2.14 us: shards(): new_weights.astype(jnp.bfloat16)]
    select_n x4, other arithmetic: 5.17 us -> 1.49 us  [merge(): return jnp.where(lane == HD, m, merged)]
    dot_general x2 -> x0, matrix products: 3.12 us -> none  [the longest x1 1.88 us: shards(): jnp.einsum('rthd,ruhd->rthu', query_heads, key_heads, preferred_element_t...]
    pallas_call x1, Pallas kernels: 10.1 us -> 12.7 us  [cache_partials(): pl.pallas_call(cache_partial_kernel, out_shape=(packed, packed), in_specs...]
    select_n x2, other arithmetic: 1.97 us -> 0.04 us  [combine_over_seq(): jnp.where(low_first, state, got)]
    broadcast_in_dim x3 -> x0, local copies, waits for them, and re-layouts: 1.89 us -> none  [the longest x1 1.02 us: pack(): weight_sum[..., None]]
  transfers between devices with their start and end apart: 4 -> 4, of which waited for: 2 -> 4; matrix products, arithmetic and copies ran while one was open for 27% -> 0% of each run, Pallas kernels for 0% -> 0%
where the time goes in v6:
time: 55.2 us; the launch traced here: 54.6 us
  Pallas kernels  12.7 us (23%)
  matrix products  12.3 us (22%)
  waiting for transfers between devices  12.1 us (22%)
  starting transfers between devices  6.23 us (11%)
  other arithmetic  5.97 us (11%)
  local copies, waits for them, and re-layouts  5.07 us (9%)
    pallas_call x1, Pallas kernels, cache_partials(): pl.pallas_call(cache_partial_kernel, out_shape=(packed, packed), in_specs...  12.7 us
    dot_general x3, matrix products, project(): jnp.dot(token_rows, weight, preferred_element_type=jnp.float32)  12.3 us
    ppermute x4, waiting for transfers between devices, exchange(): return lax.ppermute(part, 'seq', pairs)  12.1 us
    ppermute x4, starting transfers between devices, exchange(): return lax.ppermute(part, 'seq', pairs)  6.23 us
    select_n x4, other arithmetic, merge(): return jnp.where(lane == HD, m, merged)  1.49 us
    max x1, other arithmetic, merge(): m = jnp.maximum(m1, m2)  1.4 us
    reduce_sum x1, other arithmetic, rms_norm(): jnp.mean(values * values, axis=-1, keepdims=True) + epsilon  1.16 us
  transfers between devices with their start and end apart: 4, of which 4 were waited for; matrix products, arithmetic and copies ran while one was open for 0% of the time, Pallas kernels for 0%

profile of v6, /device:TPU:1, one launch (start us, length us, event | category | flops | bytes accessed | tf_op | source)
XLA Modules:
  0.0 54.6 jit_solution(7286050939318134541)
XLA Ops:
  0.0 1.2 %multiply_reduce_fusion.1 = f32[8,4]{1,0:T(8,128)S(1)} fusion(bf16[8,4,1280]{2,1,0:T(4,128)(2,1)} %param.12), kind=kLoop, calls=%fused_computation.22 | loop fusion | flops 122848 | bytes 82048 | tf_op jit(solution)/shard_map/reduce_sum | solution.py:18
  1.2 0.9 %reshape.48 = f32[32,1280]{1,0:T(8,128)S(1)} reshape(bf16[8,4,1280]{2,1,0:T(4,128)(2,1)} %param.12) | data formatting | bytes 245760 | tf_op jit(solution)/shard_map/convert_element_type | solution.py:173
  2.2 6.4 %convolution_convert_fusion.proj_ref = bf16[32,3840]{1,0:T(8,128)(2,1)} fusion(bf16[1280,3840]{1,0:T(8,128)(2,1)} %param.17, f32[32,1280]{1,0:T(8,128)S(1)} %reshape.48, f32[1280]{0:T(1024)} %param.16, f32[32]{0:T(128)S(1)} %rsqrt.20), kind=kOutput, calls=%fused_computation | convolution fusion | flops 314818560 | bytes 10245248 | tf_op jit(solution)/shard_map/dot_general | solution.py:22
  8.6 12.7 %shard_map.118 = (f32[16,32,128]{2,1,0:T(8,128)}, f32[16,32,128]{2,1,0:T(8,128)}) custom-call(s32[1]{0:T(128)} %bitcast.offset_ref, s32[8]{0:T(128)} %length_ref.1, bf16[32,3840]{1,0:T(8,128)(2,1)} %convolution_convert_fusion.proj_ref, bf16[8,128,1280]{2,1,0:T(8,128)(2,1)} %key_ref.1, bf16[8,128,1280]{2,1,0:T(8,128)(2,1)} %value_ref.1, ...), custom_call_target="tpu_custom_call" | custom-call | tf_op jit(solution)/shard_map/pallas_call | solution.py:159
  21.2 1.0 %constant_dynamic-slice_fusion.1 = (f32[1,256,128]{2,1,0:T(8,128)S(1)}, f32[1,256,128]{2,1,0:T(8,128)S(1)}) fusion(f32[2,256,128]{2,1,0:T(8,128)} %bitcast.25, s32[]{:T(128)S(6)} %select_n.91, s32[]{:T(128)S(6)} %select_n.92), kind=kLoop, calls=%fused_computation.52 | loop fusion | bytes 524296 | tf_op jit(solution)/shard_map/jit(dynamic_index_in_dim)/dynamic_slice | solution.py:73
  22.2 0.8 %copy.14 = f32[1,256,128]{1,2,0:T(8,128)} copy(f32[1,256,128]{2,1,0:T(8,128)S(1)} %get-tuple-element.27) | data formatting | bytes 262144 | tf_op jit(solution)/shard_map/jit(dynamic_index_in_dim)/dynamic_slice | solution.py:74
  23.1 1.6 %collective-permute-done = f32[256,128]{0,1:T(8,128)} collective-permute-done((f32[256,128]{0,1:T(8,128)}, f32[256,128]{0,1:T(8,128)}, u32[]{:S(2)}, u32[]{:S(2)}) %collective-permute-start) | collective-permute-done | bytes 131104 | tf_op jit(solution)/shard_map/ppermute | solution.py:64
  24.7 0.9 %bitcast_select_fusion.1 = (f32[256,128]{0,1:T(8,128)S(1)}, f32[256,128]{0,1:T(8,128)S(1)}) fusion(f32[256,128]{0,1:T(8,128)} %collective-permute-done, f32[1,256,128]{1,2,0:T(8,128)S(1)} %copy.13, pred[]{:T(512)S(6)} %eq.34), kind=kLoop, calls=%fused_computation.24 | loop fusion | flops 65536 | bytes 524289 | tf_op jit(solution)/shard_map/jit(_where)/select_n | solution.py:77
  25.7 2.5 %collective-permute-start.1 = (f32[256,128]{0,1:T(8,128)S(1)}, f32[256,128]{0,1:T(8,128)S(1)}, u32[]{:S(2)}, u32[]{:S(2)}) collective-permute-start(f32[256,128]{0,1:T(8,128)S(1)} %add_select_fusion.3), channel_id=1, source_target_pairs={{0,2},{1,3},{2,0},{3,1},{4,6},{5,7},{6,4},{7,5},{8,10},{9,11},{10,... | collective-permute-start | bytes 393224 | tf_op jit(solution)/shard_map/ppermute | solution.py:64
  28.2 3.5 %collective-permute-done.1 = f32[256,128]{0,1:T(8,128)S(1)} collective-permute-done((f32[256,128]{0,1:T(8,128)S(1)}, f32[256,128]{0,1:T(8,128)S(1)}, u32[]{:S(2)}, u32[]{:S(2)}) %collective-permute-start.1) | collective-permute-done | bytes 131104 | tf_op jit(solution)/shard_map/ppermute | solution.py:64
  31.9 2.3 %collective-permute-start.2 = (f32[256,128]{0,1:T(8,128)S(1)}, f32[256,128]{0,1:T(8,128)S(1)}, u32[]{:S(2)}, u32[]{:S(2)}) collective-permute-start(f32[256,128]{0,1:T(8,128)S(1)} %add_select_fusion.2), channel_id=1, source_target_pairs={{0,4},{1,5},{2,6},{3,7},{4,0},{5,1},{6,2},{7,3},{8,12},{9,13},{10,... | collective-permute-start | bytes 393224 | tf_op jit(solution)/shard_map/ppermute | solution.py:64
  34.1 6.0 %collective-permute-done.2 = f32[256,128]{0,1:T(8,128)S(1)} collective-permute-done((f32[256,128]{0,1:T(8,128)S(1)}, f32[256,128]{0,1:T(8,128)S(1)}, u32[]{:S(2)}, u32[]{:S(2)}) %collective-permute-start.2) | collective-permute-done | bytes 131104 | tf_op jit(solution)/shard_map/ppermute | solution.py:64
  40.3 1.5 %collective-permute-start.3 = (f32[256,128]{0,1:T(8,128)S(1)}, f32[256,128]{0,1:T(8,128)S(1)}, u32[]{:S(2)}, u32[]{:S(2)}) collective-permute-start(f32[256,128]{0,1:T(8,128)S(1)} %add_select_fusion.1), channel_id=1, source_target_pairs={{0,1},{1,0},{2,3},{3,2},{4,5},{5,4},{6,7},{7,6},{8,9},{9,8},{10,11... | collective-permute-start | bytes 393224 | tf_op jit(solution)/shard_map/ppermute | solution.py:64
  41.8 1.0 %collective-permute-done.3 = f32[256,128]{0,1:T(8,128)S(1)} collective-permute-done((f32[256,128]{0,1:T(8,128)S(1)}, f32[256,128]{0,1:T(8,128)S(1)}, u32[]{:S(2)}, u32[]{:S(2)}) %collective-permute-start.3) | collective-permute-done | bytes 131104 | tf_op jit(solution)/shard_map/ppermute | solution.py:64
  42.8 0.7 %pad_maximum_fusion = f32[512,128]{0,1:T(8,128)} fusion(f32[256,128]{0,1:T(8,128)S(1)} %get-tuple-element.19, f32[256,128]{0,1:T(8,128)S(1)} %get-tuple-element.18), kind=kLoop, calls=%fused_computation.13 | loop fusion | flops 65536 | bytes 524288 | tf_op jit(solution)/shard_map/concatenate | solution.py:87
  43.5 1.1 %copy.15 = f32[512,128]{1,0:T(8,128)S(1)} copy(f32[512,128]{0,1:T(8,128)} %pad_maximum_fusion) | data formatting | bytes 524288 | tf_op jit(solution)/shard_map/concatenate | solution.py:87
  44.6 1.4 %fusion.16 = (f32[16,32]{1,0:T(8,128)S(1)}, f32[16,32]{1,0:T(8,128)S(1)}, f32[16,32]{1,0:T(8,128)S(1)}) fusion(f32[16,32,128]{2,1,0:T(8,128)} %get-tuple-element.8, f32[16,32,128]{2,1,0:T(8,128)S(1)} %bitcast.24), kind=kLoop, calls=%fused_computation.55 | loop fusion | flops 1536 | bytes 10240 | tf_op jit(solution)/shard_map/max | solution.py:54
  46.0 1.2 %add_select_fusion = f32[16,32,128]{2,1,0:T(8,128)S(1)} fusion(f32[16,32,128]{2,1,0:T(8,128)} %get-tuple-element.8, f32[16,32]{1,0:T(8,128)S(1)} %get-tuple-element.11, f32[16,32]{1,0:T(8,128)S(1)} %get-tuple-element.10, f32[16,32]{1,0:T(8,128)S(1)} %get-tuple-element.9, pred[128]{0:T(512)(128)(4,1)S(1)} %iota_compare_fusion, f32[512,128]{1,0:T(8,128)S(1)} %copy.15), kind=kLoop, calls=%fused_computation.14 | loop fusion | flops 262144 | bytes 792704 | tf_op jit(solution)/shard_map/jit(_where)/select_n | solution.py:59
  47.2 0.3 slice_reduce_fusion
  47.5 0.1 fusion.7
  47.7 0.2 convert_element_type.58
  47.9 1.7 %multiply_reduce_fusion = (f32[32]{0:T(128)S(1)}, f32[32,1280]{1,0:T(8,128)S(1)}) fusion(f32[32,1280]{1,0:T(8,128)} %copy-done.1, bf16[32,1280]{1,0:T(8,128)(2,1)S(1)} %convert_element_type.58, bf16[1280,1280]{1,0:T(8,128)(2,1)S(1)} %copy-done), kind=kOutput, calls=%fused_computation.20 | convolution fusion | flops 105062368 | bytes 3686528 | tf_op jit(solution)/shard_map/dot_general | solution.py:22
  49.6 4.2 %fusion.2 = bf16[32,1280]{1,0:T(8,128)(2,1)S(1)} fusion(f32[32,1280]{1,0:T(8,128)S(1)} %get-tuple-element.29, bf16[1280,1280]{1,0:T(8,128)(2,1)} %param.21, bf16[1280,1280]{1,0:T(8,128)(2,1)} %param.20, f32[1280]{0:T(1024)S(1)} %copy-done.2, f32[32]{0:T(128)S(1)} %add_rsqrt_fusion.1), kind=kOutput, calls=%fused_computation.4 | convolution fusion | flops 210288640 | bytes 6804608 | tf_op jit(solution)/shard_map/dot_general | solution.py:22
  53.9 0.7 %reshape.47 = bf16[8,4,1280]{2,1,0:T(4,128)(2,1)} reshape(bf16[32,1280]{1,0:T(8,128)(2,1)S(1)} %fusion.2) | data formatting | bytes 163840 | tf_op jit(solution)/shard_map/reshape | solution.py:195
  (25 shorter events, 0.7 us)
Async XLA Ops:
  0.0 47.9 %copy-start = (bf16[1280,1280]{1,0:T(8,128)(2,1)S(1)}, bf16[1280,1280]{1,0:T(8,128)(2,1)}, u32[]{:S(2)}) copy-start(bf16[1280,1280]{1,0:T(8,128)(2,1)} %param.18) | copy-start | bytes 9830404
  2.1 6.5 %copy-start.1 = (f32[32,1280]{1,0:T(8,128)}, f32[32,1280]{1,0:T(8,128)S(1)}, u32[]{:S(2)}) copy-start(f32[32,1280]{1,0:T(8,128)S(1)} %reshape.48) | copy-start | bytes 491524
  23.0 1.7 %collective-permute-start = (f32[256,128]{0,1:T(8,128)}, f32[256,128]{0,1:T(8,128)}, u32[]{:S(2)}, u32[]{:S(2)}) collective-permute-start(f32[256,128]{0,1:T(8,128)} %bitcast.26), channel_id=1, source_target_pairs={{0,1},{1,0},{2,3},{3,2},{4,5},{5,4},{6,7},{7,6},{8,9},{9,8},{10,11... | collective-permute-start | bytes 393224 | tf_op jit(solution)/shard_map/ppermute | solution.py:64
  25.7 6.0 %collective-permute-start.1 = (f32[256,128]{0,1:T(8,128)S(1)}, f32[256,128]{0,1:T(8,128)S(1)}, u32[]{:S(2)}, u32[]{:S(2)}) collective-permute-start(f32[256,128]{0,1:T(8,128)S(1)} %add_select_fusion.3), channel_id=1, source_target_pairs={{0,2},{1,3},{2,0},{3,1},{4,6},{5,7},{6,4},{7,5},{8,10},{9,11},{10,... | collective-permute-start | bytes 393224 | tf_op jit(solution)/shard_map/ppermute | solution.py:64
  31.9 8.3 %collective-permute-start.2 = (f32[256,128]{0,1:T(8,128)S(1)}, f32[256,128]{0,1:T(8,128)S(1)}, u32[]{:S(2)}, u32[]{:S(2)}) collective-permute-start(f32[256,128]{0,1:T(8,128)S(1)} %add_select_fusion.2), channel_id=1, source_target_pairs={{0,4},{1,5},{2,6},{3,7},{4,0},{5,1},{6,2},{7,3},{8,12},{9,13},{10,... | collective-permute-start | bytes 393224 | tf_op jit(solution)/shard_map/ppermute | solution.py:64
  40.3 2.4 %collective-permute-start.3 = (f32[256,128]{0,1:T(8,128)S(1)}, f32[256,128]{0,1:T(8,128)S(1)}, u32[]{:S(2)}, u32[]{:S(2)}) collective-permute-start(f32[256,128]{0,1:T(8,128)S(1)} %add_select_fusion.1), channel_id=1, source_target_pairs={{0,1},{1,0},{2,3},{3,2},{4,5},{5,4},{6,7},{7,6},{8,9},{9,8},{10,11... | collective-permute-start | bytes 393224 | tf_op jit(solution)/shard_map/ppermute | solution.py:64
  43.5 6.1 %copy-start.2 = (f32[1280]{0:T(1024)S(1)}, f32[1280]{0:T(1024)}, u32[]{:S(2)}) copy-start(f32[1280]{0:T(1024)} %param.19) | copy-start | bytes 15364

commit v7 on v6

--- a/solution.py
+++ b/solution.py
@@ -1,3 +1,5 @@
+import functools
+
 import numpy as np
 import jax
 import jax.numpy as jnp
@@ -22,30 +24,7 @@
     return jnp.dot(token_rows, weight, preferred_element_type=jnp.float32).astype(jnp.bfloat16)
 
 
-def head_mask(heads, width):
-    return (jnp.arange(width)[None, :] // HD) == jnp.arange(heads)[:, None]
-
-
-def per_head_queries(queries, mask):
-    groups, count, width = queries.shape
-    heads = mask.shape[0]
-    blocks = jnp.where(mask[None, None], queries[:, :, None, :], jnp.zeros((), queries.dtype))
-    return blocks.reshape(groups, count * heads, width)
-
-
-def head_diagonal(rows, mask):
-    groups, count_heads, width = rows.shape
-    heads = mask.shape[0]
-    rows = rows.reshape(groups, count_heads // heads, heads, width)
-    return jnp.sum(jnp.where(mask[None, None], rows, 0.0), axis=2)
-
-
 LANES = 128
-
-
-def pack(values, peak, weight_sum):
-    pad = jnp.zeros(values.shape[:-1] + (LANES - HD - 2,), jnp.float32)
-    return jnp.concatenate([values, peak[..., None], weight_sum[..., None], pad], axis=-1)
 
 
 def merge(first, second):
@@ -87,10 +66,19 @@
     return jnp.concatenate([low_half, high_half], axis=0).reshape(heads, rows, lanes)
 
 
-def cache_partial_kernel(
-    offset_ref, length_ref, proj_ref, key_ref, value_ref, qmask_ref, fold_ref, out_ref, new_ref
-):
-    groups, slots, width = key_ref.shape
+def folded_store(target, r, rows, peak, total, qmask_float, fold, lane):
+    heads = target.shape[0]
+    count = rows.shape[0] // heads
+    folded = jnp.dot(
+        rows * qmask_float, fold, precision=lax.Precision.HIGHEST, preferred_element_type=jnp.float32
+    )
+    folded = jnp.where(lane == HD, peak, jnp.where(lane == HD + 1, total, folded))
+    for h in range(heads):
+        target[h, pl.ds(r * count, count), :] = folded[h * count:(h + 1) * count, :]
+
+
+def cache_partial_kernel(offset_ref, length_ref, query_ref, key_ref, value_ref, qmask_ref, fold_ref, out_ref):
+    groups, slots, _ = key_ref.shape
     heads = out_ref.shape[0]
     count = out_ref.shape[1] // groups
     scale_factor = HD ** (-0.5)
@@ -99,18 +87,8 @@
     fold = fold_ref[...]
     position = offset_ref[0] + lax.broadcasted_iota(jnp.int32, (1, slots), 1)
     lane = lax.broadcasted_iota(jnp.int32, (heads * count, LANES), 1)
-    patch = lax.broadcasted_iota(jnp.int32, (heads * count, 1), 0) & (count - 1)
-
-    def emit(target, r, rows, peak, total):
-        folded = jnp.dot(
-            rows * qmask_float, fold, precision=lax.Precision.HIGHEST, preferred_element_type=jnp.float32
-        )
-        folded = jnp.where(lane == HD, peak, jnp.where(lane == HD + 1, total, folded))
-        for h in range(heads):
-            target[h, pl.ds(r * count, count), :] = folded[h * count:(h + 1) * count, :]
-
     for r in range(groups):
-        queries = proj_ref[pl.ds(r * count, count), pl.ds(0, width)]
+        queries = query_ref[pl.ds(r * count, count), :]
         query_rows = jnp.concatenate([queries] * heads, axis=0) * qmask
         scores = lax.dot_general(
             query_rows, key_ref[r], (((1,), (1,)), ((), ())), preferred_element_type=jnp.float32
@@ -123,11 +101,24 @@
         value_rows = jnp.dot(
             weights.astype(jnp.bfloat16), value_ref[r], preferred_element_type=jnp.float32
         )
-        emit(out_ref, r, value_rows, peak, total)
-
-        query_float = query_rows.astype(jnp.float32)
-        keys_new = proj_ref[pl.ds(r * count, count), pl.ds(width, width)].astype(jnp.float32)
-        values_new = proj_ref[pl.ds(r * count, count), pl.ds(2 * width, width)].astype(jnp.float32)
+        folded_store(out_ref, r, value_rows, peak, total, qmask_float, fold, lane)
+
+
+def new_partial_kernel(count, query_ref, kv_ref, qmask_ref, fold_ref, out_ref):
+    rows_all, width = query_ref.shape
+    heads = out_ref.shape[0]
+    groups = rows_all // count
+    scale_factor = HD ** (-0.5)
+    qmask = qmask_ref[...]
+    qmask_float = qmask.astype(jnp.float32)
+    fold = fold_ref[...]
+    lane = lax.broadcasted_iota(jnp.int32, (heads * count, LANES), 1)
+    patch = lax.broadcasted_iota(jnp.int32, (heads * count, 1), 0) & (count - 1)
+    for r in range(groups):
+        queries = query_ref[pl.ds(r * count, count), :]
+        query_float = (jnp.concatenate([queries] * heads, axis=0) * qmask).astype(jnp.float32)
+        keys_new = kv_ref[pl.ds(r * count, count), pl.ds(0, width)].astype(jnp.float32)
+        values_new = kv_ref[pl.ds(r * count, count), pl.ds(width, width)].astype(jnp.float32)
         new_scores = []
         for u in range(count):
             score = jnp.sum(query_float * keys_new[u:u + 1, :], axis=1, keepdims=True) * scale_factor
@@ -142,29 +133,44 @@
             new_total = new_total + weight
             weight = weight.astype(jnp.bfloat16).astype(jnp.float32)
             new_rows = new_rows + weight * values_new[u:u + 1, :]
-        emit(new_ref, r, new_rows, new_peak, new_total)
-
-
-def cache_partials(offset, cache_len, projected_rows, key_cache, value_cache):
-    groups, slots, width = key_cache.shape
-    rows = projected_rows.shape[0]
-    count = rows // groups
+        folded_store(out_ref, r, new_rows, new_peak, new_total, qmask_float, fold, lane)
+
+
+def head_constants(count, width):
     row_head = np.arange(HEADS * count)[:, None] // count
     col_head = np.arange(width)[None, :] // HD
     qmask = jnp.asarray((row_head == col_head).astype(np.float32), dtype=jnp.bfloat16)
     fold = jnp.asarray((np.arange(width)[:, None] % HD == np.arange(LANES)[None, :]).astype(np.float32))
+    return qmask, fold
+
+
+def cache_partials(offset, cache_len, query_rows, key_cache, value_cache):
+    groups, _, width = key_cache.shape
+    rows = query_rows.shape[0]
+    qmask, fold = head_constants(rows // groups, width)
     smem = pl.BlockSpec(memory_space=pltpu.SMEM)
     vmem = pl.BlockSpec(memory_space=pltpu.VMEM)
-    packed = jax.ShapeDtypeStruct((HEADS, rows, LANES), jnp.float32)
     return pl.pallas_call(
         cache_partial_kernel,
-        out_shape=(packed, packed),
+        out_shape=jax.ShapeDtypeStruct((HEADS, rows, LANES), jnp.float32),
         in_specs=[smem, smem, vmem, vmem, vmem, vmem, vmem],
-        out_specs=(vmem, vmem),
-    )(offset, cache_len, projected_rows, key_cache, value_cache, qmask, fold)
-
-
-def shards(
+        out_specs=vmem,
+    )(offset, cache_len, query_rows, key_cache, value_cache, qmask, fold)
+
+
+def new_partials(query_rows, kv_rows, count):
+    rows, width = query_rows.shape
+    qmask, fold = head_constants(count, width)
+    vmem = pl.BlockSpec(memory_space=pltpu.VMEM)
+    return pl.pallas_call(
+        functools.partial(new_partial_kernel, count),
+        out_shape=jax.ShapeDtypeStruct((HEADS, rows, LANES), jnp.float32),
+        in_specs=[vmem, vmem, vmem, vmem],
+        out_specs=vmem,
+    )(query_rows, kv_rows, qmask, fold)
+
+
+def layer(
     patches, key_cache, value_cache, cache_len, attn_gain, w_qkv, w_out, ffn_gain, w_up, w_down
 ):
     groups, count_new, model_width = patches.shape
@@ -172,16 +178,12 @@
     seq_count = lax.axis_size("seq")
     inputs = patches.reshape(groups * count_new, model_width).astype(jnp.float32)
     normed = rms_norm(inputs, attn_gain).astype(jnp.bfloat16)
-    projected = project(normed, w_qkv).reshape(groups, count_new, 3 * model_width)
-    queries = projected[:, :, :model_width]
-    keys_new = projected[:, :, model_width:2 * model_width]
-    values_new = projected[:, :, 2 * model_width:]
-    scale_factor = HD ** (-0.5)
     rows = groups * count_new
+    query_rows = project(normed, w_qkv[:, :model_width])
     offset = (lax.axis_index("seq") * slots_here).astype(jnp.int32).reshape(1)
-    packed, new_packed = cache_partials(
-        offset, cache_len, projected.reshape(rows, 3 * model_width), key_cache, value_cache
-    )
+    packed = cache_partials(offset, cache_len, query_rows, key_cache, value_cache)
+    kv_rows = project(normed, w_qkv[:, model_width:])
+    new_packed = new_partials(query_rows, kv_rows, count_new)
     total = merge(combine_over_seq(packed, seq_count), new_packed)
     attended_heads = total[..., :HD] / total[..., HD + 1:HD + 2]
     attended = attended_heads.transpose(1, 0, 2).reshape(rows, model_width).astype(jnp.bfloat16)
@@ -209,5 +211,5 @@
         P(),
     )
     return jax.shard_map(
-        shards, mesh=mesh, in_specs=placed, out_specs=P("req", None, None), check_vma=False
+        layer, mesh=mesh, in_specs=placed, out_specs=P("req", None, None), check_vma=False
     )

time: 55.2 us -> 66.4 us (1.20)
  other arithmetic: 5.97 us -> 10.8 us
  local copies, waits for them, and re-layouts: 5.07 us -> 8.4 us
  Pallas kernels: 12.7 us -> 15.7 us
  matrix products: 12.3 us -> 14.1 us
  waiting for transfers between devices: 12.1 us -> 10.5 us
    pallas_call x1 -> x2, Pallas kernels: 12.7 us -> 15.7 us  [the longest x1 10 us: cache_partials(): pl.pallas_call(cache_partial_kernel, out_shape=jax.ShapeDtypeStruct((HEAD...]
    dynamic_slice x2, local copies, waits for them, and re-layouts: 1.08 us -> 3.34 us  [combine_over_seq(): kept = lax.dynamic_index_in_dim(halves, core, axis=0, keepdims=False)]
    select_n x4, other arithmetic: 1.49 us -> 3.43 us  [merge(): return jnp.where(lane == HD, m, merged)]
    select_n x2, other arithmetic: 0.04 us -> 1.97 us  [combine_over_seq(): jnp.where(low_first, state, got)]
    dot_general x3 -> x4, matrix products: 12.3 us -> 14.1 us  [project(): jnp.dot(token_rows, weight, preferred_element_type=jnp.float32)]
    ppermute x4, waiting for transfers between devices: 12.1 us -> 10.5 us  [exchange(): return lax.ppermute(part, 'seq', pairs)]
    select_n x1, other arithmetic: 0.02 us -> 0.99 us  [combine_over_seq(): low_half = jnp.where(core == 0, state, other)]
    dynamic_slice x1, local copies, waits for them, and re-layouts: 0.76 us -> 1.67 us  [combine_over_seq(): sent = lax.dynamic_index_in_dim(halves, 1 - core, axis=0, keepdims=False)]
  transfers between devices with their start and end apart: 4 -> 4, of which waited for: 4 -> 2; matrix products, arithmetic and copies ran while one was open for 0% -> 10% of each run, Pallas kernels for 0% -> 9%
where the time goes in v7:
time: 66.4 us; the launch traced here: 66 us
  Pallas kernels  15.7 us (24%)
  matrix products  14.1 us (21%)
  other arithmetic  10.8 us (16%)
  waiting for transfers between devices  10.5 us (16%)
  local copies, waits for them, and re-layouts  8.4 us (13%)
  starting transfers between devices  6.36 us (10%)
    dot_general x4, matrix products, project(): jnp.dot(token_rows, weight, preferred_element_type=jnp.float32)  14.1 us
    ppermute x4, waiting for transfers between devices, exchange(): return lax.ppermute(part, 'seq', pairs)  10.5 us
    pallas_call x1, Pallas kernels, cache_partials(): pl.pallas_call(cache_partial_kernel, out_shape=jax.ShapeDtypeStruct((HEAD...  10 us
    ppermute x4, starting transfers between devices, exchange(): return lax.ppermute(part, 'seq', pairs)  6.36 us
    pallas_call x1, Pallas kernels, new_partials(): pl.pallas_call(functools.partial(new_partial_kernel, count), out_shape=ja...  5.68 us
    select_n x4, other arithmetic, merge(): return jnp.where(lane == HD, m, merged)  3.43 us
    dynamic_slice x2, local copies, waits for them, and re-layouts, combine_over_seq(): kept = lax.dynamic_index_in_dim(halves, core, axis=0, keepdims=False)  3.34 us
    select_n x2, other arithmetic, combine_over_seq(): jnp.where(low_first, state, got)  1.97 us
  transfers between devices with their start and end apart: 4, of which 2 were waited for; matrix products, arithmetic and copies ran while one was open for 10% of the time, Pallas kernels for 9%

profile of v7, /device:TPU:1, one launch (start us, length us, event | category | flops | bytes accessed | tf_op | source)
XLA Modules:
  0.0 66.0 jit_solution(3924997321620258722)
XLA Ops:
  0.0 1.0 %reshape.48 = f32[32,1280]{1,0:T(8,128)S(1)} reshape(bf16[8,4,1280]{2,1,0:T(4,128)(2,1)} %param.14) | data formatting | bytes 245760 | tf_op jit(solution)/shard_map/convert_element_type | solution.py:179
  1.1 1.1 %multiply_reduce_fusion.1 = f32[8,4]{1,0:T(8,128)S(1)} fusion(bf16[8,4,1280]{2,1,0:T(4,128)(2,1)} %param.14), kind=kLoop, calls=%fused_computation.27 | loop fusion | flops 122848 | bytes 82048 | tf_op jit(solution)/shard_map/reduce_sum | solution.py:20
  2.2 3.3 %fusion.7.query_ref = bf16[32,1280]{1,0:T(8,128)(2,1)} fusion(bf16[1280,3840]{1,0:T(8,128)(2,1)} %param.19, f32[32,1280]{1,0:T(8,128)S(1)} %reshape.48, f32[1280]{0:T(1024)} %param.18, f32[32]{0:T(128)S(1)} %rsqrt.20), kind=kOutput, calls=%fused_computation.5 | convolution fusion | flops 105021440 | bytes 3530880 | tf_op jit(solution)/shard_map/dot_general | solution.py:24
  5.6 10.0 %shard_map.136 = f32[16,32,128]{2,1,0:T(8,128)} custom-call(s32[1]{0:T(128)} %bitcast.offset_ref, s32[8]{0:T(128)} %length_ref.1, bf16[32,1280]{1,0:T(8,128)(2,1)} %fusion.7.query_ref, bf16[8,128,1280]{2,1,0:T(8,128)(2,1)} %key_ref.1, bf16[8,128,1280]{2,1,0:T(8,128)(2,1)} %value_ref.1, bf16[64,1280]{1,0:T(8,128)(2,1)} %constant.75.clone.qmask_ref, ...), custom_call_target="tpu_custom_call" | custom-call | tf_op jit(solution)/shard_map/pallas_call | solution.py:153
  15.6 1.7 %constant_dynamic-slice_fusion.1 = (f32[1,256,128]{2,1,0:T(8,128)}, f32[1,256,128]{2,1,0:T(8,128)}) fusion(f32[2,256,128]{2,1,0:T(8,128)} %bitcast.24, s32[]{:T(128)S(6)} %select_n.91, s32[]{:T(128)S(6)} %select_n.92), kind=kLoop, calls=%fused_computation.55 | loop fusion | bytes 524296 | tf_op jit(solution)/shard_map/jit(dynamic_index_in_dim)/dynamic_slice | solution.py:52
  17.3 1.7 %copy.16 = f32[1,256,128]{1,2,0:T(8,128)} copy(f32[1,256,128]{2,1,0:T(8,128)} %get-tuple-element.23) | data formatting | bytes 262144 | tf_op jit(solution)/shard_map/jit(dynamic_index_in_dim)/dynamic_slice | solution.py:53
  19.0 1.6 %copy.15 = f32[1,256,128]{1,2,0:T(8,128)} copy(f32[1,256,128]{2,1,0:T(8,128)} %get-tuple-element.22) | data formatting | bytes 262144 | tf_op jit(solution)/shard_map/jit(dynamic_index_in_dim)/dynamic_slice | solution.py:52
  20.6 1.0 %bitcast_select_fusion.1 = (f32[256,128]{0,1:T(8,128)S(1)}, f32[256,128]{0,1:T(8,128)S(1)}) fusion(f32[256,128]{0,1:T(8,128)} %collective-permute-done, f32[1,256,128]{1,2,0:T(8,128)} %copy.15, pred[]{:T(512)S(6)} %eq.34), kind=kLoop, calls=%fused_computation.29 | loop fusion | flops 65536 | bytes 524289 | tf_op jit(solution)/shard_map/jit(_where)/select_n | solution.py:56
  22.4 2.8 %collective-permute-start.1 = (f32[256,128]{0,1:T(8,128)}, f32[256,128]{0,1:T(8,128)}, u32[]{:S(2)}, u32[]{:S(2)}) collective-permute-start(f32[256,128]{0,1:T(8,128)} %add_select_fusion.3), channel_id=1, source_target_pairs={{0,2},{1,3},{2,0},{3,1},{4,6},{5,7},{6,4},{7,5},{8,10},{9,11},{10,... | collective-permute-start | bytes 393224 | tf_op jit(solution)/shard_map/ppermute | solution.py:43
  25.1 4.2 %collective-permute-done.1 = f32[256,128]{0,1:T(8,128)} collective-permute-done((f32[256,128]{0,1:T(8,128)}, f32[256,128]{0,1:T(8,128)}, u32[]{:S(2)}, u32[]{:S(2)}) %collective-permute-start.1) | collective-permute-done | bytes 131104 | tf_op jit(solution)/shard_map/ppermute | solution.py:43
  29.3 1.0 %broadcast_select_fusion.1 = (f32[256,128]{0,1:T(8,128)S(1)}, f32[256,128]{0,1:T(8,128)S(1)}) fusion(f32[256,128]{0,1:T(8,128)} %add_select_fusion.3, f32[256,128]{0,1:T(8,128)} %collective-permute-done.1, pred[]{:T(512)S(6)} %eq.36), kind=kLoop, calls=%fused_computation.38 | loop fusion | flops 65536 | bytes 524289 | tf_op jit(solution)/shard_map/jit(_where)/select_n | solution.py:61
  31.0 2.2 %collective-permute-start.2 = (f32[256,128]{0,1:T(8,128)}, f32[256,128]{0,1:T(8,128)}, u32[]{:S(2)}, u32[]{:S(2)}) collective-permute-start(f32[256,128]{0,1:T(8,128)} %add_select_fusion.2), channel_id=1, source_target_pairs={{0,4},{1,5},{2,6},{3,7},{4,0},{5,1},{6,2},{7,3},{8,12},{9,13},{10,... | collective-permute-start | bytes 393224 | tf_op jit(solution)/shard_map/ppermute | solution.py:43
  33.2 6.3 %collective-permute-done.2 = f32[256,128]{0,1:T(8,128)} collective-permute-done((f32[256,128]{0,1:T(8,128)}, f32[256,128]{0,1:T(8,128)}, u32[]{:S(2)}, u32[]{:S(2)}) %collective-permute-start.2) | collective-permute-done | bytes 131104 | tf_op jit(solution)/shard_map/ppermute | solution.py:43
  39.6 1.0 %broadcast_select_fusion.3 = (f32[256,128]{0,1:T(8,128)S(1)}, f32[256,128]{0,1:T(8,128)S(1)}) fusion(f32[256,128]{0,1:T(8,128)} %add_select_fusion.2, f32[256,128]{0,1:T(8,128)} %collective-permute-done.2, pred[]{:T(512)S(6)} %eq.35), kind=kLoop, calls=%fused_computation.40 | loop fusion | flops 65536 | bytes 524289 | tf_op jit(solution)/shard_map/jit(_where)/select_n | solution.py:61
  40.6 0.7 %add_select_fusion.1 = f32[256,128]{0,1:T(8,128)} fusion(f32[256,128]{0,1:T(8,128)S(1)} %get-tuple-element.17, f32[256,128]{0,1:T(8,128)S(1)} %get-tuple-element.16, f32[256]{0:T(256)S(1)} %bitcast.31, f32[256]{0:T(256)S(1)} %bitcast.34, f32[256]{0:T(256)S(1)} %bitcast.28, pred[128]{0:T(512)(128)(4,1)S(1)} %iota_compare_fusion), kind=kLoop, calls=%fused_computation.30 | loop fusion | flops 131072 | bytes 396416 | tf_op jit(solution)/shard_map/jit(_where)/select_n | solution.py:38
  41.4 1.4 %collective-permute-start.3 = (f32[256,128]{0,1:T(8,128)}, f32[256,128]{0,1:T(8,128)}, u32[]{:S(2)}, u32[]{:S(2)}) collective-permute-start(f32[256,128]{0,1:T(8,128)} %add_select_fusion.1), channel_id=1, source_target_pairs={{0,1},{1,0},{2,3},{3,2},{4,5},{5,4},{6,7},{7,6},{8,9},{9,8},{10,11... | collective-permute-start | bytes 393224 | tf_op jit(solution)/shard_map/ppermute | solution.py:43
  42.8 4.8 %fusion.2.kv_ref = bf16[32,2560]{1,0:T(8,128)(2,1)} fusion(bf16[1280,3840]{1,0:T(8,128)(2,1)} %param.19, f32[32,1280]{1,0:T(8,128)S(1)} %reshape.48, f32[1280]{0:T(1024)S(1)} %copy-done.3, f32[32]{0:T(128)S(1)} %rsqrt.20), kind=kOutput, calls=%fused_computation.2 | convolution fusion | flops 209920000 | bytes 6886528 | tf_op jit(solution)/shard_map/dot_general | solution.py:24
  47.5 5.7 %shard_map.137 = f32[16,32,128]{2,1,0:T(8,128)} custom-call(bf16[32,1280]{1,0:T(8,128)(2,1)} %fusion.7.query_ref, bf16[32,2560]{1,0:T(8,128)(2,1)} %fusion.2.kv_ref, bf16[64,1280]{1,0:T(8,128)(2,1)} %constant.75.clone.qmask_ref, f32[1280,128]{1,0:T(8,128)} %constant.76.clone.fold_ref), custom_call_target="tpu_custom_call" | custom-call | tf_op jit(solution)/shard_map/pallas_call | solution.py:165
  53.2 1.0 %broadcast_select_fusion.5 = (f32[256,128]{0,1:T(8,128)S(1)}, f32[256,128]{0,1:T(8,128)S(1)}) fusion(f32[256,128]{0,1:T(8,128)} %add_select_fusion.1, f32[256,128]{0,1:T(8,128)} %collective-permute-done.3, pred[]{:T(512)S(6)} %eq.34), kind=kLoop, calls=%fused_computation.42 | loop fusion | flops 65536 | bytes 524289 | tf_op jit(solution)/shard_map/jit(_where)/select_n | solution.py:64
  54.9 1.1 %copy.17 = f32[512,128]{1,0:T(8,128)S(1)} copy(f32[512,128]{0,1:T(8,128)} %pad_maximum_fusion) | data formatting | bytes 524288 | tf_op jit(solution)/shard_map/concatenate | solution.py:66
  56.0 1.4 %fusion.24 = (f32[16,32]{1,0:T(8,128)S(1)}, f32[16,32]{1,0:T(8,128)S(1)}, f32[16,32]{1,0:T(8,128)S(1)}) fusion(f32[16,32,128]{2,1,0:T(8,128)} %shard_map.137, f32[16,32,128]{2,1,0:T(8,128)S(1)} %bitcast.23), kind=kLoop, calls=%fused_computation.58 | loop fusion | flops 1536 | bytes 10240 | tf_op jit(solution)/shard_map/max | solution.py:33
  57.4 1.2 %add_select_fusion = f32[16,32,128]{2,1,0:T(8,128)S(1)} fusion(f32[16,32,128]{2,1,0:T(8,128)} %shard_map.137, f32[16,32]{1,0:T(8,128)S(1)} %get-tuple-element.7, f32[16,32]{1,0:T(8,128)S(1)} %get-tuple-element.6, f32[16,32]{1,0:T(8,128)S(1)} %get-tuple-element.5, pred[128]{0:T(512)(128)(4,1)S(1)} %iota_compare_fusion, f32[512,128]{1,0:T(8,128)S(1)} %copy.17), kind=kLoop, calls=%fused_computation.19 | loop fusion | flops 262144 | bytes 792704 | tf_op jit(solution)/shard_map/jit(_where)/select_n | solution.py:38
  59.3 1.7 %multiply_reduce_fusion = (f32[32]{0:T(128)S(1)}, f32[32,1280]{1,0:T(8,128)S(1)}) fusion(f32[32,1280]{1,0:T(8,128)} %copy-done.1, bf16[32,1280]{1,0:T(8,128)(2,1)S(1)} %convert_element_type.62, bf16[1280,1280]{1,0:T(8,128)(2,1)S(1)} %copy-done), kind=kOutput, calls=%fused_computation.25 | convolution fusion | flops 105062368 | bytes 3686528 | tf_op jit(solution)/shard_map/dot_general | solution.py:24
  61.1 4.2 %fusion.12 = bf16[32,1280]{1,0:T(8,128)(2,1)S(1)} fusion(f32[32,1280]{1,0:T(8,128)S(1)} %get-tuple-element.25, bf16[1280,1280]{1,0:T(8,128)(2,1)} %param.23, bf16[1280,1280]{1,0:T(8,128)(2,1)} %param.22, f32[1280]{0:T(1024)S(1)} %copy-done.2, f32[32]{0:T(128)S(1)} %add_rsqrt_fusion.1), kind=kOutput, calls=%fused_computation.9 | convolution fusion | flops 210288640 | bytes 6804608 | tf_op jit(solution)/shard_map/dot_general | solution.py:24
  (29 shorter events, 3.7 us)
Async XLA Ops:
  0.0 59.3 %copy-start = (bf16[1280,1280]{1,0:T(8,128)(2,1)S(1)}, bf16[1280,1280]{1,0:T(8,128)(2,1)}, u32[]{:S(2)}) copy-start(bf16[1280,1280]{1,0:T(8,128)(2,1)} %param.20) | copy-start | bytes 9830404
  1.1 41.7 %copy-start.1 = (f32[32,1280]{1,0:T(8,128)}, f32[32,1280]{1,0:T(8,128)S(1)}, u32[]{:S(2)}) copy-start(f32[32,1280]{1,0:T(8,128)S(1)} %reshape.48) | copy-start | bytes 491524
  15.6 27.2 %copy-start.3 = (f32[1280]{0:T(1024)S(1)}, f32[1280]{0:T(1024)}, u32[]{:S(2)}) copy-start(f32[1280]{0:T(1024)} %param.18) | copy-start | bytes 15364
  18.9 1.7 %collective-permute-start = (f32[256,128]{0,1:T(8,128)}, f32[256,128]{0,1:T(8,128)}, u32[]{:S(2)}, u32[]{:S(2)}) collective-permute-start(f32[256,128]{0,1:T(8,128)} %bitcast.25), channel_id=1, source_target_pairs={{0,1},{1,0},{2,3},{3,2},{4,5},{5,4},{6,7},{7,6},{8,9},{9,8},{10,11... | collective-permute-start | bytes 393224 | tf_op jit(solution)/shard_map/ppermute | solution.py:43
  22.4 6.9 %collective-permute-start.1 = (f32[256,128]{0,1:T(8,128)}, f32[256,128]{0,1:T(8,128)}, u32[]{:S(2)}, u32[]{:S(2)}) collective-permute-start(f32[256,128]{0,1:T(8,128)} %add_select_fusion.3), channel_id=1, source_target_pairs={{0,2},{1,3},{2,0},{3,1},{4,6},{5,7},{6,4},{7,5},{8,10},{9,11},{10,... | collective-permute-start | bytes 393224 | tf_op jit(solution)/shard_map/ppermute | solution.py:43
  31.0 8.5 %collective-permute-start.2 = (f32[256,128]{0,1:T(8,128)}, f32[256,128]{0,1:T(8,128)}, u32[]{:S(2)}, u32[]{:S(2)}) collective-permute-start(f32[256,128]{0,1:T(8,128)} %add_select_fusion.2), channel_id=1, source_target_pairs={{0,4},{1,5},{2,6},{3,7},{4,0},{5,1},{6,2},{7,3},{8,12},{9,13},{10,... | collective-permute-start | bytes 393224 | tf_op jit(solution)/shard_map/ppermute | solution.py:43
  41.4 11.9 %collective-permute-start.3 = (f32[256,128]{0,1:T(8,128)}, f32[256,128]{0,1:T(8,128)}, u32[]{:S(2)}, u32[]{:S(2)}) collective-permute-start(f32[256,128]{0,1:T(8,128)} %add_select_fusion.1), channel_id=1, source_target_pairs={{0,1},{1,0},{2,3},{3,2},{4,5},{5,4},{6,7},{7,6},{8,9},{9,8},{10,11... | collective-permute-start | bytes 393224 | tf_op jit(solution)/shard_map/ppermute | solution.py:43
  54.9 6.1 %copy-start.2 = (f32[1280]{0:T(1024)S(1)}, f32[1280]{0:T(1024)}, u32[]{:S(2)}) copy-start(f32[1280]{0:T(1024)} %param.21) | copy-start | bytes 15364

commit v8 on v7

--- a/solution.py
+++ b/solution.py
@@ -5,6 +5,7 @@
 import jax.numpy as jnp
 from jax import lax
 from jax.sharding import PartitionSpec as P
+from jax.experimental.layout import Layout, with_layout_constraint
 from jax.experimental import pallas as pl
 from jax.experimental.pallas import tpu as pltpu
 
@@ -40,17 +41,17 @@
 
 def exchange(part, distance, count):
     pairs = [(i, i ^ distance) for i in range(count)]
-    return lax.ppermute(part, "seq", pairs)
-
-
-def combine_over_seq(packed, count):
-    heads, rows, lanes = packed.shape
-    half_heads = heads // 2
+    row_major = Layout(major_to_minor=(0, 1))
+    part = with_layout_constraint(part, row_major)
+    return with_layout_constraint(lax.ppermute(part, "seq", pairs), row_major)
+
+
+def combine_over_seq(kept, sent, count):
+    half_heads, rows, lanes = kept.shape
     me = lax.axis_index("seq")
     core = me % 2
-    halves = packed.reshape(2, half_heads * rows, lanes)
-    kept = lax.dynamic_index_in_dim(halves, core, axis=0, keepdims=False)
-    sent = lax.dynamic_index_in_dim(halves, 1 - core, axis=0, keepdims=False)
+    kept = kept.reshape(half_heads * rows, lanes)
+    sent = sent.reshape(half_heads * rows, lanes)
     got = exchange(sent, 1, count)
     low_first = core == 0
     state = merge(jnp.where(low_first, kept, got), jnp.where(low_first, got, kept))
@@ -63,24 +64,32 @@
     other = exchange(state, 1, count)
     low_half = jnp.where(core == 0, state, other)
     high_half = jnp.where(core == 0, other, state)
-    return jnp.concatenate([low_half, high_half], axis=0).reshape(heads, rows, lanes)
+    return low_half.reshape(half_heads, rows, lanes), high_half.reshape(half_heads, rows, lanes)
+
+
+def folded_rows(rows, peak, total, qmask_float, fold, lane):
+    folded = jnp.dot(
+        rows * qmask_float, fold, precision=lax.Precision.HIGHEST, preferred_element_type=jnp.float32
+    )
+    return jnp.where(lane == HD, peak, jnp.where(lane == HD + 1, total, folded))
 
 
 def folded_store(target, r, rows, peak, total, qmask_float, fold, lane):
     heads = target.shape[0]
     count = rows.shape[0] // heads
-    folded = jnp.dot(
-        rows * qmask_float, fold, precision=lax.Precision.HIGHEST, preferred_element_type=jnp.float32
-    )
-    folded = jnp.where(lane == HD, peak, jnp.where(lane == HD + 1, total, folded))
+    folded = folded_rows(rows, peak, total, qmask_float, fold, lane)
     for h in range(heads):
         target[h, pl.ds(r * count, count), :] = folded[h * count:(h + 1) * count, :]
 
 
-def cache_partial_kernel(offset_ref, length_ref, query_ref, key_ref, value_ref, qmask_ref, fold_ref, out_ref):
+def cache_partial_kernel(
+    offset_ref, length_ref, query_ref, key_ref, value_ref, qmask_ref, fold_ref, kept_ref, sent_ref
+):
     groups, slots, _ = key_ref.shape
-    heads = out_ref.shape[0]
-    count = out_ref.shape[1] // groups
+    half_heads = kept_ref.shape[0]
+    heads = 2 * half_heads
+    count = kept_ref.shape[1] // groups
+    core = offset_ref[1]
     scale_factor = HD ** (-0.5)
     qmask = qmask_ref[...]
     qmask_float = qmask.astype(jnp.float32)
@@ -101,7 +110,18 @@
         value_rows = jnp.dot(
             weights.astype(jnp.bfloat16), value_ref[r], preferred_element_type=jnp.float32
         )
-        folded_store(out_ref, r, value_rows, peak, total, qmask_float, fold, lane)
+        folded = folded_rows(value_rows, peak, total, qmask_float, fold, lane)
+        for h in range(heads):
+            block = folded[h * count:(h + 1) * count, :]
+            rows_here = pl.ds(r * count, count)
+
+            @pl.when(core == h // half_heads)
+            def _():
+                kept_ref[h % half_heads, rows_here, :] = block
+
+            @pl.when(core != h // half_heads)
+            def _():
+                sent_ref[h % half_heads, rows_here, :] = block
 
 
 def new_partial_kernel(count, query_ref, kv_ref, qmask_ref, fold_ref, out_ref):
@@ -150,11 +170,12 @@
     qmask, fold = head_constants(rows // groups, width)
     smem = pl.BlockSpec(memory_space=pltpu.SMEM)
     vmem = pl.BlockSpec(memory_space=pltpu.VMEM)
+    half = jax.ShapeDtypeStruct((HEADS // 2, rows, LANES), jnp.float32)
     return pl.pallas_call(
         cache_partial_kernel,
-        out_shape=jax.ShapeDtypeStruct((HEADS, rows, LANES), jnp.float32),
+        out_shape=(half, half),
         in_specs=[smem, smem, vmem, vmem, vmem, vmem, vmem],
-        out_specs=vmem,
+        out_specs=(vmem, vmem),
     )(offset, cache_len, query_rows, key_cache, value_cache, qmask, fold)
 
 
@@ -170,6 +191,43 @@
     )(query_rows, kv_rows, qmask, fold)
 
 
+def tail_kernel(low_ref, high_ref, new_ref, patch_ref, w_out_ref, gain_ref, w_up_ref, w_down_ref, out_ref):
+    half_heads, rows, _ = low_ref.shape
+    width = w_out_ref.shape[0]
+    out_sum = jnp.zeros((rows, width), jnp.float32)
+    for h in range(2 * half_heads):
+        source = low_ref if h < half_heads else high_ref
+        first = source[h % half_heads]
+        second = new_ref[h]
+        m1 = first[:, HD:HD + 1]
+        m2 = second[:, HD:HD + 1]
+        m = jnp.maximum(m1, m2)
+        merged = first * jnp.exp(m1 - m) + second * jnp.exp(m2 - m)
+        attended = (merged / merged[:, HD + 1:HD + 2]).astype(jnp.bfloat16)
+        out_sum = out_sum + jnp.dot(
+            attended[:, :HD], w_out_ref[pl.ds(h * HD, HD), :], preferred_element_type=jnp.float32
+        )
+    out_rows = out_sum.astype(jnp.bfloat16).astype(jnp.float32)
+    mixed_rows = patch_ref[...].astype(jnp.float32) + out_rows
+    normed_mixed = rms_norm(mixed_rows, gain_ref[...]).astype(jnp.bfloat16)
+    up_rows = jnp.dot(normed_mixed, w_up_ref[...], preferred_element_type=jnp.float32).astype(jnp.bfloat16)
+    up_float = up_rows.astype(jnp.float32)
+    hidden = (up_float / (1.0 + jnp.exp(-up_float))).astype(jnp.bfloat16)
+    down_rows = jnp.dot(hidden, w_down_ref[...], preferred_element_type=jnp.float32).astype(jnp.bfloat16)
+    out_ref[...] = (mixed_rows + down_rows.astype(jnp.float32)).astype(out_ref.dtype)
+
+
+def tail(low_half, high_half, new_packed, patch_rows, w_out, ffn_gain, w_up, w_down):
+    rows, width = patch_rows.shape
+    vmem = pl.BlockSpec(memory_space=pltpu.VMEM)
+    return pl.pallas_call(
+        tail_kernel,
+        out_shape=jax.ShapeDtypeStruct((rows, width), jnp.bfloat16),
+        in_specs=[vmem] * 8,
+        out_specs=vmem,
+    )(low_half, high_half, new_packed, patch_rows, w_out, ffn_gain.reshape(1, width), w_up, w_down)
+
+
 def layer(
     patches, key_cache, value_cache, cache_len, attn_gain, w_qkv, w_out, ffn_gain, w_up, w_down
 ):
@@ -180,20 +238,15 @@
     normed = rms_norm(inputs, attn_gain).astype(jnp.bfloat16)
     rows = groups * count_new
     query_rows = project(normed, w_qkv[:, :model_width])
-    offset = (lax.axis_index("seq") * slots_here).astype(jnp.int32).reshape(1)
-    packed = cache_partials(offset, cache_len, query_rows, key_cache, value_cache)
+    me = lax.axis_index("seq")
+    offset = jnp.stack([me * slots_here, me % 2]).astype(jnp.int32)
+    kept, sent = cache_partials(offset, cache_len, query_rows, key_cache, value_cache)
     kv_rows = project(normed, w_qkv[:, model_width:])
     new_packed = new_partials(query_rows, kv_rows, count_new)
-    total = merge(combine_over_seq(packed, seq_count), new_packed)
-    attended_heads = total[..., :HD] / total[..., HD + 1:HD + 2]
-    attended = attended_heads.transpose(1, 0, 2).reshape(rows, model_width).astype(jnp.bfloat16)
-    out_rows = project(attended, w_out)
-    mixed_rows = inputs + out_rows.astype(jnp.float32)
-    normed_mixed = rms_norm(mixed_rows, ffn_gain).astype(jnp.bfloat16)
-    up_rows = project(normed_mixed, w_up)
-    hidden = jax.nn.silu(up_rows.astype(jnp.float32)).astype(jnp.bfloat16)
-    down_rows = project(hidden, w_down)
-    decoded = (mixed_rows + down_rows.astype(jnp.float32)).astype(jnp.bfloat16)
+    low_half, high_half = combine_over_seq(kept, sent, seq_count)
+    decoded = tail(
+        low_half, high_half, new_packed, patches.reshape(rows, model_width), w_out, ffn_gain, w_up, w_down
+    )
     return decoded.reshape(groups, count_new, model_width)
 
 
@@ -210,6 +263,4 @@
         P(),
         P(),
     )
-    return jax.shard_map(
-        layer, mesh=mesh, in_specs=placed, out_specs=P("req", None, None), check_vma=False
-    )
+    return jax.shard_map(layer, mesh=mesh, in_specs=placed, out_specs=P("req", None, None), check_vma=False)

time: 66.4 us -> 58.3 us (0.88)
  Pallas kernels: 15.7 us -> 24.6 us
  other arithmetic: 10.8 us -> 4.74 us
  matrix products: 14.1 us -> 8.11 us
  local copies, waits for them, and re-layouts: 8.4 us -> 3.14 us
    pallas_call x1 -> x2, Pallas kernels: 10 us -> 18.9 us  [the longest x1 11.6 us: cache_partials(): pl.pallas_call(cache_partial_kernel, out_shape=(half, half), in_specs=[sm...]
    dot_general x4 -> x2, matrix products: 14.1 us -> 8.11 us  [project(): jnp.dot(token_rows, weight, preferred_element_type=jnp.float32)]
    dynamic_slice x3 -> x0, local copies, waits for them, and re-layouts: 5.02 us -> none  [the longest x2 3.34 us: combine_over_seq(): kept = lax.dynamic_index_in_dim(halves, core, axis=0, keepdims=False)]
    select_n x4 -> x3, other arithmetic: 3.43 us -> 0.52 us  [merge(): return jnp.where(lane == HD, m, merged)]
    select_n x2, other arithmetic: 1.97 us -> 0.04 us  [combine_over_seq(): jnp.where(low_first, state, got)]
    reshape x0 -> x2, local copies, waits for them, and re-layouts: none -> 1.51 us  [the longest x1 0.91 us: layer(): patches.reshape(groups * count_new, model_width).astype(jnp.float32)]
    convert_element_type x3 -> x0, local copies, waits for them, and re-layouts: 1.28 us -> none  [the longest x1 1.05 us: layer(): patches.reshape(groups * count_new, model_width).astype(jnp.float32)]
    concatenate x1 -> x0, local copies, waits for them, and re-layouts: 1.08 us -> none  [combine_over_seq(): jnp.concatenate([low_half, high_half], axis=0).reshape(heads, rows, lanes)]
  transfers between devices with their start and end apart: 4 -> 4, of which waited for: 2 -> 3; matrix products, arithmetic and copies ran while one was open for 10% -> 9% of each run, Pallas kernels for 9% -> 10%
where the time goes in v8:
time: 58.3 us; the launch traced here: 57.9 us
  Pallas kernels  24.6 us (42%)
  waiting for transfers between devices  11.1 us (19%)
  matrix products  8.11 us (14%)
  starting transfers between devices  6.25 us (11%)
  other arithmetic  4.74 us (8%)
  local copies, waits for them, and re-layouts  3.14 us (5%)
    pallas_call x1, Pallas kernels, cache_partials(): pl.pallas_call(cache_partial_kernel, out_shape=(half, half), in_specs=[sm...  11.6 us
    ppermute x4, waiting for transfers between devices, exchange(): return with_layout_constraint(lax.ppermute(part, 'seq', pairs), row_major)  11.1 us
    dot_general x2, matrix products, project(): jnp.dot(token_rows, weight, preferred_element_type=jnp.float32)  8.11 us
    pallas_call x1, Pallas kernels, tail(): pl.pallas_call(tail_kernel, out_shape=jax.ShapeDtypeStruct((rows, width),...  7.31 us
    ppermute x4, starting transfers between devices, exchange(): return with_layout_constraint(lax.ppermute(part, 'seq', pairs), row_major)  6.25 us
    pallas_call x1, Pallas kernels, new_partials(): pl.pallas_call(functools.partial(new_partial_kernel, count), out_shape=ja...  5.66 us
    reshape x1, local copies, waits for them, and re-layouts, layer(): return decoded.reshape(groups, count_new, model_width)  1.54 us
  transfers between devices with their start and end apart: 4, of which 3 were waited for; matrix products, arithmetic and copies ran while one was open for 9% of the time, Pallas kernels for 10%

profile of v8, /device:TPU:1, one launch (start us, length us, event | category | flops | bytes accessed | tf_op | source)
XLA Modules:
  0.0 57.9 jit_solution(11266110288966854527)
XLA Ops:
  0.0 0.9 %reshape.40.patch_ref = bf16[32,1280]{1,0:T(8,128)(2,1)S(1)} reshape(bf16[8,4,1280]{2,1,0:T(4,128)(2,1)} %param.14) | data formatting | bytes 163840 | tf_op jit(solution)/shard_map/reshape | solution.py:237
  0.9 1.0 %multiply_reduce_fusion = f32[8,4]{1,0:T(8,128)S(1)} fusion(bf16[8,4,1280]{2,1,0:T(4,128)(2,1)} %param.14), kind=kLoop, calls=%fused_computation.7 | loop fusion | flops 122848 | bytes 82048 | tf_op jit(solution)/shard_map/reduce_sum | solution.py:21
  2.1 0.6 %pad_add_fusion.offset_ref = s32[2]{0:T(128)} fusion(s32[1]{0:T(128)} %bitcast.1, s32[1]{0:T(128)} %bitcast), kind=kLoop, calls=%fused_computation.29 | loop fusion | flops 2 | bytes 16 | tf_op jit(solution)/shard_map/stack | solution.py:242
  2.7 3.3 %fusion.7.query_ref = bf16[32,1280]{1,0:T(8,128)(2,1)} fusion(bf16[1280,3840]{1,0:T(8,128)(2,1)} %param.19, bf16[32,1280]{1,0:T(8,128)(2,1)S(1)} %reshape.40.patch_ref, f32[1280]{0:T(1024)} %param.18, f32[32]{0:T(128)S(1)} %rsqrt.12), kind=kOutput, calls=%fused_computation.5 | convolution fusion | flops 105062400 | bytes 3448960 | tf_op jit(solution)/shard_map/dot_general | solution.py:25
  6.0 11.6 %shard_map.136 = (f32[8,32,128]{2,1,0:T(8,128)}, f32[8,32,128]{2,1,0:T(8,128)}) custom-call(s32[2]{0:T(128)} %pad_add_fusion.offset_ref, s32[8]{0:T(128)} %length_ref.1, bf16[32,1280]{1,0:T(8,128)(2,1)} %fusion.7.query_ref, bf16[8,128,1280]{2,1,0:T(8,128)(2,1)} %key_ref.1, bf16[8,128,1280]{2,1,0:T(8,128)(2,1)} %value_ref.1, ...), custom_call_target="tpu_custom_call" | custom-call | tf_op jit(solution)/shard_map/pallas_call | solution.py:174
  17.6 1.5 %collective-permute-done = f32[256,128]{1,0:T(8,128)S(1)} collective-permute-done((f32[256,128]{1,0:T(8,128)}, f32[256,128]{1,0:T(8,128)S(1)}, u32[]{:S(2)}, u32[]{:S(2)}) %collective-permute-start) | collective-permute-done | bytes 131104 | tf_op jit(solution)/shard_map/ppermute | solution.py:46
  19.2 0.9 %bitcast_select_fusion.1 = (f32[256,128]{1,0:T(8,128)S(1)}, f32[256,128]{1,0:T(8,128)S(1)}) fusion(f32[256,128]{1,0:T(8,128)S(1)} %collective-permute-done, f32[8,32,128]{2,1,0:T(8,128)} %get-tuple-element.7, pred[]{:T(512)S(6)} %eq.26), kind=kLoop, calls=%fused_computation.9 | loop fusion | flops 65536 | bytes 524289 | tf_op jit(solution)/shard_map/jit(_where)/select_n | solution.py:57
  20.1 0.3 fusion.10
  20.4 0.2 add_select_fusion.2
  20.6 2.5 %collective-permute-start.1 = (f32[256,128]{1,0:T(8,128)S(1)}, f32[256,128]{1,0:T(8,128)S(1)}, u32[]{:S(2)}, u32[]{:S(2)}) collective-permute-start(f32[256,128]{1,0:T(8,128)S(1)} %add_select_fusion.2), channel_id=1, source_target_pairs={{0,2},{1,3},{2,0},{3,1},{4,6},{5,7},{6,4},{7,5},{8,10},{9,11},{10,... | collective-permute-start | bytes 393224 | tf_op jit(solution)/shard_map/ppermute | solution.py:46
  23.1 3.5 %collective-permute-done.1 = f32[256,128]{1,0:T(8,128)S(1)} collective-permute-done((f32[256,128]{1,0:T(8,128)S(1)}, f32[256,128]{1,0:T(8,128)S(1)}, u32[]{:S(2)}, u32[]{:S(2)}) %collective-permute-start.1) | collective-permute-done | bytes 131104 | tf_op jit(solution)/shard_map/ppermute | solution.py:46
  26.6 0.3 fusion.11
  26.9 0.2 add_select_fusion.1
  27.1 2.3 %collective-permute-start.2 = (f32[256,128]{1,0:T(8,128)S(1)}, f32[256,128]{1,0:T(8,128)S(1)}, u32[]{:S(2)}, u32[]{:S(2)}) collective-permute-start(f32[256,128]{1,0:T(8,128)S(1)} %add_select_fusion.1), channel_id=1, source_target_pairs={{0,4},{1,5},{2,6},{3,7},{4,0},{5,1},{6,2},{7,3},{8,12},{9,13},{10,... | collective-permute-start | bytes 393224 | tf_op jit(solution)/shard_map/ppermute | solution.py:46
  29.3 6.0 %collective-permute-done.2 = f32[256,128]{1,0:T(8,128)S(1)} collective-permute-done((f32[256,128]{1,0:T(8,128)S(1)}, f32[256,128]{1,0:T(8,128)S(1)}, u32[]{:S(2)}, u32[]{:S(2)}) %collective-permute-start.2) | collective-permute-done | bytes 131104 | tf_op jit(solution)/shard_map/ppermute | solution.py:46
  35.4 0.3 fusion.12
  35.7 0.2 add_select_fusion
  35.9 1.5 %collective-permute-start.3 = (f32[256,128]{1,0:T(8,128)S(1)}, f32[256,128]{1,0:T(8,128)S(1)}, u32[]{:S(2)}, u32[]{:S(2)}) collective-permute-start(f32[256,128]{1,0:T(8,128)S(1)} %add_select_fusion), channel_id=1, source_target_pairs={{0,1},{1,0},{2,3},{3,2},{4,5},{5,4},{6,7},{7,6},{8,9},{9,8},{10,11... | collective-permute-start | bytes 393224 | tf_op jit(solution)/shard_map/ppermute | solution.py:46
  37.3 4.8 %fusion.2.kv_ref = bf16[32,2560]{1,0:T(8,128)(2,1)} fusion(bf16[1280,3840]{1,0:T(8,128)(2,1)} %param.19, bf16[32,1280]{1,0:T(8,128)(2,1)S(1)} %reshape.40.patch_ref, f32[1280]{0:T(1024)S(1)} %copy-done.2, f32[32]{0:T(128)S(1)} %rsqrt.12), kind=kOutput, calls=%fused_computation.2 | convolution fusion | flops 209960960 | bytes 6804608 | tf_op jit(solution)/shard_map/dot_general | solution.py:25
  42.1 5.7 %shard_map.137.new_ref = f32[16,32,128]{2,1,0:T(8,128)} custom-call(bf16[32,1280]{1,0:T(8,128)(2,1)} %fusion.7.query_ref, bf16[32,2560]{1,0:T(8,128)(2,1)} %fusion.2.kv_ref, bf16[64,1280]{1,0:T(8,128)(2,1)} %constant.64.clone.qmask_ref, f32[1280,128]{1,0:T(8,128)} %constant.65.clone.fold_ref), custom_call_target="tpu_custom_call" | custom-call | tf_op jit(solution)/shard_map/pallas_call | solution.py:186
  47.8 0.6 %reshape.45.gain_ref = f32[1,1280]{1,0:T(1,128)} reshape(f32[1280]{0:T(1024)S(1)} %copy-done.1) | data formatting | bytes 10240 | tf_op jit(solution)/shard_map/reshape | solution.py:228
  48.4 0.7 %broadcast_select_fusion.4 = (f32[256,128]{1,0:T(8,128)}, f32[256,128]{1,0:T(8,128)}) fusion(f32[256,128]{1,0:T(8,128)S(1)} %collective-permute-done.3, f32[256,128]{1,0:T(8,128)S(1)} %add_select_fusion, pred[]{:T(512)S(6)} %eq.26), kind=kLoop, calls=%fused_computation.26 | loop fusion | flops 65536 | bytes 524289 | tf_op jit(solution)/shard_map/jit(_where)/select_n | solution.py:66
  49.1 7.3 %shard_map.138 = bf16[32,1280]{1,0:T(8,128)(2,1)} custom-call(f32[8,32,128]{2,1,0:T(8,128)} %bitcast.9, f32[8,32,128]{2,1,0:T(8,128)} %bitcast.8, f32[16,32,128]{2,1,0:T(8,128)} %shard_map.137.new_ref, bf16[32,1280]{1,0:T(8,128)(2,1)} %copy-done, bf16[1280,1280]{1,0:T(8,128)(2,1)} %w_out_ref.1, f32[1,1280]{1,0:T(1,128)} %reshape.45.gain_ref, ...), custom_call_target="tpu_custom_call" | custom-call | tf_op jit(solution)/shard_map/pallas_call | solution.py:223
  56.4 1.5 %reshape.46 = bf16[8,4,1280]{2,1,0:T(4,128)(2,1)} reshape(bf16[32,1280]{1,0:T(8,128)(2,1)} %shard_map.138) | data formatting | bytes 163840 | tf_op jit(solution)/shard_map/reshape | solution.py:250
  (13 shorter events, 0.2 us)
Async XLA Ops:
  0.9 36.4 %copy-start = (bf16[32,1280]{1,0:T(8,128)(2,1)}, bf16[32,1280]{1,0:T(8,128)(2,1)S(1)}, u32[]{:S(2)}) copy-start(bf16[32,1280]{1,0:T(8,128)(2,1)S(1)} %reshape.40.patch_ref) | copy-start | bytes 245764
  2.7 34.6 %copy-start.2 = (f32[1280]{0:T(1024)S(1)}, f32[1280]{0:T(1024)}, u32[]{:S(2)}) copy-start(f32[1280]{0:T(1024)} %param.18) | copy-start | bytes 15364
  17.6 30.2 %copy-start.1 = (f32[1280]{0:T(1024)S(1)}, f32[1280]{0:T(1024)}, u32[]{:S(2)}) copy-start(f32[1280]{0:T(1024)} %param.21) | copy-start | bytes 15364
  17.6 1.6 %collective-permute-start = (f32[256,128]{1,0:T(8,128)}, f32[256,128]{1,0:T(8,128)S(1)}, u32[]{:S(2)}, u32[]{:S(2)}) collective-permute-start(f32[256,128]{1,0:T(8,128)} %bitcast.10), channel_id=1, source_target_pairs={{0,1},{1,0},{2,3},{3,2},{4,5},{5,4},{6,7},{7,6},{8,9},{9,8},{10,11... | collective-permute-start | bytes 393224 | tf_op jit(solution)/shard_map/ppermute | solution.py:46
  20.6 6.0 %collective-permute-start.1 = (f32[256,128]{1,0:T(8,128)S(1)}, f32[256,128]{1,0:T(8,128)S(1)}, u32[]{:S(2)}, u32[]{:S(2)}) collective-permute-start(f32[256,128]{1,0:T(8,128)S(1)} %add_select_fusion.2), channel_id=1, source_target_pairs={{0,2},{1,3},{2,0},{3,1},{4,6},{5,7},{6,4},{7,5},{8,10},{9,11},{10,... | collective-permute-start | bytes 393224 | tf_op jit(solution)/shard_map/ppermute | solution.py:46
  27.1 8.3 %collective-permute-start.2 = (f32[256,128]{1,0:T(8,128)S(1)}, f32[256,128]{1,0:T(8,128)S(1)}, u32[]{:S(2)}, u32[]{:S(2)}) collective-permute-start(f32[256,128]{1,0:T(8,128)S(1)} %add_select_fusion.1), channel_id=1, source_target_pairs={{0,4},{1,5},{2,6},{3,7},{4,0},{5,1},{6,2},{7,3},{8,12},{9,13},{10,... | collective-permute-start | bytes 393224 | tf_op jit(solution)/shard_map/ppermute | solution.py:46
  35.9 12.5 %collective-permute-start.3 = (f32[256,128]{1,0:T(8,128)S(1)}, f32[256,128]{1,0:T(8,128)S(1)}, u32[]{:S(2)}, u32[]{:S(2)}) collective-permute-start(f32[256,128]{1,0:T(8,128)S(1)} %add_select_fusion), channel_id=1, source_target_pairs={{0,1},{1,0},{2,3},{3,2},{4,5},{5,4},{6,7},{7,6},{8,9},{9,8},{10,11... | collective-permute-start | bytes 393224 | tf_op jit(solution)/shard_map/ppermute | solution.py:46

commit v9 on v8

--- a/solution.py
+++ b/solution.py
@@ -1,5 +1,3 @@
-import functools
-
 import numpy as np
 import jax
 import jax.numpy as jnp
@@ -97,7 +95,7 @@
     position = offset_ref[0] + lax.broadcasted_iota(jnp.int32, (1, slots), 1)
     lane = lax.broadcasted_iota(jnp.int32, (heads * count, LANES), 1)
     for r in range(groups):
-        queries = query_ref[pl.ds(r * count, count), :]
+        queries = query_ref[r]
         query_rows = jnp.concatenate([queries] * heads, axis=0) * qmask
         scores = lax.dot_general(
             query_rows, key_ref[r], (((1,), (1,)), ((), ())), preferred_element_type=jnp.float32
@@ -124,10 +122,9 @@
                 sent_ref[h % half_heads, rows_here, :] = block
 
 
-def new_partial_kernel(count, query_ref, kv_ref, qmask_ref, fold_ref, out_ref):
-    rows_all, width = query_ref.shape
+def new_partial_kernel(query_ref, kv_ref, qmask_ref, fold_ref, out_ref):
+    groups, count, width = query_ref.shape
     heads = out_ref.shape[0]
-    groups = rows_all // count
     scale_factor = HD ** (-0.5)
     qmask = qmask_ref[...]
     qmask_float = qmask.astype(jnp.float32)
@@ -135,10 +132,11 @@
     lane = lax.broadcasted_iota(jnp.int32, (heads * count, LANES), 1)
     patch = lax.broadcasted_iota(jnp.int32, (heads * count, 1), 0) & (count - 1)
     for r in range(groups):
-        queries = query_ref[pl.ds(r * count, count), :]
+        queries = query_ref[r]
         query_float = (jnp.concatenate([queries] * heads, axis=0) * qmask).astype(jnp.float32)
-        keys_new = kv_ref[pl.ds(r * count, count), pl.ds(0, width)].astype(jnp.float32)
-        values_new = kv_ref[pl.ds(r * count, count), pl.ds(width, width)].astype(jnp.float32)
+        pair = kv_ref[r]
+        keys_new = pair[:, :width].astype(jnp.float32)
+        values_new = pair[:, width:].astype(jnp.float32)
         new_scores = []
         for u in range(count):
             score = jnp.sum(query_float * keys_new[u:u + 1, :], axis=1, keepdims=True) * scale_factor
@@ -166,8 +164,9 @@
 
 def cache_partials(offset, cache_len, query_rows, key_cache, value_cache):
     groups, _, width = key_cache.shape
-    rows = query_rows.shape[0]
-    qmask, fold = head_constants(rows // groups, width)
+    count = query_rows.shape[1]
+    rows = groups * count
+    qmask, fold = head_constants(count, width)
     smem = pl.BlockSpec(memory_space=pltpu.SMEM)
     vmem = pl.BlockSpec(memory_space=pltpu.VMEM)
     half = jax.ShapeDtypeStruct((HEADS // 2, rows, LANES), jnp.float32)
@@ -179,12 +178,13 @@
     )(offset, cache_len, query_rows, key_cache, value_cache, qmask, fold)
 
 
-def new_partials(query_rows, kv_rows, count):
-    rows, width = query_rows.shape
+def new_partials(query_rows, kv_rows):
+    groups, count, width = query_rows.shape
+    rows = groups * count
     qmask, fold = head_constants(count, width)
     vmem = pl.BlockSpec(memory_space=pltpu.VMEM)
     return pl.pallas_call(
-        functools.partial(new_partial_kernel, count),
+        new_partial_kernel,
         out_shape=jax.ShapeDtypeStruct((HEADS, rows, LANES), jnp.float32),
         in_specs=[vmem, vmem, vmem, vmem],
         out_specs=vmem,
@@ -208,46 +208,45 @@
             attended[:, :HD], w_out_ref[pl.ds(h * HD, HD), :], preferred_element_type=jnp.float32
         )
     out_rows = out_sum.astype(jnp.bfloat16).astype(jnp.float32)
-    mixed_rows = patch_ref[...].astype(jnp.float32) + out_rows
+    groups, count, _ = patch_ref.shape
+    patch_rows = jnp.concatenate([patch_ref[r].astype(jnp.float32) for r in range(groups)], axis=0)
+    mixed_rows = patch_rows + out_rows
     normed_mixed = rms_norm(mixed_rows, gain_ref[...]).astype(jnp.bfloat16)
     up_rows = jnp.dot(normed_mixed, w_up_ref[...], preferred_element_type=jnp.float32).astype(jnp.bfloat16)
     up_float = up_rows.astype(jnp.float32)
     hidden = (up_float / (1.0 + jnp.exp(-up_float))).astype(jnp.bfloat16)
     down_rows = jnp.dot(hidden, w_down_ref[...], preferred_element_type=jnp.float32).astype(jnp.bfloat16)
-    out_ref[...] = (mixed_rows + down_rows.astype(jnp.float32)).astype(out_ref.dtype)
-
-
-def tail(low_half, high_half, new_packed, patch_rows, w_out, ffn_gain, w_up, w_down):
-    rows, width = patch_rows.shape
+    decoded = mixed_rows + down_rows.astype(jnp.float32)
+    for r in range(groups):
+        out_ref[r] = decoded[r * count:(r + 1) * count, :].astype(out_ref.dtype)
+
+
+def tail(low_half, high_half, new_packed, patches, w_out, ffn_gain, w_up, w_down):
+    width = patches.shape[-1]
     vmem = pl.BlockSpec(memory_space=pltpu.VMEM)
     return pl.pallas_call(
         tail_kernel,
-        out_shape=jax.ShapeDtypeStruct((rows, width), jnp.bfloat16),
+        out_shape=jax.ShapeDtypeStruct(patches.shape, jnp.bfloat16),
         in_specs=[vmem] * 8,
         out_specs=vmem,
-    )(low_half, high_half, new_packed, patch_rows, w_out, ffn_gain.reshape(1, width), w_up, w_down)
+    )(low_half, high_half, new_packed, patches, w_out, ffn_gain.reshape(1, width), w_up, w_down)
 
 
 def layer(
     patches, key_cache, value_cache, cache_len, attn_gain, w_qkv, w_out, ffn_gain, w_up, w_down
 ):
-    groups, count_new, model_width = patches.shape
+    _, _, model_width = patches.shape
     slots_here = key_cache.shape[1]
     seq_count = lax.axis_size("seq")
-    inputs = patches.reshape(groups * count_new, model_width).astype(jnp.float32)
-    normed = rms_norm(inputs, attn_gain).astype(jnp.bfloat16)
-    rows = groups * count_new
+    normed = rms_norm(patches.astype(jnp.float32), attn_gain).astype(jnp.bfloat16)
     query_rows = project(normed, w_qkv[:, :model_width])
     me = lax.axis_index("seq")
     offset = jnp.stack([me * slots_here, me % 2]).astype(jnp.int32)
     kept, sent = cache_partials(offset, cache_len, query_rows, key_cache, value_cache)
     kv_rows = project(normed, w_qkv[:, model_width:])
-    new_packed = new_partials(query_rows, kv_rows, count_new)
+    new_packed = new_partials(query_rows, kv_rows)
     low_half, high_half = combine_over_seq(kept, sent, seq_count)
-    decoded = tail(
-        low_half, high_half, new_packed, patches.reshape(rows, model_width), w_out, ffn_gain, w_up, w_down
-    )
-    return decoded.reshape(groups, count_new, model_width)
+    return tail(low_half, high_half, new_packed, patches, w_out, ffn_gain, w_up, w_down)
 
 
 def solution(mesh):

time: 58.3 us -> 55.9 us (0.959)
  local copies, waits for them, and re-layouts: 3.14 us -> 0.61 us
    reshape x2 -> x0, local copies, waits for them, and re-layouts: 2.45 us -> none  [the longest x1 1.54 us: layer(): return decoded.reshape(groups, count_new, model_width)]
  transfers between devices with their start and end apart: 4 -> 4, of which waited for: 3 -> 3; matrix products, arithmetic and copies ran while one was open for 9% -> 10% of each run, Pallas kernels for 10% -> 10%
where the time goes in v9:
time: 55.9 us; the launch traced here: 55.6 us
  Pallas kernels  24.7 us (44%)
  waiting for transfers between devices  11.1 us (20%)
  matrix products  8.24 us (15%)
  starting transfers between devices  6.25 us (11%)
  other arithmetic  4.7 us (8%)
  local copies, waits for them, and re-layouts  0.61 us (1%)
    pallas_call x1, Pallas kernels, cache_partials(): pl.pallas_call(cache_partial_kernel, out_shape=(half, half), in_specs=[sm...  11.6 us
    ppermute x4, waiting for transfers between devices, exchange(): return with_layout_constraint(lax.ppermute(part, 'seq', pairs), row_major)  11.1 us
    dot_general x2, matrix products, project(): jnp.dot(token_rows, weight, preferred_element_type=jnp.float32)  8.24 us
    pallas_call x1, Pallas kernels, tail(): pl.pallas_call(tail_kernel, out_shape=jax.ShapeDtypeStruct(patches.shape,...  7.31 us
    ppermute x4, starting transfers between devices, exchange(): return with_layout_constraint(lax.ppermute(part, 'seq', pairs), row_major)  6.25 us
    pallas_call x1, Pallas kernels, new_partials(): pl.pallas_call(new_partial_kernel, out_shape=jax.ShapeDtypeStruct((HEADS,...  5.73 us
  transfers between devices with their start and end apart: 4, of which 3 were waited for; matrix products, arithmetic and copies ran while one was open for 10% of the time, Pallas kernels for 10%

profile of v9, /device:TPU:1, one launch (start us, length us, event | category | flops | bytes accessed | tf_op | source)
XLA Modules:
  0.0 55.6 jit_solution(7613967187506075071)
XLA Ops:
  0.0 1.0 %fusion.12 = f32[8,4]{1,0:T(8,128)S(1)} fusion(bf16[8,4,1280]{2,1,0:T(4,128)(2,1)} %patch_ref.1), kind=kLoop, calls=%fused_computation.10 | loop fusion | flops 122848 | bytes 82048 | tf_op jit(solution)/shard_map/reduce_sum | solution.py:19
  1.0 0.6 %pad_add_fusion.offset_ref = s32[2]{0:T(128)} fusion(s32[1]{0:T(128)} %bitcast.1, s32[1]{0:T(128)} %bitcast), kind=kLoop, calls=%fused_computation.34 | loop fusion | flops 2 | bytes 16 | tf_op jit(solution)/shard_map/stack | solution.py:244
  1.6 3.4 %fusion.9.query_ref = bf16[8,4,1280]{2,1,0:T(4,128)(2,1)} fusion(bf16[1280,3840]{1,0:T(8,128)(2,1)} %param.19, bf16[8,4,1280]{2,1,0:T(4,128)(2,1)} %patch_ref.1, f32[1280]{0:T(1024)} %param.18, f32[8,4]{1,0:T(8,128)S(1)} %add_rsqrt_fusion), kind=kOutput, calls=%fused_computation.7 | convolution fusion | flops 105062400 | bytes 3448960 | tf_op jit(solution)/shard_map/dot_general | solution.py:23
  5.0 11.6 %shard_map.136 = (f32[8,32,128]{2,1,0:T(8,128)}, f32[8,32,128]{2,1,0:T(8,128)}) custom-call(s32[2]{0:T(128)} %pad_add_fusion.offset_ref, s32[8]{0:T(128)} %length_ref.1, bf16[8,4,1280]{2,1,0:T(4,128)(2,1)} %fusion.9.query_ref, bf16[8,128,1280]{2,1,0:T(8,128)(2,1)} %key_ref.1, bf16[8,128,1280]{2,1,0:T(8,128)(2,1)} %value_ref.1, ...), custom_call_target="tpu_custom_call" | custom-call | tf_op jit(solution)/shard_map/pallas_call | solution.py:173
  16.6 0.0 collective-permute-start
  16.7 1.5 %collective-permute-done = f32[256,128]{1,0:T(8,128)S(1)} collective-permute-done((f32[256,128]{1,0:T(8,128)}, f32[256,128]{1,0:T(8,128)S(1)}, u32[]{:S(2)}, u32[]{:S(2)}) %collective-permute-start) | collective-permute-done | bytes 131104 | tf_op jit(solution)/shard_map/ppermute | solution.py:44
  18.2 0.9 %bitcast_select_fusion.1 = (f32[256,128]{1,0:T(8,128)S(1)}, f32[256,128]{1,0:T(8,128)S(1)}) fusion(f32[256,128]{1,0:T(8,128)S(1)} %collective-permute-done, f32[8,32,128]{2,1,0:T(8,128)} %get-tuple-element.7, pred[]{:T(512)S(6)} %eq.26), kind=kLoop, calls=%fused_computation.14 | loop fusion | flops 65536 | bytes 524289 | tf_op jit(solution)/shard_map/jit(_where)/select_n | solution.py:55
  19.1 0.3 fusion.17
  19.4 0.2 add_select_fusion.2
  19.6 2.5 %collective-permute-start.1 = (f32[256,128]{1,0:T(8,128)S(1)}, f32[256,128]{1,0:T(8,128)S(1)}, u32[]{:S(2)}, u32[]{:S(2)}) collective-permute-start(f32[256,128]{1,0:T(8,128)S(1)} %add_select_fusion.2), channel_id=1, source_target_pairs={{0,2},{1,3},{2,0},{3,1},{4,6},{5,7},{6,4},{7,5},{8,10},{9,11},{10,... | collective-permute-start | bytes 393224 | tf_op jit(solution)/shard_map/ppermute | solution.py:44
  22.1 3.5 %collective-permute-done.1 = f32[256,128]{1,0:T(8,128)S(1)} collective-permute-done((f32[256,128]{1,0:T(8,128)S(1)}, f32[256,128]{1,0:T(8,128)S(1)}, u32[]{:S(2)}, u32[]{:S(2)}) %collective-permute-start.1) | collective-permute-done | bytes 131104 | tf_op jit(solution)/shard_map/ppermute | solution.py:44
  25.6 0.3 fusion.18
  25.9 0.2 add_select_fusion.1
  26.1 2.3 %collective-permute-start.2 = (f32[256,128]{1,0:T(8,128)S(1)}, f32[256,128]{1,0:T(8,128)S(1)}, u32[]{:S(2)}, u32[]{:S(2)}) collective-permute-start(f32[256,128]{1,0:T(8,128)S(1)} %add_select_fusion.1), channel_id=1, source_target_pairs={{0,4},{1,5},{2,6},{3,7},{4,0},{5,1},{6,2},{7,3},{8,12},{9,13},{10,... | collective-permute-start | bytes 393224 | tf_op jit(solution)/shard_map/ppermute | solution.py:44
  28.4 6.0 %collective-permute-done.2 = f32[256,128]{1,0:T(8,128)S(1)} collective-permute-done((f32[256,128]{1,0:T(8,128)S(1)}, f32[256,128]{1,0:T(8,128)S(1)}, u32[]{:S(2)}, u32[]{:S(2)}) %collective-permute-start.2) | collective-permute-done | bytes 131104 | tf_op jit(solution)/shard_map/ppermute | solution.py:44
  34.4 0.3 fusion.19
  34.7 0.2 add_select_fusion
  34.9 1.5 %collective-permute-start.3 = (f32[256,128]{1,0:T(8,128)S(1)}, f32[256,128]{1,0:T(8,128)S(1)}, u32[]{:S(2)}, u32[]{:S(2)}) collective-permute-start(f32[256,128]{1,0:T(8,128)S(1)} %add_select_fusion), channel_id=1, source_target_pairs={{0,1},{1,0},{2,3},{3,2},{4,5},{5,4},{6,7},{7,6},{8,9},{9,8},{10,11... | collective-permute-start | bytes 393224 | tf_op jit(solution)/shard_map/ppermute | solution.py:44
  36.4 4.9 %fusion.3.kv_ref = bf16[8,4,2560]{2,1,0:T(4,128)(2,1)} fusion(bf16[1280,3840]{1,0:T(8,128)(2,1)} %param.19, bf16[8,4,1280]{2,1,0:T(4,128)(2,1)S(1)} %copy-done, f32[1280]{0:T(1024)S(1)} %copy-done.2, f32[8,4]{1,0:T(8,128)S(1)} %add_rsqrt_fusion), kind=kOutput, calls=%fused_computation.3 | convolution fusion | flops 209960960 | bytes 6804608 | tf_op jit(solution)/shard_map/dot_general | solution.py:23
  41.2 5.7 %shard_map.137.new_ref = f32[16,32,128]{2,1,0:T(8,128)} custom-call(bf16[8,4,1280]{2,1,0:T(4,128)(2,1)} %fusion.9.query_ref, bf16[8,4,2560]{2,1,0:T(4,128)(2,1)} %fusion.3.kv_ref, bf16[64,1280]{1,0:T(8,128)(2,1)} %constant.64.clone.qmask_ref, f32[1280,128]{1,0:T(8,128)} %constant.65.clone.fold_ref), custom_call_target="tpu_custom_call" | custom-call | tf_op jit(solution)/shard_map/pallas_call | solution.py:186
  47.0 0.6 %reshape.28.gain_ref = f32[1,1280]{1,0:T(1,128)} reshape(f32[1280]{0:T(1024)S(1)} %copy-done.1) | data formatting | bytes 10240 | tf_op jit(solution)/shard_map/reshape | solution.py:232
  47.6 0.0 collective-permute-done.3
  47.6 0.7 %broadcast_select_fusion.4 = (f32[256,128]{1,0:T(8,128)}, f32[256,128]{1,0:T(8,128)}) fusion(f32[256,128]{1,0:T(8,128)S(1)} %collective-permute-done.3, f32[256,128]{1,0:T(8,128)S(1)} %add_select_fusion, pred[]{:T(512)S(6)} %eq.26), kind=kLoop, calls=%fused_computation.31 | loop fusion | flops 65536 | bytes 524289 | tf_op jit(solution)/shard_map/jit(_where)/select_n | solution.py:64
  48.3 7.3 %shard_map.138 = bf16[8,4,1280]{2,1,0:T(4,128)(2,1)} custom-call(f32[8,32,128]{2,1,0:T(8,128)} %bitcast.19, f32[8,32,128]{2,1,0:T(8,128)} %bitcast.18, f32[16,32,128]{2,1,0:T(8,128)} %shard_map.137.new_ref, bf16[8,4,1280]{2,1,0:T(4,128)(2,1)} %patch_ref.1, bf16[1280,1280]{1,0:T(8,128)(2,1)} %w_out_ref.1, f32[1,1280]{1,0:T(1,128)} %reshape.28.gain_ref, ...), custom_call_target="tpu_custom_call" | custom-call | tf_op jit(solution)/shard_map/pallas_call | solution.py:227
  (10 shorter events, 0.1 us)
Async XLA Ops:
  5.0 31.4 %copy-start = (bf16[8,4,1280]{2,1,0:T(4,128)(2,1)S(1)}, bf16[8,4,1280]{2,1,0:T(4,128)(2,1)}, u32[]{:S(2)}) copy-start(bf16[8,4,1280]{2,1,0:T(4,128)(2,1)} %patch_ref.1) | copy-start | bytes 245764
  5.0 31.4 %copy-start.2 = (f32[1280]{0:T(1024)S(1)}, f32[1280]{0:T(1024)}, u32[]{:S(2)}) copy-start(f32[1280]{0:T(1024)} %param.18) | copy-start | bytes 15364
  16.6 1.6 %collective-permute-start = (f32[256,128]{1,0:T(8,128)}, f32[256,128]{1,0:T(8,128)S(1)}, u32[]{:S(2)}, u32[]{:S(2)}) collective-permute-start(f32[256,128]{1,0:T(8,128)} %bitcast.20), channel_id=1, source_target_pairs={{0,1},{1,0},{2,3},{3,2},{4,5},{5,4},{6,7},{7,6},{8,9},{9,8},{10,11... | collective-permute-start | bytes 393224 | tf_op jit(solution)/shard_map/ppermute | solution.py:44
  19.4 27.5 %copy-start.1 = (f32[1280]{0:T(1024)S(1)}, f32[1280]{0:T(1024)}, u32[]{:S(2)}) copy-start(f32[1280]{0:T(1024)} %param.21) | copy-start | bytes 15364
  19.6 6.0 %collective-permute-start.1 = (f32[256,128]{1,0:T(8,128)S(1)}, f32[256,128]{1,0:T(8,128)S(1)}, u32[]{:S(2)}, u32[]{:S(2)}) collective-permute-start(f32[256,128]{1,0:T(8,128)S(1)} %add_select_fusion.2), channel_id=1, source_target_pairs={{0,2},{1,3},{2,0},{3,1},{4,6},{5,7},{6,4},{7,5},{8,10},{9,11},{10,... | collective-permute-start | bytes 393224 | tf_op jit(solution)/shard_map/ppermute | solution.py:44
  26.1 8.3 %collective-permute-start.2 = (f32[256,128]{1,0:T(8,128)S(1)}, f32[256,128]{1,0:T(8,128)S(1)}, u32[]{:S(2)}, u32[]{:S(2)}) collective-permute-start(f32[256,128]{1,0:T(8,128)S(1)} %add_select_fusion.1), channel_id=1, source_target_pairs={{0,4},{1,5},{2,6},{3,7},{4,0},{5,1},{6,2},{7,3},{8,12},{9,13},{10,... | collective-permute-start | bytes 393224 | tf_op jit(solution)/shard_map/ppermute | solution.py:44
  34.9 12.7 %collective-permute-start.3 = (f32[256,128]{1,0:T(8,128)S(1)}, f32[256,128]{1,0:T(8,128)S(1)}, u32[]{:S(2)}, u32[]{:S(2)}) collective-permute-start(f32[256,128]{1,0:T(8,128)S(1)} %add_select_fusion), channel_id=1, source_target_pairs={{0,1},{1,0},{2,3},{3,2},{4,5},{5,4},{6,7},{7,6},{8,9},{9,8},{10,11... | collective-permute-start | bytes 393224 | tf_op jit(solution)/shard_map/ppermute | solution.py:44

commit v10 on v9

--- a/solution.py
+++ b/solution.py
@@ -66,9 +66,15 @@
 
 
 def folded_rows(rows, peak, total, qmask_float, fold, lane):
-    folded = jnp.dot(
-        rows * qmask_float, fold, precision=lax.Precision.HIGHEST, preferred_element_type=jnp.float32
-    )
+    own = rows * qmask_float
+    high = own.astype(jnp.bfloat16)
+    rest = own - high.astype(jnp.float32)
+    middle = rest.astype(jnp.bfloat16)
+    low = (rest - middle.astype(jnp.float32)).astype(jnp.bfloat16)
+    folded = (
+        jnp.dot(high, fold, preferred_element_type=jnp.float32)
+        + jnp.dot(middle, fold, preferred_element_type=jnp.float32)
+    ) + jnp.dot(low, fold, preferred_element_type=jnp.float32)
     return jnp.where(lane == HD, peak, jnp.where(lane == HD + 1, total, folded))
 
 
@@ -89,7 +95,7 @@
     count = kept_ref.shape[1] // groups
     core = offset_ref[1]
     scale_factor = HD ** (-0.5)
-    qmask = qmask_ref[...]
+    qmask = qmask_ref[core]
     qmask_float = qmask.astype(jnp.float32)
     fold = fold_ref[...]
     position = offset_ref[0] + lax.broadcasted_iota(jnp.int32, (1, slots), 1)
@@ -110,16 +116,8 @@
         )
         folded = folded_rows(value_rows, peak, total, qmask_float, fold, lane)
         for h in range(heads):
-            block = folded[h * count:(h + 1) * count, :]
-            rows_here = pl.ds(r * count, count)
-
-            @pl.when(core == h // half_heads)
-            def _():
-                kept_ref[h % half_heads, rows_here, :] = block
-
-            @pl.when(core != h // half_heads)
-            def _():
-                sent_ref[h % half_heads, rows_here, :] = block
+            target = kept_ref if h < half_heads else sent_ref
+            target[h % half_heads, pl.ds(r * count, count), :] = folded[h * count:(h + 1) * count, :]
 
 
 def new_partial_kernel(query_ref, kv_ref, qmask_ref, fold_ref, out_ref):
@@ -158,15 +156,27 @@
     row_head = np.arange(HEADS * count)[:, None] // count
     col_head = np.arange(width)[None, :] // HD
     qmask = jnp.asarray((row_head == col_head).astype(np.float32), dtype=jnp.bfloat16)
-    fold = jnp.asarray((np.arange(width)[:, None] % HD == np.arange(LANES)[None, :]).astype(np.float32))
+    fold = jnp.asarray(
+        (np.arange(width)[:, None] % HD == np.arange(LANES)[None, :]).astype(np.float32), dtype=jnp.bfloat16
+    )
     return qmask, fold
+
+
+def ordered_masks(count, width):
+    masks = []
+    for core in range(2):
+        row_head = (np.arange(HEADS * count)[:, None] // count + core * (HEADS // 2)) % HEADS
+        col_head = np.arange(width)[None, :] // HD
+        masks.append((row_head == col_head).astype(np.float32))
+    return jnp.asarray(np.stack(masks), dtype=jnp.bfloat16)
 
 
 def cache_partials(offset, cache_len, query_rows, key_cache, value_cache):
     groups, _, width = key_cache.shape
     count = query_rows.shape[1]
     rows = groups * count
-    qmask, fold = head_constants(count, width)
+    _, fold = head_constants(count, width)
+    qmask = ordered_masks(count, width)
     smem = pl.BlockSpec(memory_space=pltpu.SMEM)
     vmem = pl.BlockSpec(memory_space=pltpu.VMEM)
     half = jax.ShapeDtypeStruct((HEADS // 2, rows, LANES), jnp.float32)

time: 55.9 us -> 52.1 us (0.932)
  Pallas kernels: 24.7 us -> 20.9 us
    pallas_call x1, Pallas kernels: 11.6 us -> 8.52 us  [cache_partials(): pl.pallas_call(cache_partial_kernel, out_shape=(half, half), in_specs=[sm...]
    pallas_call x1, Pallas kernels: 5.73 us -> 5.06 us  [new_partials(): pl.pallas_call(new_partial_kernel, out_shape=jax.ShapeDtypeStruct((HEADS,...]
  transfers between devices with their start and end apart: 4 -> 4, of which waited for: 3 -> 3; matrix products, arithmetic and copies ran while one was open for 10% -> 11% of each run, Pallas kernels for 10% -> 10%
where the time goes in v10:
time: 52.1 us; the launch traced here: 51.8 us
  Pallas kernels  20.9 us (40%)
  waiting for transfers between devices  11.1 us (21%)
  matrix products  8.27 us (16%)
  starting transfers between devices  6.23 us (12%)
  other arithmetic  4.7 us (9%)
  local copies, waits for them, and re-layouts  0.61 us (1%)
    ppermute x4, waiting for transfers between devices, exchange(): return with_layout_constraint(lax.ppermute(part, 'seq', pairs), row_major)  11.1 us
    pallas_call x1, Pallas kernels, cache_partials(): pl.pallas_call(cache_partial_kernel, out_shape=(half, half), in_specs=[sm...  8.52 us
    dot_general x2, matrix products, project(): jnp.dot(token_rows, weight, preferred_element_type=jnp.float32)  8.27 us
    pallas_call x1, Pallas kernels, tail(): pl.pallas_call(tail_kernel, out_shape=jax.ShapeDtypeStruct(patches.shape,...  7.31 us
    ppermute x4, starting transfers between devices, exchange(): return with_layout_constraint(lax.ppermute(part, 'seq', pairs), row_major)  6.23 us
    pallas_call x1, Pallas kernels, new_partials(): pl.pallas_call(new_partial_kernel, out_shape=jax.ShapeDtypeStruct((HEADS,...  5.06 us
  transfers between devices with their start and end apart: 4, of which 3 were waited for; matrix products, arithmetic and copies ran while one was open for 11% of the time, Pallas kernels for 10%

profile of v10, /device:TPU:1, one launch (start us, length us, event | category | flops | bytes accessed | tf_op | source)
XLA Modules:
  0.0 51.8 jit_solution(4369891099536717639)
XLA Ops:
  0.0 1.0 %fusion.12 = f32[8,4]{1,0:T(8,128)S(1)} fusion(bf16[8,4,1280]{2,1,0:T(4,128)(2,1)} %patch_ref.1), kind=kLoop, calls=%fused_computation.10 | loop fusion | flops 122848 | bytes 82048 | tf_op jit(solution)/shard_map/reduce_sum | solution.py:19
  1.0 0.6 %pad_add_fusion.offset_ref = s32[2]{0:T(128)} fusion(s32[1]{0:T(128)} %bitcast.1, s32[1]{0:T(128)} %bitcast), kind=kLoop, calls=%fused_computation.34 | loop fusion | flops 2 | bytes 16 | tf_op jit(solution)/shard_map/stack | solution.py:254
  1.6 3.4 %fusion.9.query_ref = bf16[8,4,1280]{2,1,0:T(4,128)(2,1)} fusion(bf16[1280,3840]{1,0:T(8,128)(2,1)} %param.19, bf16[8,4,1280]{2,1,0:T(4,128)(2,1)} %patch_ref.1, f32[1280]{0:T(1024)} %param.18, f32[8,4]{1,0:T(8,128)S(1)} %add_rsqrt_fusion), kind=kOutput, calls=%fused_computation.7 | convolution fusion | flops 105062400 | bytes 3448960 | tf_op jit(solution)/shard_map/dot_general | solution.py:23
  5.0 8.5 %shard_map.136 = (f32[8,32,128]{2,1,0:T(8,128)}, f32[8,32,128]{2,1,0:T(8,128)}) custom-call(s32[2]{0:T(128)} %pad_add_fusion.offset_ref, s32[8]{0:T(128)} %length_ref.1, bf16[8,4,1280]{2,1,0:T(4,128)(2,1)} %fusion.9.query_ref, bf16[8,128,1280]{2,1,0:T(8,128)(2,1)} %key_ref.1, bf16[8,128,1280]{2,1,0:T(8,128)(2,1)} %value_ref.1, ...), custom_call_target="tpu_custom_call" | custom-call | tf_op jit(solution)/shard_map/pallas_call | solution.py:183
  13.6 0.0 collective-permute-start
  13.6 1.5 %collective-permute-done = f32[256,128]{1,0:T(8,128)S(1)} collective-permute-done((f32[256,128]{1,0:T(8,128)}, f32[256,128]{1,0:T(8,128)S(1)}, u32[]{:S(2)}, u32[]{:S(2)}) %collective-permute-start) | collective-permute-done | bytes 131104 | tf_op jit(solution)/shard_map/ppermute | solution.py:44
  15.1 0.9 %bitcast_select_fusion.1 = (f32[256,128]{1,0:T(8,128)S(1)}, f32[256,128]{1,0:T(8,128)S(1)}) fusion(f32[256,128]{1,0:T(8,128)S(1)} %collective-permute-done, f32[8,32,128]{2,1,0:T(8,128)} %get-tuple-element.7, pred[]{:T(512)S(6)} %eq.26), kind=kLoop, calls=%fused_computation.14 | loop fusion | flops 65536 | bytes 524289 | tf_op jit(solution)/shard_map/jit(_where)/select_n | solution.py:55
  16.0 0.3 fusion.17
  16.3 0.2 add_select_fusion.2
  16.5 2.5 %collective-permute-start.1 = (f32[256,128]{1,0:T(8,128)S(1)}, f32[256,128]{1,0:T(8,128)S(1)}, u32[]{:S(2)}, u32[]{:S(2)}) collective-permute-start(f32[256,128]{1,0:T(8,128)S(1)} %add_select_fusion.2), channel_id=1, source_target_pairs={{0,2},{1,3},{2,0},{3,1},{4,6},{5,7},{6,4},{7,5},{8,10},{9,11},{10,... | collective-permute-start | bytes 393224 | tf_op jit(solution)/shard_map/ppermute | solution.py:44
  19.0 3.5 %collective-permute-done.1 = f32[256,128]{1,0:T(8,128)S(1)} collective-permute-done((f32[256,128]{1,0:T(8,128)S(1)}, f32[256,128]{1,0:T(8,128)S(1)}, u32[]{:S(2)}, u32[]{:S(2)}) %collective-permute-start.1) | collective-permute-done | bytes 131104 | tf_op jit(solution)/shard_map/ppermute | solution.py:44
  22.5 0.3 fusion.18
  22.8 0.2 add_select_fusion.1
  23.0 2.3 %collective-permute-start.2 = (f32[256,128]{1,0:T(8,128)S(1)}, f32[256,128]{1,0:T(8,128)S(1)}, u32[]{:S(2)}, u32[]{:S(2)}) collective-permute-start(f32[256,128]{1,0:T(8,128)S(1)} %add_select_fusion.1), channel_id=1, source_target_pairs={{0,4},{1,5},{2,6},{3,7},{4,0},{5,1},{6,2},{7,3},{8,12},{9,13},{10,... | collective-permute-start | bytes 393224 | tf_op jit(solution)/shard_map/ppermute | solution.py:44
  25.3 6.0 %collective-permute-done.2 = f32[256,128]{1,0:T(8,128)S(1)} collective-permute-done((f32[256,128]{1,0:T(8,128)S(1)}, f32[256,128]{1,0:T(8,128)S(1)}, u32[]{:S(2)}, u32[]{:S(2)}) %collective-permute-start.2) | collective-permute-done | bytes 131104 | tf_op jit(solution)/shard_map/ppermute | solution.py:44
  31.3 0.3 fusion.19
  31.6 0.2 add_select_fusion
  31.8 1.5 %collective-permute-start.3 = (f32[256,128]{1,0:T(8,128)S(1)}, f32[256,128]{1,0:T(8,128)S(1)}, u32[]{:S(2)}, u32[]{:S(2)}) collective-permute-start(f32[256,128]{1,0:T(8,128)S(1)} %add_select_fusion), channel_id=1, source_target_pairs={{0,1},{1,0},{2,3},{3,2},{4,5},{5,4},{6,7},{7,6},{8,9},{9,8},{10,11... | collective-permute-start | bytes 393224 | tf_op jit(solution)/shard_map/ppermute | solution.py:44
  33.3 4.9 %fusion.3.kv_ref = bf16[8,4,2560]{2,1,0:T(4,128)(2,1)} fusion(bf16[1280,3840]{1,0:T(8,128)(2,1)} %param.19, bf16[8,4,1280]{2,1,0:T(4,128)(2,1)S(1)} %copy-done, f32[1280]{0:T(1024)S(1)} %copy-done.2, f32[8,4]{1,0:T(8,128)S(1)} %add_rsqrt_fusion), kind=kOutput, calls=%fused_computation.3 | convolution fusion | flops 209960960 | bytes 6804608 | tf_op jit(solution)/shard_map/dot_general | solution.py:23
  38.1 0.6 %reshape.28.gain_ref = f32[1,1280]{1,0:T(1,128)} reshape(f32[1280]{0:T(1024)S(1)} %copy-done.1) | data formatting | bytes 10240 | tf_op jit(solution)/shard_map/reshape | solution.py:242
  38.7 5.1 %shard_map.137.new_ref = f32[16,32,128]{2,1,0:T(8,128)} custom-call(bf16[8,4,1280]{2,1,0:T(4,128)(2,1)} %fusion.9.query_ref, bf16[8,4,2560]{2,1,0:T(4,128)(2,1)} %fusion.3.kv_ref, bf16[64,1280]{1,0:T(8,128)(2,1)} %constant.68.clone.qmask_ref, bf16[1280,128]{1,0:T(8,128)(2,1)} %constant.66.clone.fold_ref), custom_call_target="tpu_custom_call" | custom-call | tf_op jit(solution)/shard_map/pallas_call | solution.py:196
  43.8 0.0 collective-permute-done.3
  43.8 0.7 %broadcast_select_fusion.4 = (f32[256,128]{1,0:T(8,128)}, f32[256,128]{1,0:T(8,128)}) fusion(f32[256,128]{1,0:T(8,128)S(1)} %collective-permute-done.3, f32[256,128]{1,0:T(8,128)S(1)} %add_select_fusion, pred[]{:T(512)S(6)} %eq.26), kind=kLoop, calls=%fused_computation.31 | loop fusion | flops 65536 | bytes 524289 | tf_op jit(solution)/shard_map/jit(_where)/select_n | solution.py:64
  44.5 7.3 %shard_map.138 = bf16[8,4,1280]{2,1,0:T(4,128)(2,1)} custom-call(f32[8,32,128]{2,1,0:T(8,128)} %bitcast.19, f32[8,32,128]{2,1,0:T(8,128)} %bitcast.18, f32[16,32,128]{2,1,0:T(8,128)} %shard_map.137.new_ref, bf16[8,4,1280]{2,1,0:T(4,128)(2,1)} %patch_ref.1, bf16[1280,1280]{1,0:T(8,128)(2,1)} %w_out_ref.1, f32[1,1280]{1,0:T(1,128)} %reshape.28.gain_ref, ...), custom_call_target="tpu_custom_call" | custom-call | tf_op jit(solution)/shard_map/pallas_call | solution.py:237
  (10 shorter events, 0.1 us)
Async XLA Ops:
  1.6 31.6 %copy-start = (bf16[8,4,1280]{2,1,0:T(4,128)(2,1)S(1)}, bf16[8,4,1280]{2,1,0:T(4,128)(2,1)}, u32[]{:S(2)}) copy-start(bf16[8,4,1280]{2,1,0:T(4,128)(2,1)} %patch_ref.1) | copy-start | bytes 245764
  1.6 31.6 %copy-start.2 = (f32[1280]{0:T(1024)S(1)}, f32[1280]{0:T(1024)}, u32[]{:S(2)}) copy-start(f32[1280]{0:T(1024)} %param.18) | copy-start | bytes 15364
  13.6 24.6 %copy-start.1 = (f32[1280]{0:T(1024)S(1)}, f32[1280]{0:T(1024)}, u32[]{:S(2)}) copy-start(f32[1280]{0:T(1024)} %param.21) | copy-start | bytes 15364
  13.6 1.6 %collective-permute-start = (f32[256,128]{1,0:T(8,128)}, f32[256,128]{1,0:T(8,128)S(1)}, u32[]{:S(2)}, u32[]{:S(2)}) collective-permute-start(f32[256,128]{1,0:T(8,128)} %bitcast.20), channel_id=1, source_target_pairs={{0,1},{1,0},{2,3},{3,2},{4,5},{5,4},{6,7},{7,6},{8,9},{9,8},{10,11... | collective-permute-start | bytes 393224 | tf_op jit(solution)/shard_map/ppermute | solution.py:44
  16.5 6.0 %collective-permute-start.1 = (f32[256,128]{1,0:T(8,128)S(1)}, f32[256,128]{1,0:T(8,128)S(1)}, u32[]{:S(2)}, u32[]{:S(2)}) collective-permute-start(f32[256,128]{1,0:T(8,128)S(1)} %add_select_fusion.2), channel_id=1, source_target_pairs={{0,2},{1,3},{2,0},{3,1},{4,6},{5,7},{6,4},{7,5},{8,10},{9,11},{10,... | collective-permute-start | bytes 393224 | tf_op jit(solution)/shard_map/ppermute | solution.py:44
  23.0 8.3 %collective-permute-start.2 = (f32[256,128]{1,0:T(8,128)S(1)}, f32[256,128]{1,0:T(8,128)S(1)}, u32[]{:S(2)}, u32[]{:S(2)}) collective-permute-start(f32[256,128]{1,0:T(8,128)S(1)} %add_select_fusion.1), channel_id=1, source_target_pairs={{0,4},{1,5},{2,6},{3,7},{4,0},{5,1},{6,2},{7,3},{8,12},{9,13},{10,... | collective-permute-start | bytes 393224 | tf_op jit(solution)/shard_map/ppermute | solution.py:44
  31.8 12.0 %collective-permute-start.3 = (f32[256,128]{1,0:T(8,128)S(1)}, f32[256,128]{1,0:T(8,128)S(1)}, u32[]{:S(2)}, u32[]{:S(2)}) collective-permute-start(f32[256,128]{1,0:T(8,128)S(1)} %add_select_fusion), channel_id=1, source_target_pairs={{0,1},{1,0},{2,3},{3,2},{4,5},{5,4},{6,7},{7,6},{8,9},{9,8},{10,11... | collective-permute-start | bytes 393224 | tf_op jit(solution)/shard_map/ppermute | solution.py:44

commit v11 on v10

--- a/solution.py
+++ b/solution.py
@@ -17,10 +17,6 @@
 
 def rms_norm(values, gain):
     return values * lax.rsqrt(jnp.mean(values * values, axis=-1, keepdims=True) + epsilon) * gain
-
-
-def project(token_rows, weight):
-    return jnp.dot(token_rows, weight, preferred_element_type=jnp.float32).astype(jnp.bfloat16)
 
 
 LANES = 128
@@ -86,19 +82,29 @@
         target[h, pl.ds(r * count, count), :] = folded[h * count:(h + 1) * count, :]
 
 
+def normed_rows(patch_ref, gain_ref):
+    groups = patch_ref.shape[0]
+    rows = jnp.concatenate([patch_ref[r].astype(jnp.float32) for r in range(groups)], axis=0)
+    return rms_norm(rows, gain_ref[...]).astype(jnp.bfloat16)
+
+
 def cache_partial_kernel(
-    offset_ref, length_ref, query_ref, key_ref, value_ref, qmask_ref, fold_ref, kept_ref, sent_ref
+    length_ref, patch_ref, gain_ref, wq_ref, key_ref, value_ref, qmask_ref, fold_ref, kept_ref, sent_ref, query_ref
 ):
     groups, slots, _ = key_ref.shape
     half_heads = kept_ref.shape[0]
     heads = 2 * half_heads
     count = kept_ref.shape[1] // groups
-    core = offset_ref[1]
+    me = lax.axis_index("seq")
+    core = me % 2
+    query_float = jnp.dot(normed_rows(patch_ref, gain_ref), wq_ref[...], preferred_element_type=jnp.float32)
+    for r in range(groups):
+        query_ref[r] = query_float[r * count:(r + 1) * count, :].astype(query_ref.dtype)
     scale_factor = HD ** (-0.5)
     qmask = qmask_ref[core]
     qmask_float = qmask.astype(jnp.float32)
     fold = fold_ref[...]
-    position = offset_ref[0] + lax.broadcasted_iota(jnp.int32, (1, slots), 1)
+    position = me * slots + lax.broadcasted_iota(jnp.int32, (1, slots), 1)
     lane = lax.broadcasted_iota(jnp.int32, (heads * count, LANES), 1)
     for r in range(groups):
         queries = query_ref[r]
@@ -120,9 +126,12 @@
             target[h % half_heads, pl.ds(r * count, count), :] = folded[h * count:(h + 1) * count, :]
 
 
-def new_partial_kernel(query_ref, kv_ref, qmask_ref, fold_ref, out_ref):
+def new_partial_kernel(patch_ref, gain_ref, wk_ref, wv_ref, query_ref, qmask_ref, fold_ref, out_ref):
     groups, count, width = query_ref.shape
     heads = out_ref.shape[0]
+    normed = normed_rows(patch_ref, gain_ref)
+    keys_all = jnp.dot(normed, wk_ref[...], preferred_element_type=jnp.float32).astype(jnp.bfloat16)
+    values_all = jnp.dot(normed, wv_ref[...], preferred_element_type=jnp.float32).astype(jnp.bfloat16)
     scale_factor = HD ** (-0.5)
     qmask = qmask_ref[...]
     qmask_float = qmask.astype(jnp.float32)
@@ -132,9 +141,8 @@
     for r in range(groups):
         queries = query_ref[r]
         query_float = (jnp.concatenate([queries] * heads, axis=0) * qmask).astype(jnp.float32)
-        pair = kv_ref[r]
-        keys_new = pair[:, :width].astype(jnp.float32)
-        values_new = pair[:, width:].astype(jnp.float32)
+        keys_new = keys_all.astype(jnp.float32)[r * count:(r + 1) * count, :]
+        values_new = values_all.astype(jnp.float32)[r * count:(r + 1) * count, :]
         new_scores = []
         for u in range(count):
             score = jnp.sum(query_float * keys_new[u:u + 1, :], axis=1, keepdims=True) * scale_factor
@@ -171,34 +179,39 @@
     return jnp.asarray(np.stack(masks), dtype=jnp.bfloat16)
 
 
-def cache_partials(offset, cache_len, query_rows, key_cache, value_cache):
+def cache_partials(cache_len, patches, attn_gain, w_qkv, key_cache, value_cache):
     groups, _, width = key_cache.shape
-    count = query_rows.shape[1]
+    count = patches.shape[1]
     rows = groups * count
     _, fold = head_constants(count, width)
     qmask = ordered_masks(count, width)
     smem = pl.BlockSpec(memory_space=pltpu.SMEM)
     vmem = pl.BlockSpec(memory_space=pltpu.VMEM)
+    query_block = pl.BlockSpec((width, width), lambda i: (0, 0))
     half = jax.ShapeDtypeStruct((HEADS // 2, rows, LANES), jnp.float32)
     return pl.pallas_call(
         cache_partial_kernel,
-        out_shape=(half, half),
-        in_specs=[smem, smem, vmem, vmem, vmem, vmem, vmem],
-        out_specs=(vmem, vmem),
-    )(offset, cache_len, query_rows, key_cache, value_cache, qmask, fold)
-
-
-def new_partials(query_rows, kv_rows):
+        grid=(1,),
+        out_shape=(half, half, jax.ShapeDtypeStruct(patches.shape, jnp.bfloat16)),
+        in_specs=[smem, vmem, vmem, query_block, vmem, vmem, vmem, vmem],
+        out_specs=(vmem, vmem, vmem),
+    )(cache_len, patches, attn_gain.reshape(1, width), w_qkv, key_cache, value_cache, qmask, fold)
+
+
+def new_partials(patches, attn_gain, w_qkv, query_rows):
     groups, count, width = query_rows.shape
     rows = groups * count
     qmask, fold = head_constants(count, width)
     vmem = pl.BlockSpec(memory_space=pltpu.VMEM)
+    key_block = pl.BlockSpec((width, width), lambda i: (0, 1))
+    value_block = pl.BlockSpec((width, width), lambda i: (0, 2))
     return pl.pallas_call(
         new_partial_kernel,
+        grid=(1,),
         out_shape=jax.ShapeDtypeStruct((HEADS, rows, LANES), jnp.float32),
-        in_specs=[vmem, vmem, vmem, vmem],
+        in_specs=[vmem, vmem, key_block, value_block, vmem, vmem, vmem],
         out_specs=vmem,
-    )(query_rows, kv_rows, qmask, fold)
+    )(patches, attn_gain.reshape(1, width), w_qkv, w_qkv, query_rows, qmask, fold)
 
 
 def tail_kernel(low_ref, high_ref, new_ref, patch_ref, w_out_ref, gain_ref, w_up_ref, w_down_ref, out_ref):
@@ -245,16 +258,9 @@
 def layer(
     patches, key_cache, value_cache, cache_len, attn_gain, w_qkv, w_out, ffn_gain, w_up, w_down
 ):
-    _, _, model_width = patches.shape
-    slots_here = key_cache.shape[1]
     seq_count = lax.axis_size("seq")
-    normed = rms_norm(patches.astype(jnp.float32), attn_gain).astype(jnp.bfloat16)
-    query_rows = project(normed, w_qkv[:, :model_width])
-    me = lax.axis_index("seq")
-    offset = jnp.stack([me * slots_here, me % 2]).astype(jnp.int32)
-    kept, sent = cache_partials(offset, cache_len, query_rows, key_cache, value_cache)
-    kv_rows = project(normed, w_qkv[:, model_width:])
-    new_packed = new_partials(query_rows, kv_rows)
+    kept, sent, query_rows = cache_partials(cache_len, patches, attn_gain, w_qkv, key_cache, value_cache)
+    new_packed = new_partials(patches, attn_gain, w_qkv, query_rows)
     low_half, high_half = combine_over_seq(kept, sent, seq_count)
     return tail(low_half, high_half, new_packed, patches, w_out, ffn_gain, w_up, w_down)
 

time: 52.1 us -> 47.8 us (0.917)
  matrix products: 8.27 us -> 0 us
  Pallas kernels: 20.9 us -> 25.2 us
  other arithmetic: 4.7 us -> 3.07 us
  local copies, waits for them, and re-layouts: 0.61 us -> 1.89 us
    dot_general x2 -> x0, matrix products: 8.27 us -> none  [project(): jnp.dot(token_rows, weight, preferred_element_type=jnp.float32)]
    pallas_call x2, Pallas kernels: 13.6 us -> 17.9 us  [the longest x1 10.3 us: cache_partials(): pl.pallas_call(cache_partial_kernel, grid=(1,), out_shape=(half, half, ja...]
    reshape x0 -> x1, local copies, waits for them, and re-layouts: none -> 1.29 us  [cache_partials(): attn_gain.reshape(1, width)]
    reduce_sum x1 -> x0, other arithmetic: 1.01 us -> none  [rms_norm(): jnp.mean(values * values, axis=-1, keepdims=True) + epsilon]
    another operation x1 -> x0, other arithmetic: 0.61 us -> none  [layer(): offset = jnp.stack([me * slots_here, me % 2]).astype(jnp.int32)]
  transfers between devices with their start and end apart: 4 -> 4, of which waited for: 3 -> 3; matrix products, arithmetic and copies ran while one was open for 11% -> 1% of each run, Pallas kernels for 10% -> 16%
where the time goes in v11:
time: 47.8 us; the launch traced here: 47.6 us
  Pallas kernels  25.2 us (53%)
  waiting for transfers between devices  11.1 us (23%)
  starting transfers between devices  6.23 us (13%)
  other arithmetic  3.07 us (6%)
  local copies, waits for them, and re-layouts  1.89 us (4%)
    ppermute x4, waiting for transfers between devices, exchange(): return with_layout_constraint(lax.ppermute(part, 'seq', pairs), row_major)  11.1 us
    pallas_call x1, Pallas kernels, cache_partials(): pl.pallas_call(cache_partial_kernel, grid=(1,), out_shape=(half, half, ja...  10.3 us
    pallas_call x1, Pallas kernels, new_partials(): pl.pallas_call(new_partial_kernel, grid=(1,), out_shape=jax.ShapeDtypeStr...  7.6 us
    pallas_call x1, Pallas kernels, tail(): pl.pallas_call(tail_kernel, out_shape=jax.ShapeDtypeStruct(patches.shape,...  7.31 us
    ppermute x4, starting transfers between devices, exchange(): return with_layout_constraint(lax.ppermute(part, 'seq', pairs), row_major)  6.23 us
    reshape x1, local copies, waits for them, and re-layouts, cache_partials(): attn_gain.reshape(1, width)  1.29 us
  transfers between devices with their start and end apart: 4, of which 3 were waited for; matrix products, arithmetic and copies ran while one was open for 1% of the time, Pallas kernels for 16%

profile of v11, /device:TPU:1, one launch (start us, length us, event | category | flops | bytes accessed | tf_op | source)
XLA Modules:
  0.0 47.6 jit_solution(10031266162007887034)
XLA Ops:
  0.0 1.3 %reshape.19.gain_ref = f32[1,1280]{1,0:T(1,128)} reshape(f32[1280]{0:T(1024)} %param.18) | data formatting | bytes 10240 | tf_op jit(solution)/shard_map/reshape | solution.py:198
  1.3 10.3 %shard_map.136 = (f32[8,32,128]{2,1,0:T(8,128)}, f32[8,32,128]{2,1,0:T(8,128)}, bf16[8,4,1280]{2,1,0:T(4,128)(2,1)}) custom-call(s32[8]{0:T(128)} %length_ref.1, bf16[8,4,1280]{2,1,0:T(4,128)(2,1)} %patch_ref.5, f32[1,1280]{1,0:T(1,128)} %reshape.19.gain_ref, bf16[1280,3840]{1,0:T(8,128)(2,1)} %wv_ref.1, bf16[8,128,1280]{2,1,0:T(8,128)(2,1)} %key_ref.1, ...), custom_call_target="tpu_custom_call" | custom-call | tf_op jit(solution)/shard_map/pallas_call | solution.py:192
  11.6 0.0 copy-start
  11.6 0.0 collective-permute-start
  11.7 1.5 %collective-permute-done = f32[256,128]{1,0:T(8,128)S(1)} collective-permute-done((f32[256,128]{1,0:T(8,128)}, f32[256,128]{1,0:T(8,128)S(1)}, u32[]{:S(2)}, u32[]{:S(2)}) %collective-permute-start) | collective-permute-done | bytes 131104 | tf_op jit(solution)/shard_map/ppermute | solution.py:40
  13.2 0.9 %bitcast_select_fusion.1 = (f32[256,128]{1,0:T(8,128)S(1)}, f32[256,128]{1,0:T(8,128)S(1)}) fusion(f32[256,128]{1,0:T(8,128)S(1)} %collective-permute-done, f32[8,32,128]{2,1,0:T(8,128)} %get-tuple-element.8, pred[]{:T(512)S(6)} %eq.25), kind=kLoop, calls=%fused_computation.1 | loop fusion | flops 65536 | bytes 524289 | tf_op jit(solution)/shard_map/jit(_where)/select_n | solution.py:51
  14.1 0.3 fusion
  14.4 0.2 add_select_fusion.2
  14.6 2.5 %collective-permute-start.1 = (f32[256,128]{1,0:T(8,128)S(1)}, f32[256,128]{1,0:T(8,128)S(1)}, u32[]{:S(2)}, u32[]{:S(2)}) collective-permute-start(f32[256,128]{1,0:T(8,128)S(1)} %add_select_fusion.2), channel_id=1, source_target_pairs={{0,2},{1,3},{2,0},{3,1},{4,6},{5,7},{6,4},{7,5},{8,10},{9,11},{10,... | collective-permute-start | bytes 393224 | tf_op jit(solution)/shard_map/ppermute | solution.py:40
  17.1 3.5 %collective-permute-done.1 = f32[256,128]{1,0:T(8,128)S(1)} collective-permute-done((f32[256,128]{1,0:T(8,128)S(1)}, f32[256,128]{1,0:T(8,128)S(1)}, u32[]{:S(2)}, u32[]{:S(2)}) %collective-permute-start.1) | collective-permute-done | bytes 131104 | tf_op jit(solution)/shard_map/ppermute | solution.py:40
  20.6 0.3 fusion.1
  20.9 0.2 add_select_fusion.1
  21.1 2.3 %collective-permute-start.2 = (f32[256,128]{1,0:T(8,128)S(1)}, f32[256,128]{1,0:T(8,128)S(1)}, u32[]{:S(2)}, u32[]{:S(2)}) collective-permute-start(f32[256,128]{1,0:T(8,128)S(1)} %add_select_fusion.1), channel_id=1, source_target_pairs={{0,4},{1,5},{2,6},{3,7},{4,0},{5,1},{6,2},{7,3},{8,12},{9,13},{10,... | collective-permute-start | bytes 393224 | tf_op jit(solution)/shard_map/ppermute | solution.py:40
  23.3 6.0 %collective-permute-done.2 = f32[256,128]{1,0:T(8,128)S(1)} collective-permute-done((f32[256,128]{1,0:T(8,128)S(1)}, f32[256,128]{1,0:T(8,128)S(1)}, u32[]{:S(2)}, u32[]{:S(2)}) %collective-permute-start.2) | collective-permute-done | bytes 131104 | tf_op jit(solution)/shard_map/ppermute | solution.py:40
  29.4 0.3 fusion.2
  29.7 0.2 add_select_fusion
  29.9 1.5 %collective-permute-start.3 = (f32[256,128]{1,0:T(8,128)S(1)}, f32[256,128]{1,0:T(8,128)S(1)}, u32[]{:S(2)}, u32[]{:S(2)}) collective-permute-start(f32[256,128]{1,0:T(8,128)S(1)} %add_select_fusion), channel_id=1, source_target_pairs={{0,1},{1,0},{2,3},{3,2},{4,5},{5,4},{6,7},{7,6},{8,9},{9,8},{10,11... | collective-permute-start | bytes 393224 | tf_op jit(solution)/shard_map/ppermute | solution.py:40
  31.3 0.0 copy-done
  31.3 0.6 %reshape.24.gain_ref = f32[1,1280]{1,0:T(1,128)} reshape(f32[1280]{0:T(1024)S(1)} %copy-done) | data formatting | bytes 10240 | tf_op jit(solution)/shard_map/reshape | solution.py:255
  31.9 7.6 %shard_map.137.new_ref = f32[16,32,128]{2,1,0:T(8,128)} custom-call(bf16[8,4,1280]{2,1,0:T(4,128)(2,1)} %patch_ref.5, f32[1,1280]{1,0:T(1,128)} %reshape.19.gain_ref, bf16[1280,3840]{1,0:T(8,128)(2,1)} %wv_ref.1, bf16[1280,3840]{1,0:T(8,128)(2,1)} %wv_ref.1, bf16[8,4,1280]{2,1,0:T(4,128)(2,1)} %get-tuple-element.10.query_ref, ...), custom_call_target="tpu_custom_call" | custom-call | tf_op jit(solution)/shard_map/pallas_call | solution.py:208
  39.5 0.0 collective-permute-done.3
  39.5 0.7 %broadcast_select_fusion.4 = (f32[256,128]{1,0:T(8,128)}, f32[256,128]{1,0:T(8,128)}) fusion(f32[256,128]{1,0:T(8,128)S(1)} %collective-permute-done.3, f32[256,128]{1,0:T(8,128)S(1)} %add_select_fusion, pred[]{:T(512)S(6)} %eq.25), kind=kLoop, calls=%fused_computation.18 | loop fusion | flops 65536 | bytes 524289 | tf_op jit(solution)/shard_map/jit(_where)/select_n | solution.py:60
  40.2 7.3 %shard_map.138 = bf16[8,4,1280]{2,1,0:T(4,128)(2,1)} custom-call(f32[8,32,128]{2,1,0:T(8,128)} %bitcast.7, f32[8,32,128]{2,1,0:T(8,128)} %bitcast.6, f32[16,32,128]{2,1,0:T(8,128)} %shard_map.137.new_ref, bf16[8,4,1280]{2,1,0:T(4,128)(2,1)} %patch_ref.5, bf16[1280,1280]{1,0:T(8,128)(2,1)} %w_out_ref.1, f32[1,1280]{1,0:T(1,128)} %reshape.24.gain_ref, ...), custom_call_target="tpu_custom_call" | custom-call | tf_op jit(solution)/shard_map/pallas_call | solution.py:250
  (3 shorter events, 0.0 us)
Async XLA Ops:
  11.6 19.7 %copy-start = (f32[1280]{0:T(1024)S(1)}, f32[1280]{0:T(1024)}, u32[]{:S(2)}) copy-start(f32[1280]{0:T(1024)} %param.21) | copy-start | bytes 15364
  11.6 1.6 %collective-permute-start = (f32[256,128]{1,0:T(8,128)}, f32[256,128]{1,0:T(8,128)S(1)}, u32[]{:S(2)}, u32[]{:S(2)}) collective-permute-start(f32[256,128]{1,0:T(8,128)} %bitcast.8), channel_id=1, source_target_pairs={{0,1},{1,0},{2,3},{3,2},{4,5},{5,4},{6,7},{7,6},{8,9},{9,8},{10,11... | collective-permute-start | bytes 393224 | tf_op jit(solution)/shard_map/ppermute | solution.py:40
  14.6 6.0 %collective-permute-start.1 = (f32[256,128]{1,0:T(8,128)S(1)}, f32[256,128]{1,0:T(8,128)S(1)}, u32[]{:S(2)}, u32[]{:S(2)}) collective-permute-start(f32[256,128]{1,0:T(8,128)S(1)} %add_select_fusion.2), channel_id=1, source_target_pairs={{0,2},{1,3},{2,0},{3,1},{4,6},{5,7},{6,4},{7,5},{8,10},{9,11},{10,... | collective-permute-start | bytes 393224 | tf_op jit(solution)/shard_map/ppermute | solution.py:40
  21.1 8.3 %collective-permute-start.2 = (f32[256,128]{1,0:T(8,128)S(1)}, f32[256,128]{1,0:T(8,128)S(1)}, u32[]{:S(2)}, u32[]{:S(2)}) collective-permute-start(f32[256,128]{1,0:T(8,128)S(1)} %add_select_fusion.1), channel_id=1, source_target_pairs={{0,4},{1,5},{2,6},{3,7},{4,0},{5,1},{6,2},{7,3},{8,12},{9,13},{10,... | collective-permute-start | bytes 393224 | tf_op jit(solution)/shard_map/ppermute | solution.py:40
  29.9 9.7 %collective-permute-start.3 = (f32[256,128]{1,0:T(8,128)S(1)}, f32[256,128]{1,0:T(8,128)S(1)}, u32[]{:S(2)}, u32[]{:S(2)}) collective-permute-start(f32[256,128]{1,0:T(8,128)S(1)} %add_select_fusion), channel_id=1, source_target_pairs={{0,1},{1,0},{2,3},{3,2},{4,5},{5,4},{6,7},{7,6},{8,9},{9,8},{10,11... | collective-permute-start | bytes 393224 | tf_op jit(solution)/shard_map/ppermute | solution.py:40

commit v12 on v11

--- a/solution.py
+++ b/solution.py
@@ -126,12 +126,17 @@
             target[h % half_heads, pl.ds(r * count, count), :] = folded[h * count:(h + 1) * count, :]
 
 
-def new_partial_kernel(patch_ref, gain_ref, wk_ref, wv_ref, query_ref, qmask_ref, fold_ref, out_ref):
+def kv_projection_kernel(patch_ref, gain_ref, wk_ref, wv_ref, key_ref, value_ref):
+    normed = normed_rows(patch_ref, gain_ref)
+    key_ref[...] = jnp.dot(normed, wk_ref[...], preferred_element_type=jnp.float32).astype(key_ref.dtype)
+    value_ref[...] = jnp.dot(normed, wv_ref[...], preferred_element_type=jnp.float32).astype(value_ref.dtype)
+
+
+def new_partial_kernel(query_ref, key_new_ref, value_new_ref, qmask_ref, fold_ref, out_ref):
     groups, count, width = query_ref.shape
     heads = out_ref.shape[0]
-    normed = normed_rows(patch_ref, gain_ref)
-    keys_all = jnp.dot(normed, wk_ref[...], preferred_element_type=jnp.float32).astype(jnp.bfloat16)
-    values_all = jnp.dot(normed, wv_ref[...], preferred_element_type=jnp.float32).astype(jnp.bfloat16)
+    keys_all = key_new_ref[...]
+    values_all = value_new_ref[...]
     scale_factor = HD ** (-0.5)
     qmask = qmask_ref[...]
     qmask_float = qmask.astype(jnp.float32)
@@ -195,23 +200,35 @@
         out_shape=(half, half, jax.ShapeDtypeStruct(patches.shape, jnp.bfloat16)),
         in_specs=[smem, vmem, vmem, query_block, vmem, vmem, vmem, vmem],
         out_specs=(vmem, vmem, vmem),
-    )(cache_len, patches, attn_gain.reshape(1, width), w_qkv, key_cache, value_cache, qmask, fold)
-
-
-def new_partials(patches, attn_gain, w_qkv, query_rows):
+    )(cache_len, patches, attn_gain, w_qkv, key_cache, value_cache, qmask, fold)
+
+
+def kv_projection(patches, attn_gain, w_qkv):
+    groups, count, width = patches.shape
+    vmem = pl.BlockSpec(memory_space=pltpu.VMEM)
+    key_block = pl.BlockSpec((width, width), lambda i: (0, 1))
+    value_block = pl.BlockSpec((width, width), lambda i: (0, 2))
+    rows = jax.ShapeDtypeStruct((groups * count, width), jnp.bfloat16)
+    return pl.pallas_call(
+        kv_projection_kernel,
+        grid=(1,),
+        out_shape=(rows, rows),
+        in_specs=[vmem, vmem, key_block, value_block],
+        out_specs=(vmem, vmem),
+    )(patches, attn_gain, w_qkv, w_qkv)
+
+
+def new_partials(query_rows, keys_new, values_new):
     groups, count, width = query_rows.shape
     rows = groups * count
     qmask, fold = head_constants(count, width)
     vmem = pl.BlockSpec(memory_space=pltpu.VMEM)
-    key_block = pl.BlockSpec((width, width), lambda i: (0, 1))
-    value_block = pl.BlockSpec((width, width), lambda i: (0, 2))
     return pl.pallas_call(
         new_partial_kernel,
-        grid=(1,),
         out_shape=jax.ShapeDtypeStruct((HEADS, rows, LANES), jnp.float32),
-        in_specs=[vmem, vmem, key_block, value_block, vmem, vmem, vmem],
+        in_specs=[vmem] * 5,
         out_specs=vmem,
-    )(patches, attn_gain.reshape(1, width), w_qkv, w_qkv, query_rows, qmask, fold)
+    )(query_rows, keys_new, values_new, qmask, fold)
 
 
 def tail_kernel(low_ref, high_ref, new_ref, patch_ref, w_out_ref, gain_ref, w_up_ref, w_down_ref, out_ref):
@@ -245,14 +262,13 @@
 
 
 def tail(low_half, high_half, new_packed, patches, w_out, ffn_gain, w_up, w_down):
-    width = patches.shape[-1]
     vmem = pl.BlockSpec(memory_space=pltpu.VMEM)
     return pl.pallas_call(
         tail_kernel,
         out_shape=jax.ShapeDtypeStruct(patches.shape, jnp.bfloat16),
         in_specs=[vmem] * 8,
         out_specs=vmem,
-    )(low_half, high_half, new_packed, patches, w_out, ffn_gain.reshape(1, width), w_up, w_down)
+    )(low_half, high_half, new_packed, patches, w_out, ffn_gain, w_up, w_down)
 
 
 def layer(
@@ -260,7 +276,8 @@
 ):
     seq_count = lax.axis_size("seq")
     kept, sent, query_rows = cache_partials(cache_len, patches, attn_gain, w_qkv, key_cache, value_cache)
-    new_packed = new_partials(patches, attn_gain, w_qkv, query_rows)
+    keys_new, values_new = kv_projection(patches, attn_gain, w_qkv)
+    new_packed = new_partials(query_rows, keys_new, values_new)
     low_half, high_half = combine_over_seq(kept, sent, seq_count)
     return tail(low_half, high_half, new_packed, patches, w_out, ffn_gain, w_up, w_down)
 

time: 47.8 us -> 48.1 us (level)
  Pallas kernels: 25.2 us -> 27.6 us
  local copies, waits for them, and re-layouts: 1.89 us -> 0 us
    pallas_call x1 -> x2, Pallas kernels: 7.6 us -> 9.9 us  [the longest x1 4.99 us: new_partials(): pl.pallas_call(new_partial_kernel, out_shape=jax.ShapeDtypeStruct((HEADS,...]
    reshape x2 -> x0, local copies, waits for them, and re-layouts: 1.89 us -> none  [the longest x1 1.29 us: cache_partials(): attn_gain.reshape(1, width)]
  transfers between devices with their start and end apart: 4 -> 4, of which waited for: 3 -> 3; matrix products, arithmetic and copies ran while one was open for 1% -> 0% of each run, Pallas kernels for 16% -> 21%
where the time goes in v12:
time: 48.1 us; the launch traced here: 48 us
  Pallas kernels  27.6 us (57%)
  waiting for transfers between devices  11.1 us (23%)
  starting transfers between devices  6.23 us (13%)
  other arithmetic  3.07 us (6%)
    ppermute x4, waiting for transfers between devices, exchange(): return with_layout_constraint(lax.ppermute(part, 'seq', pairs), row_major)  11.1 us
    pallas_call x1, Pallas kernels, cache_partials(): pl.pallas_call(cache_partial_kernel, grid=(1,), out_shape=(half, half, ja...  10.3 us
    pallas_call x1, Pallas kernels, tail(): pl.pallas_call(tail_kernel, out_shape=jax.ShapeDtypeStruct(patches.shape,...  7.31 us
    ppermute x4, starting transfers between devices, exchange(): return with_layout_constraint(lax.ppermute(part, 'seq', pairs), row_major)  6.23 us
    pallas_call x1, Pallas kernels, new_partials(): pl.pallas_call(new_partial_kernel, out_shape=jax.ShapeDtypeStruct((HEADS,...  4.99 us
    pallas_call x1, Pallas kernels, kv_projection(): pl.pallas_call(kv_projection_kernel, grid=(1,), out_shape=(rows, rows), i...  4.92 us
  transfers between devices with their start and end apart: 4, of which 3 were waited for; matrix products, arithmetic and copies ran while one was open for 0% of the time, Pallas kernels for 21%

profile of v12, /device:TPU:1, one launch (start us, length us, event | category | flops | bytes accessed | tf_op | source)
XLA Modules:
  0.0 48.0 jit_solution(17589878647893732031)
XLA Ops:
  0.0 10.3 %shard_map.136 = (f32[8,32,128]{2,1,0:T(8,128)}, f32[8,32,128]{2,1,0:T(8,128)}, bf16[8,4,1280]{2,1,0:T(4,128)(2,1)}) custom-call(s32[8]{0:T(128)} %length_ref.1, bf16[8,4,1280]{2,1,0:T(4,128)(2,1)} %patch_ref.5, f32[1280]{0:T(1024)} %gain_ref.4, bf16[1280,3840]{1,0:T(8,128)(2,1)} %wv_ref.1, bf16[8,128,1280]{2,1,0:T(8,128)(2,1)} %key_ref.1, ...), custom_call_target="tpu_custom_call" | custom-call | tf_op jit(solution)/shard_map/pallas_call | solution.py:197
  10.3 0.0 collective-permute-start
  10.4 1.5 %collective-permute-done = f32[256,128]{1,0:T(8,128)S(1)} collective-permute-done((f32[256,128]{1,0:T(8,128)}, f32[256,128]{1,0:T(8,128)S(1)}, u32[]{:S(2)}, u32[]{:S(2)}) %collective-permute-start) | collective-permute-done | bytes 131104 | tf_op jit(solution)/shard_map/ppermute | solution.py:40
  11.9 0.9 %bitcast_select_fusion.1 = (f32[256,128]{1,0:T(8,128)S(1)}, f32[256,128]{1,0:T(8,128)S(1)}) fusion(f32[256,128]{1,0:T(8,128)S(1)} %collective-permute-done, f32[8,32,128]{2,1,0:T(8,128)} %get-tuple-element.10, pred[]{:T(512)S(6)} %eq.25), kind=kLoop, calls=%fused_computation.1 | loop fusion | flops 65536 | bytes 524289 | tf_op jit(solution)/shard_map/jit(_where)/select_n | solution.py:51
  12.8 0.3 fusion
  13.1 0.2 add_select_fusion.2
  13.3 2.5 %collective-permute-start.1 = (f32[256,128]{1,0:T(8,128)S(1)}, f32[256,128]{1,0:T(8,128)S(1)}, u32[]{:S(2)}, u32[]{:S(2)}) collective-permute-start(f32[256,128]{1,0:T(8,128)S(1)} %add_select_fusion.2), channel_id=1, source_target_pairs={{0,2},{1,3},{2,0},{3,1},{4,6},{5,7},{6,4},{7,5},{8,10},{9,11},{10,... | collective-permute-start | bytes 393224 | tf_op jit(solution)/shard_map/ppermute | solution.py:40
  15.8 3.5 %collective-permute-done.1 = f32[256,128]{1,0:T(8,128)S(1)} collective-permute-done((f32[256,128]{1,0:T(8,128)S(1)}, f32[256,128]{1,0:T(8,128)S(1)}, u32[]{:S(2)}, u32[]{:S(2)}) %collective-permute-start.1) | collective-permute-done | bytes 131104 | tf_op jit(solution)/shard_map/ppermute | solution.py:40
  19.3 0.3 fusion.1
  19.6 0.2 add_select_fusion.1
  19.8 2.3 %collective-permute-start.2 = (f32[256,128]{1,0:T(8,128)S(1)}, f32[256,128]{1,0:T(8,128)S(1)}, u32[]{:S(2)}, u32[]{:S(2)}) collective-permute-start(f32[256,128]{1,0:T(8,128)S(1)} %add_select_fusion.1), channel_id=1, source_target_pairs={{0,4},{1,5},{2,6},{3,7},{4,0},{5,1},{6,2},{7,3},{8,12},{9,13},{10,... | collective-permute-start | bytes 393224 | tf_op jit(solution)/shard_map/ppermute | solution.py:40
  22.1 6.0 %collective-permute-done.2 = f32[256,128]{1,0:T(8,128)S(1)} collective-permute-done((f32[256,128]{1,0:T(8,128)S(1)}, f32[256,128]{1,0:T(8,128)S(1)}, u32[]{:S(2)}, u32[]{:S(2)}) %collective-permute-start.2) | collective-permute-done | bytes 131104 | tf_op jit(solution)/shard_map/ppermute | solution.py:40
  28.1 0.3 fusion.2
  28.4 0.2 add_select_fusion
  28.6 1.5 %collective-permute-start.3 = (f32[256,128]{1,0:T(8,128)S(1)}, f32[256,128]{1,0:T(8,128)S(1)}, u32[]{:S(2)}, u32[]{:S(2)}) collective-permute-start(f32[256,128]{1,0:T(8,128)S(1)} %add_select_fusion), channel_id=1, source_target_pairs={{0,1},{1,0},{2,3},{3,2},{4,5},{5,4},{6,7},{7,6},{8,9},{9,8},{10,11... | collective-permute-start | bytes 393224 | tf_op jit(solution)/shard_map/ppermute | solution.py:40
  30.0 4.9 %shard_map.137 = (bf16[32,1280]{1,0:T(8,128)(2,1)}, bf16[32,1280]{1,0:T(8,128)(2,1)}) custom-call(bf16[8,4,1280]{2,1,0:T(4,128)(2,1)} %patch_ref.5, f32[1280]{0:T(1024)} %gain_ref.4, bf16[1280,3840]{1,0:T(8,128)(2,1)} %wv_ref.1, bf16[1280,3840]{1,0:T(8,128)(2,1)} %wv_ref.1), custom_call_target="tpu_custom_call" | custom-call | tf_op jit(solution)/shard_map/pallas_call | solution.py:212
  35.0 5.0 %shard_map.138.new_ref = f32[16,32,128]{2,1,0:T(8,128)} custom-call(bf16[8,4,1280]{2,1,0:T(4,128)(2,1)} %get-tuple-element.12.query_ref, bf16[32,1280]{1,0:T(8,128)(2,1)} %get-tuple-element.13.key_new_ref, bf16[32,1280]{1,0:T(8,128)(2,1)} %get-tuple-element.14.value_new_ref, bf16[64,1280]{1,0:T(8,128)(2,1)} %constant.57.clone.qmask_ref, ...), custom_call_target="tpu_custom_call" | custom-call | tf_op jit(solution)/shard_map/pallas_call | solution.py:226
  40.0 0.0 collective-permute-done.3
  40.0 0.7 %broadcast_select_fusion.4 = (f32[256,128]{1,0:T(8,128)}, f32[256,128]{1,0:T(8,128)}) fusion(f32[256,128]{1,0:T(8,128)S(1)} %collective-permute-done.3, f32[256,128]{1,0:T(8,128)S(1)} %add_select_fusion, pred[]{:T(512)S(6)} %eq.25), kind=kLoop, calls=%fused_computation.18 | loop fusion | flops 65536 | bytes 524289 | tf_op jit(solution)/shard_map/jit(_where)/select_n | solution.py:60
  40.7 7.3 %shard_map.139 = bf16[8,4,1280]{2,1,0:T(4,128)(2,1)} custom-call(f32[8,32,128]{2,1,0:T(8,128)} %bitcast.7, f32[8,32,128]{2,1,0:T(8,128)} %bitcast.6, f32[16,32,128]{2,1,0:T(8,128)} %shard_map.138.new_ref, bf16[8,4,1280]{2,1,0:T(4,128)(2,1)} %patch_ref.5, bf16[1280,1280]{1,0:T(8,128)(2,1)} %w_out_ref.1, f32[1280]{0:T(1024)} %gain_ref.5, ...), custom_call_target="tpu_custom_call" | custom-call | tf_op jit(solution)/shard_map/pallas_call | solution.py:266
  (3 shorter events, 0.0 us)
Async XLA Ops:
  10.3 1.6 %collective-permute-start = (f32[256,128]{1,0:T(8,128)}, f32[256,128]{1,0:T(8,128)S(1)}, u32[]{:S(2)}, u32[]{:S(2)}) collective-permute-start(f32[256,128]{1,0:T(8,128)} %bitcast.8), channel_id=1, source_target_pairs={{0,1},{1,0},{2,3},{3,2},{4,5},{5,4},{6,7},{7,6},{8,9},{9,8},{10,11... | collective-permute-start | bytes 393224 | tf_op jit(solution)/shard_map/ppermute | solution.py:40
  13.3 6.0 %collective-permute-start.1 = (f32[256,128]{1,0:T(8,128)S(1)}, f32[256,128]{1,0:T(8,128)S(1)}, u32[]{:S(2)}, u32[]{:S(2)}) collective-permute-start(f32[256,128]{1,0:T(8,128)S(1)} %add_select_fusion.2), channel_id=1, source_target_pairs={{0,2},{1,3},{2,0},{3,1},{4,6},{5,7},{6,4},{7,5},{8,10},{9,11},{10,... | collective-permute-start | bytes 393224 | tf_op jit(solution)/shard_map/ppermute | solution.py:40
  19.8 8.3 %collective-permute-start.2 = (f32[256,128]{1,0:T(8,128)S(1)}, f32[256,128]{1,0:T(8,128)S(1)}, u32[]{:S(2)}, u32[]{:S(2)}) collective-permute-start(f32[256,128]{1,0:T(8,128)S(1)} %add_select_fusion.1), channel_id=1, source_target_pairs={{0,4},{1,5},{2,6},{3,7},{4,0},{5,1},{6,2},{7,3},{8,12},{9,13},{10,... | collective-permute-start | bytes 393224 | tf_op jit(solution)/shard_map/ppermute | solution.py:40
  28.6 11.4 %collective-permute-start.3 = (f32[256,128]{1,0:T(8,128)S(1)}, f32[256,128]{1,0:T(8,128)S(1)}, u32[]{:S(2)}, u32[]{:S(2)}) collective-permute-start(f32[256,128]{1,0:T(8,128)S(1)} %add_select_fusion), channel_id=1, source_target_pairs={{0,1},{1,0},{2,3},{3,2},{4,5},{5,4},{6,7},{7,6},{8,9},{9,8},{10,11... | collective-permute-start | bytes 393224 | tf_op jit(solution)/shard_map/ppermute | solution.py:40

commit v13 on v12

--- a/solution.py
+++ b/solution.py
@@ -56,9 +56,7 @@
         state = merge(jnp.where(low_first, state, got), jnp.where(low_first, got, state))
         distance *= 2
     other = exchange(state, 1, count)
-    low_half = jnp.where(core == 0, state, other)
-    high_half = jnp.where(core == 0, other, state)
-    return low_half.reshape(half_heads, rows, lanes), high_half.reshape(half_heads, rows, lanes)
+    return state.reshape(half_heads, rows, lanes), other.reshape(half_heads, rows, lanes)
 
 
 def folded_rows(rows, peak, total, qmask_float, fold, lane):
@@ -231,13 +229,21 @@
     )(query_rows, keys_new, values_new, qmask, fold)
 
 
-def tail_kernel(low_ref, high_ref, new_ref, patch_ref, w_out_ref, gain_ref, w_up_ref, w_down_ref, out_ref):
-    half_heads, rows, _ = low_ref.shape
+def tail_kernel(
+    state_ref, other_ref, new_ref, patch_ref, w_out_ref, gain_ref, w_up_hbm, w_down_hbm, out_ref,
+    w_up_ref, w_down_ref, copy_sems,
+):
+    copy_up = pltpu.make_async_copy(w_up_hbm, w_up_ref, copy_sems.at[0])
+    copy_down = pltpu.make_async_copy(w_down_hbm, w_down_ref, copy_sems.at[1])
+    copy_up.start()
+    copy_down.start()
+    half_heads, rows, _ = state_ref.shape
     width = w_out_ref.shape[0]
+    low_first = lax.axis_index("seq") % 2 == 0
     out_sum = jnp.zeros((rows, width), jnp.float32)
     for h in range(2 * half_heads):
-        source = low_ref if h < half_heads else high_ref
-        first = source[h % half_heads]
+        mine, theirs = state_ref[h % half_heads], other_ref[h % half_heads]
+        first = jnp.where(low_first == (h < half_heads), mine, theirs)
         second = new_ref[h]
         m1 = first[:, HD:HD + 1]
         m2 = second[:, HD:HD + 1]
@@ -252,23 +258,31 @@
     patch_rows = jnp.concatenate([patch_ref[r].astype(jnp.float32) for r in range(groups)], axis=0)
     mixed_rows = patch_rows + out_rows
     normed_mixed = rms_norm(mixed_rows, gain_ref[...]).astype(jnp.bfloat16)
+    copy_up.wait()
     up_rows = jnp.dot(normed_mixed, w_up_ref[...], preferred_element_type=jnp.float32).astype(jnp.bfloat16)
     up_float = up_rows.astype(jnp.float32)
     hidden = (up_float / (1.0 + jnp.exp(-up_float))).astype(jnp.bfloat16)
+    copy_down.wait()
     down_rows = jnp.dot(hidden, w_down_ref[...], preferred_element_type=jnp.float32).astype(jnp.bfloat16)
     decoded = mixed_rows + down_rows.astype(jnp.float32)
     for r in range(groups):
         out_ref[r] = decoded[r * count:(r + 1) * count, :].astype(out_ref.dtype)
 
 
-def tail(low_half, high_half, new_packed, patches, w_out, ffn_gain, w_up, w_down):
+def tail(state, other, new_packed, patches, w_out, ffn_gain, w_up, w_down):
     vmem = pl.BlockSpec(memory_space=pltpu.VMEM)
+    hbm = pl.BlockSpec(memory_space=pl.ANY)
     return pl.pallas_call(
         tail_kernel,
         out_shape=jax.ShapeDtypeStruct(patches.shape, jnp.bfloat16),
-        in_specs=[vmem] * 8,
+        in_specs=[vmem] * 6 + [hbm, hbm],
         out_specs=vmem,
-    )(low_half, high_half, new_packed, patches, w_out, ffn_gain, w_up, w_down)
+        scratch_shapes=[
+            pltpu.VMEM(w_up.shape, w_up.dtype),
+            pltpu.VMEM(w_down.shape, w_down.dtype),
+            pltpu.SemaphoreType.DMA((2,)),
+        ],
+    )(state, other, new_packed, patches, w_out, ffn_gain, w_up, w_down)
 
 
 def layer(
@@ -278,8 +292,8 @@
     kept, sent, query_rows = cache_partials(cache_len, patches, attn_gain, w_qkv, key_cache, value_cache)
     keys_new, values_new = kv_projection(patches, attn_gain, w_qkv)
     new_packed = new_partials(query_rows, keys_new, values_new)
-    low_half, high_half = combine_over_seq(kept, sent, seq_count)
-    return tail(low_half, high_half, new_packed, patches, w_out, ffn_gain, w_up, w_down)
+    state, other = combine_over_seq(kept, sent, seq_count)
+    return tail(state, other, new_packed, patches, w_out, ffn_gain, w_up, w_down)
 
 
 def solution(mesh):

time: 48.1 us -> 47.3 us (0.983)
  Pallas kernels: 27.6 us -> 26.7 us
  other arithmetic: 3.07 us -> 2.35 us
  local copies, waits for them, and re-layouts: 0 us -> 0.66 us
    pallas_call x1, Pallas kernels: 7.31 us -> 6.51 us  [tail(): pl.pallas_call(tail_kernel, out_shape=jax.ShapeDtypeStruct(patches.shape,...]
    select_n x1 -> x0, other arithmetic: 0.72 us -> none  [combine_over_seq(): high_half = jnp.where(core == 0, other, state)]
    unnamed x0 -> x4, local copies, waits for them, and re-layouts: none -> 0.66 us
where the time goes in v13:
time: 47.3 us; the launch traced here: 47.1 us
  Pallas kernels  26.7 us (56%)
  waiting for transfers between devices  11.1 us (23%)
  starting transfers between devices  6.23 us (13%)
  other arithmetic  2.35 us (5%)
  local copies, waits for them, and re-layouts  0.66 us (1%)
    ppermute x4, waiting for transfers between devices, exchange(): return with_layout_constraint(lax.ppermute(part, 'seq', pairs), row_major)  11.1 us
    pallas_call x1, Pallas kernels, cache_partials(): pl.pallas_call(cache_partial_kernel, grid=(1,), out_shape=(half, half, ja...  10.3 us
    pallas_call x1, Pallas kernels, tail(): pl.pallas_call(tail_kernel, out_shape=jax.ShapeDtypeStruct(patches.shape,...  6.51 us
    ppermute x4, starting transfers between devices, exchange(): return with_layout_constraint(lax.ppermute(part, 'seq', pairs), row_major)  6.23 us
    pallas_call x1, Pallas kernels, new_partials(): pl.pallas_call(new_partial_kernel, out_shape=jax.ShapeDtypeStruct((HEADS,...  4.98 us
    pallas_call x1, Pallas kernels, kv_projection(): pl.pallas_call(kv_projection_kernel, grid=(1,), out_shape=(rows, rows), i...  4.92 us
  transfers between devices with their start and end apart: 4, of which 3 were waited for; matrix products, arithmetic and copies ran while one was open for 0% of the time, Pallas kernels for 21%

profile of v13, /device:TPU:1, one launch (start us, length us, event | category | flops | bytes accessed | tf_op | source)
XLA Modules:
  0.0 47.1 jit_solution(849309431156649435)
XLA Ops:
  0.0 10.3 %shard_map.136 = (f32[8,32,128]{2,1,0:T(8,128)}, f32[8,32,128]{2,1,0:T(8,128)}, bf16[8,4,1280]{2,1,0:T(4,128)(2,1)}) custom-call(s32[8]{0:T(128)} %length_ref.1, bf16[8,4,1280]{2,1,0:T(4,128)(2,1)} %patch_ref.5, f32[1280]{0:T(1024)} %gain_ref.4, bf16[1280,3840]{1,0:T(8,128)(2,1)} %wv_ref.1, bf16[8,128,1280]{2,1,0:T(8,128)(2,1)} %key_ref.1, ...), custom_call_target="tpu_custom_call" | custom-call | tf_op jit(solution)/shard_map/pallas_call | solution.py:195
  10.3 0.0 collective-permute-start
  10.4 1.5 %collective-permute-done = f32[256,128]{1,0:T(8,128)S(1)} collective-permute-done((f32[256,128]{1,0:T(8,128)}, f32[256,128]{1,0:T(8,128)S(1)}, u32[]{:S(2)}, u32[]{:S(2)}) %collective-permute-start) | collective-permute-done | bytes 131104 | tf_op jit(solution)/shard_map/ppermute | solution.py:40
  11.9 0.9 %bitcast_select_fusion.1 = (f32[256,128]{1,0:T(8,128)S(1)}, f32[256,128]{1,0:T(8,128)S(1)}) fusion(f32[256,128]{1,0:T(8,128)S(1)} %collective-permute-done, f32[8,32,128]{2,1,0:T(8,128)} %get-tuple-element.10, pred[]{:T(512)S(6)} %eq.26), kind=kLoop, calls=%fused_computation.1 | loop fusion | flops 65536 | bytes 524289 | tf_op jit(solution)/shard_map/jit(_where)/select_n | solution.py:51
  12.8 0.3 fusion
  13.1 0.2 add_select_fusion.2
  13.3 2.5 %collective-permute-start.1 = (f32[256,128]{1,0:T(8,128)S(1)}, f32[256,128]{1,0:T(8,128)S(1)}, u32[]{:S(2)}, u32[]{:S(2)}) collective-permute-start(f32[256,128]{1,0:T(8,128)S(1)} %add_select_fusion.2), channel_id=1, source_target_pairs={{0,2},{1,3},{2,0},{3,1},{4,6},{5,7},{6,4},{7,5},{8,10},{9,11},{10,... | collective-permute-start | bytes 393224 | tf_op jit(solution)/shard_map/ppermute | solution.py:40
  15.8 3.5 %collective-permute-done.1 = f32[256,128]{1,0:T(8,128)S(1)} collective-permute-done((f32[256,128]{1,0:T(8,128)S(1)}, f32[256,128]{1,0:T(8,128)S(1)}, u32[]{:S(2)}, u32[]{:S(2)}) %collective-permute-start.1) | collective-permute-done | bytes 131104 | tf_op jit(solution)/shard_map/ppermute | solution.py:40
  19.3 0.3 fusion.1
  19.6 0.2 add_select_fusion.1
  19.8 2.3 %collective-permute-start.2 = (f32[256,128]{1,0:T(8,128)S(1)}, f32[256,128]{1,0:T(8,128)S(1)}, u32[]{:S(2)}, u32[]{:S(2)}) collective-permute-start(f32[256,128]{1,0:T(8,128)S(1)} %add_select_fusion.1), channel_id=1, source_target_pairs={{0,4},{1,5},{2,6},{3,7},{4,0},{5,1},{6,2},{7,3},{8,12},{9,13},{10,... | collective-permute-start | bytes 393224 | tf_op jit(solution)/shard_map/ppermute | solution.py:40
  22.0 6.0 %collective-permute-done.2 = f32[256,128]{1,0:T(8,128)S(1)} collective-permute-done((f32[256,128]{1,0:T(8,128)S(1)}, f32[256,128]{1,0:T(8,128)S(1)}, u32[]{:S(2)}, u32[]{:S(2)}) %collective-permute-start.2) | collective-permute-done | bytes 131104 | tf_op jit(solution)/shard_map/ppermute | solution.py:40
  28.1 0.3 fusion.2
  28.4 0.2 add_select_fusion
  28.6 0.0 copy-start
  28.6 1.5 %collective-permute-start.3 = (f32[256,128]{1,0:T(8,128)S(1)}, f32[256,128]{1,0:T(8,128)S(1)}, u32[]{:S(2)}, u32[]{:S(2)}) collective-permute-start(f32[256,128]{1,0:T(8,128)S(1)} %add_select_fusion), channel_id=1, source_target_pairs={{0,1},{1,0},{2,3},{3,2},{4,5},{5,4},{6,7},{7,6},{8,9},{9,8},{10,11... | collective-permute-start | bytes 393224 | tf_op jit(solution)/shard_map/ppermute | solution.py:40
  30.0 4.9 %shard_map.137 = (bf16[32,1280]{1,0:T(8,128)(2,1)}, bf16[32,1280]{1,0:T(8,128)(2,1)}) custom-call(bf16[8,4,1280]{2,1,0:T(4,128)(2,1)} %patch_ref.5, f32[1280]{0:T(1024)} %gain_ref.4, bf16[1280,3840]{1,0:T(8,128)(2,1)} %wv_ref.1, bf16[1280,3840]{1,0:T(8,128)(2,1)} %wv_ref.1), custom_call_target="tpu_custom_call" | custom-call | tf_op jit(solution)/shard_map/pallas_call | solution.py:210
  35.0 0.0 copy-done
  35.0 5.0 %shard_map.138.new_ref = f32[16,32,128]{2,1,0:T(8,128)} custom-call(bf16[8,4,1280]{2,1,0:T(4,128)(2,1)} %get-tuple-element.12.query_ref, bf16[32,1280]{1,0:T(8,128)(2,1)} %get-tuple-element.13.key_new_ref, bf16[32,1280]{1,0:T(8,128)(2,1)} %get-tuple-element.14.value_new_ref, bf16[64,1280]{1,0:T(8,128)(2,1)} %constant.57.clone.qmask_ref, ...), custom_call_target="tpu_custom_call" | custom-call | tf_op jit(solution)/shard_map/pallas_call | solution.py:224
  39.9 0.0 collective-permute-done.3
  40.0 0.0 copy-start.1
  40.0 0.6 %copy-done.1 = f32[256,128]{1,0:T(8,128)} copy-done((f32[256,128]{1,0:T(8,128)}, f32[256,128]{1,0:T(8,128)S(1)}, u32[]{:S(2)}) %copy-start.1) | copy-done | bytes 131096
  40.6 6.5 %shard_map.139 = bf16[8,4,1280]{2,1,0:T(4,128)(2,1)} custom-call(f32[8,32,128]{2,1,0:T(8,128)} %bitcast.6, f32[8,32,128]{2,1,0:T(8,128)} %bitcast.7, f32[16,32,128]{2,1,0:T(8,128)} %shard_map.138.new_ref, bf16[8,4,1280]{2,1,0:T(4,128)(2,1)} %patch_ref.5, bf16[1280,1280]{1,0:T(8,128)(2,1)} %w_out_ref.1, f32[1280]{0:T(1024)} %gain_ref.5, ...), custom_call_target="tpu_custom_call" | custom-call | tf_op jit(solution)/shard_map/pallas_call | solution.py:275
  (3 shorter events, 0.0 us)
Async XLA Ops:
  10.3 1.6 %collective-permute-start = (f32[256,128]{1,0:T(8,128)}, f32[256,128]{1,0:T(8,128)S(1)}, u32[]{:S(2)}, u32[]{:S(2)}) collective-permute-start(f32[256,128]{1,0:T(8,128)} %bitcast.8), channel_id=1, source_target_pairs={{0,1},{1,0},{2,3},{3,2},{4,5},{5,4},{6,7},{7,6},{8,9},{9,8},{10,11... | collective-permute-start | bytes 393224 | tf_op jit(solution)/shard_map/ppermute | solution.py:40
  13.3 6.0 %collective-permute-start.1 = (f32[256,128]{1,0:T(8,128)S(1)}, f32[256,128]{1,0:T(8,128)S(1)}, u32[]{:S(2)}, u32[]{:S(2)}) collective-permute-start(f32[256,128]{1,0:T(8,128)S(1)} %add_select_fusion.2), channel_id=1, source_target_pairs={{0,2},{1,3},{2,0},{3,1},{4,6},{5,7},{6,4},{7,5},{8,10},{9,11},{10,... | collective-permute-start | bytes 393224 | tf_op jit(solution)/shard_map/ppermute | solution.py:40
  19.8 8.3 %collective-permute-start.2 = (f32[256,128]{1,0:T(8,128)S(1)}, f32[256,128]{1,0:T(8,128)S(1)}, u32[]{:S(2)}, u32[]{:S(2)}) collective-permute-start(f32[256,128]{1,0:T(8,128)S(1)} %add_select_fusion.1), channel_id=1, source_target_pairs={{0,4},{1,5},{2,6},{3,7},{4,0},{5,1},{6,2},{7,3},{8,12},{9,13},{10,... | collective-permute-start | bytes 393224 | tf_op jit(solution)/shard_map/ppermute | solution.py:40
  28.6 6.4 %copy-start = (f32[256,128]{1,0:T(8,128)}, f32[256,128]{1,0:T(8,128)S(1)}, u32[]{:S(2)}) copy-start(f32[256,128]{1,0:T(8,128)S(1)} %add_select_fusion) | copy-start | bytes 393220
  28.6 11.4 %collective-permute-start.3 = (f32[256,128]{1,0:T(8,128)S(1)}, f32[256,128]{1,0:T(8,128)S(1)}, u32[]{:S(2)}, u32[]{:S(2)}) collective-permute-start(f32[256,128]{1,0:T(8,128)S(1)} %add_select_fusion), channel_id=1, source_target_pairs={{0,1},{1,0},{2,3},{3,2},{4,5},{5,4},{6,7},{7,6},{8,9},{9,8},{10,11... | collective-permute-start | bytes 393224 | tf_op jit(solution)/shard_map/ppermute | solution.py:40
  40.0 0.7 %copy-start.1 = (f32[256,128]{1,0:T(8,128)}, f32[256,128]{1,0:T(8,128)S(1)}, u32[]{:S(2)}) copy-start(f32[256,128]{1,0:T(8,128)S(1)} %collective-permute-done.3) | copy-start | bytes 393220

commit v14 on v13

--- a/solution.py
+++ b/solution.py
@@ -87,15 +87,28 @@
 
 
 def cache_partial_kernel(
-    length_ref, patch_ref, gain_ref, wq_ref, key_ref, value_ref, qmask_ref, fold_ref, kept_ref, sent_ref, query_ref
+    length_ref, patch_ref, gain_ref, wqkv_hbm, key_hbm, value_hbm, qmask_ref, fold_ref, kept_ref, sent_ref,
+    query_ref, wq_ref, key_ref, value_ref, copy_sems,
 ):
-    groups, slots, _ = key_ref.shape
+    groups, slots, width = key_ref.shape
     half_heads = kept_ref.shape[0]
     heads = 2 * half_heads
     count = kept_ref.shape[1] // groups
     me = lax.axis_index("seq")
     core = me % 2
-    query_float = jnp.dot(normed_rows(patch_ref, gain_ref), wq_ref[...], preferred_element_type=jnp.float32)
+    copy_wq = pltpu.make_async_copy(wqkv_hbm.at[:, pl.ds(0, width)], wq_ref, copy_sems.at[0])
+    copy_wq.start()
+    copy_keys, copy_values = [], []
+    for r in range(groups):
+        copy_keys.append(pltpu.make_async_copy(key_hbm.at[r], key_ref.at[r], copy_sems.at[1 + r]))
+        copy_values.append(
+            pltpu.make_async_copy(value_hbm.at[r], value_ref.at[r], copy_sems.at[1 + groups + r])
+        )
+        copy_keys[r].start()
+        copy_values[r].start()
+    normed = normed_rows(patch_ref, gain_ref)
+    copy_wq.wait()
+    query_float = jnp.dot(normed, wq_ref[...], preferred_element_type=jnp.float32)
     for r in range(groups):
         query_ref[r] = query_float[r * count:(r + 1) * count, :].astype(query_ref.dtype)
     scale_factor = HD ** (-0.5)
@@ -107,6 +120,7 @@
     for r in range(groups):
         queries = query_ref[r]
         query_rows = jnp.concatenate([queries] * heads, axis=0) * qmask
+        copy_keys[r].wait()
         scores = lax.dot_general(
             query_rows, key_ref[r], (((1,), (1,)), ((), ())), preferred_element_type=jnp.float32
         ) * scale_factor
@@ -115,6 +129,7 @@
         peak = jnp.max(masked, axis=1, keepdims=True)
         weights = jnp.where(live, jnp.exp(masked - peak), 0.0)
         total = jnp.sum(weights, axis=1, keepdims=True)
+        copy_values[r].wait()
         value_rows = jnp.dot(
             weights.astype(jnp.bfloat16), value_ref[r], preferred_element_type=jnp.float32
         )
@@ -190,14 +205,19 @@
     qmask = ordered_masks(count, width)
     smem = pl.BlockSpec(memory_space=pltpu.SMEM)
     vmem = pl.BlockSpec(memory_space=pltpu.VMEM)
-    query_block = pl.BlockSpec((width, width), lambda i: (0, 0))
+    hbm = pl.BlockSpec(memory_space=pl.ANY)
     half = jax.ShapeDtypeStruct((HEADS // 2, rows, LANES), jnp.float32)
     return pl.pallas_call(
         cache_partial_kernel,
-        grid=(1,),
         out_shape=(half, half, jax.ShapeDtypeStruct(patches.shape, jnp.bfloat16)),
-        in_specs=[smem, vmem, vmem, query_block, vmem, vmem, vmem, vmem],
+        in_specs=[smem, vmem, vmem, hbm, hbm, hbm, vmem, vmem],
         out_specs=(vmem, vmem, vmem),
+        scratch_shapes=[
+            pltpu.VMEM((width, width), w_qkv.dtype),
+            pltpu.VMEM(key_cache.shape, key_cache.dtype),
+            pltpu.VMEM(value_cache.shape, value_cache.dtype),
+            pltpu.SemaphoreType.DMA((1 + 2 * groups,)),
+        ],
     )(cache_len, patches, attn_gain, w_qkv, key_cache, value_cache, qmask, fold)
 
 

time: 47.3 us -> 49 us (1.036)
  Pallas kernels: 26.7 us -> 28.4 us
    pallas_call x1, Pallas kernels: 10.3 us -> 12 us  [cache_partials(): pl.pallas_call(cache_partial_kernel, out_shape=(half, half, jax.ShapeDtyp...]
  transfers between devices with their start and end apart: 4 -> 4, of which waited for: 3 -> 3; matrix products, arithmetic and copies ran while one was open for 0% -> 0% of each run, Pallas kernels for 21% -> 20%
where the time goes in v14:
time: 49 us; the launch traced here: 48.8 us
  Pallas kernels  28.4 us (58%)
  waiting for transfers between devices  11.1 us (23%)
  starting transfers between devices  6.29 us (13%)
  other arithmetic  2.35 us (5%)
  local copies, waits for them, and re-layouts  0.66 us (1%)
    pallas_call x1, Pallas kernels, cache_partials(): pl.pallas_call(cache_partial_kernel, out_shape=(half, half, jax.ShapeDtyp...  12 us
    ppermute x4, waiting for transfers between devices, exchange(): return with_layout_constraint(lax.ppermute(part, 'seq', pairs), row_major)  11.1 us
    pallas_call x1, Pallas kernels, tail(): pl.pallas_call(tail_kernel, out_shape=jax.ShapeDtypeStruct(patches.shape,...  6.51 us
    ppermute x4, starting transfers between devices, exchange(): return with_layout_constraint(lax.ppermute(part, 'seq', pairs), row_major)  6.29 us
    pallas_call x1, Pallas kernels, new_partials(): pl.pallas_call(new_partial_kernel, out_shape=jax.ShapeDtypeStruct((HEADS,...  4.98 us
    pallas_call x1, Pallas kernels, kv_projection(): pl.pallas_call(kv_projection_kernel, grid=(1,), out_shape=(rows, rows), i...  4.92 us
  transfers between devices with their start and end apart: 4, of which 3 were waited for; matrix products, arithmetic and copies ran while one was open for 0% of the time, Pallas kernels for 20%

profile of v14, /device:TPU:1, one launch (start us, length us, event | category | flops | bytes accessed | tf_op | source)
XLA Modules:
  0.0 48.8 jit_solution(8271113608023145259)
XLA Ops:
  0.0 12.0 %shard_map.136 = (f32[8,32,128]{2,1,0:T(8,128)}, f32[8,32,128]{2,1,0:T(8,128)}, bf16[8,4,1280]{2,1,0:T(4,128)(2,1)}) custom-call(s32[8]{0:T(128)} %length_ref.1, bf16[8,4,1280]{2,1,0:T(4,128)(2,1)} %patch_ref.5, f32[1280]{0:T(1024)} %gain_ref.4, bf16[1280,3840]{1,0:T(8,128)(2,1)} %wv_ref.1, bf16[8,128,1280]{2,1,0:T(8,128)(2,1)} %key_hbm.1, ...), custom_call_target="tpu_custom_call" | custom-call | tf_op jit(solution)/shard_map/pallas_call | solution.py:210
  12.0 0.1 collective-permute-start
  12.1 1.5 %collective-permute-done = f32[256,128]{1,0:T(8,128)S(1)} collective-permute-done((f32[256,128]{1,0:T(8,128)}, f32[256,128]{1,0:T(8,128)S(1)}, u32[]{:S(2)}, u32[]{:S(2)}) %collective-permute-start) | collective-permute-done | bytes 131104 | tf_op jit(solution)/shard_map/ppermute | solution.py:40
  13.6 0.9 %bitcast_select_fusion.1 = (f32[256,128]{1,0:T(8,128)S(1)}, f32[256,128]{1,0:T(8,128)S(1)}) fusion(f32[256,128]{1,0:T(8,128)S(1)} %collective-permute-done, f32[8,32,128]{2,1,0:T(8,128)} %get-tuple-element.10, pred[]{:T(512)S(6)} %eq.26), kind=kLoop, calls=%fused_computation.1 | loop fusion | flops 65536 | bytes 524289 | tf_op jit(solution)/shard_map/jit(_where)/select_n | solution.py:51
  14.5 0.3 fusion
  14.8 0.2 add_select_fusion.2
  15.0 2.5 %collective-permute-start.1 = (f32[256,128]{1,0:T(8,128)S(1)}, f32[256,128]{1,0:T(8,128)S(1)}, u32[]{:S(2)}, u32[]{:S(2)}) collective-permute-start(f32[256,128]{1,0:T(8,128)S(1)} %add_select_fusion.2), channel_id=1, source_target_pairs={{0,2},{1,3},{2,0},{3,1},{4,6},{5,7},{6,4},{7,5},{8,10},{9,11},{10,... | collective-permute-start | bytes 393224 | tf_op jit(solution)/shard_map/ppermute | solution.py:40
  17.5 3.5 %collective-permute-done.1 = f32[256,128]{1,0:T(8,128)S(1)} collective-permute-done((f32[256,128]{1,0:T(8,128)S(1)}, f32[256,128]{1,0:T(8,128)S(1)}, u32[]{:S(2)}, u32[]{:S(2)}) %collective-permute-start.1) | collective-permute-done | bytes 131104 | tf_op jit(solution)/shard_map/ppermute | solution.py:40
  21.0 0.3 fusion.1
  21.3 0.2 add_select_fusion.1
  21.5 2.3 %collective-permute-start.2 = (f32[256,128]{1,0:T(8,128)S(1)}, f32[256,128]{1,0:T(8,128)S(1)}, u32[]{:S(2)}, u32[]{:S(2)}) collective-permute-start(f32[256,128]{1,0:T(8,128)S(1)} %add_select_fusion.1), channel_id=1, source_target_pairs={{0,4},{1,5},{2,6},{3,7},{4,0},{5,1},{6,2},{7,3},{8,12},{9,13},{10,... | collective-permute-start | bytes 393224 | tf_op jit(solution)/shard_map/ppermute | solution.py:40
  23.8 6.0 %collective-permute-done.2 = f32[256,128]{1,0:T(8,128)S(1)} collective-permute-done((f32[256,128]{1,0:T(8,128)S(1)}, f32[256,128]{1,0:T(8,128)S(1)}, u32[]{:S(2)}, u32[]{:S(2)}) %collective-permute-start.2) | collective-permute-done | bytes 131104 | tf_op jit(solution)/shard_map/ppermute | solution.py:40
  29.8 0.3 fusion.2
  30.1 0.2 add_select_fusion
  30.3 0.0 copy-start
  30.3 1.5 %collective-permute-start.3 = (f32[256,128]{1,0:T(8,128)S(1)}, f32[256,128]{1,0:T(8,128)S(1)}, u32[]{:S(2)}, u32[]{:S(2)}) collective-permute-start(f32[256,128]{1,0:T(8,128)S(1)} %add_select_fusion), channel_id=1, source_target_pairs={{0,1},{1,0},{2,3},{3,2},{4,5},{5,4},{6,7},{7,6},{8,9},{9,8},{10,11... | collective-permute-start | bytes 393224 | tf_op jit(solution)/shard_map/ppermute | solution.py:40
  31.8 4.9 %shard_map.137 = (bf16[32,1280]{1,0:T(8,128)(2,1)}, bf16[32,1280]{1,0:T(8,128)(2,1)}) custom-call(bf16[8,4,1280]{2,1,0:T(4,128)(2,1)} %patch_ref.5, f32[1280]{0:T(1024)} %gain_ref.4, bf16[1280,3840]{1,0:T(8,128)(2,1)} %wv_ref.1, bf16[1280,3840]{1,0:T(8,128)(2,1)} %wv_ref.1), custom_call_target="tpu_custom_call" | custom-call | tf_op jit(solution)/shard_map/pallas_call | solution.py:230
  36.7 0.0 copy-done
  36.7 5.0 %shard_map.138.new_ref = f32[16,32,128]{2,1,0:T(8,128)} custom-call(bf16[8,4,1280]{2,1,0:T(4,128)(2,1)} %get-tuple-element.12.query_ref, bf16[32,1280]{1,0:T(8,128)(2,1)} %get-tuple-element.13.key_new_ref, bf16[32,1280]{1,0:T(8,128)(2,1)} %get-tuple-element.14.value_new_ref, bf16[64,1280]{1,0:T(8,128)(2,1)} %constant.57.clone.qmask_ref, ...), custom_call_target="tpu_custom_call" | custom-call | tf_op jit(solution)/shard_map/pallas_call | solution.py:244
  41.7 0.0 collective-permute-done.3
  41.7 0.0 copy-start.1
  41.7 0.6 %copy-done.1 = f32[256,128]{1,0:T(8,128)} copy-done((f32[256,128]{1,0:T(8,128)}, f32[256,128]{1,0:T(8,128)S(1)}, u32[]{:S(2)}) %copy-start.1) | copy-done | bytes 131096
  42.3 6.5 %shard_map.139 = bf16[8,4,1280]{2,1,0:T(4,128)(2,1)} custom-call(f32[8,32,128]{2,1,0:T(8,128)} %bitcast.6, f32[8,32,128]{2,1,0:T(8,128)} %bitcast.7, f32[16,32,128]{2,1,0:T(8,128)} %shard_map.138.new_ref, bf16[8,4,1280]{2,1,0:T(4,128)(2,1)} %patch_ref.5, bf16[1280,1280]{1,0:T(8,128)(2,1)} %w_out_ref.1, f32[1280]{0:T(1024)} %gain_ref.5, ...), custom_call_target="tpu_custom_call" | custom-call | tf_op jit(solution)/shard_map/pallas_call | solution.py:295
  (3 shorter events, 0.0 us)
Async XLA Ops:
  12.0 1.6 %collective-permute-start = (f32[256,128]{1,0:T(8,128)}, f32[256,128]{1,0:T(8,128)S(1)}, u32[]{:S(2)}, u32[]{:S(2)}) collective-permute-start(f32[256,128]{1,0:T(8,128)} %bitcast.8), channel_id=1, source_target_pairs={{0,1},{1,0},{2,3},{3,2},{4,5},{5,4},{6,7},{7,6},{8,9},{9,8},{10,11... | collective-permute-start | bytes 393224 | tf_op jit(solution)/shard_map/ppermute | solution.py:40
  15.0 6.0 %collective-permute-start.1 = (f32[256,128]{1,0:T(8,128)S(1)}, f32[256,128]{1,0:T(8,128)S(1)}, u32[]{:S(2)}, u32[]{:S(2)}) collective-permute-start(f32[256,128]{1,0:T(8,128)S(1)} %add_select_fusion.2), channel_id=1, source_target_pairs={{0,2},{1,3},{2,0},{3,1},{4,6},{5,7},{6,4},{7,5},{8,10},{9,11},{10,... | collective-permute-start | bytes 393224 | tf_op jit(solution)/shard_map/ppermute | solution.py:40
  21.5 8.3 %collective-permute-start.2 = (f32[256,128]{1,0:T(8,128)S(1)}, f32[256,128]{1,0:T(8,128)S(1)}, u32[]{:S(2)}, u32[]{:S(2)}) collective-permute-start(f32[256,128]{1,0:T(8,128)S(1)} %add_select_fusion.1), channel_id=1, source_target_pairs={{0,4},{1,5},{2,6},{3,7},{4,0},{5,1},{6,2},{7,3},{8,12},{9,13},{10,... | collective-permute-start | bytes 393224 | tf_op jit(solution)/shard_map/ppermute | solution.py:40
  30.3 6.4 %copy-start = (f32[256,128]{1,0:T(8,128)}, f32[256,128]{1,0:T(8,128)S(1)}, u32[]{:S(2)}) copy-start(f32[256,128]{1,0:T(8,128)S(1)} %add_select_fusion) | copy-start | bytes 393220
  30.3 11.4 %collective-permute-start.3 = (f32[256,128]{1,0:T(8,128)S(1)}, f32[256,128]{1,0:T(8,128)S(1)}, u32[]{:S(2)}, u32[]{:S(2)}) collective-permute-start(f32[256,128]{1,0:T(8,128)S(1)} %add_select_fusion), channel_id=1, source_target_pairs={{0,1},{1,0},{2,3},{3,2},{4,5},{5,4},{6,7},{7,6},{8,9},{9,8},{10,11... | collective-permute-start | bytes 393224 | tf_op jit(solution)/shard_map/ppermute | solution.py:40
  41.7 0.7 %copy-start.1 = (f32[256,128]{1,0:T(8,128)}, f32[256,128]{1,0:T(8,128)S(1)}, u32[]{:S(2)}) copy-start(f32[256,128]{1,0:T(8,128)S(1)} %collective-permute-done.3) | copy-start | bytes 393220

commit v15 on v13

--- a/solution.py
+++ b/solution.py
@@ -230,18 +230,30 @@
 
 
 def tail_kernel(
-    state_ref, other_ref, new_ref, patch_ref, w_out_ref, gain_ref, w_up_hbm, w_down_hbm, out_ref,
-    w_up_ref, w_down_ref, copy_sems,
+    state_ref, other_ref, new_ref, patch_ref, w_out_hbm, gain_ref, w_up_hbm, w_down_hbm, out_ref,
+    w_out_ref, w_up_ref, w_down_ref, copy_sems,
 ):
+    half_heads, rows, _ = state_ref.shape
+    width = w_out_ref.shape[0]
+    half_rows = half_heads * HD
+    copy_out = [
+        pltpu.make_async_copy(
+            w_out_hbm.at[pl.ds(i * half_rows, half_rows)], w_out_ref.at[pl.ds(i * half_rows, half_rows)],
+            copy_sems.at[2 + i],
+        )
+        for i in range(2)
+    ]
     copy_up = pltpu.make_async_copy(w_up_hbm, w_up_ref, copy_sems.at[0])
     copy_down = pltpu.make_async_copy(w_down_hbm, w_down_ref, copy_sems.at[1])
+    for copy in copy_out:
+        copy.start()
     copy_up.start()
     copy_down.start()
-    half_heads, rows, _ = state_ref.shape
-    width = w_out_ref.shape[0]
     low_first = lax.axis_index("seq") % 2 == 0
     out_sum = jnp.zeros((rows, width), jnp.float32)
     for h in range(2 * half_heads):
+        if h % half_heads == 0:
+            copy_out[h // half_heads].wait()
         mine, theirs = state_ref[h % half_heads], other_ref[h % half_heads]
         first = jnp.where(low_first == (h < half_heads), mine, theirs)
         second = new_ref[h]
@@ -275,12 +287,13 @@
     return pl.pallas_call(
         tail_kernel,
         out_shape=jax.ShapeDtypeStruct(patches.shape, jnp.bfloat16),
-        in_specs=[vmem] * 6 + [hbm, hbm],
+        in_specs=[vmem] * 4 + [hbm, vmem, hbm, hbm],
         out_specs=vmem,
         scratch_shapes=[
+            pltpu.VMEM(w_out.shape, w_out.dtype),
             pltpu.VMEM(w_up.shape, w_up.dtype),
             pltpu.VMEM(w_down.shape, w_down.dtype),
-            pltpu.SemaphoreType.DMA((2,)),
+            pltpu.SemaphoreType.DMA((4,)),
         ],
     )(state, other, new_packed, patches, w_out, ffn_gain, w_up, w_down)
 

time: 47.3 us -> 47.2 us (level)
  no operation moved by 1% of the time
where the time goes in v15:
time: 47.2 us; the launch traced here: 47 us
  Pallas kernels  26.6 us (56%)
  waiting for transfers between devices  11.1 us (24%)
  starting transfers between devices  6.23 us (13%)
  other arithmetic  2.35 us (5%)
  local copies, waits for them, and re-layouts  0.66 us (1%)
    ppermute x4, waiting for transfers between devices, exchange(): return with_layout_constraint(lax.ppermute(part, 'seq', pairs), row_major)  11.1 us
    pallas_call x1, Pallas kernels, cache_partials(): pl.pallas_call(cache_partial_kernel, grid=(1,), out_shape=(half, half, ja...  10.3 us
    pallas_call x1, Pallas kernels, tail(): pl.pallas_call(tail_kernel, out_shape=jax.ShapeDtypeStruct(patches.shape,...  6.4 us
    ppermute x4, starting transfers between devices, exchange(): return with_layout_constraint(lax.ppermute(part, 'seq', pairs), row_major)  6.23 us
    pallas_call x1, Pallas kernels, new_partials(): pl.pallas_call(new_partial_kernel, out_shape=jax.ShapeDtypeStruct((HEADS,...  4.98 us
    pallas_call x1, Pallas kernels, kv_projection(): pl.pallas_call(kv_projection_kernel, grid=(1,), out_shape=(rows, rows), i...  4.92 us
  transfers between devices with their start and end apart: 4, of which 3 were waited for; matrix products, arithmetic and copies ran while one was open for 0% of the time, Pallas kernels for 21%

profile of v15, /device:TPU:1, one launch (start us, length us, event | category | flops | bytes accessed | tf_op | source)
XLA Modules:
  0.0 47.0 jit_solution(1020315246771379541)
XLA Ops:
  0.0 10.3 %shard_map.136 = (f32[8,32,128]{2,1,0:T(8,128)}, f32[8,32,128]{2,1,0:T(8,128)}, bf16[8,4,1280]{2,1,0:T(4,128)(2,1)}) custom-call(s32[8]{0:T(128)} %length_ref.1, bf16[8,4,1280]{2,1,0:T(4,128)(2,1)} %patch_ref.5, f32[1280]{0:T(1024)} %gain_ref.4, bf16[1280,3840]{1,0:T(8,128)(2,1)} %wv_ref.1, bf16[8,128,1280]{2,1,0:T(8,128)(2,1)} %key_ref.1, ...), custom_call_target="tpu_custom_call" | custom-call | tf_op jit(solution)/shard_map/pallas_call | solution.py:195
  10.3 0.0 collective-permute-start
  10.4 1.5 %collective-permute-done = f32[256,128]{1,0:T(8,128)S(1)} collective-permute-done((f32[256,128]{1,0:T(8,128)}, f32[256,128]{1,0:T(8,128)S(1)}, u32[]{:S(2)}, u32[]{:S(2)}) %collective-permute-start) | collective-permute-done | bytes 131104 | tf_op jit(solution)/shard_map/ppermute | solution.py:40
  11.9 0.9 %bitcast_select_fusion.1 = (f32[256,128]{1,0:T(8,128)S(1)}, f32[256,128]{1,0:T(8,128)S(1)}) fusion(f32[256,128]{1,0:T(8,128)S(1)} %collective-permute-done, f32[8,32,128]{2,1,0:T(8,128)} %get-tuple-element.10, pred[]{:T(512)S(6)} %eq.26), kind=kLoop, calls=%fused_computation.1 | loop fusion | flops 65536 | bytes 524289 | tf_op jit(solution)/shard_map/jit(_where)/select_n | solution.py:51
  12.8 0.3 fusion
  13.1 0.2 add_select_fusion.2
  13.3 2.5 %collective-permute-start.1 = (f32[256,128]{1,0:T(8,128)S(1)}, f32[256,128]{1,0:T(8,128)S(1)}, u32[]{:S(2)}, u32[]{:S(2)}) collective-permute-start(f32[256,128]{1,0:T(8,128)S(1)} %add_select_fusion.2), channel_id=1, source_target_pairs={{0,2},{1,3},{2,0},{3,1},{4,6},{5,7},{6,4},{7,5},{8,10},{9,11},{10,... | collective-permute-start | bytes 393224 | tf_op jit(solution)/shard_map/ppermute | solution.py:40
  15.8 3.5 %collective-permute-done.1 = f32[256,128]{1,0:T(8,128)S(1)} collective-permute-done((f32[256,128]{1,0:T(8,128)S(1)}, f32[256,128]{1,0:T(8,128)S(1)}, u32[]{:S(2)}, u32[]{:S(2)}) %collective-permute-start.1) | collective-permute-done | bytes 131104 | tf_op jit(solution)/shard_map/ppermute | solution.py:40
  19.3 0.3 fusion.1
  19.6 0.2 add_select_fusion.1
  19.8 2.3 %collective-permute-start.2 = (f32[256,128]{1,0:T(8,128)S(1)}, f32[256,128]{1,0:T(8,128)S(1)}, u32[]{:S(2)}, u32[]{:S(2)}) collective-permute-start(f32[256,128]{1,0:T(8,128)S(1)} %add_select_fusion.1), channel_id=1, source_target_pairs={{0,4},{1,5},{2,6},{3,7},{4,0},{5,1},{6,2},{7,3},{8,12},{9,13},{10,... | collective-permute-start | bytes 393224 | tf_op jit(solution)/shard_map/ppermute | solution.py:40
  22.0 6.0 %collective-permute-done.2 = f32[256,128]{1,0:T(8,128)S(1)} collective-permute-done((f32[256,128]{1,0:T(8,128)S(1)}, f32[256,128]{1,0:T(8,128)S(1)}, u32[]{:S(2)}, u32[]{:S(2)}) %collective-permute-start.2) | collective-permute-done | bytes 131104 | tf_op jit(solution)/shard_map/ppermute | solution.py:40
  28.1 0.3 fusion.2
  28.4 0.2 add_select_fusion
  28.6 0.0 copy-start
  28.6 1.5 %collective-permute-start.3 = (f32[256,128]{1,0:T(8,128)S(1)}, f32[256,128]{1,0:T(8,128)S(1)}, u32[]{:S(2)}, u32[]{:S(2)}) collective-permute-start(f32[256,128]{1,0:T(8,128)S(1)} %add_select_fusion), channel_id=1, source_target_pairs={{0,1},{1,0},{2,3},{3,2},{4,5},{5,4},{6,7},{7,6},{8,9},{9,8},{10,11... | collective-permute-start | bytes 393224 | tf_op jit(solution)/shard_map/ppermute | solution.py:40
  30.0 4.9 %shard_map.137 = (bf16[32,1280]{1,0:T(8,128)(2,1)}, bf16[32,1280]{1,0:T(8,128)(2,1)}) custom-call(bf16[8,4,1280]{2,1,0:T(4,128)(2,1)} %patch_ref.5, f32[1280]{0:T(1024)} %gain_ref.4, bf16[1280,3840]{1,0:T(8,128)(2,1)} %wv_ref.1, bf16[1280,3840]{1,0:T(8,128)(2,1)} %wv_ref.1), custom_call_target="tpu_custom_call" | custom-call | tf_op jit(solution)/shard_map/pallas_call | solution.py:210
  35.0 0.0 copy-done
  35.0 5.0 %shard_map.138.new_ref = f32[16,32,128]{2,1,0:T(8,128)} custom-call(bf16[8,4,1280]{2,1,0:T(4,128)(2,1)} %get-tuple-element.12.query_ref, bf16[32,1280]{1,0:T(8,128)(2,1)} %get-tuple-element.13.key_new_ref, bf16[32,1280]{1,0:T(8,128)(2,1)} %get-tuple-element.14.value_new_ref, bf16[64,1280]{1,0:T(8,128)(2,1)} %constant.57.clone.qmask_ref, ...), custom_call_target="tpu_custom_call" | custom-call | tf_op jit(solution)/shard_map/pallas_call | solution.py:224
  39.9 0.0 collective-permute-done.3
  40.0 0.0 copy-start.1
  40.0 0.6 %copy-done.1 = f32[256,128]{1,0:T(8,128)} copy-done((f32[256,128]{1,0:T(8,128)}, f32[256,128]{1,0:T(8,128)S(1)}, u32[]{:S(2)}) %copy-start.1) | copy-done | bytes 131096
  40.6 6.4 %shard_map.139 = bf16[8,4,1280]{2,1,0:T(4,128)(2,1)} custom-call(f32[8,32,128]{2,1,0:T(8,128)} %bitcast.6, f32[8,32,128]{2,1,0:T(8,128)} %bitcast.7, f32[16,32,128]{2,1,0:T(8,128)} %shard_map.138.new_ref, bf16[8,4,1280]{2,1,0:T(4,128)(2,1)} %patch_ref.5, bf16[1280,1280]{1,0:T(8,128)(2,1)} %w_out_hbm.1, f32[1280]{0:T(1024)} %gain_ref.5, ...), custom_call_target="tpu_custom_call" | custom-call | tf_op jit(solution)/shard_map/pallas_call | solution.py:287
  (3 shorter events, 0.0 us)
Async XLA Ops:
  10.3 1.6 %collective-permute-start = (f32[256,128]{1,0:T(8,128)}, f32[256,128]{1,0:T(8,128)S(1)}, u32[]{:S(2)}, u32[]{:S(2)}) collective-permute-start(f32[256,128]{1,0:T(8,128)} %bitcast.8), channel_id=1, source_target_pairs={{0,1},{1,0},{2,3},{3,2},{4,5},{5,4},{6,7},{7,6},{8,9},{9,8},{10,11... | collective-permute-start | bytes 393224 | tf_op jit(solution)/shard_map/ppermute | solution.py:40
  13.3 6.0 %collective-permute-start.1 = (f32[256,128]{1,0:T(8,128)S(1)}, f32[256,128]{1,0:T(8,128)S(1)}, u32[]{:S(2)}, u32[]{:S(2)}) collective-permute-start(f32[256,128]{1,0:T(8,128)S(1)} %add_select_fusion.2), channel_id=1, source_target_pairs={{0,2},{1,3},{2,0},{3,1},{4,6},{5,7},{6,4},{7,5},{8,10},{9,11},{10,... | collective-permute-start | bytes 393224 | tf_op jit(solution)/shard_map/ppermute | solution.py:40
  19.8 8.3 %collective-permute-start.2 = (f32[256,128]{1,0:T(8,128)S(1)}, f32[256,128]{1,0:T(8,128)S(1)}, u32[]{:S(2)}, u32[]{:S(2)}) collective-permute-start(f32[256,128]{1,0:T(8,128)S(1)} %add_select_fusion.1), channel_id=1, source_target_pairs={{0,4},{1,5},{2,6},{3,7},{4,0},{5,1},{6,2},{7,3},{8,12},{9,13},{10,... | collective-permute-start | bytes 393224 | tf_op jit(solution)/shard_map/ppermute | solution.py:40
  28.6 6.4 %copy-start = (f32[256,128]{1,0:T(8,128)}, f32[256,128]{1,0:T(8,128)S(1)}, u32[]{:S(2)}) copy-start(f32[256,128]{1,0:T(8,128)S(1)} %add_select_fusion) | copy-start | bytes 393220
  28.6 11.4 %collective-permute-start.3 = (f32[256,128]{1,0:T(8,128)S(1)}, f32[256,128]{1,0:T(8,128)S(1)}, u32[]{:S(2)}, u32[]{:S(2)}) collective-permute-start(f32[256,128]{1,0:T(8,128)S(1)} %add_select_fusion), channel_id=1, source_target_pairs={{0,1},{1,0},{2,3},{3,2},{4,5},{5,4},{6,7},{7,6},{8,9},{9,8},{10,11... | collective-permute-start | bytes 393224 | tf_op jit(solution)/shard_map/ppermute | solution.py:40
  40.0 0.7 %copy-start.1 = (f32[256,128]{1,0:T(8,128)}, f32[256,128]{1,0:T(8,128)S(1)}, u32[]{:S(2)}) copy-start(f32[256,128]{1,0:T(8,128)S(1)} %collective-permute-done.3) | copy-start | bytes 393220

commit v16 on v13

--- a/solution.py
+++ b/solution.py
@@ -87,7 +87,8 @@
 
 
 def cache_partial_kernel(
-    length_ref, patch_ref, gain_ref, wq_ref, key_ref, value_ref, qmask_ref, fold_ref, kept_ref, sent_ref, query_ref
+    length_ref, patch_ref, gain_ref, wq_ref, key_hbm, value_hbm, qmask_ref, fold_ref, kept_ref, sent_ref, query_ref,
+    key_ref, value_ref, copy_sems,
 ):
     groups, slots, _ = key_ref.shape
     half_heads = kept_ref.shape[0]
@@ -95,6 +96,10 @@
     count = kept_ref.shape[1] // groups
     me = lax.axis_index("seq")
     core = me % 2
+    copy_keys = pltpu.make_async_copy(key_hbm, key_ref, copy_sems.at[0])
+    copy_values = pltpu.make_async_copy(value_hbm, value_ref, copy_sems.at[1])
+    copy_keys.start()
+    copy_values.start()
     query_float = jnp.dot(normed_rows(patch_ref, gain_ref), wq_ref[...], preferred_element_type=jnp.float32)
     for r in range(groups):
         query_ref[r] = query_float[r * count:(r + 1) * count, :].astype(query_ref.dtype)
@@ -104,6 +109,8 @@
     fold = fold_ref[...]
     position = me * slots + lax.broadcasted_iota(jnp.int32, (1, slots), 1)
     lane = lax.broadcasted_iota(jnp.int32, (heads * count, LANES), 1)
+    copy_keys.wait()
+    copy_values.wait()
     for r in range(groups):
         queries = query_ref[r]
         query_rows = jnp.concatenate([queries] * heads, axis=0) * qmask
@@ -190,14 +197,20 @@
     qmask = ordered_masks(count, width)
     smem = pl.BlockSpec(memory_space=pltpu.SMEM)
     vmem = pl.BlockSpec(memory_space=pltpu.VMEM)
+    hbm = pl.BlockSpec(memory_space=pl.ANY)
     query_block = pl.BlockSpec((width, width), lambda i: (0, 0))
     half = jax.ShapeDtypeStruct((HEADS // 2, rows, LANES), jnp.float32)
     return pl.pallas_call(
         cache_partial_kernel,
         grid=(1,),
         out_shape=(half, half, jax.ShapeDtypeStruct(patches.shape, jnp.bfloat16)),
-        in_specs=[smem, vmem, vmem, query_block, vmem, vmem, vmem, vmem],
+        in_specs=[smem, vmem, vmem, query_block, hbm, hbm, vmem, vmem],
         out_specs=(vmem, vmem, vmem),
+        scratch_shapes=[
+            pltpu.VMEM(key_cache.shape, key_cache.dtype),
+            pltpu.VMEM(value_cache.shape, value_cache.dtype),
+            pltpu.SemaphoreType.DMA((2,)),
+        ],
     )(cache_len, patches, attn_gain, w_qkv, key_cache, value_cache, qmask, fold)
 
 

time: 47.3 us -> 47.6 us (level)
  no operation moved by 1% of the time
where the time goes in v16:
time: 47.6 us; the launch traced here: 47.4 us
  Pallas kernels  27 us (57%)
  waiting for transfers between devices  11.1 us (23%)
  starting transfers between devices  6.29 us (13%)
  other arithmetic  2.35 us (5%)
  local copies, waits for them, and re-layouts  0.66 us (1%)
    ppermute x4, waiting for transfers between devices, exchange(): return with_layout_constraint(lax.ppermute(part, 'seq', pairs), row_major)  11.1 us
    pallas_call x1, Pallas kernels, cache_partials(): pl.pallas_call(cache_partial_kernel, grid=(1,), out_shape=(half, half, ja...  10.6 us
    pallas_call x1, Pallas kernels, tail(): pl.pallas_call(tail_kernel, out_shape=jax.ShapeDtypeStruct(patches.shape,...  6.51 us
    ppermute x4, starting transfers between devices, exchange(): return with_layout_constraint(lax.ppermute(part, 'seq', pairs), row_major)  6.29 us
    pallas_call x1, Pallas kernels, new_partials(): pl.pallas_call(new_partial_kernel, out_shape=jax.ShapeDtypeStruct((HEADS,...  4.98 us
    pallas_call x1, Pallas kernels, kv_projection(): pl.pallas_call(kv_projection_kernel, grid=(1,), out_shape=(rows, rows), i...  4.92 us
  transfers between devices with their start and end apart: 4, of which 3 were waited for; matrix products, arithmetic and copies ran while one was open for 0% of the time, Pallas kernels for 21%

profile of v16, /device:TPU:1, one launch (start us, length us, event | category | flops | bytes accessed | tf_op | source)
XLA Modules:
  0.0 47.4 jit_solution(5890983099701435916)
XLA Ops:
  0.0 10.6 %shard_map.136 = (f32[8,32,128]{2,1,0:T(8,128)}, f32[8,32,128]{2,1,0:T(8,128)}, bf16[8,4,1280]{2,1,0:T(4,128)(2,1)}) custom-call(s32[8]{0:T(128)} %length_ref.1, bf16[8,4,1280]{2,1,0:T(4,128)(2,1)} %patch_ref.5, f32[1280]{0:T(1024)} %gain_ref.4, bf16[1280,3840]{1,0:T(8,128)(2,1)} %wv_ref.1, bf16[8,128,1280]{2,1,0:T(8,128)(2,1)} %key_hbm.1, ...), custom_call_target="tpu_custom_call" | custom-call | tf_op jit(solution)/shard_map/pallas_call | solution.py:203
  10.6 0.1 collective-permute-start
  10.7 1.5 %collective-permute-done = f32[256,128]{1,0:T(8,128)S(1)} collective-permute-done((f32[256,128]{1,0:T(8,128)}, f32[256,128]{1,0:T(8,128)S(1)}, u32[]{:S(2)}, u32[]{:S(2)}) %collective-permute-start) | collective-permute-done | bytes 131104 | tf_op jit(solution)/shard_map/ppermute | solution.py:40
  12.2 0.9 %bitcast_select_fusion.1 = (f32[256,128]{1,0:T(8,128)S(1)}, f32[256,128]{1,0:T(8,128)S(1)}) fusion(f32[256,128]{1,0:T(8,128)S(1)} %collective-permute-done, f32[8,32,128]{2,1,0:T(8,128)} %get-tuple-element.10, pred[]{:T(512)S(6)} %eq.26), kind=kLoop, calls=%fused_computation.1 | loop fusion | flops 65536 | bytes 524289 | tf_op jit(solution)/shard_map/jit(_where)/select_n | solution.py:51
  13.1 0.3 fusion
  13.4 0.2 add_select_fusion.2
  13.6 2.5 %collective-permute-start.1 = (f32[256,128]{1,0:T(8,128)S(1)}, f32[256,128]{1,0:T(8,128)S(1)}, u32[]{:S(2)}, u32[]{:S(2)}) collective-permute-start(f32[256,128]{1,0:T(8,128)S(1)} %add_select_fusion.2), channel_id=1, source_target_pairs={{0,2},{1,3},{2,0},{3,1},{4,6},{5,7},{6,4},{7,5},{8,10},{9,11},{10,... | collective-permute-start | bytes 393224 | tf_op jit(solution)/shard_map/ppermute | solution.py:40
  16.1 3.5 %collective-permute-done.1 = f32[256,128]{1,0:T(8,128)S(1)} collective-permute-done((f32[256,128]{1,0:T(8,128)S(1)}, f32[256,128]{1,0:T(8,128)S(1)}, u32[]{:S(2)}, u32[]{:S(2)}) %collective-permute-start.1) | collective-permute-done | bytes 131104 | tf_op jit(solution)/shard_map/ppermute | solution.py:40
  19.6 0.3 fusion.1
  19.9 0.2 add_select_fusion.1
  20.1 2.3 %collective-permute-start.2 = (f32[256,128]{1,0:T(8,128)S(1)}, f32[256,128]{1,0:T(8,128)S(1)}, u32[]{:S(2)}, u32[]{:S(2)}) collective-permute-start(f32[256,128]{1,0:T(8,128)S(1)} %add_select_fusion.1), channel_id=1, source_target_pairs={{0,4},{1,5},{2,6},{3,7},{4,0},{5,1},{6,2},{7,3},{8,12},{9,13},{10,... | collective-permute-start | bytes 393224 | tf_op jit(solution)/shard_map/ppermute | solution.py:40
  22.4 6.0 %collective-permute-done.2 = f32[256,128]{1,0:T(8,128)S(1)} collective-permute-done((f32[256,128]{1,0:T(8,128)S(1)}, f32[256,128]{1,0:T(8,128)S(1)}, u32[]{:S(2)}, u32[]{:S(2)}) %collective-permute-start.2) | collective-permute-done | bytes 131104 | tf_op jit(solution)/shard_map/ppermute | solution.py:40
  28.4 0.3 fusion.2
  28.7 0.2 add_select_fusion
  28.9 0.0 copy-start
  28.9 1.5 %collective-permute-start.3 = (f32[256,128]{1,0:T(8,128)S(1)}, f32[256,128]{1,0:T(8,128)S(1)}, u32[]{:S(2)}, u32[]{:S(2)}) collective-permute-start(f32[256,128]{1,0:T(8,128)S(1)} %add_select_fusion), channel_id=1, source_target_pairs={{0,1},{1,0},{2,3},{3,2},{4,5},{5,4},{6,7},{7,6},{8,9},{9,8},{10,11... | collective-permute-start | bytes 393224 | tf_op jit(solution)/shard_map/ppermute | solution.py:40
  30.4 4.9 %shard_map.137 = (bf16[32,1280]{1,0:T(8,128)(2,1)}, bf16[32,1280]{1,0:T(8,128)(2,1)}) custom-call(bf16[8,4,1280]{2,1,0:T(4,128)(2,1)} %patch_ref.5, f32[1280]{0:T(1024)} %gain_ref.4, bf16[1280,3840]{1,0:T(8,128)(2,1)} %wv_ref.1, bf16[1280,3840]{1,0:T(8,128)(2,1)} %wv_ref.1), custom_call_target="tpu_custom_call" | custom-call | tf_op jit(solution)/shard_map/pallas_call | solution.py:223
  35.3 0.0 copy-done
  35.3 5.0 %shard_map.138.new_ref = f32[16,32,128]{2,1,0:T(8,128)} custom-call(bf16[8,4,1280]{2,1,0:T(4,128)(2,1)} %get-tuple-element.12.query_ref, bf16[32,1280]{1,0:T(8,128)(2,1)} %get-tuple-element.13.key_new_ref, bf16[32,1280]{1,0:T(8,128)(2,1)} %get-tuple-element.14.value_new_ref, bf16[64,1280]{1,0:T(8,128)(2,1)} %constant.57.clone.qmask_ref, ...), custom_call_target="tpu_custom_call" | custom-call | tf_op jit(solution)/shard_map/pallas_call | solution.py:237
  40.3 0.0 collective-permute-done.3
  40.3 0.0 copy-start.1
  40.3 0.6 %copy-done.1 = f32[256,128]{1,0:T(8,128)} copy-done((f32[256,128]{1,0:T(8,128)}, f32[256,128]{1,0:T(8,128)S(1)}, u32[]{:S(2)}) %copy-start.1) | copy-done | bytes 131096
  40.9 6.5 %shard_map.139 = bf16[8,4,1280]{2,1,0:T(4,128)(2,1)} custom-call(f32[8,32,128]{2,1,0:T(8,128)} %bitcast.6, f32[8,32,128]{2,1,0:T(8,128)} %bitcast.7, f32[16,32,128]{2,1,0:T(8,128)} %shard_map.138.new_ref, bf16[8,4,1280]{2,1,0:T(4,128)(2,1)} %patch_ref.5, bf16[1280,1280]{1,0:T(8,128)(2,1)} %w_out_ref.1, f32[1280]{0:T(1024)} %gain_ref.5, ...), custom_call_target="tpu_custom_call" | custom-call | tf_op jit(solution)/shard_map/pallas_call | solution.py:288
  (3 shorter events, 0.0 us)
Async XLA Ops:
  10.6 1.6 %collective-permute-start = (f32[256,128]{1,0:T(8,128)}, f32[256,128]{1,0:T(8,128)S(1)}, u32[]{:S(2)}, u32[]{:S(2)}) collective-permute-start(f32[256,128]{1,0:T(8,128)} %bitcast.8), channel_id=1, source_target_pairs={{0,1},{1,0},{2,3},{3,2},{4,5},{5,4},{6,7},{7,6},{8,9},{9,8},{10,11... | collective-permute-start | bytes 393224 | tf_op jit(solution)/shard_map/ppermute | solution.py:40
  13.6 6.0 %collective-permute-start.1 = (f32[256,128]{1,0:T(8,128)S(1)}, f32[256,128]{1,0:T(8,128)S(1)}, u32[]{:S(2)}, u32[]{:S(2)}) collective-permute-start(f32[256,128]{1,0:T(8,128)S(1)} %add_select_fusion.2), channel_id=1, source_target_pairs={{0,2},{1,3},{2,0},{3,1},{4,6},{5,7},{6,4},{7,5},{8,10},{9,11},{10,... | collective-permute-start | bytes 393224 | tf_op jit(solution)/shard_map/ppermute | solution.py:40
  20.1 8.3 %collective-permute-start.2 = (f32[256,128]{1,0:T(8,128)S(1)}, f32[256,128]{1,0:T(8,128)S(1)}, u32[]{:S(2)}, u32[]{:S(2)}) collective-permute-start(f32[256,128]{1,0:T(8,128)S(1)} %add_select_fusion.1), channel_id=1, source_target_pairs={{0,4},{1,5},{2,6},{3,7},{4,0},{5,1},{6,2},{7,3},{8,12},{9,13},{10,... | collective-permute-start | bytes 393224 | tf_op jit(solution)/shard_map/ppermute | solution.py:40
  28.9 6.4 %copy-start = (f32[256,128]{1,0:T(8,128)}, f32[256,128]{1,0:T(8,128)S(1)}, u32[]{:S(2)}) copy-start(f32[256,128]{1,0:T(8,128)S(1)} %add_select_fusion) | copy-start | bytes 393220
  28.9 11.4 %collective-permute-start.3 = (f32[256,128]{1,0:T(8,128)S(1)}, f32[256,128]{1,0:T(8,128)S(1)}, u32[]{:S(2)}, u32[]{:S(2)}) collective-permute-start(f32[256,128]{1,0:T(8,128)S(1)} %add_select_fusion), channel_id=1, source_target_pairs={{0,1},{1,0},{2,3},{3,2},{4,5},{5,4},{6,7},{7,6},{8,9},{9,8},{10,11... | collective-permute-start | bytes 393224 | tf_op jit(solution)/shard_map/ppermute | solution.py:40
  40.3 0.7 %copy-start.1 = (f32[256,128]{1,0:T(8,128)}, f32[256,128]{1,0:T(8,128)S(1)}, u32[]{:S(2)}) copy-start(f32[256,128]{1,0:T(8,128)S(1)} %collective-permute-done.3) | copy-start | bytes 393220

commit v17 on v13

--- a/solution.py
+++ b/solution.py
@@ -124,17 +124,16 @@
             target[h % half_heads, pl.ds(r * count, count), :] = folded[h * count:(h + 1) * count, :]
 
 
-def kv_projection_kernel(patch_ref, gain_ref, wk_ref, wv_ref, key_ref, value_ref):
+def kv_projection_kernel(patch_ref, gain_ref, w_ref, out_ref):
     normed = normed_rows(patch_ref, gain_ref)
-    key_ref[...] = jnp.dot(normed, wk_ref[...], preferred_element_type=jnp.float32).astype(key_ref.dtype)
-    value_ref[...] = jnp.dot(normed, wv_ref[...], preferred_element_type=jnp.float32).astype(value_ref.dtype)
-
-
-def new_partial_kernel(query_ref, key_new_ref, value_new_ref, qmask_ref, fold_ref, out_ref):
+    out_ref[...] = jnp.dot(normed, w_ref[...], preferred_element_type=jnp.float32).astype(out_ref.dtype)
+
+
+def new_partial_kernel(query_ref, kv_ref, qmask_ref, fold_ref, out_ref):
     groups, count, width = query_ref.shape
     heads = out_ref.shape[0]
-    keys_all = key_new_ref[...]
-    values_all = value_new_ref[...]
+    keys_all = kv_ref[:, pl.ds(0, width)]
+    values_all = kv_ref[:, pl.ds(width, width)]
     scale_factor = HD ** (-0.5)
     qmask = qmask_ref[...]
     qmask_float = qmask.astype(jnp.float32)
@@ -204,19 +203,19 @@
 def kv_projection(patches, attn_gain, w_qkv):
     groups, count, width = patches.shape
     vmem = pl.BlockSpec(memory_space=pltpu.VMEM)
-    key_block = pl.BlockSpec((width, width), lambda i: (0, 1))
-    value_block = pl.BlockSpec((width, width), lambda i: (0, 2))
-    rows = jax.ShapeDtypeStruct((groups * count, width), jnp.bfloat16)
-    return pl.pallas_call(
+    weight_block = pl.BlockSpec((width, width), lambda i: (0, 1 + i))
+    out_block = pl.BlockSpec((groups * count, width), lambda i: (0, i))
+    both = pl.pallas_call(
         kv_projection_kernel,
-        grid=(1,),
-        out_shape=(rows, rows),
-        in_specs=[vmem, vmem, key_block, value_block],
-        out_specs=(vmem, vmem),
-    )(patches, attn_gain, w_qkv, w_qkv)
-
-
-def new_partials(query_rows, keys_new, values_new):
+        grid=(2,),
+        out_shape=jax.ShapeDtypeStruct((groups * count, 2 * width), jnp.bfloat16),
+        in_specs=[vmem, vmem, weight_block],
+        out_specs=out_block,
+    )(patches, attn_gain, w_qkv)
+    return both
+
+
+def new_partials(query_rows, kv_rows):
     groups, count, width = query_rows.shape
     rows = groups * count
     qmask, fold = head_constants(count, width)
@@ -224,9 +223,9 @@
     return pl.pallas_call(
         new_partial_kernel,
         out_shape=jax.ShapeDtypeStruct((HEADS, rows, LANES), jnp.float32),
-        in_specs=[vmem] * 5,
+        in_specs=[vmem] * 4,
         out_specs=vmem,
-    )(query_rows, keys_new, values_new, qmask, fold)
+    )(query_rows, kv_rows, qmask, fold)
 
 
 def tail_kernel(
@@ -290,8 +289,8 @@
 ):
     seq_count = lax.axis_size("seq")
     kept, sent, query_rows = cache_partials(cache_len, patches, attn_gain, w_qkv, key_cache, value_cache)
-    keys_new, values_new = kv_projection(patches, attn_gain, w_qkv)
-    new_packed = new_partials(query_rows, keys_new, values_new)
+    kv_rows = kv_projection(patches, attn_gain, w_qkv)
+    new_packed = new_partials(query_rows, kv_rows)
     state, other = combine_over_seq(kept, sent, seq_count)
     return tail(state, other, new_packed, patches, w_out, ffn_gain, w_up, w_down)
 

time: 47.3 us -> 46.8 us (0.989)
  Pallas kernels: 26.7 us -> 26.2 us
    pallas_call x1, Pallas kernels: 4.92 us -> 4.37 us  [kv_projection(): pl.pallas_call(kv_projection_kernel, grid=(2,), out_shape=jax.ShapeDtypeS...]
  transfers between devices with their start and end apart: 4 -> 4, of which waited for: 3 -> 3; matrix products, arithmetic and copies ran while one was open for 0% -> 0% of each run, Pallas kernels for 21% -> 20%
where the time goes in v17:
time: 46.8 us; the launch traced here: 46.6 us
  Pallas kernels  26.2 us (56%)
  waiting for transfers between devices  11.1 us (24%)
  starting transfers between devices  6.23 us (13%)
  other arithmetic  2.35 us (5%)
  local copies, waits for them, and re-layouts  0.66 us (1%)
    ppermute x4, waiting for transfers between devices, exchange(): return with_layout_constraint(lax.ppermute(part, 'seq', pairs), row_major)  11.1 us
    pallas_call x1, Pallas kernels, cache_partials(): pl.pallas_call(cache_partial_kernel, grid=(1,), out_shape=(half, half, ja...  10.3 us
    pallas_call x1, Pallas kernels, tail(): pl.pallas_call(tail_kernel, out_shape=jax.ShapeDtypeStruct(patches.shape,...  6.51 us
    ppermute x4, starting transfers between devices, exchange(): return with_layout_constraint(lax.ppermute(part, 'seq', pairs), row_major)  6.23 us
    pallas_call x1, Pallas kernels, new_partials(): pl.pallas_call(new_partial_kernel, out_shape=jax.ShapeDtypeStruct((HEADS,...  4.99 us
    pallas_call x1, Pallas kernels, kv_projection(): pl.pallas_call(kv_projection_kernel, grid=(2,), out_shape=jax.ShapeDtypeS...  4.37 us
  transfers between devices with their start and end apart: 4, of which 3 were waited for; matrix products, arithmetic and copies ran while one was open for 0% of the time, Pallas kernels for 20%

profile of v17, /device:TPU:1, one launch (start us, length us, event | category | flops | bytes accessed | tf_op | source)
XLA Modules:
  0.0 46.6 jit_solution(12341543982235232236)
XLA Ops:
  0.0 10.3 %shard_map.136 = (f32[8,32,128]{2,1,0:T(8,128)}, f32[8,32,128]{2,1,0:T(8,128)}, bf16[8,4,1280]{2,1,0:T(4,128)(2,1)}) custom-call(s32[8]{0:T(128)} %length_ref.1, bf16[8,4,1280]{2,1,0:T(4,128)(2,1)} %patch_ref.5, f32[1280]{0:T(1024)} %gain_ref.4, bf16[1280,3840]{1,0:T(8,128)(2,1)} %w_ref.1, bf16[8,128,1280]{2,1,0:T(8,128)(2,1)} %key_ref.1, ...), custom_call_target="tpu_custom_call" | custom-call | tf_op jit(solution)/shard_map/pallas_call | solution.py:194
  10.3 0.0 collective-permute-start
  10.4 1.5 %collective-permute-done = f32[256,128]{1,0:T(8,128)S(1)} collective-permute-done((f32[256,128]{1,0:T(8,128)}, f32[256,128]{1,0:T(8,128)S(1)}, u32[]{:S(2)}, u32[]{:S(2)}) %collective-permute-start) | collective-permute-done | bytes 131104 | tf_op jit(solution)/shard_map/ppermute | solution.py:40
  11.9 0.9 %bitcast_select_fusion.1 = (f32[256,128]{1,0:T(8,128)S(1)}, f32[256,128]{1,0:T(8,128)S(1)}) fusion(f32[256,128]{1,0:T(8,128)S(1)} %collective-permute-done, f32[8,32,128]{2,1,0:T(8,128)} %get-tuple-element.8, pred[]{:T(512)S(6)} %eq.26), kind=kLoop, calls=%fused_computation.1 | loop fusion | flops 65536 | bytes 524289 | tf_op jit(solution)/shard_map/jit(_where)/select_n | solution.py:51
  12.8 0.3 fusion
  13.1 0.2 add_select_fusion.2
  13.3 2.5 %collective-permute-start.1 = (f32[256,128]{1,0:T(8,128)S(1)}, f32[256,128]{1,0:T(8,128)S(1)}, u32[]{:S(2)}, u32[]{:S(2)}) collective-permute-start(f32[256,128]{1,0:T(8,128)S(1)} %add_select_fusion.2), channel_id=1, source_target_pairs={{0,2},{1,3},{2,0},{3,1},{4,6},{5,7},{6,4},{7,5},{8,10},{9,11},{10,... | collective-permute-start | bytes 393224 | tf_op jit(solution)/shard_map/ppermute | solution.py:40
  15.8 3.5 %collective-permute-done.1 = f32[256,128]{1,0:T(8,128)S(1)} collective-permute-done((f32[256,128]{1,0:T(8,128)S(1)}, f32[256,128]{1,0:T(8,128)S(1)}, u32[]{:S(2)}, u32[]{:S(2)}) %collective-permute-start.1) | collective-permute-done | bytes 131104 | tf_op jit(solution)/shard_map/ppermute | solution.py:40
  19.3 0.3 fusion.1
  19.6 0.2 add_select_fusion.1
  19.8 2.3 %collective-permute-start.2 = (f32[256,128]{1,0:T(8,128)S(1)}, f32[256,128]{1,0:T(8,128)S(1)}, u32[]{:S(2)}, u32[]{:S(2)}) collective-permute-start(f32[256,128]{1,0:T(8,128)S(1)} %add_select_fusion.1), channel_id=1, source_target_pairs={{0,4},{1,5},{2,6},{3,7},{4,0},{5,1},{6,2},{7,3},{8,12},{9,13},{10,... | collective-permute-start | bytes 393224 | tf_op jit(solution)/shard_map/ppermute | solution.py:40
  22.0 6.0 %collective-permute-done.2 = f32[256,128]{1,0:T(8,128)S(1)} collective-permute-done((f32[256,128]{1,0:T(8,128)S(1)}, f32[256,128]{1,0:T(8,128)S(1)}, u32[]{:S(2)}, u32[]{:S(2)}) %collective-permute-start.2) | collective-permute-done | bytes 131104 | tf_op jit(solution)/shard_map/ppermute | solution.py:40
  28.1 0.3 fusion.2
  28.4 0.2 add_select_fusion
  28.6 0.0 copy-start
  28.6 1.5 %collective-permute-start.3 = (f32[256,128]{1,0:T(8,128)S(1)}, f32[256,128]{1,0:T(8,128)S(1)}, u32[]{:S(2)}, u32[]{:S(2)}) collective-permute-start(f32[256,128]{1,0:T(8,128)S(1)} %add_select_fusion), channel_id=1, source_target_pairs={{0,1},{1,0},{2,3},{3,2},{4,5},{5,4},{6,7},{7,6},{8,9},{9,8},{10,11... | collective-permute-start | bytes 393224 | tf_op jit(solution)/shard_map/ppermute | solution.py:40
  30.0 4.4 %shard_map.137.kv_ref = bf16[32,2560]{1,0:T(8,128)(2,1)} custom-call(bf16[8,4,1280]{2,1,0:T(4,128)(2,1)} %patch_ref.5, f32[1280]{0:T(1024)} %gain_ref.4, bf16[1280,3840]{1,0:T(8,128)(2,1)} %w_ref.1), custom_call_target="tpu_custom_call" | custom-call | tf_op jit(solution)/shard_map/pallas_call | solution.py:208
  34.4 0.0 copy-done
  34.4 5.0 %shard_map.138.new_ref = f32[16,32,128]{2,1,0:T(8,128)} custom-call(bf16[8,4,1280]{2,1,0:T(4,128)(2,1)} %get-tuple-element.10.query_ref, bf16[32,2560]{1,0:T(8,128)(2,1)} %shard_map.137.kv_ref, bf16[64,1280]{1,0:T(8,128)(2,1)} %constant.57.clone.qmask_ref, bf16[1280,128]{1,0:T(8,128)(2,1)} %constant.55.clone.fold_ref), custom_call_target="tpu_custom_call" | custom-call | tf_op jit(solution)/shard_map/pallas_call | solution.py:223
  39.4 0.0 collective-permute-done.3
  39.4 0.0 copy-start.1
  39.4 0.7 %copy-done.1 = f32[256,128]{1,0:T(8,128)} copy-done((f32[256,128]{1,0:T(8,128)}, f32[256,128]{1,0:T(8,128)S(1)}, u32[]{:S(2)}) %copy-start.1) | copy-done | bytes 131096
  40.1 6.5 %shard_map.139 = bf16[8,4,1280]{2,1,0:T(4,128)(2,1)} custom-call(f32[8,32,128]{2,1,0:T(8,128)} %bitcast.6, f32[8,32,128]{2,1,0:T(8,128)} %bitcast.7, f32[16,32,128]{2,1,0:T(8,128)} %shard_map.138.new_ref, bf16[8,4,1280]{2,1,0:T(4,128)(2,1)} %patch_ref.5, bf16[1280,1280]{1,0:T(8,128)(2,1)} %w_out_ref.1, f32[1280]{0:T(1024)} %gain_ref.5, ...), custom_call_target="tpu_custom_call" | custom-call | tf_op jit(solution)/shard_map/pallas_call | solution.py:274
  (3 shorter events, 0.0 us)
Async XLA Ops:
  10.3 1.6 %collective-permute-start = (f32[256,128]{1,0:T(8,128)}, f32[256,128]{1,0:T(8,128)S(1)}, u32[]{:S(2)}, u32[]{:S(2)}) collective-permute-start(f32[256,128]{1,0:T(8,128)} %bitcast.8), channel_id=1, source_target_pairs={{0,1},{1,0},{2,3},{3,2},{4,5},{5,4},{6,7},{7,6},{8,9},{9,8},{10,11... | collective-permute-start | bytes 393224 | tf_op jit(solution)/shard_map/ppermute | solution.py:40
  13.3 6.0 %collective-permute-start.1 = (f32[256,128]{1,0:T(8,128)S(1)}, f32[256,128]{1,0:T(8,128)S(1)}, u32[]{:S(2)}, u32[]{:S(2)}) collective-permute-start(f32[256,128]{1,0:T(8,128)S(1)} %add_select_fusion.2), channel_id=1, source_target_pairs={{0,2},{1,3},{2,0},{3,1},{4,6},{5,7},{6,4},{7,5},{8,10},{9,11},{10,... | collective-permute-start | bytes 393224 | tf_op jit(solution)/shard_map/ppermute | solution.py:40
  19.8 8.3 %collective-permute-start.2 = (f32[256,128]{1,0:T(8,128)S(1)}, f32[256,128]{1,0:T(8,128)S(1)}, u32[]{:S(2)}, u32[]{:S(2)}) collective-permute-start(f32[256,128]{1,0:T(8,128)S(1)} %add_select_fusion.1), channel_id=1, source_target_pairs={{0,4},{1,5},{2,6},{3,7},{4,0},{5,1},{6,2},{7,3},{8,12},{9,13},{10,... | collective-permute-start | bytes 393224 | tf_op jit(solution)/shard_map/ppermute | solution.py:40
  28.6 5.8 %copy-start = (f32[256,128]{1,0:T(8,128)}, f32[256,128]{1,0:T(8,128)S(1)}, u32[]{:S(2)}) copy-start(f32[256,128]{1,0:T(8,128)S(1)} %add_select_fusion) | copy-start | bytes 393220
  28.6 10.8 %collective-permute-start.3 = (f32[256,128]{1,0:T(8,128)S(1)}, f32[256,128]{1,0:T(8,128)S(1)}, u32[]{:S(2)}, u32[]{:S(2)}) collective-permute-start(f32[256,128]{1,0:T(8,128)S(1)} %add_select_fusion), channel_id=1, source_target_pairs={{0,1},{1,0},{2,3},{3,2},{4,5},{5,4},{6,7},{7,6},{8,9},{9,8},{10,11... | collective-permute-start | bytes 393224 | tf_op jit(solution)/shard_map/ppermute | solution.py:40
  39.4 0.7 %copy-start.1 = (f32[256,128]{1,0:T(8,128)}, f32[256,128]{1,0:T(8,128)S(1)}, u32[]{:S(2)}) copy-start(f32[256,128]{1,0:T(8,128)S(1)} %collective-permute-done.3) | copy-start | bytes 393220

commit v18 on v17

--- a/solution.py
+++ b/solution.py
@@ -93,11 +93,16 @@
     half_heads = kept_ref.shape[0]
     heads = 2 * half_heads
     count = kept_ref.shape[1] // groups
+    step = pl.program_id(0)
     me = lax.axis_index("seq")
     core = me % 2
-    query_float = jnp.dot(normed_rows(patch_ref, gain_ref), wq_ref[...], preferred_element_type=jnp.float32)
-    for r in range(groups):
-        query_ref[r] = query_float[r * count:(r + 1) * count, :].astype(query_ref.dtype)
+
+    @pl.when(step == 0)
+    def _():
+        query_float = jnp.dot(normed_rows(patch_ref, gain_ref), wq_ref[...], preferred_element_type=jnp.float32)
+        for r in range(query_ref.shape[0]):
+            query_ref[r] = query_float[r * count:(r + 1) * count, :].astype(query_ref.dtype)
+
     scale_factor = HD ** (-0.5)
     qmask = qmask_ref[core]
     qmask_float = qmask.astype(jnp.float32)
@@ -105,12 +110,12 @@
     position = me * slots + lax.broadcasted_iota(jnp.int32, (1, slots), 1)
     lane = lax.broadcasted_iota(jnp.int32, (heads * count, LANES), 1)
     for r in range(groups):
-        queries = query_ref[r]
+        queries = query_ref[step * groups + r]
         query_rows = jnp.concatenate([queries] * heads, axis=0) * qmask
         scores = lax.dot_general(
             query_rows, key_ref[r], (((1,), (1,)), ((), ())), preferred_element_type=jnp.float32
         ) * scale_factor
-        live = position < length_ref[r]
+        live = position < length_ref[step * groups + r]
         masked = jnp.where(live, scores, negative_fill)
         peak = jnp.max(masked, axis=1, keepdims=True)
         weights = jnp.where(live, jnp.exp(masked - peak), 0.0)
@@ -182,7 +187,7 @@
 
 
 def cache_partials(cache_len, patches, attn_gain, w_qkv, key_cache, value_cache):
-    groups, _, width = key_cache.shape
+    groups, slots, width = key_cache.shape
     count = patches.shape[1]
     rows = groups * count
     _, fold = head_constants(count, width)
@@ -190,13 +195,16 @@
     smem = pl.BlockSpec(memory_space=pltpu.SMEM)
     vmem = pl.BlockSpec(memory_space=pltpu.VMEM)
     query_block = pl.BlockSpec((width, width), lambda i: (0, 0))
+    steps = 4
+    cache_block = pl.BlockSpec((groups // steps, slots, width), lambda i: (i, 0, 0))
+    half_block = pl.BlockSpec((HEADS // 2, rows // steps, LANES), lambda i: (0, i, 0))
     half = jax.ShapeDtypeStruct((HEADS // 2, rows, LANES), jnp.float32)
     return pl.pallas_call(
         cache_partial_kernel,
-        grid=(1,),
+        grid=(steps,),
         out_shape=(half, half, jax.ShapeDtypeStruct(patches.shape, jnp.bfloat16)),
-        in_specs=[smem, vmem, vmem, query_block, vmem, vmem, vmem, vmem],
-        out_specs=(vmem, vmem, vmem),
+        in_specs=[smem, vmem, vmem, query_block, cache_block, cache_block, vmem, vmem],
+        out_specs=(half_block, half_block, vmem),
     )(cache_len, patches, attn_gain, w_qkv, key_cache, value_cache, qmask, fold)
 
 

time: 46.8 us -> 46.2 us (0.987)
  Pallas kernels: 26.2 us -> 25.6 us
    pallas_call x1, Pallas kernels: 10.3 us -> 9.78 us  [cache_partials(): pl.pallas_call(cache_partial_kernel, grid=(steps,), out_shape=(half, half...]
where the time goes in v18:
time: 46.2 us; the launch traced here: 46 us
  Pallas kernels  25.6 us (55%)
  waiting for transfers between devices  11.1 us (24%)
  starting transfers between devices  6.21 us (13%)
  other arithmetic  2.35 us (5%)
  local copies, waits for them, and re-layouts  0.66 us (1%)
    ppermute x4, waiting for transfers between devices, exchange(): return with_layout_constraint(lax.ppermute(part, 'seq', pairs), row_major)  11.1 us
    pallas_call x1, Pallas kernels, cache_partials(): pl.pallas_call(cache_partial_kernel, grid=(steps,), out_shape=(half, half...  9.78 us
    pallas_call x1, Pallas kernels, tail(): pl.pallas_call(tail_kernel, out_shape=jax.ShapeDtypeStruct(patches.shape,...  6.51 us
    ppermute x4, starting transfers between devices, exchange(): return with_layout_constraint(lax.ppermute(part, 'seq', pairs), row_major)  6.21 us
    pallas_call x1, Pallas kernels, new_partials(): pl.pallas_call(new_partial_kernel, out_shape=jax.ShapeDtypeStruct((HEADS,...  4.99 us
    pallas_call x1, Pallas kernels, kv_projection(): pl.pallas_call(kv_projection_kernel, grid=(2,), out_shape=jax.ShapeDtypeS...  4.37 us
  transfers between devices with their start and end apart: 4, of which 3 were waited for; matrix products, arithmetic and copies ran while one was open for 0% of the time, Pallas kernels for 20%

profile of v18, /device:TPU:1, one launch (start us, length us, event | category | flops | bytes accessed | tf_op | source)
XLA Modules:
  0.0 46.0 jit_solution(12622818611269934160)
XLA Ops:
  0.0 9.8 %shard_map.136 = (f32[8,32,128]{2,1,0:T(8,128)}, f32[8,32,128]{2,1,0:T(8,128)}, bf16[8,4,1280]{2,1,0:T(4,128)(2,1)}) custom-call(s32[8]{0:T(128)} %length_ref.1, bf16[8,4,1280]{2,1,0:T(4,128)(2,1)} %patch_ref.5, f32[1280]{0:T(1024)} %gain_ref.4, bf16[1280,3840]{1,0:T(8,128)(2,1)} %w_ref.1, bf16[8,128,1280]{2,1,0:T(8,128)(2,1)} %key_ref.1, ...), custom_call_target="tpu_custom_call" | custom-call | tf_op jit(solution)/shard_map/pallas_call | solution.py:202
  9.8 0.0 collective-permute-start
  9.8 1.5 %collective-permute-done = f32[256,128]{1,0:T(8,128)S(1)} collective-permute-done((f32[256,128]{1,0:T(8,128)}, f32[256,128]{1,0:T(8,128)S(1)}, u32[]{:S(2)}, u32[]{:S(2)}) %collective-permute-start) | collective-permute-done | bytes 131104 | tf_op jit(solution)/shard_map/ppermute | solution.py:40
  11.3 0.9 %bitcast_select_fusion.1 = (f32[256,128]{1,0:T(8,128)S(1)}, f32[256,128]{1,0:T(8,128)S(1)}) fusion(f32[256,128]{1,0:T(8,128)S(1)} %collective-permute-done, f32[8,32,128]{2,1,0:T(8,128)} %get-tuple-element.8, pred[]{:T(512)S(6)} %eq.26), kind=kLoop, calls=%fused_computation.1 | loop fusion | flops 65536 | bytes 524289 | tf_op jit(solution)/shard_map/jit(_where)/select_n | solution.py:51
  12.3 0.3 fusion
  12.6 0.2 add_select_fusion.2
  12.7 2.5 %collective-permute-start.1 = (f32[256,128]{1,0:T(8,128)S(1)}, f32[256,128]{1,0:T(8,128)S(1)}, u32[]{:S(2)}, u32[]{:S(2)}) collective-permute-start(f32[256,128]{1,0:T(8,128)S(1)} %add_select_fusion.2), channel_id=1, source_target_pairs={{0,2},{1,3},{2,0},{3,1},{4,6},{5,7},{6,4},{7,5},{8,10},{9,11},{10,... | collective-permute-start | bytes 393224 | tf_op jit(solution)/shard_map/ppermute | solution.py:40
  15.2 3.5 %collective-permute-done.1 = f32[256,128]{1,0:T(8,128)S(1)} collective-permute-done((f32[256,128]{1,0:T(8,128)S(1)}, f32[256,128]{1,0:T(8,128)S(1)}, u32[]{:S(2)}, u32[]{:S(2)}) %collective-permute-start.1) | collective-permute-done | bytes 131104 | tf_op jit(solution)/shard_map/ppermute | solution.py:40
  18.8 0.3 fusion.1
  19.1 0.2 add_select_fusion.1
  19.2 2.3 %collective-permute-start.2 = (f32[256,128]{1,0:T(8,128)S(1)}, f32[256,128]{1,0:T(8,128)S(1)}, u32[]{:S(2)}, u32[]{:S(2)}) collective-permute-start(f32[256,128]{1,0:T(8,128)S(1)} %add_select_fusion.1), channel_id=1, source_target_pairs={{0,4},{1,5},{2,6},{3,7},{4,0},{5,1},{6,2},{7,3},{8,12},{9,13},{10,... | collective-permute-start | bytes 393224 | tf_op jit(solution)/shard_map/ppermute | solution.py:40
  21.5 6.0 %collective-permute-done.2 = f32[256,128]{1,0:T(8,128)S(1)} collective-permute-done((f32[256,128]{1,0:T(8,128)S(1)}, f32[256,128]{1,0:T(8,128)S(1)}, u32[]{:S(2)}, u32[]{:S(2)}) %collective-permute-start.2) | collective-permute-done | bytes 131104 | tf_op jit(solution)/shard_map/ppermute | solution.py:40
  27.5 0.3 fusion.2
  27.8 0.2 add_select_fusion
  28.0 0.0 copy-start
  28.0 1.5 %collective-permute-start.3 = (f32[256,128]{1,0:T(8,128)S(1)}, f32[256,128]{1,0:T(8,128)S(1)}, u32[]{:S(2)}, u32[]{:S(2)}) collective-permute-start(f32[256,128]{1,0:T(8,128)S(1)} %add_select_fusion), channel_id=1, source_target_pairs={{0,1},{1,0},{2,3},{3,2},{4,5},{5,4},{6,7},{7,6},{8,9},{9,8},{10,11... | collective-permute-start | bytes 393224 | tf_op jit(solution)/shard_map/ppermute | solution.py:40
  29.5 4.4 %shard_map.137.kv_ref = bf16[32,2560]{1,0:T(8,128)(2,1)} custom-call(bf16[8,4,1280]{2,1,0:T(4,128)(2,1)} %patch_ref.5, f32[1280]{0:T(1024)} %gain_ref.4, bf16[1280,3840]{1,0:T(8,128)(2,1)} %w_ref.1), custom_call_target="tpu_custom_call" | custom-call | tf_op jit(solution)/shard_map/pallas_call | solution.py:216
  33.9 0.0 copy-done
  33.9 5.0 %shard_map.138.new_ref = f32[16,32,128]{2,1,0:T(8,128)} custom-call(bf16[8,4,1280]{2,1,0:T(4,128)(2,1)} %get-tuple-element.10.query_ref, bf16[32,2560]{1,0:T(8,128)(2,1)} %shard_map.137.kv_ref, bf16[64,1280]{1,0:T(8,128)(2,1)} %constant.57.clone.qmask_ref, bf16[1280,128]{1,0:T(8,128)(2,1)} %constant.55.clone.fold_ref), custom_call_target="tpu_custom_call" | custom-call | tf_op jit(solution)/shard_map/pallas_call | solution.py:231
  38.9 0.0 collective-permute-done.3
  38.9 0.0 copy-start.1
  38.9 0.7 %copy-done.1 = f32[256,128]{1,0:T(8,128)} copy-done((f32[256,128]{1,0:T(8,128)}, f32[256,128]{1,0:T(8,128)S(1)}, u32[]{:S(2)}) %copy-start.1) | copy-done | bytes 131096
  39.5 6.5 %shard_map.139 = bf16[8,4,1280]{2,1,0:T(4,128)(2,1)} custom-call(f32[8,32,128]{2,1,0:T(8,128)} %bitcast.6, f32[8,32,128]{2,1,0:T(8,128)} %bitcast.7, f32[16,32,128]{2,1,0:T(8,128)} %shard_map.138.new_ref, bf16[8,4,1280]{2,1,0:T(4,128)(2,1)} %patch_ref.5, bf16[1280,1280]{1,0:T(8,128)(2,1)} %w_out_ref.1, f32[1280]{0:T(1024)} %gain_ref.5, ...), custom_call_target="tpu_custom_call" | custom-call | tf_op jit(solution)/shard_map/pallas_call | solution.py:282
  (3 shorter events, 0.0 us)
Async XLA Ops:
  9.8 1.6 %collective-permute-start = (f32[256,128]{1,0:T(8,128)}, f32[256,128]{1,0:T(8,128)S(1)}, u32[]{:S(2)}, u32[]{:S(2)}) collective-permute-start(f32[256,128]{1,0:T(8,128)} %bitcast.8), channel_id=1, source_target_pairs={{0,1},{1,0},{2,3},{3,2},{4,5},{5,4},{6,7},{7,6},{8,9},{9,8},{10,11... | collective-permute-start | bytes 393224 | tf_op jit(solution)/shard_map/ppermute | solution.py:40
  12.7 6.0 %collective-permute-start.1 = (f32[256,128]{1,0:T(8,128)S(1)}, f32[256,128]{1,0:T(8,128)S(1)}, u32[]{:S(2)}, u32[]{:S(2)}) collective-permute-start(f32[256,128]{1,0:T(8,128)S(1)} %add_select_fusion.2), channel_id=1, source_target_pairs={{0,2},{1,3},{2,0},{3,1},{4,6},{5,7},{6,4},{7,5},{8,10},{9,11},{10,... | collective-permute-start | bytes 393224 | tf_op jit(solution)/shard_map/ppermute | solution.py:40
  19.2 8.3 %collective-permute-start.2 = (f32[256,128]{1,0:T(8,128)S(1)}, f32[256,128]{1,0:T(8,128)S(1)}, u32[]{:S(2)}, u32[]{:S(2)}) collective-permute-start(f32[256,128]{1,0:T(8,128)S(1)} %add_select_fusion.1), channel_id=1, source_target_pairs={{0,4},{1,5},{2,6},{3,7},{4,0},{5,1},{6,2},{7,3},{8,12},{9,13},{10,... | collective-permute-start | bytes 393224 | tf_op jit(solution)/shard_map/ppermute | solution.py:40
  28.0 5.8 %copy-start = (f32[256,128]{1,0:T(8,128)}, f32[256,128]{1,0:T(8,128)S(1)}, u32[]{:S(2)}) copy-start(f32[256,128]{1,0:T(8,128)S(1)} %add_select_fusion) | copy-start | bytes 393220
  28.0 10.8 %collective-permute-start.3 = (f32[256,128]{1,0:T(8,128)S(1)}, f32[256,128]{1,0:T(8,128)S(1)}, u32[]{:S(2)}, u32[]{:S(2)}) collective-permute-start(f32[256,128]{1,0:T(8,128)S(1)} %add_select_fusion), channel_id=1, source_target_pairs={{0,1},{1,0},{2,3},{3,2},{4,5},{5,4},{6,7},{7,6},{8,9},{9,8},{10,11... | collective-permute-start | bytes 393224 | tf_op jit(solution)/shard_map/ppermute | solution.py:40
  38.9 0.7 %copy-start.1 = (f32[256,128]{1,0:T(8,128)}, f32[256,128]{1,0:T(8,128)S(1)}, u32[]{:S(2)}) copy-start(f32[256,128]{1,0:T(8,128)S(1)} %collective-permute-done.3) | copy-start | bytes 393220

commit v19 on v18

--- a/solution.py
+++ b/solution.py
@@ -195,7 +195,7 @@
     smem = pl.BlockSpec(memory_space=pltpu.SMEM)
     vmem = pl.BlockSpec(memory_space=pltpu.VMEM)
     query_block = pl.BlockSpec((width, width), lambda i: (0, 0))
-    steps = 4
+    steps = 2
     cache_block = pl.BlockSpec((groups // steps, slots, width), lambda i: (i, 0, 0))
     half_block = pl.BlockSpec((HEADS // 2, rows // steps, LANES), lambda i: (0, i, 0))
     half = jax.ShapeDtypeStruct((HEADS // 2, rows, LANES), jnp.float32)
@@ -211,11 +211,13 @@
 def kv_projection(patches, attn_gain, w_qkv):
     groups, count, width = patches.shape
     vmem = pl.BlockSpec(memory_space=pltpu.VMEM)
-    weight_block = pl.BlockSpec((width, width), lambda i: (0, 1 + i))
-    out_block = pl.BlockSpec((groups * count, width), lambda i: (0, i))
+    pieces = 4
+    piece = 2 * width // pieces
+    weight_block = pl.BlockSpec((width, piece), lambda i: (0, pieces // 2 + i))
+    out_block = pl.BlockSpec((groups * count, piece), lambda i: (0, i))
     both = pl.pallas_call(
         kv_projection_kernel,
-        grid=(2,),
+        grid=(pieces,),
         out_shape=jax.ShapeDtypeStruct((groups * count, 2 * width), jnp.bfloat16),
         in_specs=[vmem, vmem, weight_block],
         out_specs=out_block,

time: 46.2 us -> 47.1 us (1.019)
  Pallas kernels: 25.6 us -> 26.4 us
    pallas_call x1, Pallas kernels: 4.37 us -> 5.16 us  [kv_projection(): pl.pallas_call(kv_projection_kernel, grid=(pieces,), out_shape=jax.ShapeD...]
  transfers between devices with their start and end apart: 4 -> 4, of which waited for: 3 -> 3; matrix products, arithmetic and copies ran while one was open for 0% -> 0% of each run, Pallas kernels for 20% -> 22%
where the time goes in v19:
time: 47.1 us; the launch traced here: 46.9 us
  Pallas kernels  26.4 us (56%)
  waiting for transfers between devices  11.1 us (24%)
  starting transfers between devices  6.28 us (13%)
  other arithmetic  2.35 us (5%)
  local copies, waits for them, and re-layouts  0.66 us (1%)
    ppermute x4, waiting for transfers between devices, exchange(): return with_layout_constraint(lax.ppermute(part, 'seq', pairs), row_major)  11.1 us
    pallas_call x1, Pallas kernels, cache_partials(): pl.pallas_call(cache_partial_kernel, grid=(steps,), out_shape=(half, half...  9.76 us
    pallas_call x1, Pallas kernels, tail(): pl.pallas_call(tail_kernel, out_shape=jax.ShapeDtypeStruct(patches.shape,...  6.51 us
    ppermute x4, starting transfers between devices, exchange(): return with_layout_constraint(lax.ppermute(part, 'seq', pairs), row_major)  6.28 us
    pallas_call x1, Pallas kernels, kv_projection(): pl.pallas_call(kv_projection_kernel, grid=(pieces,), out_shape=jax.ShapeD...  5.16 us
    pallas_call x1, Pallas kernels, new_partials(): pl.pallas_call(new_partial_kernel, out_shape=jax.ShapeDtypeStruct((HEADS,...  4.99 us
  transfers between devices with their start and end apart: 4, of which 3 were waited for; matrix products, arithmetic and copies ran while one was open for 0% of the time, Pallas kernels for 22%

profile of v19, /device:TPU:1, one launch (start us, length us, event | category | flops | bytes accessed | tf_op | source)
XLA Modules:
  0.0 46.9 jit_solution(3839255235981236316)
XLA Ops:
  0.0 9.8 %shard_map.136 = (f32[8,32,128]{2,1,0:T(8,128)}, f32[8,32,128]{2,1,0:T(8,128)}, bf16[8,4,1280]{2,1,0:T(4,128)(2,1)}) custom-call(s32[8]{0:T(128)} %length_ref.1, bf16[8,4,1280]{2,1,0:T(4,128)(2,1)} %patch_ref.5, f32[1280]{0:T(1024)} %gain_ref.4, bf16[1280,3840]{1,0:T(8,128)(2,1)} %w_ref.1, bf16[8,128,1280]{2,1,0:T(8,128)(2,1)} %key_ref.1, ...), custom_call_target="tpu_custom_call" | custom-call | tf_op jit(solution)/shard_map/pallas_call | solution.py:202
  9.8 0.1 collective-permute-start
  9.9 1.5 %collective-permute-done = f32[256,128]{1,0:T(8,128)S(1)} collective-permute-done((f32[256,128]{1,0:T(8,128)}, f32[256,128]{1,0:T(8,128)S(1)}, u32[]{:S(2)}, u32[]{:S(2)}) %collective-permute-start) | collective-permute-done | bytes 131104 | tf_op jit(solution)/shard_map/ppermute | solution.py:40
  11.4 0.9 %bitcast_select_fusion.1 = (f32[256,128]{1,0:T(8,128)S(1)}, f32[256,128]{1,0:T(8,128)S(1)}) fusion(f32[256,128]{1,0:T(8,128)S(1)} %collective-permute-done, f32[8,32,128]{2,1,0:T(8,128)} %get-tuple-element.8, pred[]{:T(512)S(6)} %eq.26), kind=kLoop, calls=%fused_computation.1 | loop fusion | flops 65536 | bytes 524289 | tf_op jit(solution)/shard_map/jit(_where)/select_n | solution.py:51
  12.3 0.3 fusion
  12.6 0.2 add_select_fusion.2
  12.8 2.5 %collective-permute-start.1 = (f32[256,128]{1,0:T(8,128)S(1)}, f32[256,128]{1,0:T(8,128)S(1)}, u32[]{:S(2)}, u32[]{:S(2)}) collective-permute-start(f32[256,128]{1,0:T(8,128)S(1)} %add_select_fusion.2), channel_id=1, source_target_pairs={{0,2},{1,3},{2,0},{3,1},{4,6},{5,7},{6,4},{7,5},{8,10},{9,11},{10,... | collective-permute-start | bytes 393224 | tf_op jit(solution)/shard_map/ppermute | solution.py:40
  15.3 3.5 %collective-permute-done.1 = f32[256,128]{1,0:T(8,128)S(1)} collective-permute-done((f32[256,128]{1,0:T(8,128)S(1)}, f32[256,128]{1,0:T(8,128)S(1)}, u32[]{:S(2)}, u32[]{:S(2)}) %collective-permute-start.1) | collective-permute-done | bytes 131104 | tf_op jit(solution)/shard_map/ppermute | solution.py:40
  18.8 0.3 fusion.1
  19.1 0.2 add_select_fusion.1
  19.3 2.3 %collective-permute-start.2 = (f32[256,128]{1,0:T(8,128)S(1)}, f32[256,128]{1,0:T(8,128)S(1)}, u32[]{:S(2)}, u32[]{:S(2)}) collective-permute-start(f32[256,128]{1,0:T(8,128)S(1)} %add_select_fusion.1), channel_id=1, source_target_pairs={{0,4},{1,5},{2,6},{3,7},{4,0},{5,1},{6,2},{7,3},{8,12},{9,13},{10,... | collective-permute-start | bytes 393224 | tf_op jit(solution)/shard_map/ppermute | solution.py:40
  21.5 6.0 %collective-permute-done.2 = f32[256,128]{1,0:T(8,128)S(1)} collective-permute-done((f32[256,128]{1,0:T(8,128)S(1)}, f32[256,128]{1,0:T(8,128)S(1)}, u32[]{:S(2)}, u32[]{:S(2)}) %collective-permute-start.2) | collective-permute-done | bytes 131104 | tf_op jit(solution)/shard_map/ppermute | solution.py:40
  27.6 0.3 fusion.2
  27.9 0.2 add_select_fusion
  28.1 0.0 copy-start
  28.1 1.5 %collective-permute-start.3 = (f32[256,128]{1,0:T(8,128)S(1)}, f32[256,128]{1,0:T(8,128)S(1)}, u32[]{:S(2)}, u32[]{:S(2)}) collective-permute-start(f32[256,128]{1,0:T(8,128)S(1)} %add_select_fusion), channel_id=1, source_target_pairs={{0,1},{1,0},{2,3},{3,2},{4,5},{5,4},{6,7},{7,6},{8,9},{9,8},{10,11... | collective-permute-start | bytes 393224 | tf_op jit(solution)/shard_map/ppermute | solution.py:40
  29.5 5.2 %shard_map.137.kv_ref = bf16[32,2560]{1,0:T(8,128)(2,1)} custom-call(bf16[8,4,1280]{2,1,0:T(4,128)(2,1)} %patch_ref.5, f32[1280]{0:T(1024)} %gain_ref.4, bf16[1280,3840]{1,0:T(8,128)(2,1)} %w_ref.1), custom_call_target="tpu_custom_call" | custom-call | tf_op jit(solution)/shard_map/pallas_call | solution.py:218
  34.7 0.0 copy-done
  34.7 5.0 %shard_map.138.new_ref = f32[16,32,128]{2,1,0:T(8,128)} custom-call(bf16[8,4,1280]{2,1,0:T(4,128)(2,1)} %get-tuple-element.10.query_ref, bf16[32,2560]{1,0:T(8,128)(2,1)} %shard_map.137.kv_ref, bf16[64,1280]{1,0:T(8,128)(2,1)} %constant.57.clone.qmask_ref, bf16[1280,128]{1,0:T(8,128)(2,1)} %constant.55.clone.fold_ref), custom_call_target="tpu_custom_call" | custom-call | tf_op jit(solution)/shard_map/pallas_call | solution.py:233
  39.7 0.0 collective-permute-done.3
  39.7 0.0 copy-start.1
  39.7 0.7 %copy-done.1 = f32[256,128]{1,0:T(8,128)} copy-done((f32[256,128]{1,0:T(8,128)}, f32[256,128]{1,0:T(8,128)S(1)}, u32[]{:S(2)}) %copy-start.1) | copy-done | bytes 131096
  40.4 6.5 %shard_map.139 = bf16[8,4,1280]{2,1,0:T(4,128)(2,1)} custom-call(f32[8,32,128]{2,1,0:T(8,128)} %bitcast.6, f32[8,32,128]{2,1,0:T(8,128)} %bitcast.7, f32[16,32,128]{2,1,0:T(8,128)} %shard_map.138.new_ref, bf16[8,4,1280]{2,1,0:T(4,128)(2,1)} %patch_ref.5, bf16[1280,1280]{1,0:T(8,128)(2,1)} %w_out_ref.1, f32[1280]{0:T(1024)} %gain_ref.5, ...), custom_call_target="tpu_custom_call" | custom-call | tf_op jit(solution)/shard_map/pallas_call | solution.py:284
  (3 shorter events, 0.0 us)
Async XLA Ops:
  9.8 1.6 %collective-permute-start = (f32[256,128]{1,0:T(8,128)}, f32[256,128]{1,0:T(8,128)S(1)}, u32[]{:S(2)}, u32[]{:S(2)}) collective-permute-start(f32[256,128]{1,0:T(8,128)} %bitcast.8), channel_id=1, source_target_pairs={{0,1},{1,0},{2,3},{3,2},{4,5},{5,4},{6,7},{7,6},{8,9},{9,8},{10,11... | collective-permute-start | bytes 393224 | tf_op jit(solution)/shard_map/ppermute | solution.py:40
  12.8 6.0 %collective-permute-start.1 = (f32[256,128]{1,0:T(8,128)S(1)}, f32[256,128]{1,0:T(8,128)S(1)}, u32[]{:S(2)}, u32[]{:S(2)}) collective-permute-start(f32[256,128]{1,0:T(8,128)S(1)} %add_select_fusion.2), channel_id=1, source_target_pairs={{0,2},{1,3},{2,0},{3,1},{4,6},{5,7},{6,4},{7,5},{8,10},{9,11},{10,... | collective-permute-start | bytes 393224 | tf_op jit(solution)/shard_map/ppermute | solution.py:40
  19.3 8.3 %collective-permute-start.2 = (f32[256,128]{1,0:T(8,128)S(1)}, f32[256,128]{1,0:T(8,128)S(1)}, u32[]{:S(2)}, u32[]{:S(2)}) collective-permute-start(f32[256,128]{1,0:T(8,128)S(1)} %add_select_fusion.1), channel_id=1, source_target_pairs={{0,4},{1,5},{2,6},{3,7},{4,0},{5,1},{6,2},{7,3},{8,12},{9,13},{10,... | collective-permute-start | bytes 393224 | tf_op jit(solution)/shard_map/ppermute | solution.py:40
  28.1 6.6 %copy-start = (f32[256,128]{1,0:T(8,128)}, f32[256,128]{1,0:T(8,128)S(1)}, u32[]{:S(2)}) copy-start(f32[256,128]{1,0:T(8,128)S(1)} %add_select_fusion) | copy-start | bytes 393220
  28.1 11.6 %collective-permute-start.3 = (f32[256,128]{1,0:T(8,128)S(1)}, f32[256,128]{1,0:T(8,128)S(1)}, u32[]{:S(2)}, u32[]{:S(2)}) collective-permute-start(f32[256,128]{1,0:T(8,128)S(1)} %add_select_fusion), channel_id=1, source_target_pairs={{0,1},{1,0},{2,3},{3,2},{4,5},{5,4},{6,7},{7,6},{8,9},{9,8},{10,11... | collective-permute-start | bytes 393224 | tf_op jit(solution)/shard_map/ppermute | solution.py:40
  39.7 0.7 %copy-start.1 = (f32[256,128]{1,0:T(8,128)}, f32[256,128]{1,0:T(8,128)S(1)}, u32[]{:S(2)}) copy-start(f32[256,128]{1,0:T(8,128)S(1)} %collective-permute-done.3) | copy-start | bytes 393220
